TPU v7x, 256 devices: a whole 4x4x8 slice. The times are simulated.
256 devices in a mesh: dp: 4 (over y), expert: 64 (over z, x, core).
Axes of the slice: x: 4, y: 4, z: 8, core: 2. Of those that a mesh axis runs over, the one named last changes fastest.
Arguments:
- hidden_states: bfloat16 [1024, 4, 4096], P('expert'), may hold values from -6 to 6
- routes: int32 [1024, 4, 8], P('expert'), may hold values from 0 to 63, all different within a row; in each aligned block of 64 rows (0 to 63, 64 to 127, ..., all dimensions but the last counted through in order) at most 16 rows name the same one
- route_weight: float32 [1024, 4, 8], P('expert'), may hold values from 0.05 to 1
- finish_step: int32 [1024], P('expert'), may hold values from 1 to 4
- group_keep: int32 [64], P('expert'), may hold values from 0 to 1
- dest_slot: int32 [1024], P('expert'), may hold values from 0 to 1023, as said below
- w_gate: bfloat16 [64, 4096, 1536], P('expert', None, 'dp'), may hold values from -0.09375 to 0.09375
- w_up: bfloat16 [64, 4096, 1536], P('expert', None, 'dp'), may hold values from -0.09375 to 0.09375
- w_down: bfloat16 [64, 1536, 4096], P('expert', 'dp'), may hold values from -0.15625 to 0.15625
Outputs:
- trainer_rows: bfloat16 [1024, 4, 4096], P(('dp', 'expert'))
Inputs may be any that keep to these rules, and one draw needn't show every extreme that they name: `routes`: in the 64 row-steps of one prompt group (rows g * 16 to (g + 1) * 16 - 1, all steps), no expert is named more than 16 times, a bound that some block reaches; a row names 8 different experts at each step. dest_slot is a permutation of the slots; row r of group g = r // 16 goes to a slot (d * 64 + g) * 4 + i with 0 <= d < 4 and 0 <= i < 4.
All inputs are finite; a program needn't handle non-finite values.
Results may differ from a plain program's by a relative error of at most 0.0049.
Values may be sent and summed in bfloat16 or wider, within the bound.
No kernel may reach another device: no remote copies, remote signals or barrier semaphores. Data moves between devices by JAX's collectives and lax.ppermute only.
A program may use at most 128 MiB of HBM per device.

v0:
```python
import jax
import jax.numpy as jnp
from jax import lax
from jax.sharding import PartitionSpec as P

MOST_BASE = 16


def body(
    hidden_states, routes, route_weight, finish_step, group_keep, dest_slot, w_gate, w_up, w_down
):
    expert_count = lax.axis_size("expert")
    replica_count = lax.axis_size("dp")
    row_count, step_count, model_width = hidden_states.shape
    top_count = routes.shape[2]
    tokens = row_count * step_count
    slot_count = min(tokens, max(MOST_BASE, 2 * tokens * top_count // expert_count))
    step_ids = lax.broadcasted_iota(jnp.int32, (row_count, step_count), 1)
    live_mask = ((step_ids < finish_step[:, None]) & (group_keep[0] == 1)).reshape(tokens)
    gate_share = route_weight / jnp.sum(route_weight, axis=2, keepdims=True)
    expert_ids = lax.broadcasted_iota(jnp.int32, (1, 1, expert_count), 2)
    picked = (routes.reshape(tokens, top_count, 1) == expert_ids) & live_mask[:, None, None]
    hit_mask = jnp.sum(picked.astype(jnp.int32), axis=1)
    share_wide = jnp.broadcast_to(gate_share.reshape(tokens, top_count, 1), picked.shape)
    weight = jnp.sum(jnp.where(picked, share_wide, jnp.zeros_like(share_wide)), axis=1)
    prior_hits = jnp.cumsum(hit_mask, axis=0) - hit_mask
    slot_ids = lax.broadcasted_iota(jnp.int32, (1, 1, slot_count), 2)
    placement = (hit_mask[:, :, None] == 1) & (prior_hits[:, :, None] == slot_ids)
    weighted_place = (placement.astype(jnp.float32) * weight[:, :, None]).reshape(
        tokens, expert_count * slot_count
    )
    placement = placement.reshape(tokens, expert_count * slot_count)
    flat_inputs = hidden_states.reshape(tokens, model_width)
    outgoing = lax.dot_general(
        placement.astype(jnp.bfloat16),
        flat_inputs,
        (((0,), (0,)), ((), ())),
        preferred_element_type=jnp.float32,
    ).astype(jnp.bfloat16)
    outgoing = outgoing.reshape(expert_count, slot_count, model_width)
    arrived = lax.all_to_all(outgoing, "expert", split_axis=0, concat_axis=0, tiled=True)
    sources = arrived.shape[0]
    items = arrived.shape[1]
    flattened = arrived.reshape(sources * items, model_width)
    gate_part = jnp.dot(flattened, w_gate[0], preferred_element_type=jnp.float32)
    up_part = jnp.dot(flattened, w_up[0], preferred_element_type=jnp.float32)
    activated = (jax.nn.silu(gate_part) * up_part).astype(jnp.bfloat16)
    expert_result = jnp.dot(activated, w_down[0], preferred_element_type=jnp.float32)
    partial_out = expert_result.reshape(sources, items, model_width)
    share_rows = row_count // replica_count
    flat_device = dest_slot // share_rows
    target = flat_device // expert_count * share_rows + dest_slot % share_rows
    position_ids = lax.broadcasted_iota(jnp.int32, (replica_count * share_rows, row_count), 0)
    arrangement = (target[None, :] == position_ids).astype(jnp.float32)
    returned_rows = lax.all_to_all(partial_out, "expert", split_axis=0, concat_axis=0, tiled=True)
    combined = jnp.dot(
        weighted_place,
        returned_rows.reshape(expert_count * slot_count, model_width),
        precision=lax.Precision.HIGHEST,
        preferred_element_type=jnp.float32,
    )
    arranged = jnp.dot(
        arrangement,
        combined.reshape(row_count, step_count * model_width),
        precision=lax.Precision.HIGHEST,
        preferred_element_type=jnp.float32,
    )
    arranged = arranged.reshape(replica_count, share_rows, step_count, model_width)
    summed = lax.psum_scatter(arranged, "dp", scatter_dimension=0, tiled=True)
    return summed.reshape(share_rows, step_count, model_width).astype(jnp.bfloat16)


def solution(mesh):
    in_specs = (
        P("expert", None, None),
        P("expert", None, None),
        P("expert", None, None),
        P("expert"),
        P("expert"),
        P("expert"),
        P("expert", None, "dp"),
        P("expert", None, "dp"),
        P("expert", "dp", None),
    )
    out_specs = P(("dp", "expert"), None, None)
    return jax.shard_map(body, mesh=mesh, in_specs=in_specs, out_specs=out_specs, check_vma=False)
```

profile of v0, /device:TPU:2, one launch (start us, length us, event | category | flops | bytes accessed | tf_op | source)
XLA Modules:
  0.0 656.8 jit_solution(7036065181879656285)
XLA Ops:
  0.0 0.0 copy-start
  0.0 0.9 copy.28
  1.6 0.7 fusion.16
  2.3 0.1 and.58
  2.4 0.2 convert_reduce_fusion
  2.7 0.1 reduce_window_sum.11
  2.8 0.1 copy.30
  2.9 0.1 copy.29
  3.0 2.0 reshape.115
  4.9 0.1 fusion.11
  5.1 3.4 convolution_convert_fusion
  8.4 0.0 copy-start.3
  8.4 198.2 %all_to_all.10 = bf16[64,16,4096]{2,1,0:T(8,128)(2,1)S(1)} all-to-all(bf16[64,16,4096]{2,1,0:T(8,128)(2,1)S(1)} %bitcast.43), channel_id=1, replica_groups=mesh['dp'=4,'expert'=64] {'expert'}, dimensions={0} | all-to-all | bytes 16777216 | tf_op jit(solution)/shard_map/all_to_all | solution.py:41
  206.6 0.0 copy-done.3
  206.6 0.0 copy-start.4
  206.6 4.5 fusion.4
  211.1 0.0 copy-done.4
  211.1 4.6 multiply_convert_fusion
  215.7 0.0 copy-done
  215.7 8.1 %fusion = f32[64,16,4096]{2,1,0:T(8,128)} fusion(bf16[64,16,384]{2,1,0:T(8,128)(2,1)S(1)} %bitcast.47, bf16[1,384,4096]{2,1,0:T(8,128)(2,1)S(1)} %copy-done), kind=kOutput, calls=%fused_computation.2 | convolution fusion | flops 3221225472 | bytes 20709376 | tf_op jit(solution)/shard_map/dot_general | solution.py:48
  223.7 0.0 copy-start.2
  223.7 0.0 copy-start.6
  223.7 0.0 copy-start.5
  223.8 5.9 all-to-all-start.1
  229.7 0.0 copy-done.2
  229.7 0.1 copy.31
  229.8 0.3 select_reduce_fusion
  230.1 0.1 copy.32
  230.2 0.0 copy-done.6
  230.2 0.6 dynamic-slice
  230.8 0.0 copy-done.5
  230.8 369.1 %all-to-all-done.1 = f32[64,16,4096]{2,1,0:T(8,128)} async-done(((f32[64,16,4096]{2,1,0:T(8,128)}), f32[64,16,4096]{2,1,0:T(8,128)}, u32[]{:S(2)}, u32[]{:S(2)}) %all-to-all-start.1) | async-done | bytes 16777248 | tf_op jit(solution)/shard_map/all_to_all | solution.py:55
  599.9 0.0 copy-start.1
  599.9 14.9 %convolution_bitcast_fusion = f32[64,4096]{1,0:T(8,128)} fusion(f32[64,16,4096]{2,1,0:T(8,128)} %all-to-all-done.1, f32[64,64]{0,1:T(8,128)S(1)} %copy.32, s32[64,64]{0,1:T(8,128)S(1)} %copy.30, pred[64,64]{0,1:T(8,128)(4,1)S(1)} %copy.29), kind=kOutput, calls=%fused_computation.1 | convolution fusion | flops 3221422080 | bytes 17862656 | tf_op jit(solution)/shard_map/dot_general | solution.py:56
  614.8 2.7 reshape.118
  617.5 3.1 fusion.8
  620.6 33.8 %all-reduce.2 = bf16[4,4,4,4096]{3,1,2,0:T(4,128)(2,1)} all-reduce(f32[4,4,4,4096]{3,1,2,0:T(4,128)} %fusion.8), channel_id=2, replica_groups=mesh['dp'=4,'expert'=64] {'dp'}, use_global_device_ids=true, to_apply=%region_4.5.clone | all-reduce | flops 262144 | bytes 1572864
  654.4 1.6 fusion.15
  656.0 0.8 copy.36
  656.8 0.0 copy-done.1
  (6 shorter events, 0.1 us)
Async XLA Ops:
  0.0 215.7 %copy-start = (bf16[1,384,4096]{2,1,0:T(8,128)(2,1)S(1)}, bf16[1,384,4096]{2,1,0:T(8,128)(2,1)}, u32[]{:S(2)}) copy-start(bf16[1,384,4096]{2,1,0:T(8,128)(2,1)} %param.17) | copy-start | bytes 9437188
  8.4 198.2 %copy-start.3 = (bf16[1,4096,384]{2,1,0:T(8,128)(2,1)S(1)}, bf16[1,4096,384]{2,1,0:T(8,128)(2,1)}, u32[]{:S(2)}) copy-start(bf16[1,4096,384]{2,1,0:T(8,128)(2,1)} %param.15) | copy-start | bytes 9437188
  206.6 4.5 copy-start.4
  223.7 5.9 copy-start.2
  223.7 6.4 copy-start.6
  223.7 7.0 %copy-start.5 = (s32[16]{0:T(128)S(1)}, s32[16]{0:T(128)}, u32[]{:S(2)}) copy-start(s32[16]{0:T(128)} %param.14) | copy-start | bytes 196
  223.8 376.2 %all-to-all-start.1 = ((f32[64,16,4096]{2,1,0:T(8,128)}), f32[64,16,4096]{2,1,0:T(8,128)}, u32[]{:S(2)}, u32[]{:S(2)}) async-start(f32[64,16,4096]{2,1,0:T(8,128)} %fusion), calls=%async_computation.1 | async-start | bytes 33554432 | tf_op jit(solution)/shard_map/all_to_all | solution.py:55
  599.9 56.9 %copy-start.1 = (bf16[1,384,4096]{2,1,0:T(8,128)(2,1)S(1)}, bf16[1,384,4096]{2,1,0:T(8,128)(2,1)}, u32[]{:S(2)}) copy-start(bf16[1,384,4096]{2,1,0:T(8,128)(2,1)} %param.17) | copy-start | bytes 9437188
where the time goes:
time: 658 us; the launch traced here: 657 us
  waiting for transfers between devices  369 us (56%)
  blocking collectives  232 us (35%)
  matrix products  38.4 us (6%)
  local copies, waits for them, and re-layouts  8.99 us (1%)
    all_to_all x1, waiting for transfers between devices, body(): lax.all_to_all(partial_out, 'expert', split_axis=0, concat_axis=0, tiled=...  369 us
    all_to_all x1, blocking collectives, body(): lax.all_to_all(outgoing, 'expert', split_axis=0, concat_axis=0, tiled=True)  198 us
    unnamed x1, blocking collectives  33.8 us
    dot_general x1, matrix products, body(): jnp.dot(weighted_place, returned_rows.reshape(expert_count * slot_count,...  14.9 us
  transfers between devices with their start and end apart: 1, of which 1 were waited for; matrix products, arithmetic and copies ran while one was open for 0% of the time, Pallas kernels for 0%

commit v1 on v0

--- a/solution.py
+++ b/solution.py
@@ -11,10 +11,13 @@
 ):
     expert_count = lax.axis_size("expert")
     replica_count = lax.axis_size("dp")
+    replica = lax.axis_index("dp")
     row_count, step_count, model_width = hidden_states.shape
     top_count = routes.shape[2]
     tokens = row_count * step_count
     slot_count = min(tokens, max(MOST_BASE, 2 * tokens * top_count // expert_count))
+    slot_count = -(-slot_count // replica_count) * replica_count
+    part = slot_count // replica_count
     step_ids = lax.broadcasted_iota(jnp.int32, (row_count, step_count), 1)
     live_mask = ((step_ids < finish_step[:, None]) & (group_keep[0] == 1)).reshape(tokens)
     gate_share = route_weight / jnp.sum(route_weight, axis=2, keepdims=True)
@@ -24,12 +27,12 @@
     share_wide = jnp.broadcast_to(gate_share.reshape(tokens, top_count, 1), picked.shape)
     weight = jnp.sum(jnp.where(picked, share_wide, jnp.zeros_like(share_wide)), axis=1)
     prior_hits = jnp.cumsum(hit_mask, axis=0) - hit_mask
-    slot_ids = lax.broadcasted_iota(jnp.int32, (1, 1, slot_count), 2)
+    slot_ids = replica * part + lax.broadcasted_iota(jnp.int32, (1, 1, part), 2)
     placement = (hit_mask[:, :, None] == 1) & (prior_hits[:, :, None] == slot_ids)
     weighted_place = (placement.astype(jnp.float32) * weight[:, :, None]).reshape(
-        tokens, expert_count * slot_count
+        tokens, expert_count * part
     )
-    placement = placement.reshape(tokens, expert_count * slot_count)
+    placement = placement.reshape(tokens, expert_count * part)
     flat_inputs = hidden_states.reshape(tokens, model_width)
     outgoing = lax.dot_general(
         placement.astype(jnp.bfloat16),
@@ -37,25 +40,28 @@
         (((0,), (0,)), ((), ())),
         preferred_element_type=jnp.float32,
     ).astype(jnp.bfloat16)
-    outgoing = outgoing.reshape(expert_count, slot_count, model_width)
+    outgoing = outgoing.reshape(expert_count, part, model_width)
     arrived = lax.all_to_all(outgoing, "expert", split_axis=0, concat_axis=0, tiled=True)
-    sources = arrived.shape[0]
-    items = arrived.shape[1]
-    flattened = arrived.reshape(sources * items, model_width)
+    gathered = lax.all_gather(arrived, "dp", axis=0, tiled=False)
+    flattened = gathered.reshape(replica_count * expert_count * part, model_width)
     gate_part = jnp.dot(flattened, w_gate[0], preferred_element_type=jnp.float32)
     up_part = jnp.dot(flattened, w_up[0], preferred_element_type=jnp.float32)
     activated = (jax.nn.silu(gate_part) * up_part).astype(jnp.bfloat16)
     expert_result = jnp.dot(activated, w_down[0], preferred_element_type=jnp.float32)
-    partial_out = expert_result.reshape(sources, items, model_width)
+    partial_out = expert_result.reshape(replica_count, expert_count, part, model_width)
+    reduced = lax.psum_scatter(
+        partial_out.astype(jnp.bfloat16), "dp", scatter_dimension=0, tiled=True
+    )
+    reduced = reduced.reshape(expert_count, part, model_width)
+    returned_rows = lax.all_to_all(reduced, "expert", split_axis=0, concat_axis=0, tiled=True)
     share_rows = row_count // replica_count
     flat_device = dest_slot // share_rows
     target = flat_device // expert_count * share_rows + dest_slot % share_rows
     position_ids = lax.broadcasted_iota(jnp.int32, (replica_count * share_rows, row_count), 0)
     arrangement = (target[None, :] == position_ids).astype(jnp.float32)
-    returned_rows = lax.all_to_all(partial_out, "expert", split_axis=0, concat_axis=0, tiled=True)
     combined = jnp.dot(
         weighted_place,
-        returned_rows.reshape(expert_count * slot_count, model_width),
+        returned_rows.reshape(expert_count * part, model_width).astype(jnp.float32),
         precision=lax.Precision.HIGHEST,
         preferred_element_type=jnp.float32,
     )

time: 658 us -> 408 us (0.62)
  waiting for transfers between devices: 369 us -> 217 us
  blocking collectives: 232 us -> 94.7 us
  local copies, waits for them, and re-layouts: 8.99 us -> 32.5 us
  between operations: 0.8 us -> 14.2 us
    all_to_all x1, waiting for transfers between devices: 369 us -> 50.6 us  [body(): lax.all_to_all(reduced, 'expert', split_axis=0, concat_axis=0, tiled=True)]
    all_to_all x1, blocking collectives: 198 us -> 63.4 us  [body(): lax.all_to_all(outgoing, 'expert', split_axis=0, concat_axis=0, tiled=True)]
    reduce_scatter x0 -> x1, waiting for transfers between devices: none -> 84.2 us  [body(): lax.psum_scatter(partial_out.astype(jnp.bfloat16), 'dp', scatter_dimensio...]
    all_gather x0 -> x1, waiting for transfers between devices: none -> 82.2 us  [body(): gathered = lax.all_gather(arrived, 'dp', axis=0, tiled=False)]
    reshape x0 -> x3, local copies, waits for them, and re-layouts: none -> 21.1 us  [the longest x1 12.5 us: body(): gathered.reshape(replica_count * expert_count * part, model_width)]
    dot_general x1, matrix products: 14.9 us -> 5.82 us  [body(): jnp.dot(weighted_place, returned_rows.reshape(expert_count * part, model_...]
  transfers between devices with their start and end apart: 1 -> 3, of which waited for: 1 -> 3; matrix products, arithmetic and copies ran while one was open for 0% -> 0% of each run, Pallas kernels for 0% -> 0%
where the time goes in v1:
time: 408 us; the launch traced here: 406 us
  waiting for transfers between devices  217 us (53%)
  blocking collectives  94.7 us (23%)
  matrix products  33.2 us (8%)
  local copies, waits for them, and re-layouts  32.5 us (8%)
  between operations  14.2 us (3%)
  starting transfers between devices  11.1 us (3%)
    reduce_scatter x1, waiting for transfers between devices, body(): lax.psum_scatter(partial_out.astype(jnp.bfloat16), 'dp', scatter_dimensio...  84.2 us
    all_gather x1, waiting for transfers between devices, body(): gathered = lax.all_gather(arrived, 'dp', axis=0, tiled=False)  82.2 us
    all_to_all x1, blocking collectives, body(): lax.all_to_all(outgoing, 'expert', split_axis=0, concat_axis=0, tiled=True)  63.4 us
    all_to_all x1, waiting for transfers between devices, body(): lax.all_to_all(reduced, 'expert', split_axis=0, concat_axis=0, tiled=True)  50.6 us
    unnamed x1, blocking collectives  31.3 us
    reshape x1, local copies, waits for them, and re-layouts, body(): gathered.reshape(replica_count * expert_count * part, model_width)  12.5 us
    all_to_all x1, starting transfers between devices, body(): lax.all_to_all(reduced, 'expert', split_axis=0, concat_axis=0, tiled=True)  11 us
  transfers between devices with their start and end apart: 3, of which 3 were waited for; matrix products, arithmetic and copies ran while one was open for 0% of the time, Pallas kernels for 0%

profile of v1, /device:TPU:2, one launch (start us, length us, event | category | flops | bytes accessed | tf_op | source)
XLA Modules:
  0.0 405.6 jit_solution(14676518299737943535)
XLA Ops:
  6.5 0.0 copy-start
  6.5 0.0 all-gather.3.cloned.1.call-start
  6.5 0.9 copy.30
  8.2 0.7 fusion.14
  8.9 0.1 and.59
  9.0 0.2 convert_reduce_fusion
  9.2 0.1 reduce_window_sum.11
  9.3 0.1 copy.32
  9.4 0.1 copy.31
  9.5 0.7 reduce_sum.28
  10.3 0.7 broadcast_divide_fusion
  11.0 0.1 copy.33
  11.1 0.3 select_reduce_fusion
  11.3 0.1 copy.34
  11.4 2.0 reshape.123
  13.4 0.1 broadcast_select_fusion
  13.5 3.1 convolution_convert_fusion.1
  16.6 4.1 %reshape.124 = bf16[64,4,4096]{2,1,0:T(4,128)(2,1)} reshape(bf16[256,4096]{1,0:T(8,128)(2,1)} %convolution_convert_fusion.1) | data formatting | bytes 4194304 | tf_op jit(solution)/shard_map/reshape | solution.py:43
  20.7 63.4 %all_to_all.10 = bf16[64,4,4096]{2,1,0:T(4,128)(2,1)} all-to-all(bf16[64,4,4096]{2,1,0:T(4,128)(2,1)} %reshape.124), channel_id=1, replica_groups=mesh['dp'=4,'expert'=64] {'expert'}, dimensions={0} | all-to-all | bytes 4194304 | tf_op jit(solution)/shard_map/all_to_all | solution.py:44
  84.1 0.0 all-gather.3.cloned.1.call-update
  84.1 0.0 reduce-scatter.2.cloned.1.call-start
  84.2 82.2 %all-gather.3.cloned.1.call-done = bf16[256,4,4096]{2,1,0:T(4,128)(2,1)} async-done(((bf16[64,4,4096]{2,1,0:T(4,128)(2,1)}), bf16[256,4,4096]{2,1,0:T(4,128)(2,1)}) %all-gather.3.cloned.1.call-update) | async-done | bytes 8388624 | tf_op jit(solution)/shard_map/all_gather | solution.py:45
  166.4 12.5 %reshape.125 = bf16[1024,4096]{1,0:T(8,128)(2,1)} reshape(bf16[256,4,4096]{2,1,0:T(4,128)(2,1)} %all-gather.3.cloned.1.call-done) | data formatting | bytes 16777216 | tf_op jit(solution)/shard_map/reshape | solution.py:46
  178.9 0.0 copy-start.1
  178.9 0.0 copy-start.2
  178.9 8.0 %fusion.3 = f32[1024,384]{1,0:T(8,128)S(1)} fusion(bf16[1024,4096]{1,0:T(8,128)(2,1)} %reshape.125, bf16[1,4096,384]{2,1,0:T(8,128)(2,1)} %param.15), kind=kOutput, calls=%fused_computation.6 | convolution fusion | flops 3221225472 | bytes 13107200 | tf_op jit(solution)/shard_map/dot_general | solution.py:47
  186.9 0.0 copy-done.1
  186.9 0.0 copy-done.2
  186.9 5.4 %multiply_convert_fusion = bf16[1024,384]{1,0:T(8,128)(2,1)} fusion(f32[1024,384]{1,0:T(8,128)S(1)} %fusion.3, bf16[1024,4096]{1,0:T(8,128)(2,1)S(1)} %copy-done.1, bf16[1,4096,384]{2,1,0:T(8,128)(2,1)S(1)} %copy-done.2), kind=kOutput, calls=%fused_computation.9 | convolution fusion | flops 3223584768 | bytes 13893632 | tf_op jit(solution)/shard_map/dot_general | solution.py:48
  192.3 2.4 dot_general.27
  194.7 0.0 copy-done
  194.7 7.8 %convolution_convert_fusion = bf16[4,64,4,4096]{3,1,2,0:T(8,128)(2,1)} fusion(bf16[1,384,4096]{2,1,0:T(8,128)(2,1)S(1)} %copy-done, bf16[4,64,4,384]{3,2,1,0:T(4,128)(2,1)} %dot_general.27), kind=kOutput, calls=%fused_computation | convolution fusion | flops 3225419776 | bytes 12320768 | tf_op jit(solution)/shard_map/dot_general | solution.py:50
  202.5 0.0 reduce-scatter.2.cloned.1.call-update
  202.5 84.2 %reduce-scatter.2.cloned.1.call-done = bf16[1,64,4,4096]{3,1,2,0:T(8,128)(2,1)} async-done(((bf16[4,64,4,4096]{3,1,2,0:T(8,128)(2,1)}), bf16[1,64,4,4096]{3,1,2,0:T(8,128)(2,1)}) %reduce-scatter.2.cloned.1.call-update) | async-done | bytes 2097168 | tf_op jit(solution)/shard_map/reduce_scatter | solution.py:52
  286.8 4.5 %copy.36 = bf16[64,4,4096]{2,1,0:T(4,128)(2,1)} copy(bf16[64,4,4096]{2,0,1:T(8,128)(2,1)} %bitcast.43) | data formatting | bytes 4194304 | tf_op jit(solution)/shard_map/reshape | solution.py:55
  291.3 0.0 copy-start.4
  291.3 0.0 copy-start.3
  291.3 11.0 %all-to-all-start.1 = ((bf16[64,4,4096]{2,1,0:T(4,128)(2,1)}), bf16[64,4,4096]{2,1,0:T(4,128)(2,1)}, u32[]{:S(2)}, u32[]{:S(2)}) async-start(bf16[64,4,4096]{2,1,0:T(4,128)(2,1)} %copy.36), calls=%async_computation.2 | async-start | bytes 4194304 | tf_op jit(solution)/shard_map/all_to_all | solution.py:56
  302.3 0.0 copy-done.4
  302.3 0.6 dynamic-slice
  302.9 0.0 copy-done.3
  302.9 50.6 %all-to-all-done.1 = bf16[64,4,4096]{2,1,0:T(4,128)(2,1)} async-done(((bf16[64,4,4096]{2,1,0:T(4,128)(2,1)}), bf16[64,4,4096]{2,1,0:T(4,128)(2,1)}, u32[]{:S(2)}, u32[]{:S(2)}) %all-to-all-start.1) | async-done | bytes 2097184 | tf_op jit(solution)/shard_map/all_to_all | solution.py:56
  353.5 5.8 %convolution_bitcast_fusion = f32[64,4096]{1,0:T(8,128)} fusion(bf16[64,4,4096]{2,1,0:T(4,128)(2,1)} %all-to-all-done.1, f32[64,64,4]{0,2,1:T(4,128)S(1)} %get-tuple-element.5), kind=kOutput, calls=%fused_computation.2 | convolution fusion | flops 805306368 | bytes 3211264 | tf_op jit(solution)/shard_map/dot_general | solution.py:62
  359.3 2.7 reshape.127
  362.0 3.1 fusion.8
  365.1 31.3 %all-reduce.2 = bf16[4,4,4,4096]{3,1,2,0:T(4,128)(2,1)} all-reduce(f32[4,4,4,4096]{3,1,2,0:T(4,128)} %fusion.8), channel_id=4, replica_groups=mesh['dp'=4,'expert'=64] {'dp'}, use_global_device_ids=true, to_apply=%region_5.6.clone | all-reduce | flops 262144 | bytes 1572864
  396.4 1.6 fusion.12
  398.0 0.8 copy.40
  (5 shorter events, 0.0 us)
Async XLA Ops:
  6.5 188.2 %copy-start = (bf16[1,384,4096]{2,1,0:T(8,128)(2,1)S(1)}, bf16[1,384,4096]{2,1,0:T(8,128)(2,1)}, u32[]{:S(2)}) copy-start(bf16[1,384,4096]{2,1,0:T(8,128)(2,1)} %param.17) | copy-start | bytes 9437188
  6.5 159.8 %all-gather.3.cloned.1.call-start = ((), (), s32[]{:S(2)}) async-start(), calls=%async_computation.4 | async-start | bytes 10485760 | tf_op jit(solution)/shard_map/all_gather | solution.py:45
  84.1 202.6 %reduce-scatter.2.cloned.1.call-start = ((), (), s32[]{:S(2)}) async-start(), calls=%async_computation.3 | async-start | bytes 10485760 | tf_op jit(solution)/shard_map/reduce_scatter | solution.py:52
  178.9 8.0 %copy-start.1 = (bf16[1024,4096]{1,0:T(8,128)(2,1)S(1)}, bf16[1024,4096]{1,0:T(8,128)(2,1)}, u32[]{:S(2)}) copy-start(bf16[1024,4096]{1,0:T(8,128)(2,1)} %reshape.125) | copy-start | bytes 25165828
  178.9 8.0 %copy-start.2 = (bf16[1,4096,384]{2,1,0:T(8,128)(2,1)S(1)}, bf16[1,4096,384]{2,1,0:T(8,128)(2,1)}, u32[]{:S(2)}) copy-start(bf16[1,4096,384]{2,1,0:T(8,128)(2,1)} %param.16) | copy-start | bytes 9437188
  291.3 11.1 %copy-start.4 = (u32[256]{0:T(256)S(1)}, u32[256]{0:T(256)}, u32[]{:S(2)}) copy-start(u32[256]{0:T(256)} %constant.73) | copy-start | bytes 3076
  291.3 11.7 %copy-start.3 = (s32[16]{0:T(128)S(1)}, s32[16]{0:T(128)}, u32[]{:S(2)}) copy-start(s32[16]{0:T(128)} %param.14) | copy-start | bytes 196
  291.3 62.2 %all-to-all-start.1 = ((bf16[64,4,4096]{2,1,0:T(4,128)(2,1)}), bf16[64,4,4096]{2,1,0:T(4,128)(2,1)}, u32[]{:S(2)}, u32[]{:S(2)}) async-start(bf16[64,4,4096]{2,1,0:T(4,128)(2,1)} %copy.36), calls=%async_computation.2 | async-start | bytes 4194304 | tf_op jit(solution)/shard_map/all_to_all | solution.py:56
Sparse Core Ops, SparseCore 0:
  84.3 82.0 all-gather.2
  202.7 84.0 reduce-scatter.1

commit v2 on v1

v2 whole, which is shorter than its diff:
```python
import jax
import jax.numpy as jnp
from jax import lax
from jax.sharding import PartitionSpec as P

MOST_BASE = 16


def body(
    hidden_states, routes, route_weight, finish_step, group_keep, dest_slot, w_gate, w_up, w_down
):
    expert_count = lax.axis_size("expert")
    replica_count = lax.axis_size("dp")
    replica = lax.axis_index("dp")
    row_count, step_count, model_width = hidden_states.shape
    top_count = routes.shape[2]
    tokens = row_count * step_count
    slot_count = min(tokens, max(MOST_BASE, 2 * tokens * top_count // expert_count))
    slot_count = -(-slot_count // replica_count) * replica_count
    part = slot_count // replica_count
    step_ids = lax.broadcasted_iota(jnp.int32, (row_count, step_count), 1)
    live_mask = ((step_ids < finish_step[:, None]) & (group_keep[0] == 1)).reshape(tokens)
    gate_share = route_weight / jnp.sum(route_weight, axis=2, keepdims=True)
    expert_ids = lax.broadcasted_iota(jnp.int32, (1, 1, expert_count), 2)
    picked = (routes.reshape(tokens, top_count, 1) == expert_ids) & live_mask[:, None, None]
    hit_mask = jnp.sum(picked.astype(jnp.int32), axis=1)
    share_wide = jnp.broadcast_to(gate_share.reshape(tokens, top_count, 1), picked.shape)
    weight = jnp.sum(jnp.where(picked, share_wide, jnp.zeros_like(share_wide)), axis=1)
    prior_hits = jnp.cumsum(hit_mask, axis=0) - hit_mask
    flat_inputs = hidden_states.reshape(tokens, model_width)
    chunks = 2 if part % 2 == 0 else 1
    sub = part // chunks
    combined = jnp.zeros((tokens, model_width), jnp.float32)
    for chunk in range(chunks):
        first = replica * part + chunk * sub
        slot_ids = first + lax.broadcasted_iota(jnp.int32, (1, 1, sub), 2)
        placement = (hit_mask[:, :, None] == 1) & (prior_hits[:, :, None] == slot_ids)
        weighted_place = (placement.astype(jnp.float32) * weight[:, :, None]).reshape(
            tokens, expert_count * sub
        )
        placement = placement.reshape(tokens, expert_count * sub)
        outgoing = lax.dot_general(
            placement.astype(jnp.bfloat16),
            flat_inputs,
            (((0,), (0,)), ((), ())),
            preferred_element_type=jnp.float32,
        ).astype(jnp.bfloat16)
        arrived = lax.all_to_all(outgoing, "expert", split_axis=0, concat_axis=0, tiled=True)
        gathered = lax.all_gather(arrived, "dp", axis=0, tiled=True)
        gate_part = jnp.dot(gathered, w_gate[0], preferred_element_type=jnp.float32)
        up_part = jnp.dot(gathered, w_up[0], preferred_element_type=jnp.float32)
        activated = (jax.nn.silu(gate_part) * up_part).astype(jnp.bfloat16)
        expert_result = jnp.dot(activated, w_down[0], preferred_element_type=jnp.float32)
        reduced = lax.psum_scatter(
            expert_result.astype(jnp.bfloat16), "dp", scatter_dimension=0, tiled=True
        )
        returned_rows = lax.all_to_all(reduced, "expert", split_axis=0, concat_axis=0, tiled=True)
        combined = combined + jnp.dot(
            weighted_place,
            returned_rows.astype(jnp.float32),
            precision=lax.Precision.HIGHEST,
            preferred_element_type=jnp.float32,
        )
    share_rows = row_count // replica_count
    flat_device = dest_slot // share_rows
    target = flat_device // expert_count * share_rows + dest_slot % share_rows
    position_ids = lax.broadcasted_iota(jnp.int32, (replica_count * share_rows, row_count), 0)
    arrangement = (target[None, :] == position_ids).astype(jnp.float32)
    arranged = jnp.dot(
        arrangement,
        combined.reshape(row_count, step_count * model_width),
        precision=lax.Precision.HIGHEST,
        preferred_element_type=jnp.float32,
    )
    arranged = arranged.reshape(replica_count, share_rows, step_count, model_width)
    summed = lax.psum_scatter(arranged, "dp", scatter_dimension=0, tiled=True)
    summed = summed.reshape(share_rows, step_count, model_width)
    live_rows = live_mask.reshape(row_count, step_count).astype(jnp.float32)
    live_arranged = jnp.dot(arrangement, live_rows, precision=lax.Precision.HIGHEST)
    live_mine = lax.dynamic_slice_in_dim(live_arranged, replica * share_rows, share_rows, 0)
    summed = summed * live_mine[:, :, None]
    return summed.astype(jnp.bfloat16)


def solution(mesh):
    in_specs = (
        P("expert", None, None),
        P("expert", None, None),
        P("expert", None, None),
        P("expert"),
        P("expert"),
        P("expert"),
        P("expert", None, "dp"),
        P("expert", None, "dp"),
        P("expert", "dp", None),
    )
    out_specs = P(("dp", "expert"), None, None)
    return jax.shard_map(body, mesh=mesh, in_specs=in_specs, out_specs=out_specs, check_vma=False)
```

time: 408 us -> 375 us (0.919)
  waiting for transfers between devices: 217 us -> 186 us
  blocking collectives: 94.7 us -> 75.5 us
  matrix products: 33.2 us -> 48.5 us
  starting transfers between devices: 11.1 us -> 22.2 us
  local copies, waits for them, and re-layouts: 32.5 us -> 22.1 us
    unnamed x2 -> x6, waiting for transfers between devices: 0.03 us -> 45.2 us
    all_gather x1 -> x2, waiting for transfers between devices: 82.2 us -> 42.3 us  [body(): gathered = lax.all_gather(arrived, 'dp', axis=0, tiled=True)]
    unnamed x1 -> x0, blocking collectives: 31.3 us -> none
    all_to_all x1 -> x2, waiting for transfers between devices: 50.6 us -> 24.5 us  [body(): lax.all_to_all(reduced, 'expert', split_axis=0, concat_axis=0, tiled=True)]
    reshape x3 -> x0, local copies, waits for them, and re-layouts: 21.1 us -> none  [the longest x1 12.5 us: body(): gathered.reshape(replica_count * expert_count * part, model_width)]
    all_to_all x0 -> x6, local copies, waits for them, and re-layouts: none -> 14.6 us  [the longest x4 9.57 us: body(): lax.all_to_all(outgoing, 'expert', split_axis=0, concat_axis=0, tiled=True)]
    all_to_all x1 -> x2, blocking collectives: 63.4 us -> 75.5 us  [body(): lax.all_to_all(outgoing, 'expert', split_axis=0, concat_axis=0, tiled=True)]
    dot_general x1 -> x2, matrix products: 7.78 us -> 19.5 us  [body(): jnp.dot(activated, w_down[0], preferred_element_type=jnp.float32)]
  transfers between devices with their start and end apart: 3 -> 7, of which waited for: 3 -> 6; matrix products, arithmetic and copies ran while one was open for 0% -> 11% of each run, Pallas kernels for 0% -> 0%
where the time goes in v2:
time: 375 us; the launch traced here: 374 us
  waiting for transfers between devices  186 us (50%)
  blocking collectives  75.5 us (20%)
  matrix products  48.5 us (13%)
  starting transfers between devices  22.2 us (6%)
  local copies, waits for them, and re-layouts  22.1 us (6%)
  between operations  14.1 us (4%)
  other arithmetic  4.89 us (1%)
    all_to_all x2, blocking collectives, body(): lax.all_to_all(outgoing, 'expert', split_axis=0, concat_axis=0, tiled=True)  75.5 us
    reduce_scatter x2, waiting for transfers between devices, body(): lax.psum_scatter(expert_result.astype(jnp.bfloat16), 'dp', scatter_dimens...  74.5 us
    unnamed x6, waiting for transfers between devices  45.2 us
    all_gather x2, waiting for transfers between devices, body(): gathered = lax.all_gather(arrived, 'dp', axis=0, tiled=True)  42.3 us
    all_to_all x2, waiting for transfers between devices, body(): lax.all_to_all(reduced, 'expert', split_axis=0, concat_axis=0, tiled=True)  24.5 us
    all_to_all x2, starting transfers between devices, body(): lax.all_to_all(reduced, 'expert', split_axis=0, concat_axis=0, tiled=True)  21.6 us
    dot_general x2, matrix products, body(): jnp.dot(activated, w_down[0], preferred_element_type=jnp.float32)  19.5 us
    dot_general x2, matrix products, body(): gate_part = jnp.dot(gathered, w_gate[0], preferred_element_type=jnp.float32)  12.8 us
  transfers between devices with their start and end apart: 7, of which 6 were waited for; matrix products, arithmetic and copies ran while one was open for 11% of the time, Pallas kernels for 0%

profile of v2, /device:TPU:2, one launch (start us, length us, event | category | flops | bytes accessed | tf_op | source)
XLA Modules:
  0.0 373.6 jit_solution(5819347377661006592)
XLA Ops:
  7.3 0.9 fusion.38
  8.2 0.1 and.75
  8.3 0.8 copy.36
  9.1 0.2 convert_reduce_fusion
  9.4 0.1 reduce_window_sum.11
  9.5 0.1 copy.38
  9.6 0.1 copy.37
  9.7 0.7 reduce_sum.28
  10.4 0.7 broadcast_divide_fusion
  11.1 0.1 copy.39
  11.2 0.3 select_reduce_fusion
  11.5 0.1 copy.40
  11.6 0.2 broadcast_select_fusion
  11.8 2.0 reshape.164
  13.8 2.5 convolution_convert_fusion.3
  16.3 2.5 all_to_all.28
  18.8 40.9 %all_to_all.42 = bf16[64,2,4096]{2,1,0:T(2,128)(2,1)} all-to-all(bf16[64,2,4096]{2,1,0:T(2,128)(2,1)} %all_to_all.28), channel_id=1, replica_groups=mesh['dp'=4,'expert'=64] {'expert'}, dimensions={0} | all-to-all | bytes 2097152 | tf_op jit(solution)/shard_map/all_to_all | solution.py:48
  59.7 2.3 all_to_all.30
  62.1 2.4 convolution_convert_fusion.2
  64.6 2.5 all_to_all.33
  67.1 34.6 %all_to_all.43 = bf16[64,2,4096]{2,1,0:T(2,128)(2,1)} all-to-all(bf16[64,2,4096]{2,1,0:T(2,128)(2,1)} %all_to_all.33), channel_id=1, replica_groups=mesh['dp'=4,'expert'=64] {'expert'}, dimensions={0} | all-to-all | bytes 2097152 | tf_op jit(solution)/shard_map/all_to_all | solution.py:48
  101.6 2.2 all_to_all.35
  103.9 0.0 reduce-scatter.3.cloned.1.call-start
  103.9 5.7 %all-gather.3.cloned.1.call-done = bf16[512,4096]{1,0:T(8,128)(2,1)} async-done(((bf16[128,4096]{1,0:T(8,128)(2,1)}), bf16[512,4096]{1,0:T(8,128)(2,1)}) %all-gather.3.cloned.1.call-update) | async-done | bytes 4194320 | tf_op jit(solution)/shard_map/all_gather | solution.py:49
  109.6 6.4 %fusion.9 = f32[512,384]{1,0:T(8,128)} fusion(bf16[512,4096]{1,0:T(8,128)(2,1)} %all-gather.3.cloned.1.call-done, bf16[1,4096,384]{2,1,0:T(8,128)(2,1)} %param.15), kind=kOutput, calls=%fused_computation.15 | convolution fusion | flops 1610612736 | bytes 8126464 | tf_op jit(solution)/shard_map/dot_general | solution.py:50
  116.0 9.7 %convolution_convert_fusion.1 = bf16[512,4096]{1,0:T(8,128)(2,1)} fusion(bf16[1,384,4096]{2,1,0:T(8,128)(2,1)S(1)} %copy-done, bf16[512,4096]{1,0:T(8,128)(2,1)} %all-gather.3.cloned.1.call-done, bf16[1,4096,384]{2,1,0:T(8,128)(2,1)} %param.16, f32[512,384]{1,0:T(8,128)} %fusion.9), kind=kOutput, calls=%fused_computation.1 | convolution fusion | flops 3224502272 | bytes 15466496 | tf_op jit(solution)/shard_map/dot_general | solution.py:53
  125.8 0.2 reduce-scatter.5.cloned.1.call-start
  126.0 36.6 %all-gather.5.cloned.1.call-done = bf16[512,4096]{1,0:T(8,128)(2,1)} async-done(((bf16[128,4096]{1,0:T(8,128)(2,1)}), bf16[512,4096]{1,0:T(8,128)(2,1)}) %all-gather.5.cloned.1.call-update) | async-done | bytes 4194320 | tf_op jit(solution)/shard_map/all_gather | solution.py:49
  162.6 6.4 %fusion.7 = f32[512,384]{1,0:T(8,128)} fusion(bf16[512,4096]{1,0:T(8,128)(2,1)} %all-gather.5.cloned.1.call-done, bf16[1,4096,384]{2,1,0:T(8,128)(2,1)} %param.15), kind=kOutput, calls=%fused_computation.13 | convolution fusion | flops 1610612736 | bytes 8126464 | tf_op jit(solution)/shard_map/dot_general | solution.py:50
  169.0 9.7 %convolution_convert_fusion = bf16[512,4096]{1,0:T(8,128)(2,1)} fusion(bf16[1,384,4096]{2,1,0:T(8,128)(2,1)S(1)} %copy-done, bf16[512,4096]{1,0:T(8,128)(2,1)} %all-gather.5.cloned.1.call-done, bf16[1,4096,384]{2,1,0:T(8,128)(2,1)} %param.16, f32[512,384]{1,0:T(8,128)} %fusion.7), kind=kOutput, calls=%fused_computation | convolution fusion | flops 3224502272 | bytes 15466496 | tf_op jit(solution)/shard_map/dot_general | solution.py:53
  178.8 36.2 %reduce-scatter.3.cloned.1.call-done = bf16[128,4096]{1,0:T(8,128)(2,1)} async-done(((bf16[512,4096]{1,0:T(8,128)(2,1)}), bf16[128,4096]{1,0:T(8,128)(2,1)}) %reduce-scatter.3.cloned.1.call-update) | async-done | bytes 1048592 | tf_op jit(solution)/shard_map/reduce_scatter | solution.py:54
  214.9 2.5 all_to_all.31
  217.5 10.9 %all-to-all-start.1 = ((bf16[64,2,4096]{2,1,0:T(2,128)(2,1)}), bf16[64,2,4096]{2,1,0:T(2,128)(2,1)}, u32[]{:S(2)}, u32[]{:S(2)}) async-start(bf16[64,2,4096]{2,1,0:T(2,128)(2,1)} %all_to_all.31), calls=%async_computation.2 | async-start | bytes 2097152 | tf_op jit(solution)/shard_map/all_to_all | solution.py:57
  228.3 38.3 %reduce-scatter.5.cloned.1.call-done = bf16[128,4096]{1,0:T(8,128)(2,1)} async-done(((bf16[512,4096]{1,0:T(8,128)(2,1)}), bf16[128,4096]{1,0:T(8,128)(2,1)}) %reduce-scatter.5.cloned.1.call-update) | async-done | bytes 1048592 | tf_op jit(solution)/shard_map/reduce_scatter | solution.py:54
  266.7 2.5 all_to_all.36
  269.2 10.7 %all-to-all-start.3 = ((bf16[64,2,4096]{2,1,0:T(2,128)(2,1)}), bf16[64,2,4096]{2,1,0:T(2,128)(2,1)}, u32[]{:S(2)}, u32[]{:S(2)}) async-start(bf16[64,2,4096]{2,1,0:T(2,128)(2,1)} %all_to_all.36), calls=%async_computation.5 | async-start | bytes 2097152 | tf_op jit(solution)/shard_map/all_to_all | solution.py:57
  279.9 0.3 all-reduce.3.cloned.1.call-start
  280.3 3.9 %convolution_bitcast_fusion.1 = f32[64,4096]{1,0:T(8,128)} fusion(bf16[64,2,4096]{2,1,0:T(2,128)(2,1)} %all-to-all-done.1, f32[64,64,2]{0,2,1:T(2,128)S(1)} %get-tuple-element.9), kind=kOutput, calls=%fused_computation.6 | convolution fusion | flops 402653184 | bytes 2129920 | tf_op jit(solution)/shard_map/dot_general | solution.py:58
  284.1 24.5 %all-to-all-done.3 = bf16[64,2,4096]{2,1,0:T(2,128)(2,1)} async-done(((bf16[64,2,4096]{2,1,0:T(2,128)(2,1)}), bf16[64,2,4096]{2,1,0:T(2,128)(2,1)}, u32[]{:S(2)}, u32[]{:S(2)}) %all-to-all-start.3) | async-done | bytes 1048608 | tf_op jit(solution)/shard_map/all_to_all | solution.py:57
  308.7 4.2 %fusion = f32[64,4096]{1,0:T(8,128)} fusion(f32[64,4096]{1,0:T(8,128)} %convolution_bitcast_fusion.1, bf16[64,2,4096]{2,1,0:T(2,128)(2,1)} %all-to-all-done.3, f32[64,64,2]{0,2,1:T(2,128)S(1)} %get-tuple-element.5), kind=kOutput, calls=%fused_computation.5 | convolution fusion | flops 402915328 | bytes 3178496 | tf_op jit(solution)/shard_map/dot_general | solution.py:58
  312.9 2.7 reshape.165
  315.5 3.1 fusion.23
  318.6 0.2 fusion.39
  318.8 0.1 copy.46
  318.9 0.6 dynamic-slice
  319.5 45.1 %all-reduce.3.cloned.1.call-done = f32[4,4,4,4096]{3,1,2,0:T(4,128)} async-done(((f32[4,4,4,4096]{3,1,2,0:T(4,128)}), f32[4,4,4,4096]{3,1,2,0:T(4,128)}) %all-reduce.3.cloned.1.call-update) | async-done | bytes 1048592
  364.6 1.7 fusion.34
  366.3 0.8 copy.47
  (24 shorter events, 0.3 us)
Async XLA Ops:
  6.5 109.5 %copy-start = (bf16[1,384,4096]{2,1,0:T(8,128)(2,1)S(1)}, bf16[1,384,4096]{2,1,0:T(8,128)(2,1)}, u32[]{:S(2)}) copy-start(bf16[1,384,4096]{2,1,0:T(8,128)(2,1)} %param.17) | copy-start | bytes 9437188
  6.5 103.1 %all-gather.3.cloned.1.call-start = ((), (), s32[]{:S(2)}) async-start(), calls=%async_computation.6 | async-start | bytes 5242880 | tf_op jit(solution)/shard_map/all_gather | solution.py:49
  62.0 100.6 %all-gather.5.cloned.1.call-start = ((), (), s32[]{:S(2)}) async-start(), calls=%async_computation.8 | async-start | bytes 5242880 | tf_op jit(solution)/shard_map/all_gather | solution.py:49
  103.9 111.0 %reduce-scatter.3.cloned.1.call-start = ((), (), s32[]{:S(2)}) async-start(), calls=%async_computation.7 | async-start | bytes 5242880 | tf_op jit(solution)/shard_map/reduce_scatter | solution.py:54
  125.8 140.9 %reduce-scatter.5.cloned.1.call-start = ((), (), s32[]{:S(2)}) async-start(), calls=%async_computation.9 | async-start | bytes 5242880 | tf_op jit(solution)/shard_map/reduce_scatter | solution.py:54
  217.5 62.8 %copy-start.2 = (s32[16]{0:T(128)S(1)}, s32[16]{0:T(128)}, u32[]{:S(2)}) copy-start(s32[16]{0:T(128)} %param.14) | copy-start | bytes 196
  217.5 51.7 %all-to-all-start.1 = ((bf16[64,2,4096]{2,1,0:T(2,128)(2,1)}), bf16[64,2,4096]{2,1,0:T(2,128)(2,1)}, u32[]{:S(2)}, u32[]{:S(2)}) async-start(bf16[64,2,4096]{2,1,0:T(2,128)(2,1)} %all_to_all.31), calls=%async_computation.2 | async-start | bytes 2097152 | tf_op jit(solution)/shard_map/all_to_all | solution.py:57
  269.2 39.4 %all-to-all-start.3 = ((bf16[64,2,4096]{2,1,0:T(2,128)(2,1)}), bf16[64,2,4096]{2,1,0:T(2,128)(2,1)}, u32[]{:S(2)}, u32[]{:S(2)}) async-start(bf16[64,2,4096]{2,1,0:T(2,128)(2,1)} %all_to_all.36), calls=%async_computation.5 | async-start | bytes 2097152 | tf_op jit(solution)/shard_map/all_to_all | solution.py:57
  279.9 84.7 %all-reduce.3.cloned.1.call-start = ((), (), s32[]{:S(2)}) async-start(), calls=%async_computation.10 | async-start | bytes 2097152
  312.8 5.8 %copy-start.1 = (s32[16]{0:T(128)S(1)}, s32[16]{0:T(128)}, u32[]{:S(2)}) copy-start(s32[16]{0:T(128)} %param.12) | copy-start | bytes 196
  312.9 6.1 %copy-start.3 = (u32[256]{0:T(256)S(1)}, u32[256]{0:T(256)}, u32[]{:S(2)}) copy-start(u32[256]{0:T(256)} %constant.78) | copy-start | bytes 3076
Sparse Core Ops, SparseCore 0:
  62.1 47.4 all-gather.2
  111.4 51.1 all-gather.4
  165.2 49.7 reduce-scatter.2
  217.5 49.1 reduce-scatter.4
  318.7 45.8 all-reduce.2

commit v3 on v2

--- a/solution.py
+++ b/solution.py
@@ -51,9 +51,13 @@
         up_part = jnp.dot(gathered, w_up[0], preferred_element_type=jnp.float32)
         activated = (jax.nn.silu(gate_part) * up_part).astype(jnp.bfloat16)
         expert_result = jnp.dot(activated, w_down[0], preferred_element_type=jnp.float32)
-        reduced = lax.psum_scatter(
-            expert_result.astype(jnp.bfloat16), "dp", scatter_dimension=0, tiled=True
+        quarters = lax.all_to_all(
+            expert_result.astype(jnp.bfloat16), "dp", split_axis=0, concat_axis=0, tiled=True
         )
+        reduced = jnp.sum(
+            quarters.reshape(replica_count, expert_count * sub, model_width).astype(jnp.float32),
+            axis=0,
+        ).astype(jnp.bfloat16)
         returned_rows = lax.all_to_all(reduced, "expert", split_axis=0, concat_axis=0, tiled=True)
         combined = combined + jnp.dot(
             weighted_place,
@@ -73,8 +77,7 @@
         preferred_element_type=jnp.float32,
     )
     arranged = arranged.reshape(replica_count, share_rows, step_count, model_width)
-    summed = lax.psum_scatter(arranged, "dp", scatter_dimension=0, tiled=True)
-    summed = summed.reshape(share_rows, step_count, model_width)
+    summed = jnp.sum(lax.all_to_all(arranged, "dp", split_axis=0, concat_axis=0, tiled=True), axis=0)
     live_rows = live_mask.reshape(row_count, step_count).astype(jnp.float32)
     live_arranged = jnp.dot(arrangement, live_rows, precision=lax.Precision.HIGHEST)
     live_mine = lax.dynamic_slice_in_dim(live_arranged, replica * share_rows, share_rows, 0)

time: 375 us -> 375 us (level)
  waiting for transfers between devices: 186 us -> 169 us
  starting transfers between devices: 22.2 us -> 30.7 us
  other arithmetic: 4.89 us -> 13.3 us
    reduce_scatter x2 -> x0, waiting for transfers between devices: 74.5 us -> none  [body(): lax.psum_scatter(expert_result.astype(jnp.bfloat16), 'dp', scatter_dimens...]
    all_to_all x0 -> x3, waiting for transfers between devices: none -> 57.5 us  [the longest x2 43.3 us: body(): lax.all_to_all(expert_result.astype(jnp.bfloat16), 'dp', split_axis=0, co...]
    unnamed x6 -> x2, waiting for transfers between devices: 45.2 us -> 0.03 us
    all_gather x2, waiting for transfers between devices: 42.3 us -> 65.1 us  [body(): gathered = lax.all_gather(arrived, 'dp', axis=0, tiled=True)]
    all_to_all x2, waiting for transfers between devices: 24.5 us -> 46.7 us  [body(): lax.all_to_all(reduced, 'expert', split_axis=0, concat_axis=0, tiled=True)]
    all_to_all x0 -> x3, starting transfers between devices: none -> 14.1 us  [the longest x2 9.87 us: body(): lax.all_to_all(expert_result.astype(jnp.bfloat16), 'dp', split_axis=0, co...]
    reduce_sum x0 -> x3, other arithmetic: none -> 10 us  [the longest x2 8.56 us: body(): jnp.sum(quarters.reshape(replica_count, expert_count * sub, model_width)....]
    all_to_all x2, starting transfers between devices: 21.6 us -> 16.6 us  [body(): lax.all_to_all(reduced, 'expert', split_axis=0, concat_axis=0, tiled=True)]
  transfers between devices with their start and end apart: 7 -> 7, of which waited for: 6 -> 7; matrix products, arithmetic and copies ran while one was open for 11% -> 13% of each run, Pallas kernels for 0% -> 0%
where the time goes in v3:
time: 375 us; the launch traced here: 373 us
  waiting for transfers between devices  169 us (45%)
  blocking collectives  75.5 us (20%)
  matrix products  48.5 us (13%)
  starting transfers between devices  30.7 us (8%)
  local copies, waits for them, and re-layouts  21.6 us (6%)
  between operations  14.3 us (4%)
  other arithmetic  13.3 us (4%)
    all_to_all x2, blocking collectives, body(): lax.all_to_all(outgoing, 'expert', split_axis=0, concat_axis=0, tiled=True)  75.5 us
    all_gather x2, waiting for transfers between devices, body(): gathered = lax.all_gather(arrived, 'dp', axis=0, tiled=True)  65.1 us
    all_to_all x2, waiting for transfers between devices, body(): lax.all_to_all(reduced, 'expert', split_axis=0, concat_axis=0, tiled=True)  46.7 us
    all_to_all x2, waiting for transfers between devices, body(): lax.all_to_all(expert_result.astype(jnp.bfloat16), 'dp', split_axis=0, co...  43.3 us
    dot_general x2, matrix products, body(): jnp.dot(activated, w_down[0], preferred_element_type=jnp.float32)  19.5 us
    all_to_all x2, starting transfers between devices, body(): lax.all_to_all(reduced, 'expert', split_axis=0, concat_axis=0, tiled=True)  16.6 us
    all_to_all x1, waiting for transfers between devices, body(): lax.all_to_all(arranged, 'dp', split_axis=0, concat_axis=0, tiled=True)  14.1 us
    dot_general x2, matrix products, body(): gate_part = jnp.dot(gathered, w_gate[0], preferred_element_type=jnp.float32)  12.8 us
  transfers between devices with their start and end apart: 7, of which 7 were waited for; matrix products, arithmetic and copies ran while one was open for 13% of the time, Pallas kernels for 0%

profile of v3, /device:TPU:2, one launch (start us, length us, event | category | flops | bytes accessed | tf_op | source)
XLA Modules:
  0.0 373.4 jit_solution(342440657240588606)
XLA Ops:
  7.3 0.9 fusion.36
  8.2 0.1 and.75
  8.3 0.8 copy.30
  9.1 0.2 convert_reduce_fusion
  9.4 0.1 reduce_window_sum.11
  9.6 0.1 copy.31
  9.7 0.7 reduce_sum.61
  10.4 0.7 broadcast_divide_fusion
  11.2 0.3 select_reduce_fusion
  11.6 0.2 broadcast_select_fusion
  11.8 2.0 reshape.169
  13.8 2.5 convolution_convert_fusion.3
  16.3 2.5 all_to_all.43
  18.8 40.9 %all_to_all.65 = bf16[64,2,4096]{2,1,0:T(2,128)(2,1)} all-to-all(bf16[64,2,4096]{2,1,0:T(2,128)(2,1)} %all_to_all.43), channel_id=1, replica_groups=mesh['dp'=4,'expert'=64] {'expert'}, dimensions={0} | all-to-all | bytes 2097152 | tf_op jit(solution)/shard_map/all_to_all | solution.py:48
  59.7 2.3 all_to_all.45
  62.2 2.4 convolution_convert_fusion.2
  64.6 2.5 all_to_all.50
  67.1 34.6 %all_to_all.66 = bf16[64,2,4096]{2,1,0:T(2,128)(2,1)} all-to-all(bf16[64,2,4096]{2,1,0:T(2,128)(2,1)} %all_to_all.50), channel_id=1, replica_groups=mesh['dp'=4,'expert'=64] {'expert'}, dimensions={0} | all-to-all | bytes 2097152 | tf_op jit(solution)/shard_map/all_to_all | solution.py:48
  101.7 2.3 all_to_all.52
  104.0 5.7 %all-gather.3.cloned.1.call-done = bf16[512,4096]{1,0:T(8,128)(2,1)} async-done(((bf16[128,4096]{1,0:T(8,128)(2,1)}), bf16[512,4096]{1,0:T(8,128)(2,1)}) %all-gather.3.cloned.1.call-update) | async-done | bytes 4194320 | tf_op jit(solution)/shard_map/all_gather | solution.py:49
  109.7 6.4 %fusion.9 = f32[512,384]{1,0:T(8,128)} fusion(bf16[512,4096]{1,0:T(8,128)(2,1)} %all-gather.3.cloned.1.call-done, bf16[1,4096,384]{2,1,0:T(8,128)(2,1)} %param.15), kind=kOutput, calls=%fused_computation.15 | convolution fusion | flops 1610612736 | bytes 8126464 | tf_op jit(solution)/shard_map/dot_general | solution.py:50
  116.0 9.8 %convolution_convert_fusion.1 = bf16[512,4096]{1,0:T(8,128)(2,1)} fusion(bf16[1,384,4096]{2,1,0:T(8,128)(2,1)S(1)} %copy-done, bf16[512,4096]{1,0:T(8,128)(2,1)} %all-gather.3.cloned.1.call-done, bf16[1,4096,384]{2,1,0:T(8,128)(2,1)} %param.16, f32[512,384]{1,0:T(8,128)} %fusion.9), kind=kOutput, calls=%fused_computation.1 | convolution fusion | flops 3224502272 | bytes 15466496 | tf_op jit(solution)/shard_map/dot_general | solution.py:53
  125.8 5.0 %all-to-all-start.1 = ((bf16[4,128,4096]{2,1,0:T(8,128)(2,1)}), bf16[4,128,4096]{2,1,0:T(8,128)(2,1)}, u32[]{:S(2)}, u32[]{:S(2)}) async-start(bf16[4,128,4096]{2,1,0:T(8,128)(2,1)} %bitcast.64), calls=%async_computation.1 | async-start | bytes 8388608 | tf_op jit(solution)/shard_map/all_to_all | solution.py:54
  130.8 59.5 %all-gather.5.cloned.1.call-done = bf16[512,4096]{1,0:T(8,128)(2,1)} async-done(((bf16[128,4096]{1,0:T(8,128)(2,1)}), bf16[512,4096]{1,0:T(8,128)(2,1)}) %all-gather.5.cloned.1.call-update) | async-done | bytes 4194320 | tf_op jit(solution)/shard_map/all_gather | solution.py:49
  190.3 6.4 %fusion.7 = f32[512,384]{1,0:T(8,128)} fusion(bf16[512,4096]{1,0:T(8,128)(2,1)} %all-gather.5.cloned.1.call-done, bf16[1,4096,384]{2,1,0:T(8,128)(2,1)} %param.15), kind=kOutput, calls=%fused_computation.13 | convolution fusion | flops 1610612736 | bytes 8126464 | tf_op jit(solution)/shard_map/dot_general | solution.py:50
  196.7 9.7 %convolution_convert_fusion = bf16[512,4096]{1,0:T(8,128)(2,1)} fusion(bf16[1,384,4096]{2,1,0:T(8,128)(2,1)S(1)} %copy-done, bf16[512,4096]{1,0:T(8,128)(2,1)} %all-gather.5.cloned.1.call-done, bf16[1,4096,384]{2,1,0:T(8,128)(2,1)} %param.16, f32[512,384]{1,0:T(8,128)} %fusion.7), kind=kOutput, calls=%fused_computation | convolution fusion | flops 3224502272 | bytes 15466496 | tf_op jit(solution)/shard_map/dot_general | solution.py:53
  206.4 1.2 all-to-all-done.1
  207.6 4.8 %all-to-all-start.4 = ((bf16[4,128,4096]{2,1,0:T(8,128)(2,1)}), bf16[4,128,4096]{2,1,0:T(8,128)(2,1)}, u32[]{:S(2)}, u32[]{:S(2)}) async-start(bf16[4,128,4096]{2,1,0:T(8,128)(2,1)} %bitcast.63), calls=%async_computation.4 | async-start | bytes 8388608 | tf_op jit(solution)/shard_map/all_to_all | solution.py:54
  212.5 4.3 %reduce_sum.63 = bf16[128,4096]{1,0:T(8,128)(2,1)} reduce(bf16[4,128,4096]{2,1,0:T(8,128)(2,1)} %all-to-all-done.1, bf16[]{:T(256)} %constant.68.clone.1), dimensions={0}, to_apply=%region_4.5 | reduce | flops 1572864 | bytes 5242882 | tf_op jit(solution)/shard_map/reduce_sum | solution.py:57
  216.8 2.5 all_to_all.48
  219.3 42.2 %all-to-all-done.4 = bf16[4,128,4096]{2,1,0:T(8,128)(2,1)} async-done(((bf16[4,128,4096]{2,1,0:T(8,128)(2,1)}), bf16[4,128,4096]{2,1,0:T(8,128)(2,1)}, u32[]{:S(2)}, u32[]{:S(2)}) %all-to-all-start.4) | async-done | bytes 4194336 | tf_op jit(solution)/shard_map/all_to_all | solution.py:54
  261.5 10.7 %all-to-all-start.2 = ((bf16[64,2,4096]{2,1,0:T(2,128)(2,1)}), bf16[64,2,4096]{2,1,0:T(2,128)(2,1)}, u32[]{:S(2)}, u32[]{:S(2)}) async-start(bf16[64,2,4096]{2,1,0:T(2,128)(2,1)} %all_to_all.48), calls=%async_computation.2 | async-start | bytes 2097152 | tf_op jit(solution)/shard_map/all_to_all | solution.py:61
  272.2 4.2 %reduce_sum.64 = bf16[128,4096]{1,0:T(8,128)(2,1)} reduce(bf16[4,128,4096]{2,1,0:T(8,128)(2,1)} %all-to-all-done.4, bf16[]{:T(256)} %constant.68.clone.1), dimensions={0}, to_apply=%region_5.6 | reduce | flops 1572864 | bytes 5242882 | tf_op jit(solution)/shard_map/reduce_sum | solution.py:57
  276.5 2.5 all_to_all.55
  279.0 21.9 %all-to-all-done.2 = bf16[64,2,4096]{2,1,0:T(2,128)(2,1)} async-done(((bf16[64,2,4096]{2,1,0:T(2,128)(2,1)}), bf16[64,2,4096]{2,1,0:T(2,128)(2,1)}, u32[]{:S(2)}, u32[]{:S(2)}) %all-to-all-start.2) | async-done | bytes 1048608 | tf_op jit(solution)/shard_map/all_to_all | solution.py:61
  300.9 5.9 %all-to-all-start.5 = ((bf16[64,2,4096]{2,1,0:T(2,128)(2,1)}), bf16[64,2,4096]{2,1,0:T(2,128)(2,1)}, u32[]{:S(2)}, u32[]{:S(2)}) async-start(bf16[64,2,4096]{2,1,0:T(2,128)(2,1)} %all_to_all.55), calls=%async_computation.5 | async-start | bytes 2097152 | tf_op jit(solution)/shard_map/all_to_all | solution.py:61
  306.9 3.9 %convolution_bitcast_fusion.1 = f32[64,4096]{1,0:T(8,128)} fusion(bf16[64,2,4096]{2,1,0:T(2,128)(2,1)} %all-to-all-done.2, f32[64,64,2]{0,2,1:T(2,128)S(1)} %get-tuple-element.9), kind=kOutput, calls=%fused_computation.6 | convolution fusion | flops 402653184 | bytes 2129920 | tf_op jit(solution)/shard_map/dot_general | solution.py:62
  310.7 24.8 %all-to-all-done.5 = bf16[64,2,4096]{2,1,0:T(2,128)(2,1)} async-done(((bf16[64,2,4096]{2,1,0:T(2,128)(2,1)}), bf16[64,2,4096]{2,1,0:T(2,128)(2,1)}, u32[]{:S(2)}, u32[]{:S(2)}) %all-to-all-start.5) | async-done | bytes 1048608 | tf_op jit(solution)/shard_map/all_to_all | solution.py:61
  335.5 4.2 %fusion = f32[64,4096]{1,0:T(8,128)} fusion(f32[64,4096]{1,0:T(8,128)} %convolution_bitcast_fusion.1, bf16[64,2,4096]{2,1,0:T(2,128)(2,1)} %all-to-all-done.5, f32[64,64,2]{0,2,1:T(2,128)S(1)} %get-tuple-element.5), kind=kOutput, calls=%fused_computation.5 | convolution fusion | flops 402915328 | bytes 3178496 | tf_op jit(solution)/shard_map/dot_general | solution.py:62
  339.7 2.7 reshape.170
  342.4 3.1 fusion.23
  345.5 4.2 %all-to-all-start.6 = ((f32[4,4,4,4096]{3,1,2,0:T(4,128)}), f32[4,4,4,4096]{3,1,2,0:T(4,128)}, u32[]{:S(2)}, u32[]{:S(2)}) async-start(f32[4,4,4,4096]{3,1,2,0:T(4,128)} %fusion.23), calls=%async_computation.6 | async-start | bytes 2097152 | tf_op jit(solution)/shard_map/all_to_all | solution.py:80
  349.7 0.2 fusion.37
  349.9 0.1 copy.40
  350.0 14.1 %all-to-all-done.6 = f32[4,4,4,4096]{3,1,2,0:T(4,128)} async-done(((f32[4,4,4,4096]{3,1,2,0:T(4,128)}), f32[4,4,4,4096]{3,1,2,0:T(4,128)}, u32[]{:S(2)}, u32[]{:S(2)}) %all-to-all-start.6) | async-done | bytes 1048608 | tf_op jit(solution)/shard_map/all_to_all | solution.py:80
  364.2 1.5 reduce_sum.65
  365.6 0.1 multiply_convert_fusion
  365.8 0.8 copy.41
  (21 shorter events, 0.5 us)
Async XLA Ops:
  6.5 109.5 %copy-start = (bf16[1,384,4096]{2,1,0:T(8,128)(2,1)S(1)}, bf16[1,384,4096]{2,1,0:T(8,128)(2,1)}, u32[]{:S(2)}) copy-start(bf16[1,384,4096]{2,1,0:T(8,128)(2,1)} %param.17) | copy-start | bytes 9437188
  6.5 103.1 %all-gather.3.cloned.1.call-start = ((), (), s32[]{:S(2)}) async-start(), calls=%async_computation.7 | async-start | bytes 5242880 | tf_op jit(solution)/shard_map/all_gather | solution.py:49
  62.1 128.2 %all-gather.5.cloned.1.call-start = ((), (), s32[]{:S(2)}) async-start(), calls=%async_computation.8 | async-start | bytes 5242880 | tf_op jit(solution)/shard_map/all_gather | solution.py:49
  125.8 81.8 %all-to-all-start.1 = ((bf16[4,128,4096]{2,1,0:T(8,128)(2,1)}), bf16[4,128,4096]{2,1,0:T(8,128)(2,1)}, u32[]{:S(2)}, u32[]{:S(2)}) async-start(bf16[4,128,4096]{2,1,0:T(8,128)(2,1)} %bitcast.64), calls=%async_computation.1 | async-start | bytes 8388608 | tf_op jit(solution)/shard_map/all_to_all | solution.py:54
  207.6 53.9 %all-to-all-start.4 = ((bf16[4,128,4096]{2,1,0:T(8,128)(2,1)}), bf16[4,128,4096]{2,1,0:T(8,128)(2,1)}, u32[]{:S(2)}, u32[]{:S(2)}) async-start(bf16[4,128,4096]{2,1,0:T(8,128)(2,1)} %bitcast.63), calls=%async_computation.4 | async-start | bytes 8388608 | tf_op jit(solution)/shard_map/all_to_all | solution.py:54
  261.5 39.4 %all-to-all-start.2 = ((bf16[64,2,4096]{2,1,0:T(2,128)(2,1)}), bf16[64,2,4096]{2,1,0:T(2,128)(2,1)}, u32[]{:S(2)}, u32[]{:S(2)}) async-start(bf16[64,2,4096]{2,1,0:T(2,128)(2,1)} %all_to_all.48), calls=%async_computation.2 | async-start | bytes 2097152 | tf_op jit(solution)/shard_map/all_to_all | solution.py:61
  276.5 30.3 %copy-start.2 = (s32[16]{0:T(128)S(1)}, s32[16]{0:T(128)}, u32[]{:S(2)}) copy-start(s32[16]{0:T(128)} %param.14) | copy-start | bytes 196
  300.9 34.6 %all-to-all-start.5 = ((bf16[64,2,4096]{2,1,0:T(2,128)(2,1)}), bf16[64,2,4096]{2,1,0:T(2,128)(2,1)}, u32[]{:S(2)}, u32[]{:S(2)}) async-start(bf16[64,2,4096]{2,1,0:T(2,128)(2,1)} %all_to_all.55), calls=%async_computation.5 | async-start | bytes 2097152 | tf_op jit(solution)/shard_map/all_to_all | solution.py:61
  339.7 10.0 %copy-start.1 = (s32[16]{0:T(128)S(1)}, s32[16]{0:T(128)}, u32[]{:S(2)}) copy-start(s32[16]{0:T(128)} %param.12) | copy-start | bytes 196
  345.5 18.7 %all-to-all-start.6 = ((f32[4,4,4,4096]{3,1,2,0:T(4,128)}), f32[4,4,4,4096]{3,1,2,0:T(4,128)}, u32[]{:S(2)}, u32[]{:S(2)}) async-start(f32[4,4,4,4096]{3,1,2,0:T(4,128)} %fusion.23), calls=%async_computation.6 | async-start | bytes 2097152 | tf_op jit(solution)/shard_map/all_to_all | solution.py:80
Sparse Core Ops, SparseCore 0:
  62.2 47.4 all-gather.2
  111.5 78.8 all-gather.4

commit v4 on v2

--- a/solution.py
+++ b/solution.py
@@ -4,6 +4,17 @@
 from jax.sharding import PartitionSpec as P
 
 MOST_BASE = 16
+
+
+def exchange_sum(blocks, replica, replica_count):
+    total = lax.dynamic_index_in_dim(blocks, replica, 0, keepdims=False).astype(jnp.float32)
+    for shift in range(1, replica_count):
+        outgoing = lax.dynamic_index_in_dim(
+            blocks, (replica + shift) % replica_count, 0, keepdims=False
+        )
+        pairs = [(i, (i + shift) % replica_count) for i in range(replica_count)]
+        total = total + lax.ppermute(outgoing, "dp", pairs).astype(jnp.float32)
+    return total
 
 
 def body(
@@ -51,9 +62,10 @@
         up_part = jnp.dot(gathered, w_up[0], preferred_element_type=jnp.float32)
         activated = (jax.nn.silu(gate_part) * up_part).astype(jnp.bfloat16)
         expert_result = jnp.dot(activated, w_down[0], preferred_element_type=jnp.float32)
-        reduced = lax.psum_scatter(
-            expert_result.astype(jnp.bfloat16), "dp", scatter_dimension=0, tiled=True
+        blocks = expert_result.astype(jnp.bfloat16).reshape(
+            replica_count, expert_count * sub, model_width
         )
+        reduced = exchange_sum(blocks, replica, replica_count).astype(jnp.bfloat16)
         returned_rows = lax.all_to_all(reduced, "expert", split_axis=0, concat_axis=0, tiled=True)
         combined = combined + jnp.dot(
             weighted_place,
@@ -73,8 +85,7 @@
         preferred_element_type=jnp.float32,
     )
     arranged = arranged.reshape(replica_count, share_rows, step_count, model_width)
-    summed = lax.psum_scatter(arranged, "dp", scatter_dimension=0, tiled=True)
-    summed = summed.reshape(share_rows, step_count, model_width)
+    summed = exchange_sum(arranged, replica, replica_count)
     live_rows = live_mask.reshape(row_count, step_count).astype(jnp.float32)
     live_arranged = jnp.dot(arrangement, live_rows, precision=lax.Precision.HIGHEST)
     live_mine = lax.dynamic_slice_in_dim(live_arranged, replica * share_rows, share_rows, 0)

time: 375 us -> 375 us (level)
  waiting for transfers between devices: 186 us -> 166 us
  starting transfers between devices: 22.2 us -> 32 us
  other arithmetic: 4.89 us -> 10.8 us
  local copies, waits for them, and re-layouts: 22.1 us -> 27.4 us
    reduce_scatter x2 -> x0, waiting for transfers between devices: 74.5 us -> none  [body(): lax.psum_scatter(expert_result.astype(jnp.bfloat16), 'dp', scatter_dimens...]
    ppermute x0 -> x9, waiting for transfers between devices: none -> 60 us  [exchange_sum(): total = total + lax.ppermute(outgoing, 'dp', pairs).astype(jnp.float32)]
    unnamed x6 -> x2, waiting for transfers between devices: 45.2 us -> 0.03 us
    all_gather x2, waiting for transfers between devices: 42.3 us -> 80.9 us  [body(): gathered = lax.all_gather(arrived, 'dp', axis=0, tiled=True)]
    ppermute x0 -> x9, starting transfers between devices: none -> 10.7 us  [exchange_sum(): total = total + lax.ppermute(outgoing, 'dp', pairs).astype(jnp.float32)]
    convert_element_type x0 -> x2, other arithmetic: none -> 6.67 us  [body(): reduced = exchange_sum(blocks, replica, replica_count).astype(jnp.bfloat16)]
    squeeze x0 -> x2, local copies, waits for them, and re-layouts: none -> 6.1 us  [exchange_sum(): lax.dynamic_index_in_dim(blocks, (replica + shift) % replica_count, 0, ke...]
  transfers between devices with their start and end apart: 7 -> 13, of which waited for: 6 -> 8; matrix products, arithmetic and copies ran while one was open for 11% -> 13% of each run, Pallas kernels for 0% -> 0%
where the time goes in v4:
time: 375 us; the launch traced here: 373 us
  waiting for transfers between devices  166 us (44%)
  blocking collectives  75.5 us (20%)
  matrix products  47.5 us (13%)
  starting transfers between devices  32 us (9%)
  local copies, waits for them, and re-layouts  27.4 us (7%)
  between operations  14.3 us (4%)
  other arithmetic  10.8 us (3%)
    all_gather x2, waiting for transfers between devices, body(): gathered = lax.all_gather(arrived, 'dp', axis=0, tiled=True)  80.9 us
    all_to_all x2, blocking collectives, body(): lax.all_to_all(outgoing, 'expert', split_axis=0, concat_axis=0, tiled=True)  75.5 us
    ppermute x9, waiting for transfers between devices, exchange_sum(): total = total + lax.ppermute(outgoing, 'dp', pairs).astype(jnp.float32)  60 us
    all_to_all x2, waiting for transfers between devices, body(): lax.all_to_all(reduced, 'expert', split_axis=0, concat_axis=0, tiled=True)  24.8 us
    all_to_all x2, starting transfers between devices, body(): lax.all_to_all(reduced, 'expert', split_axis=0, concat_axis=0, tiled=True)  21.2 us
    dot_general x2, matrix products, body(): jnp.dot(activated, w_down[0], preferred_element_type=jnp.float32)  19.5 us
    dot_general x2, matrix products, body(): gate_part = jnp.dot(gathered, w_gate[0], preferred_element_type=jnp.float32)  12.8 us
    ppermute x9, starting transfers between devices, exchange_sum(): total = total + lax.ppermute(outgoing, 'dp', pairs).astype(jnp.float32)  10.7 us
  transfers between devices with their start and end apart: 13, of which 8 were waited for; matrix products, arithmetic and copies ran while one was open for 13% of the time, Pallas kernels for 0%

profile of v4, /device:TPU:2, one launch (start us, length us, event | category | flops | bytes accessed | tf_op | source)
XLA Modules:
  0.0 373.0 jit_solution(10202069643291321383)
XLA Ops:
  6.5 0.9 reduce_sum.28
  7.4 0.8 broadcast_divide_fusion
  8.3 0.8 copy.36
  9.8 0.7 fusion.46
  10.6 0.2 convert_reduce_fusion
  10.8 0.3 select_reduce_fusion
  11.7 2.0 reshape.171
  13.7 2.4 convolution_convert_fusion.3
  16.2 2.5 all_to_all.28
  18.7 40.9 %all_to_all.42 = bf16[64,2,4096]{2,1,0:T(2,128)(2,1)} all-to-all(bf16[64,2,4096]{2,1,0:T(2,128)(2,1)} %all_to_all.28), channel_id=1, replica_groups=mesh['dp'=4,'expert'=64] {'expert'}, dimensions={0} | all-to-all | bytes 2097152 | tf_op jit(solution)/shard_map/all_to_all | solution.py:59
  59.6 2.2 all_to_all.30
  62.0 2.4 convolution_convert_fusion.2
  64.4 2.5 all_to_all.33
  67.0 34.6 %all_to_all.43 = bf16[64,2,4096]{2,1,0:T(2,128)(2,1)} all-to-all(bf16[64,2,4096]{2,1,0:T(2,128)(2,1)} %all_to_all.33), channel_id=1, replica_groups=mesh['dp'=4,'expert'=64] {'expert'}, dimensions={0} | all-to-all | bytes 2097152 | tf_op jit(solution)/shard_map/all_to_all | solution.py:59
  101.5 2.3 all_to_all.35
  103.9 5.6 %all-gather.3.cloned.1.call-done = bf16[512,4096]{1,0:T(8,128)(2,1)} async-done(((bf16[128,4096]{1,0:T(8,128)(2,1)}), bf16[512,4096]{1,0:T(8,128)(2,1)}) %all-gather.3.cloned.1.call-update) | async-done | bytes 4194320 | tf_op jit(solution)/shard_map/all_gather | solution.py:60
  109.5 6.4 %fusion.9 = f32[512,384]{1,0:T(8,128)} fusion(bf16[512,4096]{1,0:T(8,128)(2,1)} %all-gather.3.cloned.1.call-done, bf16[1,4096,384]{2,1,0:T(8,128)(2,1)} %param.15), kind=kOutput, calls=%fused_computation.15 | convolution fusion | flops 1610612736 | bytes 8126464 | tf_op jit(solution)/shard_map/dot_general | solution.py:61
  115.9 9.7 %convolution_convert_fusion.1 = bf16[512,4096]{1,0:T(8,128)(2,1)} fusion(bf16[1,384,4096]{2,1,0:T(8,128)(2,1)S(1)} %copy-done, bf16[512,4096]{1,0:T(8,128)(2,1)} %all-gather.3.cloned.1.call-done, bf16[1,4096,384]{2,1,0:T(8,128)(2,1)} %param.16, f32[512,384]{1,0:T(8,128)} %fusion.9), kind=kOutput, calls=%fused_computation.1 | convolution fusion | flops 3224502272 | bytes 15466496 | tf_op jit(solution)/shard_map/dot_general | solution.py:64
  125.6 3.9 %dynamic-slice_bitcast_fusion.5 = (bf16[128,4096]{1,0:T(8,128)(2,1)}, bf16[128,4096]{1,0:T(8,128)(2,1)}, bf16[128,4096]{1,0:T(8,128)(2,1)}) fusion(bf16[4,128,4096]{2,1,0:T(8,128)(2,1)} %bitcast.103, s32[]{:T(128)S(6)} %select_n.76, s32[]{:T(128)S(6)} %select_n.80, s32[]{:T(128)S(6)} %select_n.78), kind=kLoop, calls=%fused_computation.39 | loop fusion | bytes 6291468 | tf_op jit(solution)/shard_map/jit(dynamic_index_in_dim)/squeeze | solution.py:12
  129.5 1.1 collective-permute-start.2
  130.6 1.8 collective-permute-start.1
  132.4 0.6 collective-permute-start
  132.9 75.3 %all-gather.5.cloned.1.call-done = bf16[512,4096]{1,0:T(8,128)(2,1)} async-done(((bf16[128,4096]{1,0:T(8,128)(2,1)}), bf16[512,4096]{1,0:T(8,128)(2,1)}) %all-gather.5.cloned.1.call-update) | async-done | bytes 4194320 | tf_op jit(solution)/shard_map/all_gather | solution.py:60
  208.2 6.4 %fusion.7 = f32[512,384]{1,0:T(8,128)} fusion(bf16[512,4096]{1,0:T(8,128)(2,1)} %all-gather.5.cloned.1.call-done, bf16[1,4096,384]{2,1,0:T(8,128)(2,1)} %param.15), kind=kOutput, calls=%fused_computation.13 | convolution fusion | flops 1610612736 | bytes 8126464 | tf_op jit(solution)/shard_map/dot_general | solution.py:61
  214.6 9.7 %convolution_convert_fusion = bf16[512,4096]{1,0:T(8,128)(2,1)} fusion(bf16[1,384,4096]{2,1,0:T(8,128)(2,1)S(1)} %copy-done, bf16[512,4096]{1,0:T(8,128)(2,1)} %all-gather.5.cloned.1.call-done, bf16[1,4096,384]{2,1,0:T(8,128)(2,1)} %param.16, f32[512,384]{1,0:T(8,128)} %fusion.7), kind=kOutput, calls=%fused_computation | convolution fusion | flops 3224502272 | bytes 15466496 | tf_op jit(solution)/shard_map/dot_general | solution.py:64
  224.4 3.8 %fusion.16 = bf16[128,4096]{1,0:T(8,128)(2,1)} fusion(bf16[128,4096]{1,0:T(8,128)(2,1)} %collective-permute-done.2, bf16[128,4096]{1,0:T(8,128)(2,1)} %collective-permute-done.1, bf16[128,4096]{1,0:T(8,128)(2,1)} %collective-permute-done, bf16[4,128,4096]{2,1,0:T(8,128)(2,1)} %bitcast.104, s32[]{:T(128)S(6)} %select_n.74), kind=kLoop, calls=%fused_computation.24 | loop fusion | flops 4194304 | bytes 5242884 | tf_op jit(solution)/shard_map/convert_element_type | solution.py:68
  228.2 2.5 all_to_all.31
  230.7 10.7 %all-to-all-start.1 = ((bf16[64,2,4096]{2,1,0:T(2,128)(2,1)}), bf16[64,2,4096]{2,1,0:T(2,128)(2,1)}, u32[]{:S(2)}, u32[]{:S(2)}) async-start(bf16[64,2,4096]{2,1,0:T(2,128)(2,1)} %all_to_all.31), calls=%async_computation.1 | async-start | bytes 2097152 | tf_op jit(solution)/shard_map/all_to_all | solution.py:69
  241.4 2.2 dynamic-slice_bitcast_fusion.2
  243.7 4.0 %collective-permute-start.5 = (bf16[128,4096]{1,0:T(8,128)(2,1)S(1)}, bf16[128,4096]{1,0:T(8,128)(2,1)S(1)}, u32[]{:S(2)}, u32[]{:S(2)}) collective-permute-start(bf16[128,4096]{1,0:T(8,128)(2,1)S(1)} %get-tuple-element.10), channel_id=1, source_target_pairs={{0,192},{64,0},{128,64},{192,128},{1,193},{65,1},{129,65},{193,129... | collective-permute-start | bytes 3145736 | tf_op jit(solution)/shard_map/ppermute | solution.py:16
  247.8 0.9 collective-permute-start.3
  248.6 44.2 %collective-permute-done.5 = bf16[128,4096]{1,0:T(8,128)(2,1)S(1)} collective-permute-done((bf16[128,4096]{1,0:T(8,128)(2,1)S(1)}, bf16[128,4096]{1,0:T(8,128)(2,1)S(1)}, u32[]{:S(2)}, u32[]{:S(2)}) %collective-permute-start.5) | collective-permute-done | bytes 1048608 | tf_op jit(solution)/shard_map/ppermute | solution.py:16
  292.9 3.4 collective-permute-done.3
  296.3 2.9 fusion.13
  299.2 2.5 all_to_all.36
  301.7 10.5 %all-to-all-start.3 = ((bf16[64,2,4096]{2,1,0:T(2,128)(2,1)}), bf16[64,2,4096]{2,1,0:T(2,128)(2,1)}, u32[]{:S(2)}, u32[]{:S(2)}) async-start(bf16[64,2,4096]{2,1,0:T(2,128)(2,1)} %all_to_all.36), calls=%async_computation.3 | async-start | bytes 2097152 | tf_op jit(solution)/shard_map/all_to_all | solution.py:69
  312.3 3.9 %convolution_bitcast_fusion.1 = f32[64,4096]{1,0:T(8,128)} fusion(bf16[64,2,4096]{2,1,0:T(2,128)(2,1)} %all-to-all-done.1, f32[64,64,2]{0,2,1:T(2,128)S(1)} %get-tuple-element.19), kind=kOutput, calls=%fused_computation.6 | convolution fusion | flops 402653184 | bytes 2129920 | tf_op jit(solution)/shard_map/dot_general | solution.py:70
  316.1 24.8 %all-to-all-done.3 = bf16[64,2,4096]{2,1,0:T(2,128)(2,1)} async-done(((bf16[64,2,4096]{2,1,0:T(2,128)(2,1)}), bf16[64,2,4096]{2,1,0:T(2,128)(2,1)}, u32[]{:S(2)}, u32[]{:S(2)}) %all-to-all-start.3) | async-done | bytes 1048608 | tf_op jit(solution)/shard_map/all_to_all | solution.py:69
  340.9 4.2 %fusion = f32[64,4096]{1,0:T(8,128)} fusion(f32[64,4096]{1,0:T(8,128)} %convolution_bitcast_fusion.1, bf16[64,2,4096]{2,1,0:T(2,128)(2,1)} %all-to-all-done.3, f32[64,64,2]{0,2,1:T(2,128)S(1)} %get-tuple-element.5), kind=kOutput, calls=%fused_computation.5 | convolution fusion | flops 402915328 | bytes 3178496 | tf_op jit(solution)/shard_map/dot_general | solution.py:70
  345.1 2.7 reshape.174
  347.8 2.1 fusion.29
  350.1 1.0 collective-permute-start.8
  351.3 0.4 collective-permute-start.7
  351.8 0.9 collective-permute-start.6
  353.0 6.5 %collective-permute-done.8 = f32[4,4,4096]{2,1,0:T(4,128)S(1)} collective-permute-done((f32[4,4,4096]{2,1,0:T(4,128)S(1)}, f32[4,4,4096]{2,1,0:T(4,128)S(1)}, u32[]{:S(2)}, u32[]{:S(2)}) %collective-permute-start.8) | collective-permute-done | bytes 262176 | tf_op jit(solution)/shard_map/ppermute | solution.py:16
  359.4 2.7 collective-permute-done.7
  362.1 3.1 collective-permute-done.6
  365.2 0.9 fusion.42
  (36 shorter events, 1.8 us)
Async XLA Ops:
  6.5 109.3 %copy-start = (bf16[1,384,4096]{2,1,0:T(8,128)(2,1)S(1)}, bf16[1,384,4096]{2,1,0:T(8,128)(2,1)}, u32[]{:S(2)}) copy-start(bf16[1,384,4096]{2,1,0:T(8,128)(2,1)} %param.17) | copy-start | bytes 9437188
  6.5 103.0 %all-gather.3.cloned.1.call-start = ((), (), s32[]{:S(2)}) async-start(), calls=%async_computation.4 | async-start | bytes 5242880 | tf_op jit(solution)/shard_map/all_gather | solution.py:60
  61.9 146.3 %all-gather.5.cloned.1.call-start = ((), (), s32[]{:S(2)}) async-start(), calls=%async_computation.5 | async-start | bytes 5242880 | tf_op jit(solution)/shard_map/all_gather | solution.py:60
  129.5 94.8 %collective-permute-start.2 = (bf16[128,4096]{1,0:T(8,128)(2,1)}, bf16[128,4096]{1,0:T(8,128)(2,1)}, u32[]{:S(2)}, u32[]{:S(2)}) collective-permute-start(bf16[128,4096]{1,0:T(8,128)(2,1)} %get-tuple-element.13), channel_id=1, source_target_pairs={{0,192},{64,0},{128,64},{192,128},{1,193},{65,1},{129,65},{193,129... | collective-permute-start | bytes 3145736 | tf_op jit(solution)/shard_map/ppermute | solution.py:16
  130.6 93.8 %collective-permute-start.1 = (bf16[128,4096]{1,0:T(8,128)(2,1)}, bf16[128,4096]{1,0:T(8,128)(2,1)}, u32[]{:S(2)}, u32[]{:S(2)}) collective-permute-start(bf16[128,4096]{1,0:T(8,128)(2,1)} %get-tuple-element.14), channel_id=1, source_target_pairs={{0,128},{64,192},{128,0},{192,64},{1,129},{65,193},{129,1},{193,65... | collective-permute-start | bytes 3145736 | tf_op jit(solution)/shard_map/ppermute | solution.py:16
  132.4 92.0 %collective-permute-start = (bf16[128,4096]{1,0:T(8,128)(2,1)}, bf16[128,4096]{1,0:T(8,128)(2,1)}, u32[]{:S(2)}, u32[]{:S(2)}) collective-permute-start(bf16[128,4096]{1,0:T(8,128)(2,1)} %get-tuple-element.12), channel_id=1, source_target_pairs={{0,64},{64,128},{128,192},{192,0},{1,65},{65,129},{129,193},{193,1... | collective-permute-start | bytes 3145736 | tf_op jit(solution)/shard_map/ppermute | solution.py:16
  230.7 71.0 %all-to-all-start.1 = ((bf16[64,2,4096]{2,1,0:T(2,128)(2,1)}), bf16[64,2,4096]{2,1,0:T(2,128)(2,1)}, u32[]{:S(2)}, u32[]{:S(2)}) async-start(bf16[64,2,4096]{2,1,0:T(2,128)(2,1)} %all_to_all.31), calls=%async_computation.1 | async-start | bytes 2097152 | tf_op jit(solution)/shard_map/all_to_all | solution.py:69
  243.7 49.2 %collective-permute-start.5 = (bf16[128,4096]{1,0:T(8,128)(2,1)S(1)}, bf16[128,4096]{1,0:T(8,128)(2,1)S(1)}, u32[]{:S(2)}, u32[]{:S(2)}) collective-permute-start(bf16[128,4096]{1,0:T(8,128)(2,1)S(1)} %get-tuple-element.10), channel_id=1, source_target_pairs={{0,192},{64,0},{128,64},{192,128},{1,193},{65,1},{129,65},{193,129... | collective-permute-start | bytes 3145736 | tf_op jit(solution)/shard_map/ppermute | solution.py:16
  247.7 45.2 %collective-permute-start.4 = (bf16[128,4096]{1,0:T(8,128)(2,1)S(1)}, bf16[128,4096]{1,0:T(8,128)(2,1)S(1)}, u32[]{:S(2)}, u32[]{:S(2)}) collective-permute-start(bf16[128,4096]{1,0:T(8,128)(2,1)S(1)} %get-tuple-element.11), channel_id=1, source_target_pairs={{0,128},{64,192},{128,0},{192,64},{1,129},{65,193},{129,1},{193,65... | collective-permute-start | bytes 3145736 | tf_op jit(solution)/shard_map/ppermute | solution.py:16
  247.8 48.6 %collective-permute-start.3 = (bf16[128,4096]{1,0:T(8,128)(2,1)S(1)}, bf16[128,4096]{1,0:T(8,128)(2,1)S(1)}, u32[]{:S(2)}, u32[]{:S(2)}) collective-permute-start(bf16[128,4096]{1,0:T(8,128)(2,1)S(1)} %get-tuple-element.9), channel_id=1, source_target_pairs={{0,64},{64,128},{128,192},{192,0},{1,65},{65,129},{129,193},{193,1... | collective-permute-start | bytes 3145736 | tf_op jit(solution)/shard_map/ppermute | solution.py:16
  299.2 13.1 %copy-start.2 = (s32[16]{0:T(128)S(1)}, s32[16]{0:T(128)}, u32[]{:S(2)}) copy-start(s32[16]{0:T(128)} %param.14) | copy-start | bytes 196
  301.7 39.2 %all-to-all-start.3 = ((bf16[64,2,4096]{2,1,0:T(2,128)(2,1)}), bf16[64,2,4096]{2,1,0:T(2,128)(2,1)}, u32[]{:S(2)}, u32[]{:S(2)}) async-start(bf16[64,2,4096]{2,1,0:T(2,128)(2,1)} %all_to_all.36), calls=%async_computation.3 | async-start | bytes 2097152 | tf_op jit(solution)/shard_map/all_to_all | solution.py:69
  347.8 5.0 %copy-start.1 = (s32[16]{0:T(128)S(1)}, s32[16]{0:T(128)}, u32[]{:S(2)}) copy-start(s32[16]{0:T(128)} %param.12) | copy-start | bytes 196
  350.1 9.3 %collective-permute-start.8 = (f32[4,4,4096]{2,1,0:T(4,128)S(1)}, f32[4,4,4096]{2,1,0:T(4,128)S(1)}, u32[]{:S(2)}, u32[]{:S(2)}) collective-permute-start(f32[4,4,4096]{2,1,0:T(4,128)S(1)} %bitcast.107), channel_id=1, source_target_pairs={{0,192},{64,0},{128,64},{192,128},{1,193},{65,1},{129,65},{193,129... | collective-permute-start | bytes 786440 | tf_op jit(solution)/shard_map/ppermute | solution.py:16
  351.3 10.8 %collective-permute-start.7 = (f32[4,4,4096]{2,1,0:T(4,128)S(1)}, f32[4,4,4096]{2,1,0:T(4,128)S(1)}, u32[]{:S(2)}, u32[]{:S(2)}) collective-permute-start(f32[4,4,4096]{2,1,0:T(4,128)S(1)} %bitcast.108), channel_id=1, source_target_pairs={{0,128},{64,192},{128,0},{192,64},{1,129},{65,193},{129,1},{193,65... | collective-permute-start | bytes 786440 | tf_op jit(solution)/shard_map/ppermute | solution.py:16
  351.8 13.4 %collective-permute-start.6 = (f32[4,4,4096]{2,1,0:T(4,128)S(1)}, f32[4,4,4096]{2,1,0:T(4,128)S(1)}, u32[]{:S(2)}, u32[]{:S(2)}) collective-permute-start(f32[4,4,4096]{2,1,0:T(4,128)S(1)} %bitcast.109), channel_id=1, source_target_pairs={{0,64},{64,128},{128,192},{192,0},{1,65},{65,129},{129,193},{193,1... | collective-permute-start | bytes 786440 | tf_op jit(solution)/shard_map/ppermute | solution.py:16
Sparse Core Ops, SparseCore 0:
  62.0 47.4 all-gather.2
  111.3 96.8 all-gather.4

commit v5 on v4

v5 whole, which is shorter than its diff:
```python
import jax
import jax.numpy as jnp
from jax import lax
from jax.sharding import PartitionSpec as P

MOST_BASE = 16


def exchange_gather(blocks, replica, replica_count):
    pieces = [None] * replica_count
    pieces[0] = lax.dynamic_index_in_dim(blocks, replica, 0, keepdims=False)
    for shift in range(1, replica_count):
        outgoing = lax.dynamic_index_in_dim(
            blocks, (replica + shift) % replica_count, 0, keepdims=False
        )
        pairs = [(i, (i + shift) % replica_count) for i in range(replica_count)]
        pieces[shift] = lax.ppermute(outgoing, "dp", pairs)
    stacked = jnp.stack(pieces, axis=0)
    order = (replica - lax.broadcasted_iota(jnp.int32, (replica_count,), 0)) % replica_count
    return jnp.take(stacked, order, axis=0)


def body(
    hidden_states, routes, route_weight, finish_step, group_keep, dest_slot, w_gate, w_up, w_down
):
    expert_count = lax.axis_size("expert")
    replica_count = lax.axis_size("dp")
    replica = lax.axis_index("dp")
    row_count, step_count, model_width = hidden_states.shape
    top_count = routes.shape[2]
    hidden_part = w_down.shape[1]
    columns = model_width // replica_count
    tokens = row_count * step_count
    slot_count = min(tokens, max(MOST_BASE, 2 * tokens * top_count // expert_count))
    slot_count = -(-slot_count // replica_count) * replica_count
    part = slot_count // replica_count
    down_blocks = w_down[0].reshape(hidden_part, replica_count, columns).transpose(1, 0, 2)
    down_cols = exchange_gather(down_blocks, replica, replica_count)
    step_ids = lax.broadcasted_iota(jnp.int32, (row_count, step_count), 1)
    live_mask = ((step_ids < finish_step[:, None]) & (group_keep[0] == 1)).reshape(tokens)
    gate_share = route_weight / jnp.sum(route_weight, axis=2, keepdims=True)
    expert_ids = lax.broadcasted_iota(jnp.int32, (1, 1, expert_count), 2)
    picked = (routes.reshape(tokens, top_count, 1) == expert_ids) & live_mask[:, None, None]
    hit_mask = jnp.sum(picked.astype(jnp.int32), axis=1)
    share_wide = jnp.broadcast_to(gate_share.reshape(tokens, top_count, 1), picked.shape)
    weight = jnp.sum(jnp.where(picked, share_wide, jnp.zeros_like(share_wide)), axis=1)
    prior_hits = jnp.cumsum(hit_mask, axis=0) - hit_mask
    flat_inputs = hidden_states.reshape(tokens, model_width)
    chunks = 2 if part % 2 == 0 else 1
    sub = part // chunks
    member_ids = lax.broadcasted_iota(jnp.int32, (1, 1, replica_count, 1), 2)
    within_ids = lax.broadcasted_iota(jnp.int32, (1, 1, 1, sub), 3)
    combined = jnp.zeros((tokens, columns), jnp.float32)
    for chunk in range(chunks):
        slot_ids = replica * part + chunk * sub + lax.broadcasted_iota(jnp.int32, (1, 1, sub), 2)
        placement = (hit_mask[:, :, None] == 1) & (prior_hits[:, :, None] == slot_ids)
        placement = placement.reshape(tokens, expert_count * sub)
        outgoing = lax.dot_general(
            placement.astype(jnp.bfloat16),
            flat_inputs,
            (((0,), (0,)), ((), ())),
            preferred_element_type=jnp.float32,
        ).astype(jnp.bfloat16)
        arrived = lax.all_to_all(outgoing, "expert", split_axis=0, concat_axis=0, tiled=True)
        gathered = lax.all_gather(arrived, "dp", axis=0, tiled=True)
        gate_part = jnp.dot(gathered, w_gate[0], preferred_element_type=jnp.float32)
        up_part = jnp.dot(gathered, w_up[0], preferred_element_type=jnp.float32)
        activated = (jax.nn.silu(gate_part) * up_part).astype(jnp.bfloat16)
        hidden_all = lax.all_gather(activated, "dp", axis=0, tiled=False)
        expert_cols = lax.dot_general(
            hidden_all,
            down_cols,
            (((0, 2), (0, 1)), ((), ())),
            preferred_element_type=jnp.float32,
        ).astype(jnp.bfloat16)
        by_source = expert_cols.reshape(replica_count, expert_count, sub, columns).transpose(
            1, 0, 2, 3
        )
        returned_rows = lax.all_to_all(by_source, "expert", split_axis=0, concat_axis=0, tiled=True)
        all_slot_ids = member_ids * part + chunk * sub + within_ids
        weighted_place = jnp.where(
            (hit_mask[:, :, None, None] == 1) & (prior_hits[:, :, None, None] == all_slot_ids),
            weight[:, :, None, None],
            0.0,
        ).reshape(tokens, expert_count * replica_count * sub)
        combined = combined + jnp.dot(
            weighted_place,
            returned_rows.reshape(expert_count * replica_count * sub, columns).astype(jnp.float32),
            precision=lax.Precision.HIGHEST,
            preferred_element_type=jnp.float32,
        )
    share_rows = row_count // replica_count
    flat_device = dest_slot // share_rows
    target = flat_device // expert_count * share_rows + dest_slot % share_rows
    position_ids = lax.broadcasted_iota(jnp.int32, (replica_count * share_rows, row_count), 0)
    arrangement = (target[None, :] == position_ids).astype(jnp.float32)
    arranged = jnp.dot(
        arrangement,
        combined.reshape(row_count, step_count * columns),
        precision=lax.Precision.HIGHEST,
        preferred_element_type=jnp.float32,
    ).astype(jnp.bfloat16)
    arranged = arranged.reshape(replica_count, share_rows, step_count, columns)
    quarters = lax.all_to_all(arranged, "dp", split_axis=0, concat_axis=0, tiled=True)
    return quarters.transpose(1, 2, 0, 3).reshape(share_rows, step_count, model_width)


def solution(mesh):
    in_specs = (
        P("expert", None, None),
        P("expert", None, None),
        P("expert", None, None),
        P("expert"),
        P("expert"),
        P("expert"),
        P("expert", None, "dp"),
        P("expert", None, "dp"),
        P("expert", "dp", None),
    )
    out_specs = P(("dp", "expert"), None, None)
    return jax.shard_map(body, mesh=mesh, in_specs=in_specs, out_specs=out_specs, check_vma=False)
```

time: 375 us -> 332 us (0.89)
  waiting for transfers between devices: 166 us -> 120 us
  local copies, waits for them, and re-layouts: 27.4 us -> 48.4 us
  starting transfers between devices: 32 us -> 19.9 us
  matrix products: 47.5 us -> 38.7 us
  blocking collectives: 75.5 us -> 84.3 us
  other arithmetic: 10.8 us -> 5 us
    ppermute x9 -> x3, waiting for transfers between devices: 60 us -> 0.01 us  [exchange_gather(): pieces[shift] = lax.ppermute(outgoing, 'dp', pairs)]
    all_gather x0 -> x2, waiting for transfers between devices: none -> 21.6 us  [body(): hidden_all = lax.all_gather(activated, 'dp', axis=0, tiled=False)]
    all_gather x2, waiting for transfers between devices: 80.9 us -> 65.5 us  [body(): gathered = lax.all_gather(arrived, 'dp', axis=0, tiled=True)]
    another operation x0 -> x5, local copies, waits for them, and re-layouts: none -> 13.3 us
    reshape x1 -> x7, local copies, waits for them, and re-layouts: 2.68 us -> 13.1 us  [the longest x4 11.3 us: body(): expert_cols.reshape(replica_count, expert_count, sub, columns)]
    all_to_all x0 -> x1, blocking collectives: none -> 8.84 us  [body(): lax.all_to_all(arranged, 'dp', split_axis=0, concat_axis=0, tiled=True)]
    all_to_all x2, waiting for transfers between devices: 24.8 us -> 32.9 us  [body(): lax.all_to_all(by_source, 'expert', split_axis=0, concat_axis=0, tiled=True)]
    convert_element_type x3 -> x0, other arithmetic: 7.6 us -> none  [the longest x2 6.67 us: body(): reduced = exchange_sum(blocks, replica, replica_count).astype(jnp.bfloat16)]
  transfers between devices with their start and end apart: 13 -> 9, of which waited for: 8 -> 6; matrix products, arithmetic and copies ran while one was open for 13% -> 21% of each run, Pallas kernels for 0% -> 0%
where the time goes in v5:
time: 332 us; the launch traced here: 330 us
  waiting for transfers between devices  120 us (36%)
  blocking collectives  84.3 us (25%)
  local copies, waits for them, and re-layouts  48.4 us (15%)
  matrix products  38.7 us (12%)
  starting transfers between devices  19.9 us (6%)
  between operations  14 us (4%)
  other arithmetic  5 us (2%)
    all_to_all x2, blocking collectives, body(): lax.all_to_all(outgoing, 'expert', split_axis=0, concat_axis=0, tiled=True)  75.5 us
    all_gather x2, waiting for transfers between devices, body(): gathered = lax.all_gather(arrived, 'dp', axis=0, tiled=True)  65.5 us
    all_to_all x2, waiting for transfers between devices, body(): lax.all_to_all(by_source, 'expert', split_axis=0, concat_axis=0, tiled=True)  32.9 us
    all_gather x2, waiting for transfers between devices, body(): hidden_all = lax.all_gather(activated, 'dp', axis=0, tiled=False)  21.6 us
    all_to_all x2, starting transfers between devices, body(): lax.all_to_all(by_source, 'expert', split_axis=0, concat_axis=0, tiled=True)  16.6 us
    another operation x5, local copies, waits for them, and re-layouts  13.3 us
    reshape x4, local copies, waits for them, and re-layouts, body(): expert_cols.reshape(replica_count, expert_count, sub, columns)  11.3 us
    dot_general x2, matrix products, body(): lax.dot_general(hidden_all, down_cols, (((0, 2), (0, 1)), ((), ())), pref...  10.5 us
  transfers between devices with their start and end apart: 9, of which 6 were waited for; matrix products, arithmetic and copies ran while one was open for 21% of the time, Pallas kernels for 0%

profile of v5, /device:TPU:2, one launch (start us, length us, event | category | flops | bytes accessed | tf_op | source)
XLA Modules:
  0.0 330.4 jit_solution(6307096701580997879)
XLA Ops:
  6.5 0.9 copy.46
  8.2 0.7 fusion.40
  9.0 0.2 convert_reduce_fusion
  9.7 2.0 reshape.270
  11.7 2.5 convolution_convert_fusion
  14.2 2.5 all_to_all.29
  16.7 40.9 %all_to_all.39 = bf16[64,2,4096]{2,1,0:T(2,128)(2,1)} all-to-all(bf16[64,2,4096]{2,1,0:T(2,128)(2,1)} %all_to_all.29), channel_id=1, replica_groups=mesh['dp'=4,'expert'=64] {'expert'}, dimensions={0} | all-to-all | bytes 2097152 | tf_op jit(solution)/shard_map/all_to_all | solution.py:64
  57.6 2.2 all_to_all.31
  60.0 2.5 convolution_convert_fusion.1
  62.5 2.5 all_to_all.25
  65.0 34.6 %all_to_all.40 = bf16[64,2,4096]{2,1,0:T(2,128)(2,1)} all-to-all(bf16[64,2,4096]{2,1,0:T(2,128)(2,1)} %all_to_all.25), channel_id=1, replica_groups=mesh['dp'=4,'expert'=64] {'expert'}, dimensions={0} | all-to-all | bytes 2097152 | tf_op jit(solution)/shard_map/all_to_all | solution.py:64
  99.6 2.3 all_to_all.27
  101.9 5.6 %all-gather.9.cloned.1.call-done = bf16[512,4096]{1,0:T(8,128)(2,1)} async-done(((bf16[128,4096]{1,0:T(8,128)(2,1)}), bf16[512,4096]{1,0:T(8,128)(2,1)}) %all-gather.9.cloned.1.call-update) | async-done | bytes 4194320 | tf_op jit(solution)/shard_map/all_gather | solution.py:65
  107.5 4.7 %fusion.4 = f32[512,384]{1,0:T(8,128)S(1)} fusion(bf16[512,4096]{1,0:T(8,128)(2,1)} %all-gather.9.cloned.1.call-done, bf16[1,4096,384]{2,1,0:T(8,128)(2,1)S(1)} %copy-done), kind=kOutput, calls=%fused_computation.9 | convolution fusion | flops 1610612736 | bytes 8126464 | tf_op jit(solution)/shard_map/dot_general | solution.py:66
  112.2 3.1 fusion.14
  115.4 4.7 %copy.50 = bf16[1,384,4096]{1,2,0:T(8,128)(2,1)} copy(bf16[1,384,4096]{2,1,0:T(8,128)(2,1)} %param.17) | data formatting | bytes 6291456 | tf_op args[8]
  120.0 3.9 %constant_dynamic-slice_fusion.3 = (bf16[384,1,1024]{0,2,1:T(8,128)(2,1)}, bf16[384,1,1024]{0,2,1:T(8,128)(2,1)}, bf16[384,1,1024]{0,2,1:T(8,128)(2,1)}, bf16[384,1,1024]{0,2,1:T(8,128)(2,1)}) fusion(bf16[384,4,1024]{0,2,1:T(8,128)(2,1)} %bitcast.71, s32[]{:T(128)S(6)} %select_n.97, s32[]{:T(128)S(6)} %select_n.103, s32[]{:T(128)S(6)} %select_n.101, ...), kind=kLoop, calls=%fused_computation.79 | loop fusion | bytes 6291472 | tf_op jit(solution)/shard_map/dynamic-slice
  124.0 2.4 copy.54
  126.3 0.8 collective-permute-start.2
  127.2 2.3 copy.53
  129.5 1.9 collective-permute-start.1
  131.4 2.3 copy.52
  133.7 0.5 collective-permute-start
  134.2 60.0 %all-gather.7.cloned.1.call-done = bf16[512,4096]{1,0:T(8,128)(2,1)} async-done(((bf16[128,4096]{1,0:T(8,128)(2,1)}), bf16[512,4096]{1,0:T(8,128)(2,1)}) %all-gather.7.cloned.1.call-update) | async-done | bytes 4194320 | tf_op jit(solution)/shard_map/all_gather | solution.py:65
  194.2 4.7 %fusion.6 = f32[512,384]{1,0:T(8,128)S(1)} fusion(bf16[512,4096]{1,0:T(8,128)(2,1)} %all-gather.7.cloned.1.call-done, bf16[1,4096,384]{2,1,0:T(8,128)(2,1)S(1)} %copy-done), kind=kOutput, calls=%fused_computation.11 | convolution fusion | flops 1610612736 | bytes 8126464 | tf_op jit(solution)/shard_map/dot_general | solution.py:66
  198.9 3.1 fusion.17
  202.0 2.3 copy.51
  204.4 3.2 pad_maximum_fusion
  207.6 4.4 %gather_fusion = bf16[4,384,1024]{2,1,0:T(8,128)(2,1)} fusion(bf16[4,384,1024]{2,1,0:T(8,128)(2,1)} %pad_maximum_fusion, s32[1024]{0:T(1024)S(1)} %pad_clamp_fusion), kind=kCustom, calls=%fused_computation | custom fusion | bytes 6291472 | tf_op jit(solution)/shard_map/jit(_take)/gather | solution.py:20
  212.0 12.2 %all-gather.13.cloned.1.call-done = bf16[2048,384]{1,0:T(8,128)(2,1)} async-done(((bf16[512,384]{1,0:T(8,128)(2,1)}), bf16[2048,384]{1,0:T(8,128)(2,1)}) %all-gather.13.cloned.1.call-update) | async-done | bytes 1572880 | tf_op jit(solution)/shard_map/all_gather | solution.py:69
  224.3 5.2 %bitcast_convert_fusion = bf16[512,1024]{1,0:T(8,128)(2,1)} fusion(bf16[4,512,384]{2,1,0:T(8,128)(2,1)} %bitcast.82, bf16[4,384,1024]{2,1,0:T(8,128)(2,1)} %gather_fusion, pred[4]{0:T(512)(128)(4,1)S(1)} %compare_and_fusion.2), kind=kOutput, calls=%fused_computation.14 | convolution fusion | flops 1612709888 | bytes 5767172 | tf_op jit(solution)/shard_map/dot_general | solution.py:70
  229.5 2.3 reshape.272
  231.8 3.4 %copy.69 = bf16[4,64,2,1024]{3,2,0,1:T(2,128)(2,1)} copy(bf16[4,64,2,1024]{3,2,1,0:T(2,128)(2,1)} %reshape.272) | data formatting | bytes 2097152 | tf_op jit(solution)/shard_map/reshape | solution.py:76
  235.1 10.7 %all-to-all-start.3 = ((bf16[64,4,2,1024]{3,2,1,0:T(2,128)(2,1)}), bf16[64,4,2,1024]{3,2,1,0:T(2,128)(2,1)}, u32[]{:S(2)}, u32[]{:S(2)}) async-start(bf16[64,4,2,1024]{3,2,1,0:T(2,128)(2,1)} %bitcast.73), calls=%async_computation.3 | async-start | bytes 2097152 | tf_op jit(solution)/shard_map/all_to_all | solution.py:79
  245.9 9.3 %all-gather.11.cloned.1.call-done = bf16[2048,384]{1,0:T(8,128)(2,1)} async-done(((bf16[512,384]{1,0:T(8,128)(2,1)}), bf16[2048,384]{1,0:T(8,128)(2,1)}) %all-gather.11.cloned.1.call-update) | async-done | bytes 1572880 | tf_op jit(solution)/shard_map/all_gather | solution.py:69
  255.2 5.2 %bitcast_convert_fusion.1 = bf16[512,1024]{1,0:T(8,128)(2,1)} fusion(bf16[4,512,384]{2,1,0:T(8,128)(2,1)} %bitcast.83, bf16[4,384,1024]{2,1,0:T(8,128)(2,1)} %gather_fusion, pred[4]{0:T(512)(128)(4,1)S(1)} %compare_and_fusion.2), kind=kOutput, calls=%fused_computation.15 | convolution fusion | flops 1612709888 | bytes 5767172 | tf_op jit(solution)/shard_map/dot_general | solution.py:70
  260.4 2.3 reshape.271
  262.7 3.4 %copy.70 = bf16[4,64,2,1024]{3,2,0,1:T(2,128)(2,1)} copy(bf16[4,64,2,1024]{3,2,1,0:T(2,128)(2,1)} %reshape.271) | data formatting | bytes 2097152 | tf_op jit(solution)/shard_map/reshape | solution.py:76
  266.1 8.5 %all-to-all-done.3 = bf16[64,4,2,1024]{3,2,1,0:T(2,128)(2,1)} async-done(((bf16[64,4,2,1024]{3,2,1,0:T(2,128)(2,1)}), bf16[64,4,2,1024]{3,2,1,0:T(2,128)(2,1)}, u32[]{:S(2)}, u32[]{:S(2)}) %all-to-all-start.3) | async-done | bytes 1048608 | tf_op jit(solution)/shard_map/all_to_all | solution.py:79
  274.6 5.9 %all-to-all-start.1 = ((bf16[64,4,2,1024]{3,2,1,0:T(2,128)(2,1)}), bf16[64,4,2,1024]{3,2,1,0:T(2,128)(2,1)}, u32[]{:S(2)}, u32[]{:S(2)}) async-start(bf16[64,4,2,1024]{3,2,1,0:T(2,128)(2,1)} %bitcast.72), calls=%async_computation.1 | async-start | bytes 2097152 | tf_op jit(solution)/shard_map/all_to_all | solution.py:79
  280.6 0.3 select_reduce_fusion
  281.0 3.7 %convolution_bitcast_fusion = f32[64,1024]{1,0:T(8,128)} fusion(bf16[64,4,2,1024]{3,2,1,0:T(2,128)(2,1)} %all-to-all-done.3, s32[4,2]{1,0:T(4,128)S(1)} %iota_add_fusion, f32[64,64]{1,0:T(8,128)S(1)} %select_reduce_fusion, s32[64,64]{1,0:T(8,128)S(1)} %sub.39, pred[64,64]{1,0:T(8,128)(4,1)S(1)} %broadcast_compare_fusion), kind=kOutput, calls=%fused_computation.20 | convolution fusion | flops 402751488 | bytes 1347616 | tf_op jit(solution)/shard_map/dot_general | solution.py:86
  284.7 24.4 %all-to-all-done.1 = bf16[64,4,2,1024]{3,2,1,0:T(2,128)(2,1)} async-done(((bf16[64,4,2,1024]{3,2,1,0:T(2,128)(2,1)}), bf16[64,4,2,1024]{3,2,1,0:T(2,128)(2,1)}, u32[]{:S(2)}, u32[]{:S(2)}) %all-to-all-start.1) | async-done | bytes 1048608 | tf_op jit(solution)/shard_map/all_to_all | solution.py:79
  309.1 3.8 %fusion.20 = f32[64,1024]{1,0:T(8,128)} fusion(f32[64,1024]{1,0:T(8,128)} %convolution_bitcast_fusion, bf16[64,4,2,1024]{3,2,1,0:T(2,128)(2,1)} %all-to-all-done.1, f32[64,64]{1,0:T(8,128)S(1)} %select_reduce_fusion, s32[4,2]{1,0:T(4,128)S(1)} %iota_add_fusion.1, s32[64,64]{1,0:T(8,128)S(1)} %sub.39, pred[64,64]{1,0:T(8,128)(4,1)S(1)} %broadcast_compare_fusion), kind=kOutput, calls=%fused_computation.22 | convolution fusion | flops 402817024 | bytes 1609760 | tf_op jit(solution)/shard_map/dot_general | solution.py:86
  312.9 1.1 reshape.273
  314.0 0.3 convolution_convert_fusion.2
  314.3 8.8 %all_to_all.41 = bf16[4,4,4,1024]{3,2,1,0:T(4,128)(2,1)S(1)} all-to-all(bf16[4,4,4,1024]{3,2,1,0:T(4,128)(2,1)S(1)} %reshape.274), channel_id=1, replica_groups=mesh['dp'=4,'expert'=64] {'dp'}, dimensions={0} | all-to-all | bytes 262144 | tf_op jit(solution)/shard_map/all_to_all | solution.py:104
  323.1 0.7 copy.62
  (47 shorter events, 1.3 us)
Async XLA Ops:
  6.5 100.9 %copy-start = (bf16[1,4096,384]{2,1,0:T(8,128)(2,1)S(1)}, bf16[1,4096,384]{2,1,0:T(8,128)(2,1)}, u32[]{:S(2)}) copy-start(bf16[1,4096,384]{2,1,0:T(8,128)(2,1)} %param.15) | copy-start | bytes 9437188
  6.5 100.9 %all-gather.9.cloned.1.call-start = ((), (), s32[]{:S(2)}) async-start(), calls=%async_computation.6 | async-start | bytes 5242880 | tf_op jit(solution)/shard_map/all_gather | solution.py:65
  59.9 134.3 %all-gather.7.cloned.1.call-start = ((), (), s32[]{:S(2)}) async-start(), calls=%async_computation.5 | async-start | bytes 5242880 | tf_op jit(solution)/shard_map/all_gather | solution.py:65
  101.9 122.4 %all-gather.13.cloned.1.call-start = ((), (), s32[]{:S(2)}) async-start(), calls=%async_computation.8 | async-start | bytes 1966080 | tf_op jit(solution)/shard_map/all_gather | solution.py:69
  107.5 4.7 %copy-start.3 = (bf16[512,4096]{1,0:T(8,128)(2,1)S(1)}, bf16[512,4096]{1,0:T(8,128)(2,1)}, u32[]{:S(2)}) copy-start(bf16[512,4096]{1,0:T(8,128)(2,1)} %all-gather.9.cloned.1.call-done) | copy-start | bytes 12582916
  107.5 4.7 %copy-start.4 = (bf16[1,4096,384]{2,1,0:T(8,128)(2,1)S(1)}, bf16[1,4096,384]{2,1,0:T(8,128)(2,1)}, u32[]{:S(2)}) copy-start(bf16[1,4096,384]{2,1,0:T(8,128)(2,1)} %param.16) | copy-start | bytes 9437188
  115.3 139.9 %all-gather.11.cloned.1.call-start = ((), (), s32[]{:S(2)}) async-start(), calls=%async_computation.7 | async-start | bytes 1966080 | tf_op jit(solution)/shard_map/all_gather | solution.py:69
  126.3 78.0 %collective-permute-start.2 = (bf16[384,1024]{1,0:T(8,128)(2,1)}, bf16[384,1024]{1,0:T(8,128)(2,1)}, u32[]{:S(2)}, u32[]{:S(2)}) collective-permute-start(bf16[384,1024]{1,0:T(8,128)(2,1)} %bitcast.75), channel_id=1, source_target_pairs={{0,192},{64,0},{128,64},{192,128},{1,193},{65,1},{129,65},{193,129... | collective-permute-start | bytes 2359304 | tf_op jit(solution)/shard_map/ppermute | solution.py:17
  129.5 74.8 %collective-permute-start.1 = (bf16[384,1024]{1,0:T(8,128)(2,1)}, bf16[384,1024]{1,0:T(8,128)(2,1)}, u32[]{:S(2)}, u32[]{:S(2)}) collective-permute-start(bf16[384,1024]{1,0:T(8,128)(2,1)} %bitcast.76), channel_id=1, source_target_pairs={{0,128},{64,192},{128,0},{192,64},{1,129},{65,193},{129,1},{193,65... | collective-permute-start | bytes 2359304 | tf_op jit(solution)/shard_map/ppermute | solution.py:17
  133.7 70.6 %collective-permute-start = (bf16[384,1024]{1,0:T(8,128)(2,1)}, bf16[384,1024]{1,0:T(8,128)(2,1)}, u32[]{:S(2)}, u32[]{:S(2)}) collective-permute-start(bf16[384,1024]{1,0:T(8,128)(2,1)} %bitcast.77), channel_id=1, source_target_pairs={{0,64},{64,128},{128,192},{192,0},{1,65},{65,129},{129,193},{193,1... | collective-permute-start | bytes 2359304 | tf_op jit(solution)/shard_map/ppermute | solution.py:17
  194.2 4.7 %copy-start.2 = (bf16[512,4096]{1,0:T(8,128)(2,1)S(1)}, bf16[512,4096]{1,0:T(8,128)(2,1)}, u32[]{:S(2)}) copy-start(bf16[512,4096]{1,0:T(8,128)(2,1)} %all-gather.7.cloned.1.call-done) | copy-start | bytes 12582916
  194.2 4.7 %copy-start.5 = (bf16[1,4096,384]{2,1,0:T(8,128)(2,1)S(1)}, bf16[1,4096,384]{2,1,0:T(8,128)(2,1)}, u32[]{:S(2)}) copy-start(bf16[1,4096,384]{2,1,0:T(8,128)(2,1)} %param.16) | copy-start | bytes 9437188
  235.1 39.4 %all-to-all-start.3 = ((bf16[64,4,2,1024]{3,2,1,0:T(2,128)(2,1)}), bf16[64,4,2,1024]{3,2,1,0:T(2,128)(2,1)}, u32[]{:S(2)}, u32[]{:S(2)}) async-start(bf16[64,4,2,1024]{3,2,1,0:T(2,128)(2,1)} %bitcast.73), calls=%async_computation.3 | async-start | bytes 2097152 | tf_op jit(solution)/shard_map/all_to_all | solution.py:79
  260.4 20.0 %copy-start.1 = (f32[16,4,8]{0,2,1:T(8,128)S(1)}, f32[16,4,8]{0,2,1:T(8,128)}, u32[]{:S(2)}) copy-start(f32[16,4,8]{0,2,1:T(8,128)} %param.11) | copy-start | bytes 6148
  260.4 20.4 %copy-start.6 = (s32[16]{0:T(128)S(1)}, s32[16]{0:T(128)}, u32[]{:S(2)}) copy-start(s32[16]{0:T(128)} %param.14) | copy-start | bytes 196
  274.6 34.6 %all-to-all-start.1 = ((bf16[64,4,2,1024]{3,2,1,0:T(2,128)(2,1)}), bf16[64,4,2,1024]{3,2,1,0:T(2,128)(2,1)}, u32[]{:S(2)}, u32[]{:S(2)}) async-start(bf16[64,4,2,1024]{3,2,1,0:T(2,128)(2,1)} %bitcast.72), calls=%async_computation.1 | async-start | bytes 2097152 | tf_op jit(solution)/shard_map/all_to_all | solution.py:79
Sparse Core Ops, SparseCore 0:
  60.0 47.4 all-gather.8
  109.3 84.8 all-gather.6
  196.0 28.1 all-gather.12
  225.9 29.2 all-gather.10

commit v6 on v5

--- a/solution.py
+++ b/solution.py
@@ -7,17 +7,22 @@
 
 
 def exchange_gather(blocks, replica, replica_count):
-    pieces = [None] * replica_count
-    pieces[0] = lax.dynamic_index_in_dim(blocks, replica, 0, keepdims=False)
+    pieces = [lax.dynamic_index_in_dim(blocks, replica, 0, keepdims=False)]
     for shift in range(1, replica_count):
         outgoing = lax.dynamic_index_in_dim(
             blocks, (replica + shift) % replica_count, 0, keepdims=False
         )
         pairs = [(i, (i + shift) % replica_count) for i in range(replica_count)]
-        pieces[shift] = lax.ppermute(outgoing, "dp", pairs)
-    stacked = jnp.stack(pieces, axis=0)
-    order = (replica - lax.broadcasted_iota(jnp.int32, (replica_count,), 0)) % replica_count
-    return jnp.take(stacked, order, axis=0)
+        pieces.append(lax.ppermute(outgoing, "dp", pairs))
+    return jnp.stack(pieces, axis=0)
+
+
+def exchange_all(block, replica_count):
+    pieces = [block]
+    for shift in range(1, replica_count):
+        pairs = [(i, (i + shift) % replica_count) for i in range(replica_count)]
+        pieces.append(lax.ppermute(block, "dp", pairs))
+    return jnp.stack(pieces, axis=0)
 
 
 def body(
@@ -61,12 +66,14 @@
             (((0,), (0,)), ((), ())),
             preferred_element_type=jnp.float32,
         ).astype(jnp.bfloat16)
+        if chunk == 1:
+            down_cols, outgoing = lax.optimization_barrier((down_cols, outgoing))
         arrived = lax.all_to_all(outgoing, "expert", split_axis=0, concat_axis=0, tiled=True)
         gathered = lax.all_gather(arrived, "dp", axis=0, tiled=True)
         gate_part = jnp.dot(gathered, w_gate[0], preferred_element_type=jnp.float32)
         up_part = jnp.dot(gathered, w_up[0], preferred_element_type=jnp.float32)
         activated = (jax.nn.silu(gate_part) * up_part).astype(jnp.bfloat16)
-        hidden_all = lax.all_gather(activated, "dp", axis=0, tiled=False)
+        hidden_all = exchange_all(activated, replica_count)
         expert_cols = lax.dot_general(
             hidden_all,
             down_cols,

time: 332 us -> 326 us (0.982)
  waiting for transfers between devices: 120 us -> 101 us
  starting transfers between devices: 19.9 us -> 37.1 us
  matrix products: 38.7 us -> 33.8 us
    ppermute x3 -> x9, waiting for transfers between devices: 0.01 us -> 67.2 us  [the longest x6 44.6 us: exchange_all(): pieces.append(lax.ppermute(block, 'dp', pairs))]
    all_gather x2, waiting for transfers between devices: 65.5 us -> 9.23 us  [body(): gathered = lax.all_gather(arrived, 'dp', axis=0, tiled=True)]
    all_gather x2 -> x0, waiting for transfers between devices: 21.6 us -> none  [body(): hidden_all = lax.all_gather(activated, 'dp', axis=0, tiled=False)]
    ppermute x3 -> x9, starting transfers between devices: 3.23 us -> 15.6 us  [the longest x6 9.77 us: exchange_all(): pieces.append(lax.ppermute(block, 'dp', pairs))]
    all_to_all x2, waiting for transfers between devices: 32.9 us -> 24.4 us  [body(): lax.all_to_all(by_source, 'expert', split_axis=0, concat_axis=0, tiled=True)]
    all_to_all x2, starting transfers between devices: 16.6 us -> 21.5 us  [body(): lax.all_to_all(by_source, 'expert', split_axis=0, concat_axis=0, tiled=True)]
    another operation x5 -> x2, local copies, waits for them, and re-layouts: 13.3 us -> 17.8 us
    gather x1 -> x0, local copies, waits for them, and re-layouts: 4.42 us -> none  [exchange_gather(): return jnp.take(stacked, order, axis=0)]
  transfers between devices with their start and end apart: 9 -> 13, of which waited for: 6 -> 11; matrix products, arithmetic and copies ran while one was open for 21% -> 15% of each run, Pallas kernels for 0% -> 0%
where the time goes in v6:
time: 326 us; the launch traced here: 324 us
  waiting for transfers between devices  101 us (31%)
  blocking collectives  84.9 us (26%)
  local copies, waits for them, and re-layouts  49.2 us (15%)
  starting transfers between devices  37.1 us (11%)
  matrix products  33.8 us (10%)
  between operations  14.3 us (4%)
  other arithmetic  4.31 us (1%)
    all_to_all x2, blocking collectives, body(): lax.all_to_all(outgoing, 'expert', split_axis=0, concat_axis=0, tiled=True)  75.5 us
    ppermute x6, waiting for transfers between devices, exchange_all(): pieces.append(lax.ppermute(block, 'dp', pairs))  44.6 us
    all_to_all x2, waiting for transfers between devices, body(): lax.all_to_all(by_source, 'expert', split_axis=0, concat_axis=0, tiled=True)  24.4 us
    ppermute x3, waiting for transfers between devices, exchange_gather(): pieces.append(lax.ppermute(outgoing, 'dp', pairs))  22.6 us
    all_to_all x2, starting transfers between devices, body(): lax.all_to_all(by_source, 'expert', split_axis=0, concat_axis=0, tiled=True)  21.5 us
    another operation x1, local copies, waits for them, and re-layouts  11.5 us
    reshape x4, local copies, waits for them, and re-layouts, body(): expert_cols.reshape(replica_count, expert_count, sub, columns)  11.2 us
    ppermute x6, starting transfers between devices, exchange_all(): pieces.append(lax.ppermute(block, 'dp', pairs))  9.77 us
  transfers between devices with their start and end apart: 13, of which 11 were waited for; matrix products, arithmetic and copies ran while one was open for 15% of the time, Pallas kernels for 0%

profile of v6, /device:TPU:2, one launch (start us, length us, event | category | flops | bytes accessed | tf_op | source)
XLA Modules:
  0.0 324.5 jit_solution(1667784092942975115)
XLA Ops:
  6.5 6.3 %reshape_squeeze.3 = bf16[384,4,1024]{2,1,0:T(4,128)(2,1)} reshape(bf16[1,384,4096]{2,1,0:T(8,128)(2,1)} %param.17) | data formatting | bytes 6291456 | tf_op jit(solution)/shard_map/reshape;squeeze | solution.py:42
  12.9 11.5 %constant_dynamic-slice_fusion.3 = (bf16[384,1,1024]{2,1,0:T(2,128)(2,1)}, bf16[384,1,1024]{2,1,0:T(2,128)(2,1)S(1)}, bf16[384,1,1024]{2,1,0:T(2,128)(2,1)S(1)}, bf16[384,1,1024]{2,1,0:T(2,128)(2,1)S(1)}) fusion(bf16[384,4,1024]{2,1,0:T(4,128)(2,1)} %reshape_squeeze.3, s32[]{:T(128)S(6)} %select_n.58, s32[]{:T(128)S(6)} %select_n.62, s32[]{:T(128)S(6)} %select_n.60, ...), kind=kLoop, calls=%fused_computation.85 | loop fusion | bytes 6291472 | tf_op jit(solution)/shard_map/dynamic-slice
  24.3 1.2 copy.75
  25.5 1.6 collective-permute-start.3
  27.1 1.2 copy.74
  28.3 2.9 collective-permute-start.4
  31.2 1.2 copy.73
  32.3 1.3 collective-permute-start.5
  33.7 2.6 copy.76
  37.7 2.0 reshape.216
  39.9 2.4 convolution_convert_fusion
  42.4 4.0 %collective-permute-done.3 = bf16[384,1024]{1,0:T(8,128)(2,1)} collective-permute-done((bf16[384,1024]{1,0:T(8,128)(2,1)}, bf16[384,1024]{1,0:T(8,128)(2,1)}, u32[]{:S(2)}, u32[]{:S(2)}) %collective-permute-start.3) | collective-permute-done | bytes 786464 | tf_op jit(solution)/shard_map/ppermute | solution.py:16
  46.4 18.0 %collective-permute-done.4 = bf16[384,1024]{1,0:T(8,128)(2,1)} collective-permute-done((bf16[384,1024]{1,0:T(8,128)(2,1)}, bf16[384,1024]{1,0:T(8,128)(2,1)}, u32[]{:S(2)}, u32[]{:S(2)}) %collective-permute-start.4) | collective-permute-done | bytes 786464 | tf_op jit(solution)/shard_map/ppermute | solution.py:16
  65.0 3.3 %pad_maximum_fusion = bf16[4,384,1024]{2,1,0:T(8,128)(2,1)} fusion(bf16[1,384,1024]{2,1,0:T(8,128)(2,1)} %bitcast.15, bf16[1,384,1024]{2,1,0:T(8,128)(2,1)} %bitcast.13, bf16[1,384,1024]{2,1,0:T(8,128)(2,1)} %bitcast.11, bf16[1,384,1024]{2,1,0:T(8,128)(2,1)} %bitcast.83), kind=kLoop, calls=%fused_computation.3 | loop fusion | flops 4718592 | bytes 6291456 | tf_op jit(solution)/shard_map/stack | solution.py:17
  68.3 2.5 all_to_all.29
  70.8 40.9 %all_to_all.39 = bf16[64,2,4096]{2,1,0:T(2,128)(2,1)} all-to-all(bf16[64,2,4096]{2,1,0:T(2,128)(2,1)} %all_to_all.29), channel_id=1, replica_groups=mesh['dp'=4,'expert'=64] {'expert'}, dimensions={0} | all-to-all | bytes 2097152 | tf_op jit(solution)/shard_map/all_to_all | solution.py:71
  111.7 2.3 all_to_all.31
  114.1 2.4 convolution_convert_fusion.1
  116.6 2.5 all_to_all.25
  119.1 34.6 %all_to_all.40 = bf16[64,2,4096]{2,1,0:T(2,128)(2,1)} all-to-all(bf16[64,2,4096]{2,1,0:T(2,128)(2,1)} %all_to_all.25), channel_id=1, replica_groups=mesh['dp'=4,'expert'=64] {'expert'}, dimensions={0} | all-to-all | bytes 2097152 | tf_op jit(solution)/shard_map/all_to_all | solution.py:71
  153.7 2.3 all_to_all.27
  156.0 5.6 %all-gather.5.cloned.1.call-done = bf16[512,4096]{1,0:T(8,128)(2,1)} async-done(((bf16[128,4096]{1,0:T(8,128)(2,1)}), bf16[512,4096]{1,0:T(8,128)(2,1)}) %all-gather.5.cloned.1.call-update) | async-done | bytes 4194320 | tf_op jit(solution)/shard_map/all_gather | solution.py:72
  161.6 4.7 %fusion.4 = f32[512,384]{1,0:T(8,128)S(1)} fusion(bf16[512,4096]{1,0:T(8,128)(2,1)} %all-gather.5.cloned.1.call-done, bf16[1,4096,384]{2,1,0:T(8,128)(2,1)S(1)} %copy-done), kind=kOutput, calls=%fused_computation.8 | convolution fusion | flops 1610612736 | bytes 8126464 | tf_op jit(solution)/shard_map/dot_general | solution.py:73
  166.3 2.3 fusion.28
  169.5 1.7 collective-permute-start.7
  171.2 2.1 collective-permute-start.8
  173.4 12.8 %collective-permute-done.6 = bf16[512,384]{1,0:T(8,128)(2,1)S(1)} collective-permute-done((bf16[512,384]{1,0:T(8,128)(2,1)S(1)}, bf16[512,384]{1,0:T(8,128)(2,1)S(1)}, u32[]{:S(2)}, u32[]{:S(2)}) %collective-permute-start.6) | collective-permute-done | bytes 393248 | tf_op jit(solution)/shard_map/ppermute | solution.py:24
  186.1 11.1 %collective-permute-done.7 = bf16[512,384]{1,0:T(8,128)(2,1)S(1)} collective-permute-done((bf16[512,384]{1,0:T(8,128)(2,1)S(1)}, bf16[512,384]{1,0:T(8,128)(2,1)S(1)}, u32[]{:S(2)}, u32[]{:S(2)}) %collective-permute-start.7) | collective-permute-done | bytes 393248 | tf_op jit(solution)/shard_map/ppermute | solution.py:24
  197.3 3.8 %collective-permute-done.8 = bf16[512,384]{1,0:T(8,128)(2,1)S(1)} collective-permute-done((bf16[512,384]{1,0:T(8,128)(2,1)S(1)}, bf16[512,384]{1,0:T(8,128)(2,1)S(1)}, u32[]{:S(2)}, u32[]{:S(2)}) %collective-permute-start.8) | collective-permute-done | bytes 393248 | tf_op jit(solution)/shard_map/ppermute | solution.py:24
  201.1 2.8 bitcast_convert_fusion
  203.9 2.2 reshape.218
  206.1 3.4 %copy.71 = bf16[4,64,2,1024]{3,2,0,1:T(2,128)(2,1)} copy(bf16[4,64,2,1024]{3,2,1,0:T(2,128)(2,1)} %reshape.218) | data formatting | bytes 2097152 | tf_op jit(solution)/shard_map/reshape | solution.py:83
  209.5 10.7 %all-to-all-start.3 = ((bf16[64,4,2,1024]{3,2,1,0:T(2,128)(2,1)}), bf16[64,4,2,1024]{3,2,1,0:T(2,128)(2,1)}, u32[]{:S(2)}, u32[]{:S(2)}) async-start(bf16[64,4,2,1024]{3,2,1,0:T(2,128)(2,1)} %bitcast.81), calls=%async_computation.3 | async-start | bytes 2097152 | tf_op jit(solution)/shard_map/all_to_all | solution.py:86
  220.2 3.6 %all-gather.3.cloned.1.call-done = bf16[512,4096]{1,0:T(8,128)(2,1)} async-done(((bf16[128,4096]{1,0:T(8,128)(2,1)}), bf16[512,4096]{1,0:T(8,128)(2,1)}) %all-gather.3.cloned.1.call-update) | async-done | bytes 4194320 | tf_op jit(solution)/shard_map/all_gather | solution.py:72
  223.9 4.7 %fusion.6 = f32[512,384]{1,0:T(8,128)S(1)} fusion(bf16[512,4096]{1,0:T(8,128)(2,1)} %all-gather.3.cloned.1.call-done, bf16[1,4096,384]{2,1,0:T(8,128)(2,1)S(1)} %copy-done), kind=kOutput, calls=%fused_computation.10 | convolution fusion | flops 1610612736 | bytes 8126464 | tf_op jit(solution)/shard_map/dot_general | solution.py:73
  228.6 2.3 fusion.31
  230.9 1.7 collective-permute-start
  232.6 2.7 collective-permute-start.1
  235.9 7.6 %collective-permute-done = bf16[512,384]{1,0:T(8,128)(2,1)S(1)} collective-permute-done((bf16[512,384]{1,0:T(8,128)(2,1)S(1)}, bf16[512,384]{1,0:T(8,128)(2,1)S(1)}, u32[]{:S(2)}, u32[]{:S(2)}) %collective-permute-start) | collective-permute-done | bytes 393248 | tf_op jit(solution)/shard_map/ppermute | solution.py:24
  243.5 9.3 %collective-permute-done.1 = bf16[512,384]{1,0:T(8,128)(2,1)S(1)} collective-permute-done((bf16[512,384]{1,0:T(8,128)(2,1)S(1)}, bf16[512,384]{1,0:T(8,128)(2,1)S(1)}, u32[]{:S(2)}, u32[]{:S(2)}) %collective-permute-start.1) | collective-permute-done | bytes 393248 | tf_op jit(solution)/shard_map/ppermute | solution.py:24
  252.8 4.4 %bitcast_convert_fusion.1 = bf16[512,1024]{1,0:T(8,128)(2,1)} fusion(bf16[1,512,384]{2,1,0:T(8,128)(2,1)S(1)} %bitcast.95, bf16[1,512,384]{2,1,0:T(8,128)(2,1)S(1)} %bitcast.93, bf16[1,512,384]{2,1,0:T(8,128)(2,1)S(1)} %bitcast.91, bf16[1,512,384]{2,1,0:T(8,128)(2,1)S(1)} %bitcast.89, bf16[1,384,1024]{2,1,0:T(8,128)(2,1)} %bitcast.15, ...), kind=kOutput, calls=%fused_computation.13 | convolution fusion | flops 1618214912 | bytes 5767168 | tf_op jit(solution)/shard_map/dot_general | solution.py:77
  257.2 2.3 reshape.217
  259.5 3.4 %copy.72 = bf16[4,64,2,1024]{3,2,0,1:T(2,128)(2,1)} copy(bf16[4,64,2,1024]{3,2,1,0:T(2,128)(2,1)} %reshape.217) | data formatting | bytes 2097152 | tf_op jit(solution)/shard_map/reshape | solution.py:83
  262.9 10.7 %all-to-all-start.1 = ((bf16[64,4,2,1024]{3,2,1,0:T(2,128)(2,1)}), bf16[64,4,2,1024]{3,2,1,0:T(2,128)(2,1)}, u32[]{:S(2)}, u32[]{:S(2)}) async-start(bf16[64,4,2,1024]{3,2,1,0:T(2,128)(2,1)} %bitcast.82), calls=%async_computation.1 | async-start | bytes 2097152 | tf_op jit(solution)/shard_map/all_to_all | solution.py:86
  274.2 3.7 %convolution_bitcast_fusion = f32[64,1024]{1,0:T(8,128)} fusion(bf16[64,4,2,1024]{3,2,1,0:T(2,128)(2,1)} %all-to-all-done.3, s32[4,2]{1,0:T(4,128)S(1)} %iota_add_fusion, f32[64,64]{1,0:T(8,128)S(1)} %select_reduce_fusion, s32[64,64]{1,0:T(8,128)S(1)} %sub.20, pred[64,64]{1,0:T(8,128)(4,1)S(1)} %broadcast_compare_fusion), kind=kOutput, calls=%fused_computation.32 | convolution fusion | flops 402751488 | bytes 1347616 | tf_op jit(solution)/shard_map/dot_general | solution.py:93
  277.9 24.4 %all-to-all-done.1 = bf16[64,4,2,1024]{3,2,1,0:T(2,128)(2,1)} async-done(((bf16[64,4,2,1024]{3,2,1,0:T(2,128)(2,1)}), bf16[64,4,2,1024]{3,2,1,0:T(2,128)(2,1)}, u32[]{:S(2)}, u32[]{:S(2)}) %all-to-all-start.1) | async-done | bytes 1048608 | tf_op jit(solution)/shard_map/all_to_all | solution.py:86
  302.3 3.7 %fusion.34 = f32[64,1024]{1,0:T(8,128)} fusion(f32[64,1024]{1,0:T(8,128)} %convolution_bitcast_fusion, bf16[64,4,2,1024]{3,2,1,0:T(2,128)(2,1)} %all-to-all-done.1, f32[64,64]{1,0:T(8,128)S(1)} %select_reduce_fusion, s32[4,2]{1,0:T(4,128)S(1)} %iota_add_fusion.1, s32[64,64]{1,0:T(8,128)S(1)} %sub.20, pred[64,64]{1,0:T(8,128)(4,1)S(1)} %broadcast_compare_fusion), kind=kOutput, calls=%fused_computation.34 | convolution fusion | flops 402817024 | bytes 1609760 | tf_op jit(solution)/shard_map/dot_general | solution.py:93
  307.5 9.4 %all_to_all.41 = bf16[4,4,4,1024]{3,2,1,0:T(4,128)(2,1)S(1)} all-to-all(bf16[4,4,4,1024]{3,2,1,0:T(4,128)(2,1)S(1)} %reshape.220), channel_id=1, replica_groups=mesh['dp'=4,'expert'=64] {'dp'}, dimensions={0} | all-to-all | bytes 262144 | tf_op jit(solution)/shard_map/all_to_all | solution.py:111
  (57 shorter events, 5.9 us)
Async XLA Ops:
  6.5 155.0 %copy-start = (bf16[1,4096,384]{2,1,0:T(8,128)(2,1)S(1)}, bf16[1,4096,384]{2,1,0:T(8,128)(2,1)}, u32[]{:S(2)}) copy-start(bf16[1,4096,384]{2,1,0:T(8,128)(2,1)} %param.15) | copy-start | bytes 9437188
  6.5 155.0 %all-gather.5.cloned.1.call-start = ((), (), s32[]{:S(2)}) async-start(), calls=%async_computation.6 | async-start | bytes 5242880 | tf_op jit(solution)/shard_map/all_gather | solution.py:72
  25.5 20.9 %collective-permute-start.3 = (bf16[384,1024]{1,0:T(8,128)(2,1)}, bf16[384,1024]{1,0:T(8,128)(2,1)}, u32[]{:S(2)}, u32[]{:S(2)}) collective-permute-start(bf16[384,1024]{1,0:T(8,128)(2,1)} %bitcast.79), channel_id=1, source_target_pairs={{0,64},{64,128},{128,192},{192,0},{1,65},{65,129},{129,193},{193,1... | collective-permute-start | bytes 2359304 | tf_op jit(solution)/shard_map/ppermute | solution.py:16
  27.1 9.2 %copy-start.4 = (s32[16,4,8]{0,2,1:T(8,128)S(1)}, s32[16,4,8]{0,2,1:T(8,128)}, u32[]{:S(2)}) copy-start(s32[16,4,8]{0,2,1:T(8,128)} %param.10) | copy-start | bytes 6148
  27.1 9.9 %copy-start.5 = (s32[16]{0:T(128)S(1)}, s32[16]{0:T(128)}, u32[]{:S(2)}) copy-start(s32[16]{0:T(128)} %param.12) | copy-start | bytes 196
  28.3 36.2 %collective-permute-start.4 = (bf16[384,1024]{1,0:T(8,128)(2,1)}, bf16[384,1024]{1,0:T(8,128)(2,1)}, u32[]{:S(2)}, u32[]{:S(2)}) collective-permute-start(bf16[384,1024]{1,0:T(8,128)(2,1)} %bitcast.78), channel_id=1, source_target_pairs={{0,128},{64,192},{128,0},{192,64},{1,129},{65,193},{129,1},{193,65... | collective-permute-start | bytes 2359304 | tf_op jit(solution)/shard_map/ppermute | solution.py:16
  32.3 32.7 %collective-permute-start.5 = (bf16[384,1024]{1,0:T(8,128)(2,1)}, bf16[384,1024]{1,0:T(8,128)(2,1)}, u32[]{:S(2)}, u32[]{:S(2)}) collective-permute-start(bf16[384,1024]{1,0:T(8,128)(2,1)} %bitcast.77), channel_id=1, source_target_pairs={{0,192},{64,0},{128,64},{192,128},{1,193},{65,1},{129,65},{193,129... | collective-permute-start | bytes 2359304 | tf_op jit(solution)/shard_map/ppermute | solution.py:16
  114.0 109.9 %all-gather.3.cloned.1.call-start = ((), (), s32[]{:S(2)}) async-start(), calls=%async_computation.5 | async-start | bytes 5242880 | tf_op jit(solution)/shard_map/all_gather | solution.py:72
  161.6 4.7 %copy-start.7 = (bf16[512,4096]{1,0:T(8,128)(2,1)S(1)}, bf16[512,4096]{1,0:T(8,128)(2,1)}, u32[]{:S(2)}) copy-start(bf16[512,4096]{1,0:T(8,128)(2,1)} %all-gather.5.cloned.1.call-done) | copy-start | bytes 12582916
  161.6 4.7 %copy-start.8 = (bf16[1,4096,384]{2,1,0:T(8,128)(2,1)S(1)}, bf16[1,4096,384]{2,1,0:T(8,128)(2,1)}, u32[]{:S(2)}) copy-start(bf16[1,4096,384]{2,1,0:T(8,128)(2,1)} %param.16) | copy-start | bytes 9437188
  166.2 34.8 %copy-start.1 = (bf16[4,384,1024]{2,1,0:T(8,128)(2,1)S(1)}, bf16[4,384,1024]{2,1,0:T(8,128)(2,1)}, u32[]{:S(2)}) copy-start(bf16[4,384,1024]{2,1,0:T(8,128)(2,1)} %pad_maximum_fusion) | copy-start | bytes 9437188
  168.6 17.5 %collective-permute-start.6 = (bf16[512,384]{1,0:T(8,128)(2,1)S(1)}, bf16[512,384]{1,0:T(8,128)(2,1)S(1)}, u32[]{:S(2)}, u32[]{:S(2)}) collective-permute-start(bf16[512,384]{1,0:T(8,128)(2,1)S(1)} %fusion.28), channel_id=1, source_target_pairs={{0,64},{64,128},{128,192},{192,0},{1,65},{65,129},{129,193},{193,1... | collective-permute-start | bytes 1179656 | tf_op jit(solution)/shard_map/ppermute | solution.py:24
  169.5 27.8 %collective-permute-start.7 = (bf16[512,384]{1,0:T(8,128)(2,1)S(1)}, bf16[512,384]{1,0:T(8,128)(2,1)S(1)}, u32[]{:S(2)}, u32[]{:S(2)}) collective-permute-start(bf16[512,384]{1,0:T(8,128)(2,1)S(1)} %fusion.28), channel_id=1, source_target_pairs={{0,128},{64,192},{128,0},{192,64},{1,129},{65,193},{129,1},{193,65... | collective-permute-start | bytes 1179656 | tf_op jit(solution)/shard_map/ppermute | solution.py:24
  171.2 29.8 %collective-permute-start.8 = (bf16[512,384]{1,0:T(8,128)(2,1)S(1)}, bf16[512,384]{1,0:T(8,128)(2,1)S(1)}, u32[]{:S(2)}, u32[]{:S(2)}) collective-permute-start(bf16[512,384]{1,0:T(8,128)(2,1)S(1)} %fusion.28), channel_id=1, source_target_pairs={{0,192},{64,0},{128,64},{192,128},{1,193},{65,1},{129,65},{193,129... | collective-permute-start | bytes 1179656 | tf_op jit(solution)/shard_map/ppermute | solution.py:24
  209.5 53.4 %all-to-all-start.3 = ((bf16[64,4,2,1024]{3,2,1,0:T(2,128)(2,1)}), bf16[64,4,2,1024]{3,2,1,0:T(2,128)(2,1)}, u32[]{:S(2)}, u32[]{:S(2)}) async-start(bf16[64,4,2,1024]{3,2,1,0:T(2,128)(2,1)} %bitcast.81), calls=%async_computation.3 | async-start | bytes 2097152 | tf_op jit(solution)/shard_map/all_to_all | solution.py:86
  223.9 4.7 %copy-start.6 = (bf16[512,4096]{1,0:T(8,128)(2,1)S(1)}, bf16[512,4096]{1,0:T(8,128)(2,1)}, u32[]{:S(2)}) copy-start(bf16[512,4096]{1,0:T(8,128)(2,1)} %all-gather.3.cloned.1.call-done) | copy-start | bytes 12582916
  223.9 4.7 %copy-start.9 = (bf16[1,4096,384]{2,1,0:T(8,128)(2,1)S(1)}, bf16[1,4096,384]{2,1,0:T(8,128)(2,1)}, u32[]{:S(2)}) copy-start(bf16[1,4096,384]{2,1,0:T(8,128)(2,1)} %param.16) | copy-start | bytes 9437188
  228.6 24.2 %copy-start.2 = (bf16[384,1,1024]{2,0,1:T(8,128)(2,1)S(1)}, bf16[384,1,1024]{2,0,1:T(8,128)(2,1)}, u32[]{:S(2)}) copy-start(bf16[384,1,1024]{2,0,1:T(8,128)(2,1)} %copy.76) | copy-start | bytes 2359300
  230.9 12.6 %collective-permute-start = (bf16[512,384]{1,0:T(8,128)(2,1)S(1)}, bf16[512,384]{1,0:T(8,128)(2,1)S(1)}, u32[]{:S(2)}, u32[]{:S(2)}) collective-permute-start(bf16[512,384]{1,0:T(8,128)(2,1)S(1)} %fusion.31), channel_id=1, source_target_pairs={{0,64},{64,128},{128,192},{192,0},{1,65},{65,129},{129,193},{193,1... | collective-permute-start | bytes 1179656 | tf_op jit(solution)/shard_map/ppermute | solution.py:24
  232.6 20.2 %collective-permute-start.1 = (bf16[512,384]{1,0:T(8,128)(2,1)S(1)}, bf16[512,384]{1,0:T(8,128)(2,1)S(1)}, u32[]{:S(2)}, u32[]{:S(2)}) collective-permute-start(bf16[512,384]{1,0:T(8,128)(2,1)S(1)} %fusion.31), channel_id=1, source_target_pairs={{0,128},{64,192},{128,0},{192,64},{1,129},{65,193},{129,1},{193,65... | collective-permute-start | bytes 1179656 | tf_op jit(solution)/shard_map/ppermute | solution.py:24
  235.3 17.5 %collective-permute-start.2 = (bf16[512,384]{1,0:T(8,128)(2,1)S(1)}, bf16[512,384]{1,0:T(8,128)(2,1)S(1)}, u32[]{:S(2)}, u32[]{:S(2)}) collective-permute-start(bf16[512,384]{1,0:T(8,128)(2,1)S(1)} %fusion.31), channel_id=1, source_target_pairs={{0,192},{64,0},{128,64},{192,128},{1,193},{65,1},{129,65},{193,129... | collective-permute-start | bytes 1179656 | tf_op jit(solution)/shard_map/ppermute | solution.py:24
  257.2 16.4 %copy-start.3 = (f32[16,4,8]{0,2,1:T(8,128)S(1)}, f32[16,4,8]{0,2,1:T(8,128)}, u32[]{:S(2)}) copy-start(f32[16,4,8]{0,2,1:T(8,128)} %param.11) | copy-start | bytes 6148
  257.2 16.8 %copy-start.10 = (s32[16]{0:T(128)S(1)}, s32[16]{0:T(128)}, u32[]{:S(2)}) copy-start(s32[16]{0:T(128)} %param.14) | copy-start | bytes 196
  262.9 39.4 %all-to-all-start.1 = ((bf16[64,4,2,1024]{3,2,1,0:T(2,128)(2,1)}), bf16[64,4,2,1024]{3,2,1,0:T(2,128)(2,1)}, u32[]{:S(2)}, u32[]{:S(2)}) async-start(bf16[64,4,2,1024]{3,2,1,0:T(2,128)(2,1)} %bitcast.82), calls=%async_computation.1 | async-start | bytes 2097152 | tf_op jit(solution)/shard_map/all_to_all | solution.py:86
Sparse Core Ops, SparseCore 0:
  114.2 47.3 all-gather.4
  163.4 60.4 all-gather.2

commit v7 on v6

--- a/solution.py
+++ b/solution.py
@@ -6,15 +6,15 @@
 MOST_BASE = 16
 
 
-def exchange_gather(blocks, replica, replica_count):
-    pieces = [lax.dynamic_index_in_dim(blocks, replica, 0, keepdims=False)]
+def exchange_columns(matrix, replica, replica_count):
+    width = matrix.shape[1] // replica_count
+    pieces = [lax.dynamic_slice_in_dim(matrix, replica * width, width, axis=1)]
     for shift in range(1, replica_count):
-        outgoing = lax.dynamic_index_in_dim(
-            blocks, (replica + shift) % replica_count, 0, keepdims=False
-        )
+        start = ((replica + shift) % replica_count) * width
+        outgoing = lax.dynamic_slice_in_dim(matrix, start, width, axis=1)
         pairs = [(i, (i + shift) % replica_count) for i in range(replica_count)]
         pieces.append(lax.ppermute(outgoing, "dp", pairs))
-    return jnp.stack(pieces, axis=0)
+    return pieces
 
 
 def exchange_all(block, replica_count):
@@ -22,7 +22,7 @@
     for shift in range(1, replica_count):
         pairs = [(i, (i + shift) % replica_count) for i in range(replica_count)]
         pieces.append(lax.ppermute(block, "dp", pairs))
-    return jnp.stack(pieces, axis=0)
+    return pieces
 
 
 def body(
@@ -39,8 +39,7 @@
     slot_count = min(tokens, max(MOST_BASE, 2 * tokens * top_count // expert_count))
     slot_count = -(-slot_count // replica_count) * replica_count
     part = slot_count // replica_count
-    down_blocks = w_down[0].reshape(hidden_part, replica_count, columns).transpose(1, 0, 2)
-    down_cols = exchange_gather(down_blocks, replica, replica_count)
+    down_cols = exchange_columns(w_down[0], replica, replica_count)
     step_ids = lax.broadcasted_iota(jnp.int32, (row_count, step_count), 1)
     live_mask = ((step_ids < finish_step[:, None]) & (group_keep[0] == 1)).reshape(tokens)
     gate_share = route_weight / jnp.sum(route_weight, axis=2, keepdims=True)
@@ -66,20 +65,20 @@
             (((0,), (0,)), ((), ())),
             preferred_element_type=jnp.float32,
         ).astype(jnp.bfloat16)
-        if chunk == 1:
-            down_cols, outgoing = lax.optimization_barrier((down_cols, outgoing))
         arrived = lax.all_to_all(outgoing, "expert", split_axis=0, concat_axis=0, tiled=True)
+        if chunk == 0:
+            down_cols, arrived = lax.optimization_barrier((down_cols, arrived))
         gathered = lax.all_gather(arrived, "dp", axis=0, tiled=True)
         gate_part = jnp.dot(gathered, w_gate[0], preferred_element_type=jnp.float32)
         up_part = jnp.dot(gathered, w_up[0], preferred_element_type=jnp.float32)
         activated = (jax.nn.silu(gate_part) * up_part).astype(jnp.bfloat16)
         hidden_all = exchange_all(activated, replica_count)
-        expert_cols = lax.dot_general(
-            hidden_all,
-            down_cols,
-            (((0, 2), (0, 1)), ((), ())),
-            preferred_element_type=jnp.float32,
-        ).astype(jnp.bfloat16)
+        expert_cols = jnp.dot(hidden_all[0], down_cols[0], preferred_element_type=jnp.float32)
+        for shift in range(1, replica_count):
+            expert_cols = expert_cols + jnp.dot(
+                hidden_all[shift], down_cols[shift], preferred_element_type=jnp.float32
+            )
+        expert_cols = expert_cols.astype(jnp.bfloat16)
         by_source = expert_cols.reshape(replica_count, expert_count, sub, columns).transpose(
             1, 0, 2, 3
         )

time: 326 us -> 334 us (1.025)
  waiting for transfers between devices: 101 us -> 149 us
  blocking collectives: 84.9 us -> 49.3 us
  local copies, waits for them, and re-layouts: 49.2 us -> 29.9 us
  matrix products: 33.8 us -> 46.5 us
  starting transfers between devices: 37.1 us -> 42.1 us
    all_gather x2, waiting for transfers between devices: 9.23 us -> 51 us  [body(): gathered = lax.all_gather(arrived, 'dp', axis=0, tiled=True)]
    all_to_all x2 -> x1, blocking collectives: 75.5 us -> 40.9 us  [body(): lax.all_to_all(outgoing, 'expert', split_axis=0, concat_axis=0, tiled=True)]
    ppermute x6, waiting for transfers between devices: 44.6 us -> 14.5 us  [exchange_all(): pieces.append(lax.ppermute(block, 'dp', pairs))]
    all_to_all x0 -> x1, waiting for transfers between devices: none -> 19.1 us  [body(): lax.all_to_all(outgoing, 'expert', split_axis=0, concat_axis=0, tiled=True)]
    another operation x2 -> x0, local copies, waits for them, and re-layouts: 17.8 us -> none
    ppermute x3, waiting for transfers between devices: 22.6 us -> 39.4 us  [exchange_columns(): pieces.append(lax.ppermute(outgoing, 'dp', pairs))]
    dot_general x2 -> x8, matrix products: 7.23 us -> 15.8 us  [the longest x6 13.3 us: body(): jnp.dot(hidden_all[shift], down_cols[shift], preferred_element_type=jnp.f...]
    all_to_all x0 -> x1, starting transfers between devices: none -> 5.85 us  [body(): lax.all_to_all(outgoing, 'expert', split_axis=0, concat_axis=0, tiled=True)]
  transfers between devices with their start and end apart: 13 -> 14, of which waited for: 11 -> 7; matrix products, arithmetic and copies ran while one was open for 15% -> 14% of each run, Pallas kernels for 0% -> 0%
where the time goes in v7:
time: 334 us; the launch traced here: 333 us
  waiting for transfers between devices  149 us (45%)
  blocking collectives  49.3 us (15%)
  matrix products  46.5 us (14%)
  starting transfers between devices  42.1 us (13%)
  local copies, waits for them, and re-layouts  29.9 us (9%)
  between operations  14.4 us (4%)
    all_gather x2, waiting for transfers between devices, body(): gathered = lax.all_gather(arrived, 'dp', axis=0, tiled=True)  51 us
    all_to_all x1, blocking collectives, body(): lax.all_to_all(outgoing, 'expert', split_axis=0, concat_axis=0, tiled=True)  40.9 us
    ppermute x3, waiting for transfers between devices, exchange_columns(): pieces.append(lax.ppermute(outgoing, 'dp', pairs))  39.4 us
    all_to_all x2, waiting for transfers between devices, body(): lax.all_to_all(by_source, 'expert', split_axis=0, concat_axis=0, tiled=True)  25.1 us
    all_to_all x2, starting transfers between devices, body(): lax.all_to_all(by_source, 'expert', split_axis=0, concat_axis=0, tiled=True)  21.2 us
    all_to_all x1, waiting for transfers between devices, body(): lax.all_to_all(outgoing, 'expert', split_axis=0, concat_axis=0, tiled=True)  19.1 us
    ppermute x6, waiting for transfers between devices, exchange_all(): pieces.append(lax.ppermute(block, 'dp', pairs))  14.5 us
    dot_general x6, matrix products, body(): jnp.dot(hidden_all[shift], down_cols[shift], preferred_element_type=jnp.f...  13.3 us
  transfers between devices with their start and end apart: 14, of which 7 were waited for; matrix products, arithmetic and copies ran while one was open for 14% of the time, Pallas kernels for 0%

profile of v7, /device:TPU:2, one launch (start us, length us, event | category | flops | bytes accessed | tf_op | source)
XLA Modules:
  0.0 332.9 jit_solution(12972941955087734242)
XLA Ops:
  6.5 0.9 copy.29
  8.2 0.7 fusion.40
  9.5 2.0 reshape.213
  11.7 2.4 convolution_convert_fusion
  14.1 2.5 all_to_all.29
  16.7 40.9 %all_to_all.39 = bf16[64,2,4096]{2,1,0:T(2,128)(2,1)} all-to-all(bf16[64,2,4096]{2,1,0:T(2,128)(2,1)} %all_to_all.29), channel_id=1, replica_groups=mesh['dp'=4,'expert'=64] {'expert'}, dimensions={0} | all-to-all | bytes 2097152 | tf_op jit(solution)/shard_map/all_to_all | solution.py:68
  57.6 2.3 all_to_all.31
  59.9 2.4 convolution_convert_fusion.1
  62.4 2.5 all_to_all.25
  64.9 5.8 %all-to-all-start = ((bf16[64,2,4096]{2,1,0:T(2,128)(2,1)}), bf16[64,2,4096]{2,1,0:T(2,128)(2,1)}, u32[]{:S(2)}, u32[]{:S(2)}) async-start(bf16[64,2,4096]{2,1,0:T(2,128)(2,1)} %all_to_all.25), calls=%async_computation | async-start | bytes 2097152 | tf_op jit(solution)/shard_map/all_to_all | solution.py:68
  70.9 3.7 %dynamic-slice_bitcast_fusion = (bf16[384,1024]{1,0:T(8,128)(2,1)}, bf16[384,1024]{1,0:T(8,128)(2,1)}, bf16[384,1024]{1,0:T(8,128)(2,1)}, bf16[384,1024]{1,0:T(8,128)(2,1)}) fusion(bf16[1,384,4096]{2,1,0:T(8,128)(2,1)} %param.17, s32[]{:T(128)S(6)} %select_n.63, s32[]{:T(128)S(6)} %select_n.59, s32[]{:T(128)S(6)} %select_n.57, s32[]{:T(128)S(6)} %select_n.61), kind=kLoop, calls=%fused_computation.24 | loop fusion | bytes 6291472 | tf_op jit(solution)/shard_map/dynamic_slice | solution.py:14
  74.6 1.6 collective-permute-start
  76.2 2.9 collective-permute-start.1
  79.0 1.4 collective-permute-start.2
  80.4 19.1 %all-to-all-done = bf16[64,2,4096]{2,1,0:T(2,128)(2,1)} async-done(((bf16[64,2,4096]{2,1,0:T(2,128)(2,1)}), bf16[64,2,4096]{2,1,0:T(2,128)(2,1)}, u32[]{:S(2)}, u32[]{:S(2)}) %all-to-all-start) | async-done | bytes 1048608 | tf_op jit(solution)/shard_map/all_to_all | solution.py:68
  99.5 2.3 all_to_all.27
  101.8 11.3 %collective-permute-done = bf16[384,1024]{1,0:T(8,128)(2,1)} collective-permute-done((bf16[384,1024]{1,0:T(8,128)(2,1)}, bf16[384,1024]{1,0:T(8,128)(2,1)}, u32[]{:S(2)}, u32[]{:S(2)}) %collective-permute-start) | collective-permute-done | bytes 786464 | tf_op jit(solution)/shard_map/ppermute | solution.py:16
  113.1 28.1 %collective-permute-done.1 = bf16[384,1024]{1,0:T(8,128)(2,1)} collective-permute-done((bf16[384,1024]{1,0:T(8,128)(2,1)}, bf16[384,1024]{1,0:T(8,128)(2,1)}, u32[]{:S(2)}, u32[]{:S(2)}) %collective-permute-start.1) | collective-permute-done | bytes 786464 | tf_op jit(solution)/shard_map/ppermute | solution.py:16
  141.3 4.7 %fusion.4 = f32[512,384]{1,0:T(8,128)S(1)} fusion(bf16[512,4096]{1,0:T(8,128)(2,1)} %all-gather.5.cloned.1.call-done, bf16[1,4096,384]{2,1,0:T(8,128)(2,1)S(1)} %copy-done), kind=kOutput, calls=%fused_computation.7 | convolution fusion | flops 1610612736 | bytes 8126464 | tf_op jit(solution)/shard_map/dot_general | solution.py:72
  145.9 3.1 fusion.14
  149.1 0.8 collective-permute-start.6
  149.8 1.7 collective-permute-start.7
  151.6 1.9 collective-permute-start.8
  153.5 51.0 %all-gather.3.cloned.1.call-done = bf16[512,4096]{1,0:T(8,128)(2,1)} async-done(((bf16[128,4096]{1,0:T(8,128)(2,1)}), bf16[512,4096]{1,0:T(8,128)(2,1)}) %all-gather.3.cloned.1.call-update) | async-done | bytes 4194320 | tf_op jit(solution)/shard_map/all_gather | solution.py:71
  204.5 5.5 %fusion.6 = f32[512,384]{1,0:T(8,128)} fusion(bf16[512,4096]{1,0:T(8,128)(2,1)} %all-gather.3.cloned.1.call-done, bf16[1,4096,384]{2,1,0:T(8,128)(2,1)S(1)} %copy-done), kind=kOutput, calls=%fused_computation.9 | convolution fusion | flops 1610612736 | bytes 8126464 | tf_op jit(solution)/shard_map/dot_general | solution.py:72
  210.0 1.7 fusion.48
  211.7 2.0 fusion.49
  213.7 2.0 fusion.50
  215.6 2.9 add_convert_fusion
  218.5 2.2 reshape.215
  220.7 3.3 %copy.47 = bf16[4,64,2,1024]{3,2,0,1:T(2,128)(2,1)} copy(bf16[4,64,2,1024]{3,2,1,0:T(2,128)(2,1)} %reshape.215) | data formatting | bytes 2097152 | tf_op jit(solution)/shard_map/reshape | solution.py:82
  224.1 10.7 %all-to-all-start.3 = ((bf16[64,4,2,1024]{3,2,1,0:T(2,128)(2,1)}), bf16[64,4,2,1024]{3,2,1,0:T(2,128)(2,1)}, u32[]{:S(2)}, u32[]{:S(2)}) async-start(bf16[64,4,2,1024]{3,2,1,0:T(2,128)(2,1)} %bitcast.77), calls=%async_computation.3 | async-start | bytes 2097152 | tf_op jit(solution)/shard_map/all_to_all | solution.py:85
  234.8 5.7 %fusion.17 = bf16[512,384]{1,0:T(8,128)(2,1)S(1)} fusion(bf16[512,4096]{1,0:T(8,128)(2,1)} %all-gather.3.cloned.1.call-done, bf16[1,4096,384]{2,1,0:T(8,128)(2,1)} %param.16, f32[512,384]{1,0:T(8,128)} %fusion.6), kind=kOutput, calls=%fused_computation.16 | convolution fusion | flops 1611792384 | bytes 8519680 | tf_op jit(solution)/shard_map/dot_general | solution.py:73
  240.5 1.1 collective-permute-start.3
  241.7 3.0 collective-permute-start.4
  246.0 7.0 %collective-permute-done.3 = bf16[512,384]{1,0:T(8,128)(2,1)S(1)} collective-permute-done((bf16[512,384]{1,0:T(8,128)(2,1)S(1)}, bf16[512,384]{1,0:T(8,128)(2,1)S(1)}, u32[]{:S(2)}, u32[]{:S(2)}) %collective-permute-start.3) | collective-permute-done | bytes 393248 | tf_op jit(solution)/shard_map/ppermute | solution.py:24
  253.0 1.8 fusion.46
  254.8 7.4 %collective-permute-done.4 = bf16[512,384]{1,0:T(8,128)(2,1)S(1)} collective-permute-done((bf16[512,384]{1,0:T(8,128)(2,1)S(1)}, bf16[512,384]{1,0:T(8,128)(2,1)S(1)}, u32[]{:S(2)}, u32[]{:S(2)}) %collective-permute-start.4) | collective-permute-done | bytes 393248 | tf_op jit(solution)/shard_map/ppermute | solution.py:24
  262.3 1.8 fusion.47
  264.1 2.9 add_convert_fusion.1
  267.0 2.3 reshape.214
  269.3 3.4 %copy.48 = bf16[4,64,2,1024]{3,2,0,1:T(2,128)(2,1)} copy(bf16[4,64,2,1024]{3,2,1,0:T(2,128)(2,1)} %reshape.214) | data formatting | bytes 2097152 | tf_op jit(solution)/shard_map/reshape | solution.py:82
  272.7 10.5 %all-to-all-start.1 = ((bf16[64,4,2,1024]{3,2,1,0:T(2,128)(2,1)}), bf16[64,4,2,1024]{3,2,1,0:T(2,128)(2,1)}, u32[]{:S(2)}, u32[]{:S(2)}) async-start(bf16[64,4,2,1024]{3,2,1,0:T(2,128)(2,1)} %bitcast.78), calls=%async_computation.1 | async-start | bytes 2097152 | tf_op jit(solution)/shard_map/all_to_all | solution.py:85
  283.8 3.0 convolution_bitcast_fusion
  286.8 25.1 %all-to-all-done.1 = bf16[64,4,2,1024]{3,2,1,0:T(2,128)(2,1)} async-done(((bf16[64,4,2,1024]{3,2,1,0:T(2,128)(2,1)}), bf16[64,4,2,1024]{3,2,1,0:T(2,128)(2,1)}, u32[]{:S(2)}, u32[]{:S(2)}) %all-to-all-start.1) | async-done | bytes 1048608 | tf_op jit(solution)/shard_map/all_to_all | solution.py:85
  311.9 3.7 %fusion.20 = f32[64,1024]{1,0:T(8,128)} fusion(f32[64,1024]{1,0:T(8,128)S(1)} %convolution_bitcast_fusion, bf16[64,4,2,1024]{3,2,1,0:T(2,128)(2,1)} %all-to-all-done.1, f32[64,64]{1,0:T(8,128)S(1)} %select_reduce_fusion, s32[4,2]{1,0:T(4,128)S(1)} %iota_add_fusion.1, s32[64,64]{1,0:T(8,128)S(1)} %copy-done.6, pred[64,64]{1,0:T(8,128)(4,1)S(1)} %broadcast_compare_fusion), kind=kOutput, calls=%fused_computation.19 | convolution fusion | flops 402817024 | bytes 1609760 | tf_op jit(solution)/shard_map/dot_general | solution.py:92
  315.6 1.1 reshape.216
  317.0 8.4 %all_to_all.40 = bf16[4,4,4,1024]{3,2,1,0:T(4,128)(2,1)S(1)} all-to-all(bf16[4,4,4,1024]{3,2,1,0:T(4,128)(2,1)S(1)} %reshape.217), channel_id=1, replica_groups=mesh['dp'=4,'expert'=64] {'dp'}, dimensions={0} | all-to-all | bytes 262144 | tf_op jit(solution)/shard_map/all_to_all | solution.py:110
  (58 shorter events, 3.9 us)
Async XLA Ops:
  6.5 134.7 %copy-start = (bf16[1,4096,384]{2,1,0:T(8,128)(2,1)S(1)}, bf16[1,4096,384]{2,1,0:T(8,128)(2,1)}, u32[]{:S(2)}) copy-start(bf16[1,4096,384]{2,1,0:T(8,128)(2,1)} %param.15) | copy-start | bytes 9437188
  6.5 134.7 %all-gather.5.cloned.1.call-start = ((), (), s32[]{:S(2)}) async-start(), calls=%async_computation.6 | async-start | bytes 5242880 | tf_op jit(solution)/shard_map/all_gather | solution.py:71
  7.5 50.1 %copy-start.3 = (s32[16,4,8]{2,1,0:T(4,128)}, s32[16,4,8]{2,1,0:T(4,128)S(1)}, u32[]{:S(2)}) copy-start(s32[16,4,8]{2,1,0:T(4,128)S(1)} %copy.29) | copy-start | bytes 6148
  9.3 48.2 %copy-start.5 = (s32[64,64]{1,0:T(8,128)}, s32[64,64]{1,0:T(8,128)S(1)}, u32[]{:S(2)}) copy-start(s32[64,64]{1,0:T(8,128)S(1)} %sub.20) | copy-start | bytes 49156
  64.9 34.6 %all-to-all-start = ((bf16[64,2,4096]{2,1,0:T(2,128)(2,1)}), bf16[64,2,4096]{2,1,0:T(2,128)(2,1)}, u32[]{:S(2)}, u32[]{:S(2)}) async-start(bf16[64,2,4096]{2,1,0:T(2,128)(2,1)} %all_to_all.25), calls=%async_computation | async-start | bytes 2097152 | tf_op jit(solution)/shard_map/all_to_all | solution.py:68
  70.8 133.7 %all-gather.3.cloned.1.call-start = ((), (), s32[]{:S(2)}) async-start(), calls=%async_computation.5 | async-start | bytes 5242880 | tf_op jit(solution)/shard_map/all_gather | solution.py:71
  74.6 38.5 %collective-permute-start = (bf16[384,1024]{1,0:T(8,128)(2,1)}, bf16[384,1024]{1,0:T(8,128)(2,1)}, u32[]{:S(2)}, u32[]{:S(2)}) collective-permute-start(bf16[384,1024]{1,0:T(8,128)(2,1)} %get-tuple-element.16), channel_id=1, source_target_pairs={{0,64},{64,128},{128,192},{192,0},{1,65},{65,129},{129,193},{193,1... | collective-permute-start | bytes 2359304 | tf_op jit(solution)/shard_map/ppermute | solution.py:16
  76.2 65.0 %collective-permute-start.1 = (bf16[384,1024]{1,0:T(8,128)(2,1)}, bf16[384,1024]{1,0:T(8,128)(2,1)}, u32[]{:S(2)}, u32[]{:S(2)}) collective-permute-start(bf16[384,1024]{1,0:T(8,128)(2,1)} %get-tuple-element.18), channel_id=1, source_target_pairs={{0,128},{64,192},{128,0},{192,64},{1,129},{65,193},{129,1},{193,65... | collective-permute-start | bytes 2359304 | tf_op jit(solution)/shard_map/ppermute | solution.py:16
  79.0 62.1 %collective-permute-start.2 = (bf16[384,1024]{1,0:T(8,128)(2,1)}, bf16[384,1024]{1,0:T(8,128)(2,1)}, u32[]{:S(2)}, u32[]{:S(2)}) collective-permute-start(bf16[384,1024]{1,0:T(8,128)(2,1)} %get-tuple-element.15), channel_id=1, source_target_pairs={{0,192},{64,0},{128,64},{192,128},{1,193},{65,1},{129,65},{193,129... | collective-permute-start | bytes 2359304 | tf_op jit(solution)/shard_map/ppermute | solution.py:16
  141.2 4.7 %copy-start.8 = (bf16[512,4096]{1,0:T(8,128)(2,1)S(1)}, bf16[512,4096]{1,0:T(8,128)(2,1)}, u32[]{:S(2)}) copy-start(bf16[512,4096]{1,0:T(8,128)(2,1)} %all-gather.5.cloned.1.call-done) | copy-start | bytes 12582916
  141.2 4.7 %copy-start.9 = (bf16[1,4096,384]{2,1,0:T(8,128)(2,1)S(1)}, bf16[1,4096,384]{2,1,0:T(8,128)(2,1)}, u32[]{:S(2)}) copy-start(bf16[1,4096,384]{2,1,0:T(8,128)(2,1)} %param.16) | copy-start | bytes 9437188
  149.1 62.6 %collective-permute-start.6 = (bf16[512,384]{1,0:T(8,128)(2,1)}, bf16[512,384]{1,0:T(8,128)(2,1)}, u32[]{:S(2)}, u32[]{:S(2)}) collective-permute-start(bf16[512,384]{1,0:T(8,128)(2,1)} %fusion.14), channel_id=1, source_target_pairs={{0,64},{64,128},{128,192},{192,0},{1,65},{65,129},{129,193},{193,1... | collective-permute-start | bytes 1179656 | tf_op jit(solution)/shard_map/ppermute | solution.py:24
  149.8 63.8 %collective-permute-start.7 = (bf16[512,384]{1,0:T(8,128)(2,1)}, bf16[512,384]{1,0:T(8,128)(2,1)}, u32[]{:S(2)}, u32[]{:S(2)}) collective-permute-start(bf16[512,384]{1,0:T(8,128)(2,1)} %fusion.14), channel_id=1, source_target_pairs={{0,128},{64,192},{128,0},{192,64},{1,129},{65,193},{129,1},{193,65... | collective-permute-start | bytes 1179656 | tf_op jit(solution)/shard_map/ppermute | solution.py:24
  151.6 64.1 %collective-permute-start.8 = (bf16[512,384]{1,0:T(8,128)(2,1)}, bf16[512,384]{1,0:T(8,128)(2,1)S(1)}, u32[]{:S(2)}, u32[]{:S(2)}) collective-permute-start(bf16[512,384]{1,0:T(8,128)(2,1)} %fusion.14), channel_id=1, source_target_pairs={{0,192},{64,0},{128,64},{192,128},{1,193},{65,1},{129,65},{193,129... | collective-permute-start | bytes 1179656 | tf_op jit(solution)/shard_map/ppermute | solution.py:24
  204.5 5.5 %copy-start.1 = (bf16[384,1024]{1,0:T(8,128)(2,1)S(1)}, bf16[384,1024]{1,0:T(8,128)(2,1)}, u32[]{:S(2)}) copy-start(bf16[384,1024]{1,0:T(8,128)(2,1)} %get-tuple-element.11) | copy-start | bytes 2359300
  224.1 48.6 %all-to-all-start.3 = ((bf16[64,4,2,1024]{3,2,1,0:T(2,128)(2,1)}), bf16[64,4,2,1024]{3,2,1,0:T(2,128)(2,1)}, u32[]{:S(2)}, u32[]{:S(2)}) async-start(bf16[64,4,2,1024]{3,2,1,0:T(2,128)(2,1)} %bitcast.77), calls=%async_computation.3 | async-start | bytes 2097152 | tf_op jit(solution)/shard_map/all_to_all | solution.py:85
  234.8 9.9 %copy-start.2 = (bf16[384,1024]{1,0:T(8,128)(2,1)S(1)}, bf16[384,1024]{1,0:T(8,128)(2,1)}, u32[]{:S(2)}) copy-start(bf16[384,1024]{1,0:T(8,128)(2,1)} %get-tuple-element.11) | copy-start | bytes 2359300
  240.5 12.5 %collective-permute-start.3 = (bf16[512,384]{1,0:T(8,128)(2,1)S(1)}, bf16[512,384]{1,0:T(8,128)(2,1)S(1)}, u32[]{:S(2)}, u32[]{:S(2)}) collective-permute-start(bf16[512,384]{1,0:T(8,128)(2,1)S(1)} %fusion.17), channel_id=1, source_target_pairs={{0,64},{64,128},{128,192},{192,0},{1,65},{65,129},{129,193},{193,1... | collective-permute-start | bytes 1179656 | tf_op jit(solution)/shard_map/ppermute | solution.py:24
  241.7 20.6 %collective-permute-start.4 = (bf16[512,384]{1,0:T(8,128)(2,1)S(1)}, bf16[512,384]{1,0:T(8,128)(2,1)S(1)}, u32[]{:S(2)}, u32[]{:S(2)}) collective-permute-start(bf16[512,384]{1,0:T(8,128)(2,1)S(1)} %fusion.17), channel_id=1, source_target_pairs={{0,128},{64,192},{128,0},{192,64},{1,129},{65,193},{129,1},{193,65... | collective-permute-start | bytes 1179656 | tf_op jit(solution)/shard_map/ppermute | solution.py:24
  245.4 18.7 %collective-permute-start.5 = (bf16[512,384]{1,0:T(8,128)(2,1)S(1)}, bf16[512,384]{1,0:T(8,128)(2,1)S(1)}, u32[]{:S(2)}, u32[]{:S(2)}) collective-permute-start(bf16[512,384]{1,0:T(8,128)(2,1)S(1)} %fusion.17), channel_id=1, source_target_pairs={{0,192},{64,0},{128,64},{192,128},{1,193},{65,1},{129,65},{193,129... | collective-permute-start | bytes 1179656 | tf_op jit(solution)/shard_map/ppermute | solution.py:24
  267.0 16.2 %copy-start.7 = (f32[16,4,8]{0,2,1:T(8,128)S(1)}, f32[16,4,8]{0,2,1:T(8,128)}, u32[]{:S(2)}) copy-start(f32[16,4,8]{0,2,1:T(8,128)} %param.11) | copy-start | bytes 6148
  267.0 16.3 %copy-start.4 = (s32[16,4,8]{2,1,0:T(4,128)S(1)}, s32[16,4,8]{2,1,0:T(4,128)}, u32[]{:S(2)}) copy-start(s32[16,4,8]{2,1,0:T(4,128)} %copy-done.3) | copy-start | bytes 6148
  267.0 16.6 %copy-start.10 = (s32[16]{0:T(128)S(1)}, s32[16]{0:T(128)}, u32[]{:S(2)}) copy-start(s32[16]{0:T(128)} %param.14) | copy-start | bytes 196
  267.0 16.8 %copy-start.6 = (s32[64,64]{1,0:T(8,128)S(1)}, s32[64,64]{1,0:T(8,128)}, u32[]{:S(2)}) copy-start(s32[64,64]{1,0:T(8,128)} %copy-done.5) | copy-start | bytes 49156
  272.7 39.2 %all-to-all-start.1 = ((bf16[64,4,2,1024]{3,2,1,0:T(2,128)(2,1)}), bf16[64,4,2,1024]{3,2,1,0:T(2,128)(2,1)}, u32[]{:S(2)}, u32[]{:S(2)}) async-start(bf16[64,4,2,1024]{3,2,1,0:T(2,128)(2,1)} %bitcast.78), calls=%async_computation.1 | async-start | bytes 2097152 | tf_op jit(solution)/shard_map/all_to_all | solution.py:85
Sparse Core Ops, SparseCore 0:
  60.0 78.2 all-gather.4
  141.3 63.1 all-gather.2

commit v8 on v7

--- a/solution.py
+++ b/solution.py
@@ -65,9 +65,9 @@
             (((0,), (0,)), ((), ())),
             preferred_element_type=jnp.float32,
         ).astype(jnp.bfloat16)
+        if chunk == 1:
+            down_cols, outgoing = lax.optimization_barrier((down_cols, outgoing))
         arrived = lax.all_to_all(outgoing, "expert", split_axis=0, concat_axis=0, tiled=True)
-        if chunk == 0:
-            down_cols, arrived = lax.optimization_barrier((down_cols, arrived))
         gathered = lax.all_gather(arrived, "dp", axis=0, tiled=True)
         gate_part = jnp.dot(gathered, w_gate[0], preferred_element_type=jnp.float32)
         up_part = jnp.dot(gathered, w_up[0], preferred_element_type=jnp.float32)

time: 334 us -> 338 us (1.012)
  blocking collectives: 49.3 us -> 84.1 us
  waiting for transfers between devices: 149 us -> 127 us
  starting transfers between devices: 42.1 us -> 37.3 us
    all_to_all x1 -> x2, blocking collectives: 40.9 us -> 75.5 us  [body(): lax.all_to_all(outgoing, 'expert', split_axis=0, concat_axis=0, tiled=True)]
    all_to_all x1 -> x0, waiting for transfers between devices: 19.1 us -> none  [body(): lax.all_to_all(outgoing, 'expert', split_axis=0, concat_axis=0, tiled=True)]
    ppermute x3, waiting for transfers between devices: 39.4 us -> 27 us  [exchange_columns(): pieces.append(lax.ppermute(outgoing, 'dp', pairs))]
    ppermute x6, waiting for transfers between devices: 14.5 us -> 24.4 us  [exchange_all(): pieces.append(lax.ppermute(block, 'dp', pairs))]
    all_to_all x1 -> x0, starting transfers between devices: 5.85 us -> none  [body(): lax.all_to_all(outgoing, 'expert', split_axis=0, concat_axis=0, tiled=True)]
  transfers between devices with their start and end apart: 14 -> 13, of which waited for: 7 -> 9; matrix products, arithmetic and copies ran while one was open for 14% -> 14% of each run, Pallas kernels for 0% -> 0%
where the time goes in v8:
time: 338 us; the launch traced here: 337 us
  waiting for transfers between devices  127 us (38%)
  blocking collectives  84.1 us (25%)
  matrix products  44.7 us (13%)
  starting transfers between devices  37.3 us (11%)
  local copies, waits for them, and re-layouts  29 us (9%)
  between operations  14.3 us (4%)
    all_to_all x2, blocking collectives, body(): lax.all_to_all(outgoing, 'expert', split_axis=0, concat_axis=0, tiled=True)  75.5 us
    all_gather x2, waiting for transfers between devices, body(): gathered = lax.all_gather(arrived, 'dp', axis=0, tiled=True)  50.4 us
    ppermute x3, waiting for transfers between devices, exchange_columns(): pieces.append(lax.ppermute(outgoing, 'dp', pairs))  27 us
    all_to_all x2, waiting for transfers between devices, body(): lax.all_to_all(by_source, 'expert', split_axis=0, concat_axis=0, tiled=True)  25.1 us
    ppermute x6, waiting for transfers between devices, exchange_all(): pieces.append(lax.ppermute(block, 'dp', pairs))  24.4 us
    all_to_all x2, starting transfers between devices, body(): lax.all_to_all(by_source, 'expert', split_axis=0, concat_axis=0, tiled=True)  21.2 us
    dot_general x6, matrix products, body(): jnp.dot(hidden_all[shift], down_cols[shift], preferred_element_type=jnp.f...  13.2 us
    reshape x4, local copies, waits for them, and re-layouts, body(): expert_cols.reshape(replica_count, expert_count, sub, columns)  11.3 us
  transfers between devices with their start and end apart: 13, of which 9 were waited for; matrix products, arithmetic and copies ran while one was open for 14% of the time, Pallas kernels for 0%

profile of v8, /device:TPU:2, one launch (start us, length us, event | category | flops | bytes accessed | tf_op | source)
XLA Modules:
  0.0 337.2 jit_solution(3354540780657556418)
XLA Ops:
  6.5 3.7 %dynamic-slice_bitcast_fusion = (bf16[384,1024]{1,0:T(8,128)(2,1)}, bf16[384,1024]{1,0:T(8,128)(2,1)}, bf16[384,1024]{1,0:T(8,128)(2,1)}, bf16[384,1024]{1,0:T(8,128)(2,1)}) fusion(bf16[1,384,4096]{2,1,0:T(8,128)(2,1)} %param.17, s32[]{:T(128)S(6)} %select_n.63, s32[]{:T(128)S(6)} %select_n.59, s32[]{:T(128)S(6)} %select_n.57, s32[]{:T(128)S(6)} %select_n.61), kind=kLoop, calls=%fused_computation.24 | loop fusion | bytes 6291472 | tf_op jit(solution)/shard_map/dynamic_slice | solution.py:14
  10.2 1.6 collective-permute-start.1
  11.8 2.9 collective-permute-start.3
  14.7 1.3 collective-permute-start.5
  17.5 2.0 reshape.213
  19.7 2.5 convolution_convert_fusion
  22.2 8.9 %collective-permute-done.1 = bf16[384,1024]{1,0:T(8,128)(2,1)} collective-permute-done((bf16[384,1024]{1,0:T(8,128)(2,1)}, bf16[384,1024]{1,0:T(8,128)(2,1)}, u32[]{:S(2)}, u32[]{:S(2)}) %collective-permute-start.1) | collective-permute-done | bytes 786464 | tf_op jit(solution)/shard_map/ppermute | solution.py:16
  31.1 18.0 %collective-permute-done.3 = bf16[384,1024]{1,0:T(8,128)(2,1)} collective-permute-done((bf16[384,1024]{1,0:T(8,128)(2,1)}, bf16[384,1024]{1,0:T(8,128)(2,1)}, u32[]{:S(2)}, u32[]{:S(2)}) %collective-permute-start.3) | collective-permute-done | bytes 786464 | tf_op jit(solution)/shard_map/ppermute | solution.py:16
  49.1 2.5 all_to_all.29
  51.7 40.9 %all_to_all.39 = bf16[64,2,4096]{2,1,0:T(2,128)(2,1)} all-to-all(bf16[64,2,4096]{2,1,0:T(2,128)(2,1)} %all_to_all.29), channel_id=1, replica_groups=mesh['dp'=4,'expert'=64] {'expert'}, dimensions={0} | all-to-all | bytes 2097152 | tf_op jit(solution)/shard_map/all_to_all | solution.py:70
  92.6 2.3 all_to_all.31
  95.0 2.5 convolution_convert_fusion.1
  97.5 2.5 all_to_all.25
  100.0 34.6 %all_to_all.40 = bf16[64,2,4096]{2,1,0:T(2,128)(2,1)} all-to-all(bf16[64,2,4096]{2,1,0:T(2,128)(2,1)} %all_to_all.25), channel_id=1, replica_groups=mesh['dp'=4,'expert'=64] {'expert'}, dimensions={0} | all-to-all | bytes 2097152 | tf_op jit(solution)/shard_map/all_to_all | solution.py:70
  134.6 2.3 all_to_all.27
  136.9 5.0 %all-gather.5.cloned.1.call-done = bf16[512,4096]{1,0:T(8,128)(2,1)} async-done(((bf16[128,4096]{1,0:T(8,128)(2,1)}), bf16[512,4096]{1,0:T(8,128)(2,1)}) %all-gather.5.cloned.1.call-update) | async-done | bytes 4194320 | tf_op jit(solution)/shard_map/all_gather | solution.py:71
  141.9 4.7 %fusion.4 = f32[512,384]{1,0:T(8,128)S(1)} fusion(bf16[512,4096]{1,0:T(8,128)(2,1)} %all-gather.5.cloned.1.call-done, bf16[1,4096,384]{2,1,0:T(8,128)(2,1)S(1)} %copy-done), kind=kOutput, calls=%fused_computation.7 | convolution fusion | flops 1610612736 | bytes 8126464 | tf_op jit(solution)/shard_map/dot_general | solution.py:72
  146.6 2.3 fusion.14
  148.9 1.1 collective-permute-start.6
  150.0 45.3 %all-gather.3.cloned.1.call-done = bf16[512,4096]{1,0:T(8,128)(2,1)} async-done(((bf16[128,4096]{1,0:T(8,128)(2,1)}), bf16[512,4096]{1,0:T(8,128)(2,1)}) %all-gather.3.cloned.1.call-update) | async-done | bytes 4194320 | tf_op jit(solution)/shard_map/all_gather | solution.py:71
  195.4 5.5 %fusion.6 = f32[512,384]{1,0:T(8,128)} fusion(bf16[512,4096]{1,0:T(8,128)(2,1)} %all-gather.3.cloned.1.call-done, bf16[1,4096,384]{2,1,0:T(8,128)(2,1)S(1)} %copy-done), kind=kOutput, calls=%fused_computation.9 | convolution fusion | flops 1610612736 | bytes 8126464 | tf_op jit(solution)/shard_map/dot_general | solution.py:72
  200.8 1.6 collective-permute-start.7
  202.5 1.4 collective-permute-start.8
  204.6 2.0 fusion.49
  206.6 6.8 %collective-permute-done.7 = bf16[512,384]{1,0:T(8,128)(2,1)S(1)} collective-permute-done((bf16[512,384]{1,0:T(8,128)(2,1)S(1)}, bf16[512,384]{1,0:T(8,128)(2,1)S(1)}, u32[]{:S(2)}, u32[]{:S(2)}) %collective-permute-start.7) | collective-permute-done | bytes 393248 | tf_op jit(solution)/shard_map/ppermute | solution.py:24
  213.4 1.8 fusion.50
  215.3 4.4 %collective-permute-done.8 = bf16[512,384]{1,0:T(8,128)(2,1)S(1)} collective-permute-done((bf16[512,384]{1,0:T(8,128)(2,1)S(1)}, bf16[512,384]{1,0:T(8,128)(2,1)S(1)}, u32[]{:S(2)}, u32[]{:S(2)}) %collective-permute-start.8) | collective-permute-done | bytes 393248 | tf_op jit(solution)/shard_map/ppermute | solution.py:24
  219.6 2.9 add_convert_fusion
  222.5 2.2 reshape.215
  224.8 3.4 copy.47
  228.1 10.7 %all-to-all-start.3 = ((bf16[64,4,2,1024]{3,2,1,0:T(2,128)(2,1)}), bf16[64,4,2,1024]{3,2,1,0:T(2,128)(2,1)}, u32[]{:S(2)}, u32[]{:S(2)}) async-start(bf16[64,4,2,1024]{3,2,1,0:T(2,128)(2,1)} %bitcast.77), calls=%async_computation.3 | async-start | bytes 2097152 | tf_op jit(solution)/shard_map/all_to_all | solution.py:85
  238.9 5.7 %fusion.17 = bf16[512,384]{1,0:T(8,128)(2,1)S(1)} fusion(bf16[512,4096]{1,0:T(8,128)(2,1)} %all-gather.3.cloned.1.call-done, bf16[1,4096,384]{2,1,0:T(8,128)(2,1)} %param.16, f32[512,384]{1,0:T(8,128)} %fusion.6), kind=kOutput, calls=%fused_computation.16 | convolution fusion | flops 1611792384 | bytes 8519680 | tf_op jit(solution)/shard_map/dot_general | solution.py:73
  244.6 2.2 collective-permute-start
  246.8 1.9 collective-permute-start.2
  249.4 1.9 collective-permute-start.4
  251.3 5.7 %collective-permute-done = bf16[512,384]{1,0:T(8,128)(2,1)S(1)} collective-permute-done((bf16[512,384]{1,0:T(8,128)(2,1)S(1)}, bf16[512,384]{1,0:T(8,128)(2,1)S(1)}, u32[]{:S(2)}, u32[]{:S(2)}) %collective-permute-start) | collective-permute-done | bytes 393248 | tf_op jit(solution)/shard_map/ppermute | solution.py:24
  257.0 1.8 fusion.46
  258.9 7.4 %collective-permute-done.2 = bf16[512,384]{1,0:T(8,128)(2,1)S(1)} collective-permute-done((bf16[512,384]{1,0:T(8,128)(2,1)S(1)}, bf16[512,384]{1,0:T(8,128)(2,1)S(1)}, u32[]{:S(2)}, u32[]{:S(2)}) %collective-permute-start.2) | collective-permute-done | bytes 393248 | tf_op jit(solution)/shard_map/ppermute | solution.py:24
  266.3 1.8 fusion.47
  268.2 2.9 add_convert_fusion.1
  271.1 2.3 reshape.214
  273.4 3.4 %copy.48 = bf16[4,64,2,1024]{3,2,0,1:T(2,128)(2,1)} copy(bf16[4,64,2,1024]{3,2,1,0:T(2,128)(2,1)} %reshape.214) | data formatting | bytes 2097152 | tf_op jit(solution)/shard_map/reshape | solution.py:82
  276.7 10.5 %all-to-all-start.1 = ((bf16[64,4,2,1024]{3,2,1,0:T(2,128)(2,1)}), bf16[64,4,2,1024]{3,2,1,0:T(2,128)(2,1)}, u32[]{:S(2)}, u32[]{:S(2)}) async-start(bf16[64,4,2,1024]{3,2,1,0:T(2,128)(2,1)} %bitcast.78), calls=%async_computation.1 | async-start | bytes 2097152 | tf_op jit(solution)/shard_map/all_to_all | solution.py:85
  287.9 3.0 convolution_bitcast_fusion
  290.8 25.1 %all-to-all-done.1 = bf16[64,4,2,1024]{3,2,1,0:T(2,128)(2,1)} async-done(((bf16[64,4,2,1024]{3,2,1,0:T(2,128)(2,1)}), bf16[64,4,2,1024]{3,2,1,0:T(2,128)(2,1)}, u32[]{:S(2)}, u32[]{:S(2)}) %all-to-all-start.1) | async-done | bytes 1048608 | tf_op jit(solution)/shard_map/all_to_all | solution.py:85
  315.9 3.7 %fusion.20 = f32[64,1024]{1,0:T(8,128)} fusion(f32[64,1024]{1,0:T(8,128)S(1)} %convolution_bitcast_fusion, bf16[64,4,2,1024]{3,2,1,0:T(2,128)(2,1)} %all-to-all-done.1, f32[64,64]{1,0:T(8,128)S(1)} %select_reduce_fusion, s32[4,2]{1,0:T(4,128)S(1)} %iota_add_fusion.1, s32[64,64]{1,0:T(8,128)S(1)} %copy-done.6, pred[64,64]{1,0:T(8,128)(4,1)S(1)} %broadcast_compare_fusion), kind=kOutput, calls=%fused_computation.19 | convolution fusion | flops 402817024 | bytes 1609760 | tf_op jit(solution)/shard_map/dot_general | solution.py:92
  319.6 1.1 reshape.216
  321.1 8.6 %all_to_all.41 = bf16[4,4,4,1024]{3,2,1,0:T(4,128)(2,1)S(1)} all-to-all(bf16[4,4,4,1024]{3,2,1,0:T(4,128)(2,1)S(1)} %reshape.217), channel_id=1, replica_groups=mesh['dp'=4,'expert'=64] {'dp'}, dimensions={0} | all-to-all | bytes 262144 | tf_op jit(solution)/shard_map/all_to_all | solution.py:110
  (61 shorter events, 4.2 us)
Async XLA Ops:
  6.5 135.4 %copy-start = (bf16[1,4096,384]{2,1,0:T(8,128)(2,1)S(1)}, bf16[1,4096,384]{2,1,0:T(8,128)(2,1)}, u32[]{:S(2)}) copy-start(bf16[1,4096,384]{2,1,0:T(8,128)(2,1)} %param.15) | copy-start | bytes 9437188
  6.5 135.3 %all-gather.5.cloned.1.call-start = ((), (), s32[]{:S(2)}) async-start(), calls=%async_computation.6 | async-start | bytes 5242880 | tf_op jit(solution)/shard_map/all_gather | solution.py:71
  6.5 9.5 %copy-start.8 = (s32[16,4,8]{0,2,1:T(8,128)S(1)}, s32[16,4,8]{0,2,1:T(8,128)}, u32[]{:S(2)}) copy-start(s32[16,4,8]{0,2,1:T(8,128)} %param.10) | copy-start | bytes 6148
  6.5 10.3 %copy-start.9 = (s32[16]{0:T(128)S(1)}, s32[16]{0:T(128)}, u32[]{:S(2)}) copy-start(s32[16]{0:T(128)} %param.12) | copy-start | bytes 196
  10.2 20.9 %collective-permute-start.1 = (bf16[384,1024]{1,0:T(8,128)(2,1)}, bf16[384,1024]{1,0:T(8,128)(2,1)}, u32[]{:S(2)}, u32[]{:S(2)}) collective-permute-start(bf16[384,1024]{1,0:T(8,128)(2,1)} %get-tuple-element.16), channel_id=1, source_target_pairs={{0,64},{64,128},{128,192},{192,0},{1,65},{65,129},{129,193},{193,1... | collective-permute-start | bytes 2359304 | tf_op jit(solution)/shard_map/ppermute | solution.py:16
  11.8 37.3 %collective-permute-start.3 = (bf16[384,1024]{1,0:T(8,128)(2,1)}, bf16[384,1024]{1,0:T(8,128)(2,1)}, u32[]{:S(2)}, u32[]{:S(2)}) collective-permute-start(bf16[384,1024]{1,0:T(8,128)(2,1)} %get-tuple-element.18), channel_id=1, source_target_pairs={{0,128},{64,192},{128,0},{192,64},{1,129},{65,193},{129,1},{193,65... | collective-permute-start | bytes 2359304 | tf_op jit(solution)/shard_map/ppermute | solution.py:16
  14.7 34.4 %collective-permute-start.5 = (bf16[384,1024]{1,0:T(8,128)(2,1)}, bf16[384,1024]{1,0:T(8,128)(2,1)}, u32[]{:S(2)}, u32[]{:S(2)}) collective-permute-start(bf16[384,1024]{1,0:T(8,128)(2,1)} %get-tuple-element.15), channel_id=1, source_target_pairs={{0,192},{64,0},{128,64},{192,128},{1,193},{65,1},{129,65},{193,129... | collective-permute-start | bytes 2359304 | tf_op jit(solution)/shard_map/ppermute | solution.py:16
  16.1 76.5 %copy-start.3 = (s32[16,4,8]{2,1,0:T(4,128)}, s32[16,4,8]{2,1,0:T(4,128)S(1)}, u32[]{:S(2)}) copy-start(s32[16,4,8]{2,1,0:T(4,128)S(1)} %copy.29) | copy-start | bytes 6148
  17.3 75.3 %copy-start.5 = (s32[64,64]{1,0:T(8,128)}, s32[64,64]{1,0:T(8,128)S(1)}, u32[]{:S(2)}) copy-start(s32[64,64]{1,0:T(8,128)S(1)} %sub.20) | copy-start | bytes 49156
  94.9 100.4 %all-gather.3.cloned.1.call-start = ((), (), s32[]{:S(2)}) async-start(), calls=%async_computation.5 | async-start | bytes 5242880 | tf_op jit(solution)/shard_map/all_gather | solution.py:71
  141.9 4.7 %copy-start.10 = (bf16[512,4096]{1,0:T(8,128)(2,1)S(1)}, bf16[512,4096]{1,0:T(8,128)(2,1)}, u32[]{:S(2)}) copy-start(bf16[512,4096]{1,0:T(8,128)(2,1)} %all-gather.5.cloned.1.call-done) | copy-start | bytes 12582916
  141.9 4.7 %copy-start.11 = (bf16[1,4096,384]{2,1,0:T(8,128)(2,1)S(1)}, bf16[1,4096,384]{2,1,0:T(8,128)(2,1)}, u32[]{:S(2)}) copy-start(bf16[1,4096,384]{2,1,0:T(8,128)(2,1)} %param.16) | copy-start | bytes 9437188
  148.9 55.7 %collective-permute-start.6 = (bf16[512,384]{1,0:T(8,128)(2,1)S(1)}, bf16[512,384]{1,0:T(8,128)(2,1)}, u32[]{:S(2)}, u32[]{:S(2)}) collective-permute-start(bf16[512,384]{1,0:T(8,128)(2,1)S(1)} %fusion.14), channel_id=1, source_target_pairs={{0,64},{64,128},{128,192},{192,0},{1,65},{65,129},{129,193},{193,1... | collective-permute-start | bytes 1179656 | tf_op jit(solution)/shard_map/ppermute | solution.py:24
  195.4 8.5 %copy-start.1 = (bf16[384,1024]{1,0:T(8,128)(2,1)S(1)}, bf16[384,1024]{1,0:T(8,128)(2,1)}, u32[]{:S(2)}) copy-start(bf16[384,1024]{1,0:T(8,128)(2,1)} %get-tuple-element.11) | copy-start | bytes 2359300
  200.8 12.6 %collective-permute-start.7 = (bf16[512,384]{1,0:T(8,128)(2,1)S(1)}, bf16[512,384]{1,0:T(8,128)(2,1)S(1)}, u32[]{:S(2)}, u32[]{:S(2)}) collective-permute-start(bf16[512,384]{1,0:T(8,128)(2,1)S(1)} %fusion.14), channel_id=1, source_target_pairs={{0,128},{64,192},{128,0},{192,64},{1,129},{65,193},{129,1},{193,65... | collective-permute-start | bytes 1179656 | tf_op jit(solution)/shard_map/ppermute | solution.py:24
  202.5 17.2 %collective-permute-start.8 = (bf16[512,384]{1,0:T(8,128)(2,1)S(1)}, bf16[512,384]{1,0:T(8,128)(2,1)S(1)}, u32[]{:S(2)}, u32[]{:S(2)}) collective-permute-start(bf16[512,384]{1,0:T(8,128)(2,1)S(1)} %fusion.14), channel_id=1, source_target_pairs={{0,192},{64,0},{128,64},{192,128},{1,193},{65,1},{129,65},{193,129... | collective-permute-start | bytes 1179656 | tf_op jit(solution)/shard_map/ppermute | solution.py:24
  228.1 48.6 %all-to-all-start.3 = ((bf16[64,4,2,1024]{3,2,1,0:T(2,128)(2,1)}), bf16[64,4,2,1024]{3,2,1,0:T(2,128)(2,1)}, u32[]{:S(2)}, u32[]{:S(2)}) async-start(bf16[64,4,2,1024]{3,2,1,0:T(2,128)(2,1)} %bitcast.77), calls=%async_computation.3 | async-start | bytes 2097152 | tf_op jit(solution)/shard_map/all_to_all | solution.py:85
  238.9 9.9 %copy-start.2 = (bf16[384,1024]{1,0:T(8,128)(2,1)S(1)}, bf16[384,1024]{1,0:T(8,128)(2,1)}, u32[]{:S(2)}) copy-start(bf16[384,1024]{1,0:T(8,128)(2,1)} %get-tuple-element.11) | copy-start | bytes 2359300
  244.6 12.5 %collective-permute-start = (bf16[512,384]{1,0:T(8,128)(2,1)S(1)}, bf16[512,384]{1,0:T(8,128)(2,1)S(1)}, u32[]{:S(2)}, u32[]{:S(2)}) collective-permute-start(bf16[512,384]{1,0:T(8,128)(2,1)S(1)} %fusion.17), channel_id=1, source_target_pairs={{0,64},{64,128},{128,192},{192,0},{1,65},{65,129},{129,193},{193,1... | collective-permute-start | bytes 1179656 | tf_op jit(solution)/shard_map/ppermute | solution.py:24
  246.8 19.5 %collective-permute-start.2 = (bf16[512,384]{1,0:T(8,128)(2,1)S(1)}, bf16[512,384]{1,0:T(8,128)(2,1)S(1)}, u32[]{:S(2)}, u32[]{:S(2)}) collective-permute-start(bf16[512,384]{1,0:T(8,128)(2,1)S(1)} %fusion.17), channel_id=1, source_target_pairs={{0,128},{64,192},{128,0},{192,64},{1,129},{65,193},{129,1},{193,65... | collective-permute-start | bytes 1179656 | tf_op jit(solution)/shard_map/ppermute | solution.py:24
  249.4 18.7 %collective-permute-start.4 = (bf16[512,384]{1,0:T(8,128)(2,1)S(1)}, bf16[512,384]{1,0:T(8,128)(2,1)S(1)}, u32[]{:S(2)}, u32[]{:S(2)}) collective-permute-start(bf16[512,384]{1,0:T(8,128)(2,1)S(1)} %fusion.17), channel_id=1, source_target_pairs={{0,192},{64,0},{128,64},{192,128},{1,193},{65,1},{129,65},{193,129... | collective-permute-start | bytes 1179656 | tf_op jit(solution)/shard_map/ppermute | solution.py:24
  271.0 16.2 %copy-start.7 = (f32[16,4,8]{0,2,1:T(8,128)S(1)}, f32[16,4,8]{0,2,1:T(8,128)}, u32[]{:S(2)}) copy-start(f32[16,4,8]{0,2,1:T(8,128)} %param.11) | copy-start | bytes 6148
  271.0 16.3 %copy-start.4 = (s32[16,4,8]{2,1,0:T(4,128)S(1)}, s32[16,4,8]{2,1,0:T(4,128)}, u32[]{:S(2)}) copy-start(s32[16,4,8]{2,1,0:T(4,128)} %copy-done.3) | copy-start | bytes 6148
  271.0 16.6 %copy-start.12 = (s32[16]{0:T(128)S(1)}, s32[16]{0:T(128)}, u32[]{:S(2)}) copy-start(s32[16]{0:T(128)} %param.14) | copy-start | bytes 196
  271.0 16.8 %copy-start.6 = (s32[64,64]{1,0:T(8,128)S(1)}, s32[64,64]{1,0:T(8,128)}, u32[]{:S(2)}) copy-start(s32[64,64]{1,0:T(8,128)} %copy-done.5) | copy-start | bytes 49156
  276.7 39.2 %all-to-all-start.1 = ((bf16[64,4,2,1024]{3,2,1,0:T(2,128)(2,1)}), bf16[64,4,2,1024]{3,2,1,0:T(2,128)(2,1)}, u32[]{:S(2)}, u32[]{:S(2)}) async-start(bf16[64,4,2,1024]{3,2,1,0:T(2,128)(2,1)} %bitcast.78), calls=%async_computation.1 | async-start | bytes 2097152 | tf_op jit(solution)/shard_map/all_to_all | solution.py:85
Sparse Core Ops, SparseCore 0:
  95.0 46.8 all-gather.4
  143.7 51.6 all-gather.2

commit v9 on v8

--- a/solution.py
+++ b/solution.py
@@ -72,7 +72,13 @@
         gate_part = jnp.dot(gathered, w_gate[0], preferred_element_type=jnp.float32)
         up_part = jnp.dot(gathered, w_up[0], preferred_element_type=jnp.float32)
         activated = (jax.nn.silu(gate_part) * up_part).astype(jnp.bfloat16)
-        hidden_all = exchange_all(activated, replica_count)
+        gathered_hidden = lax.all_gather(activated, "dp", axis=0, tiled=False)
+        hidden_all = [
+            lax.dynamic_index_in_dim(
+                gathered_hidden, (replica - shift) % replica_count, 0, keepdims=False
+            )
+            for shift in range(replica_count)
+        ]
         expert_cols = jnp.dot(hidden_all[0], down_cols[0], preferred_element_type=jnp.float32)
         for shift in range(1, replica_count):
             expert_cols = expert_cols + jnp.dot(

time: 338 us -> 335 us (level)
  starting transfers between devices: 37.3 us -> 23.3 us
  waiting for transfers between devices: 127 us -> 138 us
    all_gather x0 -> x2, waiting for transfers between devices: none -> 30.4 us  [body(): gathered_hidden = lax.all_gather(activated, 'dp', axis=0, tiled=False)]
    ppermute x6 -> x0, waiting for transfers between devices: 24.4 us -> none  [exchange_all(): pieces.append(lax.ppermute(block, 'dp', pairs))]
    ppermute x6 -> x0, starting transfers between devices: 10.2 us -> none  [exchange_all(): pieces.append(lax.ppermute(block, 'dp', pairs))]
    all_to_all x2, waiting for transfers between devices: 25.1 us -> 31.8 us  [body(): lax.all_to_all(by_source, 'expert', split_axis=0, concat_axis=0, tiled=True)]
    all_to_all x2, starting transfers between devices: 21.2 us -> 16.6 us  [body(): lax.all_to_all(by_source, 'expert', split_axis=0, concat_axis=0, tiled=True)]
  transfers between devices with their start and end apart: 13 -> 9, of which waited for: 9 -> 9; matrix products, arithmetic and copies ran while one was open for 14% -> 16% of each run, Pallas kernels for 0% -> 0%
where the time goes in v9:
time: 335 us; the launch traced here: 334 us
  waiting for transfers between devices  138 us (41%)
  blocking collectives  84.3 us (25%)
  matrix products  44.3 us (13%)
  local copies, waits for them, and re-layouts  29 us (9%)
  starting transfers between devices  23.3 us (7%)
  between operations  14.1 us (4%)
    all_to_all x2, blocking collectives, body(): lax.all_to_all(outgoing, 'expert', split_axis=0, concat_axis=0, tiled=True)  75.5 us
    all_gather x2, waiting for transfers between devices, body(): gathered = lax.all_gather(arrived, 'dp', axis=0, tiled=True)  50 us
    all_to_all x2, waiting for transfers between devices, body(): lax.all_to_all(by_source, 'expert', split_axis=0, concat_axis=0, tiled=True)  31.8 us
    all_gather x2, waiting for transfers between devices, body(): gathered_hidden = lax.all_gather(activated, 'dp', axis=0, tiled=False)  30.4 us
    ppermute x3, waiting for transfers between devices, exchange_columns(): pieces.append(lax.ppermute(outgoing, 'dp', pairs))  25.8 us
    all_to_all x2, starting transfers between devices, body(): lax.all_to_all(by_source, 'expert', split_axis=0, concat_axis=0, tiled=True)  16.6 us
    dot_general x6, matrix products, body(): jnp.dot(hidden_all[shift], down_cols[shift], preferred_element_type=jnp.f...  13.4 us
    reshape x4, local copies, waits for them, and re-layouts, body(): expert_cols.reshape(replica_count, expert_count, sub, columns)  11.2 us
  transfers between devices with their start and end apart: 9, of which 9 were waited for; matrix products, arithmetic and copies ran while one was open for 16% of the time, Pallas kernels for 0%

profile of v9, /device:TPU:2, one launch (start us, length us, event | category | flops | bytes accessed | tf_op | source)
XLA Modules:
  0.0 334.2 jit_solution(4981041073009181782)
XLA Ops:
  6.5 3.8 %dynamic-slice_bitcast_fusion = (bf16[384,1024]{1,0:T(8,128)(2,1)}, bf16[384,1024]{1,0:T(8,128)(2,1)}, bf16[384,1024]{1,0:T(8,128)(2,1)}, bf16[384,1024]{1,0:T(8,128)(2,1)}) fusion(bf16[1,384,4096]{2,1,0:T(8,128)(2,1)} %param.17, s32[]{:T(128)S(6)} %select_n.112, s32[]{:T(128)S(6)} %select_n.104, s32[]{:T(128)S(6)} %select_n.100, s32[]{:T(128)S(6)} %select_n.108), kind=kLoop, calls=%fused_computation.24 | loop fusion | bytes 6291472 | tf_op jit(solution)/shard_map/dynamic_slice | solution.py:14
  10.3 3.2 collective-permute-start.1
  13.5 0.7 collective-permute-start
  14.2 2.6 collective-permute-start.2
  18.2 2.0 reshape.213
  20.4 2.5 convolution_convert_fusion
  22.8 9.8 %collective-permute-done.1 = bf16[384,1024]{1,0:T(8,128)(2,1)} collective-permute-done((bf16[384,1024]{1,0:T(8,128)(2,1)}, bf16[384,1024]{1,0:T(8,128)(2,1)}, u32[]{:S(2)}, u32[]{:S(2)}) %collective-permute-start.1) | collective-permute-done | bytes 786464 | tf_op jit(solution)/shard_map/ppermute | solution.py:16
  32.6 15.7 %collective-permute-done = bf16[384,1024]{1,0:T(8,128)(2,1)} collective-permute-done((bf16[384,1024]{1,0:T(8,128)(2,1)}, bf16[384,1024]{1,0:T(8,128)(2,1)}, u32[]{:S(2)}, u32[]{:S(2)}) %collective-permute-start) | collective-permute-done | bytes 786464 | tf_op jit(solution)/shard_map/ppermute | solution.py:16
  48.3 0.4 collective-permute-done.2
  48.6 2.5 all_to_all.29
  51.2 40.9 %all_to_all.39 = bf16[64,2,4096]{2,1,0:T(2,128)(2,1)} all-to-all(bf16[64,2,4096]{2,1,0:T(2,128)(2,1)} %all_to_all.29), channel_id=1, replica_groups=mesh['dp'=4,'expert'=64] {'expert'}, dimensions={0} | all-to-all | bytes 2097152 | tf_op jit(solution)/shard_map/all_to_all | solution.py:70
  92.1 2.3 all_to_all.31
  94.5 2.4 convolution_convert_fusion.1
  97.0 2.5 all_to_all.25
  99.5 34.6 %all_to_all.40 = bf16[64,2,4096]{2,1,0:T(2,128)(2,1)} all-to-all(bf16[64,2,4096]{2,1,0:T(2,128)(2,1)} %all_to_all.25), channel_id=1, replica_groups=mesh['dp'=4,'expert'=64] {'expert'}, dimensions={0} | all-to-all | bytes 2097152 | tf_op jit(solution)/shard_map/all_to_all | solution.py:70
  134.1 2.3 all_to_all.27
  136.4 5.0 %all-gather.9.cloned.1.call-done = bf16[512,4096]{1,0:T(8,128)(2,1)} async-done(((bf16[128,4096]{1,0:T(8,128)(2,1)}), bf16[512,4096]{1,0:T(8,128)(2,1)}) %all-gather.9.cloned.1.call-update) | async-done | bytes 4194320 | tf_op jit(solution)/shard_map/all_gather | solution.py:71
  141.4 4.7 %fusion.4 = f32[512,384]{1,0:T(8,128)S(1)} fusion(bf16[512,4096]{1,0:T(8,128)(2,1)} %all-gather.9.cloned.1.call-done, bf16[1,4096,384]{2,1,0:T(8,128)(2,1)S(1)} %copy-done), kind=kOutput, calls=%fused_computation.7 | convolution fusion | flops 1610612736 | bytes 8126464 | tf_op jit(solution)/shard_map/dot_general | solution.py:72
  146.1 3.1 fusion.14
  149.3 0.2 all-gather.11.cloned.1.call-start
  149.5 45.0 %all-gather.7.cloned.1.call-done = bf16[512,4096]{1,0:T(8,128)(2,1)} async-done(((bf16[128,4096]{1,0:T(8,128)(2,1)}), bf16[512,4096]{1,0:T(8,128)(2,1)}) %all-gather.7.cloned.1.call-update) | async-done | bytes 4194320 | tf_op jit(solution)/shard_map/all_gather | solution.py:71
  194.5 4.7 %fusion.6 = f32[512,384]{1,0:T(8,128)S(1)} fusion(bf16[512,4096]{1,0:T(8,128)(2,1)} %all-gather.7.cloned.1.call-done, bf16[1,4096,384]{2,1,0:T(8,128)(2,1)S(1)} %copy-done), kind=kOutput, calls=%fused_computation.9 | convolution fusion | flops 1610612736 | bytes 8126464 | tf_op jit(solution)/shard_map/dot_general | solution.py:72
  199.2 3.1 fusion.17
  202.4 23.4 %all-gather.13.cloned.1.call-done = bf16[2048,384]{1,0:T(8,128)(2,1)} async-done(((bf16[512,384]{1,0:T(8,128)(2,1)}), bf16[2048,384]{1,0:T(8,128)(2,1)}) %all-gather.13.cloned.1.call-update) | async-done | bytes 1572880 | tf_op jit(solution)/shard_map/all_gather | solution.py:75
  225.8 2.1 fusion.29
  227.9 0.7 fusion.31
  228.6 1.9 fusion.27
  230.5 2.9 add_convert_fusion
  233.3 2.2 reshape.215
  235.6 3.3 %copy.47 = bf16[4,64,2,1024]{3,2,0,1:T(2,128)(2,1)} copy(bf16[4,64,2,1024]{3,2,1,0:T(2,128)(2,1)} %reshape.215) | data formatting | bytes 2097152 | tf_op jit(solution)/shard_map/reshape | solution.py:88
  238.9 10.7 %all-to-all-start.3 = ((bf16[64,4,2,1024]{3,2,1,0:T(2,128)(2,1)}), bf16[64,4,2,1024]{3,2,1,0:T(2,128)(2,1)}, u32[]{:S(2)}, u32[]{:S(2)}) async-start(bf16[64,4,2,1024]{3,2,1,0:T(2,128)(2,1)} %bitcast.100), calls=%async_computation.3 | async-start | bytes 2097152 | tf_op jit(solution)/shard_map/all_to_all | solution.py:91
  249.7 7.0 %all-gather.11.cloned.1.call-done = bf16[2048,384]{1,0:T(8,128)(2,1)} async-done(((bf16[512,384]{1,0:T(8,128)(2,1)}), bf16[2048,384]{1,0:T(8,128)(2,1)}) %all-gather.11.cloned.1.call-update) | async-done | bytes 1572880 | tf_op jit(solution)/shard_map/all_gather | solution.py:75
  256.6 2.1 fusion.41
  258.7 1.9 fusion.37
  260.6 1.9 fusion.39
  262.5 2.9 add_convert_fusion.1
  265.4 2.2 reshape.214
  267.6 3.4 %copy.48 = bf16[4,64,2,1024]{3,2,0,1:T(2,128)(2,1)} copy(bf16[4,64,2,1024]{3,2,1,0:T(2,128)(2,1)} %reshape.214) | data formatting | bytes 2097152 | tf_op jit(solution)/shard_map/reshape | solution.py:88
  271.0 7.4 %all-to-all-done.3 = bf16[64,4,2,1024]{3,2,1,0:T(2,128)(2,1)} async-done(((bf16[64,4,2,1024]{3,2,1,0:T(2,128)(2,1)}), bf16[64,4,2,1024]{3,2,1,0:T(2,128)(2,1)}, u32[]{:S(2)}, u32[]{:S(2)}) %all-to-all-start.3) | async-done | bytes 1048608 | tf_op jit(solution)/shard_map/all_to_all | solution.py:91
  278.4 5.9 %all-to-all-start.1 = ((bf16[64,4,2,1024]{3,2,1,0:T(2,128)(2,1)}), bf16[64,4,2,1024]{3,2,1,0:T(2,128)(2,1)}, u32[]{:S(2)}, u32[]{:S(2)}) async-start(bf16[64,4,2,1024]{3,2,1,0:T(2,128)(2,1)} %bitcast.99), calls=%async_computation.1 | async-start | bytes 2097152 | tf_op jit(solution)/shard_map/all_to_all | solution.py:91
  284.4 0.3 select_reduce_fusion
  284.8 3.7 %convolution_bitcast_fusion = f32[64,1024]{1,0:T(8,128)} fusion(bf16[64,4,2,1024]{3,2,1,0:T(2,128)(2,1)} %all-to-all-done.3, s32[4,2]{1,0:T(4,128)S(1)} %iota_add_fusion, f32[64,64]{1,0:T(8,128)S(1)} %select_reduce_fusion, s32[64,64]{1,0:T(8,128)S(1)} %sub.32, pred[64,64]{1,0:T(8,128)(4,1)S(1)} %broadcast_compare_fusion), kind=kOutput, calls=%fused_computation.17 | convolution fusion | flops 402751488 | bytes 1347616 | tf_op jit(solution)/shard_map/dot_general | solution.py:98
  288.5 24.4 %all-to-all-done.1 = bf16[64,4,2,1024]{3,2,1,0:T(2,128)(2,1)} async-done(((bf16[64,4,2,1024]{3,2,1,0:T(2,128)(2,1)}), bf16[64,4,2,1024]{3,2,1,0:T(2,128)(2,1)}, u32[]{:S(2)}, u32[]{:S(2)}) %all-to-all-start.1) | async-done | bytes 1048608 | tf_op jit(solution)/shard_map/all_to_all | solution.py:91
  312.9 3.7 %fusion.20 = f32[64,1024]{1,0:T(8,128)} fusion(f32[64,1024]{1,0:T(8,128)} %convolution_bitcast_fusion, bf16[64,4,2,1024]{3,2,1,0:T(2,128)(2,1)} %all-to-all-done.1, f32[64,64]{1,0:T(8,128)S(1)} %select_reduce_fusion, s32[4,2]{1,0:T(4,128)S(1)} %iota_add_fusion.1, s32[64,64]{1,0:T(8,128)S(1)} %sub.32, pred[64,64]{1,0:T(8,128)(4,1)S(1)} %broadcast_compare_fusion), kind=kOutput, calls=%fused_computation.19 | convolution fusion | flops 402817024 | bytes 1609760 | tf_op jit(solution)/shard_map/dot_general | solution.py:98
  316.7 1.1 reshape.216
  317.7 0.2 convolution_convert_fusion.2
  318.1 8.8 %all_to_all.41 = bf16[4,4,4,1024]{3,2,1,0:T(4,128)(2,1)S(1)} all-to-all(bf16[4,4,4,1024]{3,2,1,0:T(4,128)(2,1)S(1)} %reshape.217), channel_id=1, replica_groups=mesh['dp'=4,'expert'=64] {'dp'}, dimensions={0} | all-to-all | bytes 262144 | tf_op jit(solution)/shard_map/all_to_all | solution.py:116
  326.9 0.7 copy.40
  (53 shorter events, 1.6 us)
Async XLA Ops:
  6.5 134.9 %copy-start = (bf16[1,4096,384]{2,1,0:T(8,128)(2,1)S(1)}, bf16[1,4096,384]{2,1,0:T(8,128)(2,1)}, u32[]{:S(2)}) copy-start(bf16[1,4096,384]{2,1,0:T(8,128)(2,1)} %param.15) | copy-start | bytes 9437188
  6.5 134.9 %all-gather.9.cloned.1.call-start = ((), (), s32[]{:S(2)}) async-start(), calls=%async_computation.6 | async-start | bytes 5242880 | tf_op jit(solution)/shard_map/all_gather | solution.py:71
  6.5 10.2 %copy-start.5 = (s32[16,4,8]{0,2,1:T(8,128)S(1)}, s32[16,4,8]{0,2,1:T(8,128)}, u32[]{:S(2)}) copy-start(s32[16,4,8]{0,2,1:T(8,128)} %param.10) | copy-start | bytes 6148
  6.5 10.9 %copy-start.6 = (s32[16]{0:T(128)S(1)}, s32[16]{0:T(128)}, u32[]{:S(2)}) copy-start(s32[16]{0:T(128)} %param.12) | copy-start | bytes 196
  10.3 22.3 %collective-permute-start.1 = (bf16[384,1024]{1,0:T(8,128)(2,1)}, bf16[384,1024]{1,0:T(8,128)(2,1)}, u32[]{:S(2)}, u32[]{:S(2)}) collective-permute-start(bf16[384,1024]{1,0:T(8,128)(2,1)} %get-tuple-element.18), channel_id=1, source_target_pairs={{0,128},{64,192},{128,0},{192,64},{1,129},{65,193},{129,1},{193,65... | collective-permute-start | bytes 2359304 | tf_op jit(solution)/shard_map/ppermute | solution.py:16
  13.5 34.8 %collective-permute-start = (bf16[384,1024]{1,0:T(8,128)(2,1)}, bf16[384,1024]{1,0:T(8,128)(2,1)}, u32[]{:S(2)}, u32[]{:S(2)}) collective-permute-start(bf16[384,1024]{1,0:T(8,128)(2,1)} %get-tuple-element.16), channel_id=1, source_target_pairs={{0,64},{64,128},{128,192},{192,0},{1,65},{65,129},{129,193},{193,1... | collective-permute-start | bytes 2359304 | tf_op jit(solution)/shard_map/ppermute | solution.py:16
  14.2 34.5 %collective-permute-start.2 = (bf16[384,1024]{1,0:T(8,128)(2,1)}, bf16[384,1024]{1,0:T(8,128)(2,1)}, u32[]{:S(2)}, u32[]{:S(2)}) collective-permute-start(bf16[384,1024]{1,0:T(8,128)(2,1)} %get-tuple-element.15), channel_id=1, source_target_pairs={{0,192},{64,0},{128,64},{192,128},{1,193},{65,1},{129,65},{193,129... | collective-permute-start | bytes 2359304 | tf_op jit(solution)/shard_map/ppermute | solution.py:16
  94.4 100.1 %all-gather.7.cloned.1.call-start = ((), (), s32[]{:S(2)}) async-start(), calls=%async_computation.5 | async-start | bytes 5242880 | tf_op jit(solution)/shard_map/all_gather | solution.py:71
  136.4 89.4 %all-gather.13.cloned.1.call-start = ((), (), s32[]{:S(2)}) async-start(), calls=%async_computation.8 | async-start | bytes 1966080 | tf_op jit(solution)/shard_map/all_gather | solution.py:75
  141.4 4.7 %copy-start.7 = (bf16[512,4096]{1,0:T(8,128)(2,1)S(1)}, bf16[512,4096]{1,0:T(8,128)(2,1)}, u32[]{:S(2)}) copy-start(bf16[512,4096]{1,0:T(8,128)(2,1)} %all-gather.9.cloned.1.call-done) | copy-start | bytes 12582916
  141.4 4.7 %copy-start.9 = (bf16[1,4096,384]{2,1,0:T(8,128)(2,1)S(1)}, bf16[1,4096,384]{2,1,0:T(8,128)(2,1)}, u32[]{:S(2)}) copy-start(bf16[1,4096,384]{2,1,0:T(8,128)(2,1)} %param.16) | copy-start | bytes 9437188
  149.3 107.4 %all-gather.11.cloned.1.call-start = ((), (), s32[]{:S(2)}) async-start(), calls=%async_computation.7 | async-start | bytes 1966080 | tf_op jit(solution)/shard_map/all_gather | solution.py:75
  194.5 4.7 %copy-start.8 = (bf16[512,4096]{1,0:T(8,128)(2,1)S(1)}, bf16[512,4096]{1,0:T(8,128)(2,1)}, u32[]{:S(2)}) copy-start(bf16[512,4096]{1,0:T(8,128)(2,1)} %all-gather.7.cloned.1.call-done) | copy-start | bytes 12582916
  194.5 4.7 %copy-start.10 = (bf16[1,4096,384]{2,1,0:T(8,128)(2,1)S(1)}, bf16[1,4096,384]{2,1,0:T(8,128)(2,1)}, u32[]{:S(2)}) copy-start(bf16[1,4096,384]{2,1,0:T(8,128)(2,1)} %param.16) | copy-start | bytes 9437188
  225.8 2.1 copy-start.1
  225.8 2.1 copy-start.3
  238.9 39.5 %all-to-all-start.3 = ((bf16[64,4,2,1024]{3,2,1,0:T(2,128)(2,1)}), bf16[64,4,2,1024]{3,2,1,0:T(2,128)(2,1)}, u32[]{:S(2)}, u32[]{:S(2)}) async-start(bf16[64,4,2,1024]{3,2,1,0:T(2,128)(2,1)} %bitcast.100), calls=%async_computation.3 | async-start | bytes 2097152 | tf_op jit(solution)/shard_map/all_to_all | solution.py:91
  256.6 2.1 copy-start.2
  267.6 16.6 %copy-start.4 = (f32[16,4,8]{0,2,1:T(8,128)S(1)}, f32[16,4,8]{0,2,1:T(8,128)}, u32[]{:S(2)}) copy-start(f32[16,4,8]{0,2,1:T(8,128)} %param.11) | copy-start | bytes 6148
  267.6 17.1 %copy-start.11 = (s32[16]{0:T(128)S(1)}, s32[16]{0:T(128)}, u32[]{:S(2)}) copy-start(s32[16]{0:T(128)} %param.14) | copy-start | bytes 196
  278.4 34.6 %all-to-all-start.1 = ((bf16[64,4,2,1024]{3,2,1,0:T(2,128)(2,1)}), bf16[64,4,2,1024]{3,2,1,0:T(2,128)(2,1)}, u32[]{:S(2)}, u32[]{:S(2)}) async-start(bf16[64,4,2,1024]{3,2,1,0:T(2,128)(2,1)} %bitcast.99), calls=%async_computation.1 | async-start | bytes 2097152 | tf_op jit(solution)/shard_map/all_to_all | solution.py:91
Sparse Core Ops, SparseCore 0:
  94.5 46.8 all-gather.8
  143.2 51.1 all-gather.6
  196.3 29.4 all-gather.12
  227.4 29.1 all-gather.10

commit v10 on v9

--- a/solution.py
+++ b/solution.py
@@ -55,19 +55,26 @@
     member_ids = lax.broadcasted_iota(jnp.int32, (1, 1, replica_count, 1), 2)
     within_ids = lax.broadcasted_iota(jnp.int32, (1, 1, 1, sub), 3)
     combined = jnp.zeros((tokens, columns), jnp.float32)
+    outgoings = []
     for chunk in range(chunks):
         slot_ids = replica * part + chunk * sub + lax.broadcasted_iota(jnp.int32, (1, 1, sub), 2)
         placement = (hit_mask[:, :, None] == 1) & (prior_hits[:, :, None] == slot_ids)
         placement = placement.reshape(tokens, expert_count * sub)
-        outgoing = lax.dot_general(
-            placement.astype(jnp.bfloat16),
-            flat_inputs,
-            (((0,), (0,)), ((), ())),
-            preferred_element_type=jnp.float32,
-        ).astype(jnp.bfloat16)
-        if chunk == 1:
-            down_cols, outgoing = lax.optimization_barrier((down_cols, outgoing))
-        arrived = lax.all_to_all(outgoing, "expert", split_axis=0, concat_axis=0, tiled=True)
+        outgoings.append(
+            lax.dot_general(
+                placement.astype(jnp.bfloat16),
+                flat_inputs,
+                (((0,), (0,)), ((), ())),
+                preferred_element_type=jnp.float32,
+            ).astype(jnp.bfloat16)
+        )
+    arrivals = [lax.all_to_all(outgoings[0], "expert", split_axis=0, concat_axis=0, tiled=True)]
+    fenced = lax.optimization_barrier((down_cols, arrivals[0], outgoings[1:]))
+    down_cols, arrivals[0], rest = fenced
+    for outgoing in rest:
+        arrivals.append(lax.all_to_all(outgoing, "expert", split_axis=0, concat_axis=0, tiled=True))
+    for chunk in range(chunks):
+        arrived = arrivals[chunk]
         gathered = lax.all_gather(arrived, "dp", axis=0, tiled=True)
         gate_part = jnp.dot(gathered, w_gate[0], preferred_element_type=jnp.float32)
         up_part = jnp.dot(gathered, w_up[0], preferred_element_type=jnp.float32)

time: 335 us -> 357 us (1.066)
  waiting for transfers between devices: 138 us -> 184 us
  blocking collectives: 84.3 us -> 48 us
  starting transfers between devices: 23.3 us -> 35 us
    all_gather x2, waiting for transfers between devices: 50 us -> 91.1 us  [body(): gathered = lax.all_gather(arrived, 'dp', axis=0, tiled=True)]
    all_to_all x2 -> x1, blocking collectives: 75.5 us -> 39.2 us  [body(): lax.all_to_all(outgoing, 'expert', split_axis=0, concat_axis=0, tiled=True)]
    all_to_all x0 -> x1, waiting for transfers between devices: none -> 16.8 us  [body(): lax.all_to_all(outgoings[0], 'expert', split_axis=0, concat_axis=0, tiled...]
    ppermute x3, waiting for transfers between devices: 25.8 us -> 11.9 us  [exchange_columns(): pieces.append(lax.ppermute(outgoing, 'dp', pairs))]
    all_to_all x0 -> x1, starting transfers between devices: none -> 12.2 us  [body(): lax.all_to_all(outgoings[0], 'expert', split_axis=0, concat_axis=0, tiled...]
    all_to_all x4 -> x2, local copies, waits for them, and re-layouts: 9.65 us -> 4.8 us  [body(): lax.all_to_all(outgoing, 'expert', split_axis=0, concat_axis=0, tiled=True)]
    all_to_all x0 -> x2, local copies, waits for them, and re-layouts: none -> 4.83 us  [body(): lax.all_to_all(outgoings[0], 'expert', split_axis=0, concat_axis=0, tiled...]
  transfers between devices with their start and end apart: 9 -> 10, of which waited for: 9 -> 8; matrix products, arithmetic and copies ran while one was open for 16% -> 15% of each run, Pallas kernels for 0% -> 0%
where the time goes in v10:
time: 357 us; the launch traced here: 355 us
  waiting for transfers between devices  184 us (52%)
  blocking collectives  48 us (13%)
  matrix products  43.2 us (12%)
  starting transfers between devices  35 us (10%)
  local copies, waits for them, and re-layouts  29.6 us (8%)
  between operations  14.2 us (4%)
    all_gather x2, waiting for transfers between devices, body(): gathered = lax.all_gather(arrived, 'dp', axis=0, tiled=True)  91.1 us
    all_to_all x1, blocking collectives, body(): lax.all_to_all(outgoing, 'expert', split_axis=0, concat_axis=0, tiled=True)  39.2 us
    all_to_all x2, waiting for transfers between devices, body(): lax.all_to_all(by_source, 'expert', split_axis=0, concat_axis=0, tiled=True)  32.9 us
    all_gather x2, waiting for transfers between devices, body(): gathered_hidden = lax.all_gather(activated, 'dp', axis=0, tiled=False)  30.4 us
    all_to_all x1, waiting for transfers between devices, body(): lax.all_to_all(outgoings[0], 'expert', split_axis=0, concat_axis=0, tiled...  16.8 us
    all_to_all x2, starting transfers between devices, body(): lax.all_to_all(by_source, 'expert', split_axis=0, concat_axis=0, tiled=True)  16.6 us
    dot_general x6, matrix products, body(): jnp.dot(hidden_all[shift], down_cols[shift], preferred_element_type=jnp.f...  13.7 us
    all_to_all x1, starting transfers between devices, body(): lax.all_to_all(outgoings[0], 'expert', split_axis=0, concat_axis=0, tiled...  12.2 us
  transfers between devices with their start and end apart: 10, of which 8 were waited for; matrix products, arithmetic and copies ran while one was open for 15% of the time, Pallas kernels for 0%

profile of v10, /device:TPU:2, one launch (start us, length us, event | category | flops | bytes accessed | tf_op | source)
XLA Modules:
  0.0 355.5 jit_solution(1705867965900836746)
XLA Ops:
  6.5 0.9 copy.29
  8.2 0.7 fusion.68
  9.7 1.9 reshape.213
  11.7 2.5 convolution_convert_fusion.1
  14.1 2.5 all_to_all.25
  16.7 12.2 %all-to-all-start = ((bf16[64,2,4096]{2,1,0:T(2,128)(2,1)}), bf16[64,2,4096]{2,1,0:T(2,128)(2,1)}, u32[]{:S(2)}, u32[]{:S(2)}) async-start(bf16[64,2,4096]{2,1,0:T(2,128)(2,1)} %all_to_all.25), calls=%async_computation | async-start | bytes 2097152 | tf_op jit(solution)/shard_map/all_to_all | solution.py:71
  29.0 3.6 dynamic-slice_bitcast_fusion
  32.5 1.6 collective-permute-start
  34.1 2.9 collective-permute-start.1
  37.0 1.3 collective-permute-start.2
  38.4 2.4 convolution_convert_fusion
  40.8 16.8 %all-to-all-done = bf16[64,2,4096]{2,1,0:T(2,128)(2,1)} async-done(((bf16[64,2,4096]{2,1,0:T(2,128)(2,1)}), bf16[64,2,4096]{2,1,0:T(2,128)(2,1)}, u32[]{:S(2)}, u32[]{:S(2)}) %all-to-all-start) | async-done | bytes 1048608 | tf_op jit(solution)/shard_map/all_to_all | solution.py:71
  57.6 2.3 all_to_all.27
  59.9 11.9 %collective-permute-done.1 = bf16[384,1024]{1,0:T(8,128)(2,1)} collective-permute-done((bf16[384,1024]{1,0:T(8,128)(2,1)}, bf16[384,1024]{1,0:T(8,128)(2,1)}, u32[]{:S(2)}, u32[]{:S(2)}) %collective-permute-start.1) | collective-permute-done | bytes 786464 | tf_op jit(solution)/shard_map/ppermute | solution.py:16
  71.7 2.5 all_to_all.29
  74.3 39.2 %all_to_all.39 = bf16[64,2,4096]{2,1,0:T(2,128)(2,1)} all-to-all(bf16[64,2,4096]{2,1,0:T(2,128)(2,1)} %all_to_all.29), channel_id=1, replica_groups=mesh['dp'=4,'expert'=64] {'expert'}, dimensions={0} | all-to-all | bytes 2097152 | tf_op jit(solution)/shard_map/all_to_all | solution.py:75
  113.5 2.3 all_to_all.31
  115.8 0.7 all-gather.7.cloned.1.call-update
  116.6 46.2 %all-gather.9.cloned.1.call-done = bf16[512,4096]{1,0:T(8,128)(2,1)} async-done(((bf16[128,4096]{1,0:T(8,128)(2,1)}), bf16[512,4096]{1,0:T(8,128)(2,1)}) %all-gather.9.cloned.1.call-update) | async-done | bytes 4194320 | tf_op jit(solution)/shard_map/all_gather | solution.py:78
  162.7 4.7 %fusion.4 = f32[512,384]{1,0:T(8,128)S(1)} fusion(bf16[512,4096]{1,0:T(8,128)(2,1)} %all-gather.9.cloned.1.call-done, bf16[1,4096,384]{2,1,0:T(8,128)(2,1)S(1)} %copy-done), kind=kOutput, calls=%fused_computation.7 | convolution fusion | flops 1610612736 | bytes 8126464 | tf_op jit(solution)/shard_map/dot_general | solution.py:79
  167.4 3.1 fusion.14
  170.8 45.0 %all-gather.7.cloned.1.call-done = bf16[512,4096]{1,0:T(8,128)(2,1)} async-done(((bf16[128,4096]{1,0:T(8,128)(2,1)}), bf16[512,4096]{1,0:T(8,128)(2,1)}) %all-gather.7.cloned.1.call-update) | async-done | bytes 4194320 | tf_op jit(solution)/shard_map/all_gather | solution.py:78
  215.8 4.7 %fusion.6 = f32[512,384]{1,0:T(8,128)S(1)} fusion(bf16[512,4096]{1,0:T(8,128)(2,1)} %all-gather.7.cloned.1.call-done, bf16[1,4096,384]{2,1,0:T(8,128)(2,1)S(1)} %copy-done), kind=kOutput, calls=%fused_computation.9 | convolution fusion | flops 1610612736 | bytes 8126464 | tf_op jit(solution)/shard_map/dot_general | solution.py:79
  220.4 3.1 fusion.17
  223.6 23.4 %all-gather.13.cloned.1.call-done = bf16[2048,384]{1,0:T(8,128)(2,1)} async-done(((bf16[512,384]{1,0:T(8,128)(2,1)}), bf16[2048,384]{1,0:T(8,128)(2,1)}) %all-gather.13.cloned.1.call-update) | async-done | bytes 1572880 | tf_op jit(solution)/shard_map/all_gather | solution.py:82
  247.1 2.1 fusion.29
  249.2 0.7 fusion.31
  249.9 1.9 fusion.27
  251.8 2.9 add_convert_fusion
  254.6 2.2 reshape.215
  256.9 3.4 copy.47
  260.2 10.7 %all-to-all-start.3 = ((bf16[64,4,2,1024]{3,2,1,0:T(2,128)(2,1)}), bf16[64,4,2,1024]{3,2,1,0:T(2,128)(2,1)}, u32[]{:S(2)}, u32[]{:S(2)}) async-start(bf16[64,4,2,1024]{3,2,1,0:T(2,128)(2,1)} %bitcast.100), calls=%async_computation.3 | async-start | bytes 2097152 | tf_op jit(solution)/shard_map/all_to_all | solution.py:98
  271.0 7.0 %all-gather.11.cloned.1.call-done = bf16[2048,384]{1,0:T(8,128)(2,1)} async-done(((bf16[512,384]{1,0:T(8,128)(2,1)}), bf16[2048,384]{1,0:T(8,128)(2,1)}) %all-gather.11.cloned.1.call-update) | async-done | bytes 1572880 | tf_op jit(solution)/shard_map/all_gather | solution.py:82
  277.9 2.1 fusion.39
  280.1 0.7 fusion.41
  280.8 1.9 fusion.37
  282.7 2.9 add_convert_fusion.1
  285.5 2.2 reshape.214
  287.8 3.4 copy.48
  291.2 8.5 %all-to-all-done.3 = bf16[64,4,2,1024]{3,2,1,0:T(2,128)(2,1)} async-done(((bf16[64,4,2,1024]{3,2,1,0:T(2,128)(2,1)}), bf16[64,4,2,1024]{3,2,1,0:T(2,128)(2,1)}, u32[]{:S(2)}, u32[]{:S(2)}) %all-to-all-start.3) | async-done | bytes 1048608 | tf_op jit(solution)/shard_map/all_to_all | solution.py:98
  299.7 5.9 %all-to-all-start.1 = ((bf16[64,4,2,1024]{3,2,1,0:T(2,128)(2,1)}), bf16[64,4,2,1024]{3,2,1,0:T(2,128)(2,1)}, u32[]{:S(2)}, u32[]{:S(2)}) async-start(bf16[64,4,2,1024]{3,2,1,0:T(2,128)(2,1)} %bitcast.99), calls=%async_computation.1 | async-start | bytes 2097152 | tf_op jit(solution)/shard_map/all_to_all | solution.py:98
  305.7 0.3 select_reduce_fusion
  306.2 3.7 %convolution_bitcast_fusion = f32[64,1024]{1,0:T(8,128)} fusion(bf16[64,4,2,1024]{3,2,1,0:T(2,128)(2,1)} %all-to-all-done.3, s32[4,2]{1,0:T(4,128)S(1)} %iota_add_fusion, f32[64,64]{1,0:T(8,128)S(1)} %select_reduce_fusion, s32[64,64]{1,0:T(8,128)S(1)} %sub.32, pred[64,64]{1,0:T(8,128)(4,1)S(1)} %broadcast_compare_fusion), kind=kOutput, calls=%fused_computation.17 | convolution fusion | flops 402751488 | bytes 1347616 | tf_op jit(solution)/shard_map/dot_general | solution.py:105
  309.8 24.4 %all-to-all-done.1 = bf16[64,4,2,1024]{3,2,1,0:T(2,128)(2,1)} async-done(((bf16[64,4,2,1024]{3,2,1,0:T(2,128)(2,1)}), bf16[64,4,2,1024]{3,2,1,0:T(2,128)(2,1)}, u32[]{:S(2)}, u32[]{:S(2)}) %all-to-all-start.1) | async-done | bytes 1048608 | tf_op jit(solution)/shard_map/all_to_all | solution.py:98
  334.3 3.7 %fusion.20 = f32[64,1024]{1,0:T(8,128)} fusion(f32[64,1024]{1,0:T(8,128)} %convolution_bitcast_fusion, bf16[64,4,2,1024]{3,2,1,0:T(2,128)(2,1)} %all-to-all-done.1, f32[64,64]{1,0:T(8,128)S(1)} %select_reduce_fusion, s32[4,2]{1,0:T(4,128)S(1)} %iota_add_fusion.1, s32[64,64]{1,0:T(8,128)S(1)} %sub.32, pred[64,64]{1,0:T(8,128)(4,1)S(1)} %broadcast_compare_fusion), kind=kOutput, calls=%fused_computation.19 | convolution fusion | flops 402817024 | bytes 1609760 | tf_op jit(solution)/shard_map/dot_general | solution.py:105
  338.0 1.1 reshape.216
  339.4 8.8 %all_to_all.40 = bf16[4,4,4,1024]{3,2,1,0:T(4,128)(2,1)S(1)} all-to-all(bf16[4,4,4,1024]{3,2,1,0:T(4,128)(2,1)S(1)} %reshape.217), channel_id=1, replica_groups=mesh['dp'=4,'expert'=64] {'dp'}, dimensions={0} | all-to-all | bytes 262144 | tf_op jit(solution)/shard_map/all_to_all | solution.py:123
  348.2 0.7 copy.40
  (52 shorter events, 1.9 us)
Async XLA Ops:
  6.5 156.2 %copy-start = (bf16[1,4096,384]{2,1,0:T(8,128)(2,1)S(1)}, bf16[1,4096,384]{2,1,0:T(8,128)(2,1)}, u32[]{:S(2)}) copy-start(bf16[1,4096,384]{2,1,0:T(8,128)(2,1)} %param.15) | copy-start | bytes 9437188
  16.7 40.9 %all-to-all-start = ((bf16[64,2,4096]{2,1,0:T(2,128)(2,1)}), bf16[64,2,4096]{2,1,0:T(2,128)(2,1)}, u32[]{:S(2)}, u32[]{:S(2)}) async-start(bf16[64,2,4096]{2,1,0:T(2,128)(2,1)} %all_to_all.25), calls=%async_computation | async-start | bytes 2097152 | tf_op jit(solution)/shard_map/all_to_all | solution.py:71
  28.9 133.8 %all-gather.9.cloned.1.call-start = ((), (), s32[]{:S(2)}) async-start(), calls=%async_computation.6 | async-start | bytes 5242880 | tf_op jit(solution)/shard_map/all_gather | solution.py:78
  32.5 27.4 %collective-permute-start = (bf16[384,1024]{1,0:T(8,128)(2,1)}, bf16[384,1024]{1,0:T(8,128)(2,1)}, u32[]{:S(2)}, u32[]{:S(2)}) collective-permute-start(bf16[384,1024]{1,0:T(8,128)(2,1)} %get-tuple-element.18), channel_id=1, source_target_pairs={{0,64},{64,128},{128,192},{192,0},{1,65},{65,129},{129,193},{193,1... | collective-permute-start | bytes 2359304 | tf_op jit(solution)/shard_map/ppermute | solution.py:16
  34.1 37.6 %collective-permute-start.1 = (bf16[384,1024]{1,0:T(8,128)(2,1)}, bf16[384,1024]{1,0:T(8,128)(2,1)}, u32[]{:S(2)}, u32[]{:S(2)}) collective-permute-start(bf16[384,1024]{1,0:T(8,128)(2,1)} %get-tuple-element.20), channel_id=1, source_target_pairs={{0,128},{64,192},{128,0},{192,64},{1,129},{65,193},{129,1},{193,65... | collective-permute-start | bytes 2359304 | tf_op jit(solution)/shard_map/ppermute | solution.py:16
  37.0 34.7 %collective-permute-start.2 = (bf16[384,1024]{1,0:T(8,128)(2,1)}, bf16[384,1024]{1,0:T(8,128)(2,1)}, u32[]{:S(2)}, u32[]{:S(2)}) collective-permute-start(bf16[384,1024]{1,0:T(8,128)(2,1)} %get-tuple-element.17), channel_id=1, source_target_pairs={{0,192},{64,0},{128,64},{192,128},{1,193},{65,1},{129,65},{193,129... | collective-permute-start | bytes 2359304 | tf_op jit(solution)/shard_map/ppermute | solution.py:16
  115.8 100.0 %all-gather.7.cloned.1.call-start = ((), (), s32[]{:S(2)}) async-start(), calls=%async_computation.5 | async-start | bytes 5242880 | tf_op jit(solution)/shard_map/all_gather | solution.py:78
  116.5 130.5 %all-gather.13.cloned.1.call-start = ((), (), s32[]{:S(2)}) async-start(), calls=%async_computation.8 | async-start | bytes 1966080 | tf_op jit(solution)/shard_map/all_gather | solution.py:82
  162.7 4.7 %copy-start.7 = (bf16[512,4096]{1,0:T(8,128)(2,1)S(1)}, bf16[512,4096]{1,0:T(8,128)(2,1)}, u32[]{:S(2)}) copy-start(bf16[512,4096]{1,0:T(8,128)(2,1)} %all-gather.9.cloned.1.call-done) | copy-start | bytes 12582916
  162.7 4.7 %copy-start.8 = (bf16[1,4096,384]{2,1,0:T(8,128)(2,1)S(1)}, bf16[1,4096,384]{2,1,0:T(8,128)(2,1)}, u32[]{:S(2)}) copy-start(bf16[1,4096,384]{2,1,0:T(8,128)(2,1)} %param.16) | copy-start | bytes 9437188
  170.6 107.4 %all-gather.11.cloned.1.call-start = ((), (), s32[]{:S(2)}) async-start(), calls=%async_computation.7 | async-start | bytes 1966080 | tf_op jit(solution)/shard_map/all_gather | solution.py:82
  215.8 4.7 %copy-start.6 = (bf16[512,4096]{1,0:T(8,128)(2,1)S(1)}, bf16[512,4096]{1,0:T(8,128)(2,1)}, u32[]{:S(2)}) copy-start(bf16[512,4096]{1,0:T(8,128)(2,1)} %all-gather.7.cloned.1.call-done) | copy-start | bytes 12582916
  215.8 4.7 %copy-start.9 = (bf16[1,4096,384]{2,1,0:T(8,128)(2,1)S(1)}, bf16[1,4096,384]{2,1,0:T(8,128)(2,1)}, u32[]{:S(2)}) copy-start(bf16[1,4096,384]{2,1,0:T(8,128)(2,1)} %param.16) | copy-start | bytes 9437188
  247.1 2.1 copy-start.1
  247.1 2.1 copy-start.4
  260.2 39.5 %all-to-all-start.3 = ((bf16[64,4,2,1024]{3,2,1,0:T(2,128)(2,1)}), bf16[64,4,2,1024]{3,2,1,0:T(2,128)(2,1)}, u32[]{:S(2)}, u32[]{:S(2)}) async-start(bf16[64,4,2,1024]{3,2,1,0:T(2,128)(2,1)} %bitcast.100), calls=%async_computation.3 | async-start | bytes 2097152 | tf_op jit(solution)/shard_map/all_to_all | solution.py:98
  277.9 2.1 copy-start.2
  277.9 2.1 copy-start.3
  287.8 17.8 %copy-start.5 = (f32[16,4,8]{0,2,1:T(8,128)S(1)}, f32[16,4,8]{0,2,1:T(8,128)}, u32[]{:S(2)}) copy-start(f32[16,4,8]{0,2,1:T(8,128)} %param.11) | copy-start | bytes 6148
  287.8 18.2 %copy-start.10 = (s32[16]{0:T(128)S(1)}, s32[16]{0:T(128)}, u32[]{:S(2)}) copy-start(s32[16]{0:T(128)} %param.14) | copy-start | bytes 196
  299.7 34.6 %all-to-all-start.1 = ((bf16[64,4,2,1024]{3,2,1,0:T(2,128)(2,1)}), bf16[64,4,2,1024]{3,2,1,0:T(2,128)(2,1)}, u32[]{:S(2)}, u32[]{:S(2)}) async-start(bf16[64,4,2,1024]{3,2,1,0:T(2,128)(2,1)} %bitcast.99), calls=%async_computation.1 | async-start | bytes 2097152 | tf_op jit(solution)/shard_map/all_to_all | solution.py:98
Sparse Core Ops, SparseCore 0:
  115.9 46.8 all-gather.8
  164.5 51.1 all-gather.6
  217.6 29.4 all-gather.12
  248.7 29.1 all-gather.10

commit v11 on v6

--- a/solution.py
+++ b/solution.py
@@ -6,12 +6,12 @@
 MOST_BASE = 16
 
 
-def exchange_gather(blocks, replica, replica_count):
-    pieces = [lax.dynamic_index_in_dim(blocks, replica, 0, keepdims=False)]
+def exchange_gather(matrix, replica, replica_count):
+    width = matrix.shape[1] // replica_count
+    pieces = [lax.dynamic_slice_in_dim(matrix, replica * width, width, axis=1)]
     for shift in range(1, replica_count):
-        outgoing = lax.dynamic_index_in_dim(
-            blocks, (replica + shift) % replica_count, 0, keepdims=False
-        )
+        start = ((replica + shift) % replica_count) * width
+        outgoing = lax.dynamic_slice_in_dim(matrix, start, width, axis=1)
         pairs = [(i, (i + shift) % replica_count) for i in range(replica_count)]
         pieces.append(lax.ppermute(outgoing, "dp", pairs))
     return jnp.stack(pieces, axis=0)
@@ -39,8 +39,7 @@
     slot_count = min(tokens, max(MOST_BASE, 2 * tokens * top_count // expert_count))
     slot_count = -(-slot_count // replica_count) * replica_count
     part = slot_count // replica_count
-    down_blocks = w_down[0].reshape(hidden_part, replica_count, columns).transpose(1, 0, 2)
-    down_cols = exchange_gather(down_blocks, replica, replica_count)
+    down_cols = exchange_gather(w_down[0], replica, replica_count)
     step_ids = lax.broadcasted_iota(jnp.int32, (row_count, step_count), 1)
     live_mask = ((step_ids < finish_step[:, None]) & (group_keep[0] == 1)).reshape(tokens)
     gate_share = route_weight / jnp.sum(route_weight, axis=2, keepdims=True)

time: 326 us -> 309 us (0.948)
  local copies, waits for them, and re-layouts: 49.2 us -> 28.9 us
  waiting for transfers between devices: 101 us -> 105 us
    another operation x2 -> x0, local copies, waits for them, and re-layouts: 17.8 us -> none
    unnamed x27 -> x23, local copies, waits for them, and re-layouts: 6.2 us -> 0.12 us
    ppermute x3, waiting for transfers between devices: 22.6 us -> 27 us  [exchange_gather(): pieces.append(lax.ppermute(outgoing, 'dp', pairs))]
    dynamic_slice x0 -> x1, local copies, waits for them, and re-layouts: none -> 3.71 us  [exchange_gather(): pieces = [lax.dynamic_slice_in_dim(matrix, replica * width, width, axis=1)]]
  transfers between devices with their start and end apart: 13 -> 13, of which waited for: 11 -> 10; matrix products, arithmetic and copies ran while one was open for 15% -> 14% of each run, Pallas kernels for 0% -> 0%
where the time goes in v11:
time: 309 us; the launch traced here: 308 us
  waiting for transfers between devices  105 us (34%)
  blocking collectives  84.9 us (27%)
  starting transfers between devices  36.9 us (12%)
  matrix products  33.8 us (11%)
  local copies, waits for them, and re-layouts  28.9 us (9%)
  between operations  14.3 us (5%)
  other arithmetic  4.31 us (1%)
    all_to_all x2, blocking collectives, body(): lax.all_to_all(outgoing, 'expert', split_axis=0, concat_axis=0, tiled=True)  75.5 us
    ppermute x6, waiting for transfers between devices, exchange_all(): pieces.append(lax.ppermute(block, 'dp', pairs))  44.6 us
    ppermute x3, waiting for transfers between devices, exchange_gather(): pieces.append(lax.ppermute(outgoing, 'dp', pairs))  27 us
    all_to_all x2, waiting for transfers between devices, body(): lax.all_to_all(by_source, 'expert', split_axis=0, concat_axis=0, tiled=True)  24.4 us
    all_to_all x2, starting transfers between devices, body(): lax.all_to_all(by_source, 'expert', split_axis=0, concat_axis=0, tiled=True)  21.4 us
    reshape x4, local copies, waits for them, and re-layouts, body(): expert_cols.reshape(replica_count, expert_count, sub, columns)  11.2 us
    all_to_all x4, local copies, waits for them, and re-layouts, body(): lax.all_to_all(outgoing, 'expert', split_axis=0, concat_axis=0, tiled=True)  9.63 us
    ppermute x6, starting transfers between devices, exchange_all(): pieces.append(lax.ppermute(block, 'dp', pairs))  9.55 us
  transfers between devices with their start and end apart: 13, of which 10 were waited for; matrix products, arithmetic and copies ran while one was open for 14% of the time, Pallas kernels for 0%

profile of v11, /device:TPU:2, one launch (start us, length us, event | category | flops | bytes accessed | tf_op | source)
XLA Modules:
  0.0 307.8 jit_solution(12428345920649276187)
XLA Ops:
  6.5 3.7 %constant_dynamic-slice_fusion = (bf16[1,384,1024]{2,1,0:T(8,128)(2,1)}, bf16[384,1024]{1,0:T(8,128)(2,1)}, bf16[384,1024]{1,0:T(8,128)(2,1)}, bf16[384,1024]{1,0:T(8,128)(2,1)}) fusion(bf16[1,384,4096]{2,1,0:T(8,128)(2,1)} %param.17, s32[]{:T(128)S(6)} %select_n.57, s32[]{:T(128)S(6)} %select_n.59, s32[]{:T(128)S(6)} %select_n.63, s32[]{:T(128)S(6)} %select_n.61), kind=kLoop, calls=%fused_computation.81 | loop fusion | bytes 6291472 | tf_op jit(solution)/shard_map/dynamic_slice | solution.py:11
  10.3 1.6 collective-permute-start.3
  11.8 2.9 collective-permute-start.4
  14.7 1.3 collective-permute-start.5
  17.5 2.0 reshape.214
  19.7 2.5 convolution_convert_fusion
  22.2 9.0 %collective-permute-done.3 = bf16[384,1024]{1,0:T(8,128)(2,1)} collective-permute-done((bf16[384,1024]{1,0:T(8,128)(2,1)}, bf16[384,1024]{1,0:T(8,128)(2,1)}, u32[]{:S(2)}, u32[]{:S(2)}) %collective-permute-start.3) | collective-permute-done | bytes 786464 | tf_op jit(solution)/shard_map/ppermute | solution.py:16
  31.1 18.0 %collective-permute-done.4 = bf16[384,1024]{1,0:T(8,128)(2,1)} collective-permute-done((bf16[384,1024]{1,0:T(8,128)(2,1)}, bf16[384,1024]{1,0:T(8,128)(2,1)}, u32[]{:S(2)}, u32[]{:S(2)}) %collective-permute-start.4) | collective-permute-done | bytes 786464 | tf_op jit(solution)/shard_map/ppermute | solution.py:16
  49.2 3.3 %pad_maximum_fusion = bf16[4,384,1024]{2,1,0:T(8,128)(2,1)} fusion(bf16[1,384,1024]{2,1,0:T(8,128)(2,1)} %bitcast.14, bf16[1,384,1024]{2,1,0:T(8,128)(2,1)} %bitcast.12, bf16[1,384,1024]{2,1,0:T(8,128)(2,1)} %bitcast.10, bf16[1,384,1024]{2,1,0:T(8,128)(2,1)} %get-tuple-element.9), kind=kLoop, calls=%fused_computation.3 | loop fusion | flops 4718592 | bytes 6291456 | tf_op jit(solution)/shard_map/stack | solution.py:17
  52.4 2.5 all_to_all.29
  55.0 40.9 %all_to_all.39 = bf16[64,2,4096]{2,1,0:T(2,128)(2,1)} all-to-all(bf16[64,2,4096]{2,1,0:T(2,128)(2,1)} %all_to_all.29), channel_id=1, replica_groups=mesh['dp'=4,'expert'=64] {'expert'}, dimensions={0} | all-to-all | bytes 2097152 | tf_op jit(solution)/shard_map/all_to_all | solution.py:70
  95.9 2.3 all_to_all.31
  98.3 2.5 convolution_convert_fusion.1
  100.7 2.5 all_to_all.25
  103.3 34.6 %all_to_all.40 = bf16[64,2,4096]{2,1,0:T(2,128)(2,1)} all-to-all(bf16[64,2,4096]{2,1,0:T(2,128)(2,1)} %all_to_all.25), channel_id=1, replica_groups=mesh['dp'=4,'expert'=64] {'expert'}, dimensions={0} | all-to-all | bytes 2097152 | tf_op jit(solution)/shard_map/all_to_all | solution.py:70
  137.8 2.3 all_to_all.27
  140.1 5.0 %all-gather.5.cloned.1.call-done = bf16[512,4096]{1,0:T(8,128)(2,1)} async-done(((bf16[128,4096]{1,0:T(8,128)(2,1)}), bf16[512,4096]{1,0:T(8,128)(2,1)}) %all-gather.5.cloned.1.call-update) | async-done | bytes 4194320 | tf_op jit(solution)/shard_map/all_gather | solution.py:71
  145.1 4.7 %fusion.4 = f32[512,384]{1,0:T(8,128)S(1)} fusion(bf16[512,4096]{1,0:T(8,128)(2,1)} %all-gather.5.cloned.1.call-done, bf16[1,4096,384]{2,1,0:T(8,128)(2,1)S(1)} %copy-done), kind=kOutput, calls=%fused_computation.8 | convolution fusion | flops 1610612736 | bytes 8126464 | tf_op jit(solution)/shard_map/dot_general | solution.py:72
  149.8 2.3 fusion.28
  152.2 0.9 collective-permute-start.6
  153.1 1.7 collective-permute-start.7
  154.8 2.1 collective-permute-start.8
  157.0 12.8 %collective-permute-done.6 = bf16[512,384]{1,0:T(8,128)(2,1)S(1)} collective-permute-done((bf16[512,384]{1,0:T(8,128)(2,1)S(1)}, bf16[512,384]{1,0:T(8,128)(2,1)S(1)}, u32[]{:S(2)}, u32[]{:S(2)}) %collective-permute-start.6) | collective-permute-done | bytes 393248 | tf_op jit(solution)/shard_map/ppermute | solution.py:24
  169.7 11.1 %collective-permute-done.7 = bf16[512,384]{1,0:T(8,128)(2,1)S(1)} collective-permute-done((bf16[512,384]{1,0:T(8,128)(2,1)S(1)}, bf16[512,384]{1,0:T(8,128)(2,1)S(1)}, u32[]{:S(2)}, u32[]{:S(2)}) %collective-permute-start.7) | collective-permute-done | bytes 393248 | tf_op jit(solution)/shard_map/ppermute | solution.py:24
  180.8 3.8 %collective-permute-done.8 = bf16[512,384]{1,0:T(8,128)(2,1)S(1)} collective-permute-done((bf16[512,384]{1,0:T(8,128)(2,1)S(1)}, bf16[512,384]{1,0:T(8,128)(2,1)S(1)}, u32[]{:S(2)}, u32[]{:S(2)}) %collective-permute-start.8) | collective-permute-done | bytes 393248 | tf_op jit(solution)/shard_map/ppermute | solution.py:24
  184.7 2.8 bitcast_convert_fusion
  187.5 2.2 reshape.216
  189.7 3.4 %copy.47 = bf16[4,64,2,1024]{3,2,0,1:T(2,128)(2,1)} copy(bf16[4,64,2,1024]{3,2,1,0:T(2,128)(2,1)} %reshape.216) | data formatting | bytes 2097152 | tf_op jit(solution)/shard_map/reshape | solution.py:82
  193.1 10.7 %all-to-all-start.3 = ((bf16[64,4,2,1024]{3,2,1,0:T(2,128)(2,1)}), bf16[64,4,2,1024]{3,2,1,0:T(2,128)(2,1)}, u32[]{:S(2)}, u32[]{:S(2)}) async-start(bf16[64,4,2,1024]{3,2,1,0:T(2,128)(2,1)} %bitcast.75), calls=%async_computation.3 | async-start | bytes 2097152 | tf_op jit(solution)/shard_map/all_to_all | solution.py:85
  203.8 3.6 %all-gather.3.cloned.1.call-done = bf16[512,4096]{1,0:T(8,128)(2,1)} async-done(((bf16[128,4096]{1,0:T(8,128)(2,1)}), bf16[512,4096]{1,0:T(8,128)(2,1)}) %all-gather.3.cloned.1.call-update) | async-done | bytes 4194320 | tf_op jit(solution)/shard_map/all_gather | solution.py:71
  207.5 4.7 %fusion.6 = f32[512,384]{1,0:T(8,128)S(1)} fusion(bf16[512,4096]{1,0:T(8,128)(2,1)} %all-gather.3.cloned.1.call-done, bf16[1,4096,384]{2,1,0:T(8,128)(2,1)S(1)} %copy-done), kind=kOutput, calls=%fused_computation.10 | convolution fusion | flops 1610612736 | bytes 8126464 | tf_op jit(solution)/shard_map/dot_general | solution.py:72
  212.2 2.3 fusion.31
  214.5 1.5 collective-permute-start
  216.0 2.7 collective-permute-start.1
  218.7 0.6 collective-permute-start.2
  219.3 7.6 %collective-permute-done = bf16[512,384]{1,0:T(8,128)(2,1)S(1)} collective-permute-done((bf16[512,384]{1,0:T(8,128)(2,1)S(1)}, bf16[512,384]{1,0:T(8,128)(2,1)S(1)}, u32[]{:S(2)}, u32[]{:S(2)}) %collective-permute-start) | collective-permute-done | bytes 393248 | tf_op jit(solution)/shard_map/ppermute | solution.py:24
  226.9 9.3 %collective-permute-done.1 = bf16[512,384]{1,0:T(8,128)(2,1)S(1)} collective-permute-done((bf16[512,384]{1,0:T(8,128)(2,1)S(1)}, bf16[512,384]{1,0:T(8,128)(2,1)S(1)}, u32[]{:S(2)}, u32[]{:S(2)}) %collective-permute-start.1) | collective-permute-done | bytes 393248 | tf_op jit(solution)/shard_map/ppermute | solution.py:24
  236.2 4.4 %bitcast_convert_fusion.1 = bf16[512,1024]{1,0:T(8,128)(2,1)} fusion(bf16[1,512,384]{2,1,0:T(8,128)(2,1)S(1)} %bitcast.87, bf16[1,512,384]{2,1,0:T(8,128)(2,1)S(1)} %bitcast.85, bf16[1,512,384]{2,1,0:T(8,128)(2,1)S(1)} %bitcast.83, bf16[1,512,384]{2,1,0:T(8,128)(2,1)S(1)} %bitcast.81, bf16[1,384,1024]{2,1,0:T(8,128)(2,1)} %bitcast.14, ...), kind=kOutput, calls=%fused_computation.13 | convolution fusion | flops 1618214912 | bytes 5767168 | tf_op jit(solution)/shard_map/dot_general | solution.py:76
  240.6 2.3 reshape.215
  242.9 3.4 %copy.48 = bf16[4,64,2,1024]{3,2,0,1:T(2,128)(2,1)} copy(bf16[4,64,2,1024]{3,2,1,0:T(2,128)(2,1)} %reshape.215) | data formatting | bytes 2097152 | tf_op jit(solution)/shard_map/reshape | solution.py:82
  246.2 10.7 %all-to-all-start.1 = ((bf16[64,4,2,1024]{3,2,1,0:T(2,128)(2,1)}), bf16[64,4,2,1024]{3,2,1,0:T(2,128)(2,1)}, u32[]{:S(2)}, u32[]{:S(2)}) async-start(bf16[64,4,2,1024]{3,2,1,0:T(2,128)(2,1)} %bitcast.76), calls=%async_computation.1 | async-start | bytes 2097152 | tf_op jit(solution)/shard_map/all_to_all | solution.py:85
  257.1 0.3 select_reduce_fusion
  257.6 3.7 %convolution_bitcast_fusion = f32[64,1024]{1,0:T(8,128)} fusion(bf16[64,4,2,1024]{3,2,1,0:T(2,128)(2,1)} %all-to-all-done.3, s32[4,2]{1,0:T(4,128)S(1)} %iota_add_fusion, f32[64,64]{1,0:T(8,128)S(1)} %select_reduce_fusion, s32[64,64]{1,0:T(8,128)S(1)} %sub.20, pred[64,64]{1,0:T(8,128)(4,1)S(1)} %broadcast_compare_fusion), kind=kOutput, calls=%fused_computation.32 | convolution fusion | flops 402751488 | bytes 1347616 | tf_op jit(solution)/shard_map/dot_general | solution.py:92
  261.3 24.4 %all-to-all-done.1 = bf16[64,4,2,1024]{3,2,1,0:T(2,128)(2,1)} async-done(((bf16[64,4,2,1024]{3,2,1,0:T(2,128)(2,1)}), bf16[64,4,2,1024]{3,2,1,0:T(2,128)(2,1)}, u32[]{:S(2)}, u32[]{:S(2)}) %all-to-all-start.1) | async-done | bytes 1048608 | tf_op jit(solution)/shard_map/all_to_all | solution.py:85
  285.7 3.7 %fusion.34 = f32[64,1024]{1,0:T(8,128)} fusion(f32[64,1024]{1,0:T(8,128)} %convolution_bitcast_fusion, bf16[64,4,2,1024]{3,2,1,0:T(2,128)(2,1)} %all-to-all-done.1, f32[64,64]{1,0:T(8,128)S(1)} %select_reduce_fusion, s32[4,2]{1,0:T(4,128)S(1)} %iota_add_fusion.1, s32[64,64]{1,0:T(8,128)S(1)} %sub.20, pred[64,64]{1,0:T(8,128)(4,1)S(1)} %broadcast_compare_fusion), kind=kOutput, calls=%fused_computation.34 | convolution fusion | flops 402817024 | bytes 1609760 | tf_op jit(solution)/shard_map/dot_general | solution.py:92
  289.4 1.1 reshape.217
  290.8 9.4 %all_to_all.41 = bf16[4,4,4,1024]{3,2,1,0:T(4,128)(2,1)S(1)} all-to-all(bf16[4,4,4,1024]{3,2,1,0:T(4,128)(2,1)S(1)} %reshape.218), channel_id=1, replica_groups=mesh['dp'=4,'expert'=64] {'dp'}, dimensions={0} | all-to-all | bytes 262144 | tf_op jit(solution)/shard_map/all_to_all | solution.py:110
  300.3 0.7 copy.40
  (52 shorter events, 1.7 us)
Async XLA Ops:
  6.5 138.6 %copy-start = (bf16[1,4096,384]{2,1,0:T(8,128)(2,1)S(1)}, bf16[1,4096,384]{2,1,0:T(8,128)(2,1)}, u32[]{:S(2)}) copy-start(bf16[1,4096,384]{2,1,0:T(8,128)(2,1)} %param.15) | copy-start | bytes 9437188
  6.5 138.6 %all-gather.5.cloned.1.call-start = ((), (), s32[]{:S(2)}) async-start(), calls=%async_computation.6 | async-start | bytes 5242880 | tf_op jit(solution)/shard_map/all_gather | solution.py:71
  6.5 9.5 %copy-start.4 = (s32[16,4,8]{0,2,1:T(8,128)S(1)}, s32[16,4,8]{0,2,1:T(8,128)}, u32[]{:S(2)}) copy-start(s32[16,4,8]{0,2,1:T(8,128)} %param.10) | copy-start | bytes 6148
  6.5 10.3 %copy-start.5 = (s32[16]{0:T(128)S(1)}, s32[16]{0:T(128)}, u32[]{:S(2)}) copy-start(s32[16]{0:T(128)} %param.12) | copy-start | bytes 196
  10.3 20.9 %collective-permute-start.3 = (bf16[384,1024]{1,0:T(8,128)(2,1)}, bf16[384,1024]{1,0:T(8,128)(2,1)}, u32[]{:S(2)}, u32[]{:S(2)}) collective-permute-start(bf16[384,1024]{1,0:T(8,128)(2,1)} %get-tuple-element.10), channel_id=1, source_target_pairs={{0,64},{64,128},{128,192},{192,0},{1,65},{65,129},{129,193},{193,1... | collective-permute-start | bytes 2359304 | tf_op jit(solution)/shard_map/ppermute | solution.py:16
  11.8 37.3 %collective-permute-start.4 = (bf16[384,1024]{1,0:T(8,128)(2,1)}, bf16[384,1024]{1,0:T(8,128)(2,1)}, u32[]{:S(2)}, u32[]{:S(2)}) collective-permute-start(bf16[384,1024]{1,0:T(8,128)(2,1)} %get-tuple-element.12), channel_id=1, source_target_pairs={{0,128},{64,192},{128,0},{192,64},{1,129},{65,193},{129,1},{193,65... | collective-permute-start | bytes 2359304 | tf_op jit(solution)/shard_map/ppermute | solution.py:16
  14.7 34.4 %collective-permute-start.5 = (bf16[384,1024]{1,0:T(8,128)(2,1)}, bf16[384,1024]{1,0:T(8,128)(2,1)}, u32[]{:S(2)}, u32[]{:S(2)}) collective-permute-start(bf16[384,1024]{1,0:T(8,128)(2,1)} %get-tuple-element.11), channel_id=1, source_target_pairs={{0,192},{64,0},{128,64},{192,128},{1,193},{65,1},{129,65},{193,129... | collective-permute-start | bytes 2359304 | tf_op jit(solution)/shard_map/ppermute | solution.py:16
  98.2 109.3 %all-gather.3.cloned.1.call-start = ((), (), s32[]{:S(2)}) async-start(), calls=%async_computation.5 | async-start | bytes 5242880 | tf_op jit(solution)/shard_map/all_gather | solution.py:71
  145.1 4.7 %copy-start.7 = (bf16[512,4096]{1,0:T(8,128)(2,1)S(1)}, bf16[512,4096]{1,0:T(8,128)(2,1)}, u32[]{:S(2)}) copy-start(bf16[512,4096]{1,0:T(8,128)(2,1)} %all-gather.5.cloned.1.call-done) | copy-start | bytes 12582916
  145.1 4.7 %copy-start.8 = (bf16[1,4096,384]{2,1,0:T(8,128)(2,1)S(1)}, bf16[1,4096,384]{2,1,0:T(8,128)(2,1)}, u32[]{:S(2)}) copy-start(bf16[1,4096,384]{2,1,0:T(8,128)(2,1)} %param.16) | copy-start | bytes 9437188
  149.8 34.8 %copy-start.1 = (bf16[4,384,1024]{2,1,0:T(8,128)(2,1)S(1)}, bf16[4,384,1024]{2,1,0:T(8,128)(2,1)}, u32[]{:S(2)}) copy-start(bf16[4,384,1024]{2,1,0:T(8,128)(2,1)} %pad_maximum_fusion) | copy-start | bytes 9437188
  152.2 17.6 %collective-permute-start.6 = (bf16[512,384]{1,0:T(8,128)(2,1)S(1)}, bf16[512,384]{1,0:T(8,128)(2,1)S(1)}, u32[]{:S(2)}, u32[]{:S(2)}) collective-permute-start(bf16[512,384]{1,0:T(8,128)(2,1)S(1)} %fusion.28), channel_id=1, source_target_pairs={{0,64},{64,128},{128,192},{192,0},{1,65},{65,129},{129,193},{193,1... | collective-permute-start | bytes 1179656 | tf_op jit(solution)/shard_map/ppermute | solution.py:24
  153.1 27.8 %collective-permute-start.7 = (bf16[512,384]{1,0:T(8,128)(2,1)S(1)}, bf16[512,384]{1,0:T(8,128)(2,1)S(1)}, u32[]{:S(2)}, u32[]{:S(2)}) collective-permute-start(bf16[512,384]{1,0:T(8,128)(2,1)S(1)} %fusion.28), channel_id=1, source_target_pairs={{0,128},{64,192},{128,0},{192,64},{1,129},{65,193},{129,1},{193,65... | collective-permute-start | bytes 1179656 | tf_op jit(solution)/shard_map/ppermute | solution.py:24
  154.8 29.8 %collective-permute-start.8 = (bf16[512,384]{1,0:T(8,128)(2,1)S(1)}, bf16[512,384]{1,0:T(8,128)(2,1)S(1)}, u32[]{:S(2)}, u32[]{:S(2)}) collective-permute-start(bf16[512,384]{1,0:T(8,128)(2,1)S(1)} %fusion.28), channel_id=1, source_target_pairs={{0,192},{64,0},{128,64},{192,128},{1,193},{65,1},{129,65},{193,129... | collective-permute-start | bytes 1179656 | tf_op jit(solution)/shard_map/ppermute | solution.py:24
  193.1 53.2 %all-to-all-start.3 = ((bf16[64,4,2,1024]{3,2,1,0:T(2,128)(2,1)}), bf16[64,4,2,1024]{3,2,1,0:T(2,128)(2,1)}, u32[]{:S(2)}, u32[]{:S(2)}) async-start(bf16[64,4,2,1024]{3,2,1,0:T(2,128)(2,1)} %bitcast.75), calls=%async_computation.3 | async-start | bytes 2097152 | tf_op jit(solution)/shard_map/all_to_all | solution.py:85
  207.5 4.7 %copy-start.6 = (bf16[512,4096]{1,0:T(8,128)(2,1)S(1)}, bf16[512,4096]{1,0:T(8,128)(2,1)}, u32[]{:S(2)}) copy-start(bf16[512,4096]{1,0:T(8,128)(2,1)} %all-gather.3.cloned.1.call-done) | copy-start | bytes 12582916
  207.5 4.7 %copy-start.9 = (bf16[1,4096,384]{2,1,0:T(8,128)(2,1)S(1)}, bf16[1,4096,384]{2,1,0:T(8,128)(2,1)}, u32[]{:S(2)}) copy-start(bf16[1,4096,384]{2,1,0:T(8,128)(2,1)} %param.16) | copy-start | bytes 9437188
  212.1 24.0 %copy-start.2 = (bf16[1,384,1024]{2,1,0:T(8,128)(2,1)S(1)}, bf16[1,384,1024]{2,1,0:T(8,128)(2,1)}, u32[]{:S(2)}) copy-start(bf16[1,384,1024]{2,1,0:T(8,128)(2,1)} %get-tuple-element.9) | copy-start | bytes 2359300
  214.5 12.4 %collective-permute-start = (bf16[512,384]{1,0:T(8,128)(2,1)S(1)}, bf16[512,384]{1,0:T(8,128)(2,1)S(1)}, u32[]{:S(2)}, u32[]{:S(2)}) collective-permute-start(bf16[512,384]{1,0:T(8,128)(2,1)S(1)} %fusion.31), channel_id=1, source_target_pairs={{0,64},{64,128},{128,192},{192,0},{1,65},{65,129},{129,193},{193,1... | collective-permute-start | bytes 1179656 | tf_op jit(solution)/shard_map/ppermute | solution.py:24
  216.0 20.2 %collective-permute-start.1 = (bf16[512,384]{1,0:T(8,128)(2,1)S(1)}, bf16[512,384]{1,0:T(8,128)(2,1)S(1)}, u32[]{:S(2)}, u32[]{:S(2)}) collective-permute-start(bf16[512,384]{1,0:T(8,128)(2,1)S(1)} %fusion.31), channel_id=1, source_target_pairs={{0,128},{64,192},{128,0},{192,64},{1,129},{65,193},{129,1},{193,65... | collective-permute-start | bytes 1179656 | tf_op jit(solution)/shard_map/ppermute | solution.py:24
  218.7 17.5 %collective-permute-start.2 = (bf16[512,384]{1,0:T(8,128)(2,1)S(1)}, bf16[512,384]{1,0:T(8,128)(2,1)S(1)}, u32[]{:S(2)}, u32[]{:S(2)}) collective-permute-start(bf16[512,384]{1,0:T(8,128)(2,1)S(1)} %fusion.31), channel_id=1, source_target_pairs={{0,192},{64,0},{128,64},{192,128},{1,193},{65,1},{129,65},{193,129... | collective-permute-start | bytes 1179656 | tf_op jit(solution)/shard_map/ppermute | solution.py:24
  240.6 16.4 %copy-start.3 = (f32[16,4,8]{0,2,1:T(8,128)S(1)}, f32[16,4,8]{0,2,1:T(8,128)}, u32[]{:S(2)}) copy-start(f32[16,4,8]{0,2,1:T(8,128)} %param.11) | copy-start | bytes 6148
  240.6 16.8 %copy-start.10 = (s32[16]{0:T(128)S(1)}, s32[16]{0:T(128)}, u32[]{:S(2)}) copy-start(s32[16]{0:T(128)} %param.14) | copy-start | bytes 196
  246.2 39.4 %all-to-all-start.1 = ((bf16[64,4,2,1024]{3,2,1,0:T(2,128)(2,1)}), bf16[64,4,2,1024]{3,2,1,0:T(2,128)(2,1)}, u32[]{:S(2)}, u32[]{:S(2)}) async-start(bf16[64,4,2,1024]{3,2,1,0:T(2,128)(2,1)} %bitcast.76), calls=%async_computation.1 | async-start | bytes 2097152 | tf_op jit(solution)/shard_map/all_to_all | solution.py:85
Sparse Core Ops, SparseCore 0:
  98.3 46.7 all-gather.4
  146.9 60.4 all-gather.2

commit v12 on v11

--- a/solution.py
+++ b/solution.py
@@ -54,6 +54,27 @@
     sub = part // chunks
     member_ids = lax.broadcasted_iota(jnp.int32, (1, 1, replica_count, 1), 2)
     within_ids = lax.broadcasted_iota(jnp.int32, (1, 1, 1, sub), 3)
+    share_rows = row_count // replica_count
+    flat_device = dest_slot // share_rows
+    target = flat_device // expert_count * share_rows + dest_slot % share_rows
+    position_ids = lax.broadcasted_iota(jnp.int32, (replica_count * share_rows, row_count), 0)
+    arrangement = (target[None, :] == position_ids).astype(jnp.float32)
+    weight = jnp.dot(
+        arrangement,
+        weight.reshape(row_count, step_count * expert_count),
+        precision=lax.Precision.HIGHEST,
+        preferred_element_type=jnp.float32,
+    ).reshape(tokens, expert_count)
+    hit_arranged = jnp.dot(
+        arrangement,
+        hit_mask.reshape(row_count, step_count * expert_count).astype(jnp.float32),
+        precision=lax.Precision.HIGHEST,
+    ).reshape(tokens, expert_count)
+    prior_arranged = jnp.dot(
+        arrangement,
+        prior_hits.reshape(row_count, step_count * expert_count).astype(jnp.float32),
+        precision=lax.Precision.HIGHEST,
+    ).reshape(tokens, expert_count)
     combined = jnp.zeros((tokens, columns), jnp.float32)
     for chunk in range(chunks):
         slot_ids = replica * part + chunk * sub + lax.broadcasted_iota(jnp.int32, (1, 1, sub), 2)
@@ -85,28 +106,20 @@
         returned_rows = lax.all_to_all(by_source, "expert", split_axis=0, concat_axis=0, tiled=True)
         all_slot_ids = member_ids * part + chunk * sub + within_ids
         weighted_place = jnp.where(
-            (hit_mask[:, :, None, None] == 1) & (prior_hits[:, :, None, None] == all_slot_ids),
+            (hit_arranged[:, :, None, None] == 1.0)
+            & (prior_arranged[:, :, None, None] == all_slot_ids.astype(jnp.float32)),
             weight[:, :, None, None],
             0.0,
         ).reshape(tokens, expert_count * replica_count * sub)
-        combined = combined + jnp.dot(
-            weighted_place,
-            returned_rows.reshape(expert_count * replica_count * sub, columns).astype(jnp.float32),
-            precision=lax.Precision.HIGHEST,
-            preferred_element_type=jnp.float32,
+        place_high = weighted_place.astype(jnp.bfloat16)
+        place_low = (weighted_place - place_high.astype(jnp.float32)).astype(jnp.bfloat16)
+        rows_flat = returned_rows.reshape(expert_count * replica_count * sub, columns)
+        combined = (
+            combined
+            + jnp.dot(place_high, rows_flat, preferred_element_type=jnp.float32)
+            + jnp.dot(place_low, rows_flat, preferred_element_type=jnp.float32)
         )
-    share_rows = row_count // replica_count
-    flat_device = dest_slot // share_rows
-    target = flat_device // expert_count * share_rows + dest_slot % share_rows
-    position_ids = lax.broadcasted_iota(jnp.int32, (replica_count * share_rows, row_count), 0)
-    arrangement = (target[None, :] == position_ids).astype(jnp.float32)
-    arranged = jnp.dot(
-        arrangement,
-        combined.reshape(row_count, step_count * columns),
-        precision=lax.Precision.HIGHEST,
-        preferred_element_type=jnp.float32,
-    ).astype(jnp.bfloat16)
-    arranged = arranged.reshape(replica_count, share_rows, step_count, columns)
+    arranged = combined.astype(jnp.bfloat16).reshape(replica_count, share_rows, step_count, columns)
     quarters = lax.all_to_all(arranged, "dp", split_axis=0, concat_axis=0, tiled=True)
     return quarters.transpose(1, 2, 0, 3).reshape(share_rows, step_count, model_width)
 

time: 309 us -> 341 us (1.10)
  waiting for transfers between devices: 105 us -> 132 us
  matrix products: 33.8 us -> 39.9 us
  starting transfers between devices: 36.9 us -> 33.4 us
    ppermute x3, waiting for transfers between devices: 27 us -> 59.4 us  [exchange_gather(): pieces.append(lax.ppermute(outgoing, 'dp', pairs))]
    all_gather x2, waiting for transfers between devices: 8.67 us -> 1.68 us  [body(): gathered = lax.all_gather(arrived, 'dp', axis=0, tiled=True)]
    all_to_all x2, starting transfers between devices: 21.4 us -> 15 us  [body(): lax.all_to_all(by_source, 'expert', split_axis=0, concat_axis=0, tiled=True)]
    dot_general x3 -> x7, matrix products: 7.69 us -> 10.6 us  [the longest x2 5.14 us: body(): jnp.dot(place_high, rows_flat, preferred_element_type=jnp.float32)]
  transfers between devices with their start and end apart: 13 -> 13, of which waited for: 10 -> 9; matrix products, arithmetic and copies ran while one was open for 14% -> 14% of each run, Pallas kernels for 0% -> 0%
where the time goes in v12:
time: 341 us; the launch traced here: 340 us
  waiting for transfers between devices  132 us (39%)
  blocking collectives  86.1 us (25%)
  matrix products  39.9 us (12%)
  starting transfers between devices  33.4 us (10%)
  local copies, waits for them, and re-layouts  29.1 us (9%)
  between operations  14.4 us (4%)
  other arithmetic  4.97 us (1%)
    all_to_all x2, blocking collectives, body(): lax.all_to_all(outgoing, 'expert', split_axis=0, concat_axis=0, tiled=True)  75.5 us
    ppermute x3, waiting for transfers between devices, exchange_gather(): pieces.append(lax.ppermute(outgoing, 'dp', pairs))  59.4 us
    ppermute x6, waiting for transfers between devices, exchange_all(): pieces.append(lax.ppermute(block, 'dp', pairs))  45.9 us
    all_to_all x2, waiting for transfers between devices, body(): lax.all_to_all(by_source, 'expert', split_axis=0, concat_axis=0, tiled=True)  24.8 us
    all_to_all x2, starting transfers between devices, body(): lax.all_to_all(by_source, 'expert', split_axis=0, concat_axis=0, tiled=True)  15 us
    ppermute x6, starting transfers between devices, exchange_all(): pieces.append(lax.ppermute(block, 'dp', pairs))  12.5 us
    reshape x4, local copies, waits for them, and re-layouts, body(): expert_cols.reshape(replica_count, expert_count, sub, columns)  11.2 us
    all_to_all x1, blocking collectives, body(): lax.all_to_all(arranged, 'dp', split_axis=0, concat_axis=0, tiled=True)  10.6 us
  transfers between devices with their start and end apart: 13, of which 9 were waited for; matrix products, arithmetic and copies ran while one was open for 14% of the time, Pallas kernels for 0%

profile of v12, /device:TPU:2, one launch (start us, length us, event | category | flops | bytes accessed | tf_op | source)
XLA Modules:
  0.0 339.6 jit_solution(14683748627386282405)
XLA Ops:
  6.5 0.9 copy.31
  8.2 0.7 fusion.69
  9.7 2.0 reshape.259
  11.7 2.4 convolution_convert_fusion.1
  14.1 2.5 all_to_all.25
  16.6 40.9 %all_to_all.39 = bf16[64,2,4096]{2,1,0:T(2,128)(2,1)} all-to-all(bf16[64,2,4096]{2,1,0:T(2,128)(2,1)} %all_to_all.25), channel_id=1, replica_groups=mesh['dp'=4,'expert'=64] {'expert'}, dimensions={0} | all-to-all | bytes 2097152 | tf_op jit(solution)/shard_map/all_to_all | solution.py:91
  57.6 2.3 all_to_all.27
  59.9 3.6 %constant_dynamic-slice_fusion = (bf16[1,384,1024]{2,1,0:T(8,128)(2,1)}, bf16[384,1024]{1,0:T(8,128)(2,1)}, bf16[384,1024]{1,0:T(8,128)(2,1)}, bf16[384,1024]{1,0:T(8,128)(2,1)}) fusion(bf16[1,384,4096]{2,1,0:T(8,128)(2,1)} %param.17, s32[]{:T(128)S(6)} %select_n.63, s32[]{:T(128)S(6)} %select_n.65, s32[]{:T(128)S(6)} %select_n.69, s32[]{:T(128)S(6)} %select_n.67), kind=kLoop, calls=%fused_computation.104 | loop fusion | bytes 6291472 | tf_op jit(solution)/shard_map/dynamic_slice | solution.py:11
  63.5 1.6 collective-permute-start.3
  65.1 2.9 collective-permute-start.4
  68.0 1.3 collective-permute-start.5
  69.4 2.5 convolution_convert_fusion
  71.9 25.0 %collective-permute-done.3 = bf16[384,1024]{1,0:T(8,128)(2,1)} collective-permute-done((bf16[384,1024]{1,0:T(8,128)(2,1)}, bf16[384,1024]{1,0:T(8,128)(2,1)}, u32[]{:S(2)}, u32[]{:S(2)}) %collective-permute-start.3) | collective-permute-done | bytes 786464 | tf_op jit(solution)/shard_map/ppermute | solution.py:16
  96.9 34.4 %collective-permute-done.4 = bf16[384,1024]{1,0:T(8,128)(2,1)} collective-permute-done((bf16[384,1024]{1,0:T(8,128)(2,1)}, bf16[384,1024]{1,0:T(8,128)(2,1)}, u32[]{:S(2)}, u32[]{:S(2)}) %collective-permute-start.4) | collective-permute-done | bytes 786464 | tf_op jit(solution)/shard_map/ppermute | solution.py:16
  131.3 3.3 pad_maximum_fusion
  134.5 2.5 all_to_all.29
  137.1 34.6 %all_to_all.40 = bf16[64,2,4096]{2,1,0:T(2,128)(2,1)} all-to-all(bf16[64,2,4096]{2,1,0:T(2,128)(2,1)} %all_to_all.29), channel_id=1, replica_groups=mesh['dp'=4,'expert'=64] {'expert'}, dimensions={0} | all-to-all | bytes 2097152 | tf_op jit(solution)/shard_map/all_to_all | solution.py:91
  171.7 2.3 all_to_all.31
  174.0 4.7 %fusion.6 = f32[512,384]{1,0:T(8,128)S(1)} fusion(bf16[512,4096]{1,0:T(8,128)(2,1)} %all-gather.3.cloned.1.call-done, bf16[1,4096,384]{2,1,0:T(8,128)(2,1)S(1)} %copy-done), kind=kOutput, calls=%fused_computation.9 | convolution fusion | flops 1610612736 | bytes 8126464 | tf_op jit(solution)/shard_map/dot_general | solution.py:93
  178.7 2.3 fusion.31
  181.2 3.7 %collective-permute-start.1 = (bf16[512,384]{1,0:T(8,128)(2,1)S(1)}, bf16[512,384]{1,0:T(8,128)(2,1)S(1)}, u32[]{:S(2)}, u32[]{:S(2)}) collective-permute-start(bf16[512,384]{1,0:T(8,128)(2,1)S(1)} %fusion.31), channel_id=1, source_target_pairs={{0,128},{64,192},{128,0},{192,64},{1,129},{65,193},{129,1},{193,65... | collective-permute-start | bytes 1179656 | tf_op jit(solution)/shard_map/ppermute | solution.py:24
  184.8 2.5 collective-permute-start.2
  187.4 13.0 %collective-permute-done = bf16[512,384]{1,0:T(8,128)(2,1)S(1)} collective-permute-done((bf16[512,384]{1,0:T(8,128)(2,1)S(1)}, bf16[512,384]{1,0:T(8,128)(2,1)S(1)}, u32[]{:S(2)}, u32[]{:S(2)}) %collective-permute-start) | collective-permute-done | bytes 393248 | tf_op jit(solution)/shard_map/ppermute | solution.py:24
  200.4 15.8 %collective-permute-done.1 = bf16[512,384]{1,0:T(8,128)(2,1)S(1)} collective-permute-done((bf16[512,384]{1,0:T(8,128)(2,1)S(1)}, bf16[512,384]{1,0:T(8,128)(2,1)S(1)}, u32[]{:S(2)}, u32[]{:S(2)}) %collective-permute-start.1) | collective-permute-done | bytes 393248 | tf_op jit(solution)/shard_map/ppermute | solution.py:24
  216.2 1.5 collective-permute-done.2
  217.7 4.5 %bitcast_convert_fusion.1 = bf16[512,1024]{1,0:T(8,128)(2,1)} fusion(bf16[1,512,384]{2,1,0:T(8,128)(2,1)S(1)} %bitcast.100, bf16[1,512,384]{2,1,0:T(8,128)(2,1)S(1)} %bitcast.99, bf16[1,512,384]{2,1,0:T(8,128)(2,1)S(1)} %bitcast.98, bf16[1,512,384]{2,1,0:T(8,128)(2,1)S(1)} %bitcast.97, bf16[1,384,1024]{2,1,0:T(8,128)(2,1)} %bitcast.14, ...), kind=kOutput, calls=%fused_computation.12 | convolution fusion | flops 1618214912 | bytes 5767168 | tf_op jit(solution)/shard_map/dot_general | solution.py:97
  222.2 2.2 reshape.260
  224.4 3.4 copy.58
  227.8 5.8 %all-to-all-start.1 = ((bf16[64,4,2,1024]{3,2,1,0:T(2,128)(2,1)}), bf16[64,4,2,1024]{3,2,1,0:T(2,128)(2,1)}, u32[]{:S(2)}, u32[]{:S(2)}) async-start(bf16[64,4,2,1024]{3,2,1,0:T(2,128)(2,1)} %bitcast.91), calls=%async_computation.1 | async-start | bytes 2097152 | tf_op jit(solution)/shard_map/all_to_all | solution.py:106
  233.6 1.7 all-gather.5.cloned.1.call-done
  235.3 4.7 %fusion.4 = f32[512,384]{1,0:T(8,128)S(1)} fusion(bf16[512,4096]{1,0:T(8,128)(2,1)} %all-gather.5.cloned.1.call-done, bf16[1,4096,384]{2,1,0:T(8,128)(2,1)S(1)} %copy-done), kind=kOutput, calls=%fused_computation.7 | convolution fusion | flops 1610612736 | bytes 8126464 | tf_op jit(solution)/shard_map/dot_general | solution.py:93
  240.0 3.1 fusion.28
  243.1 1.7 collective-permute-start.6
  244.8 2.4 collective-permute-start.7
  247.2 2.1 collective-permute-start.8
  249.4 6.3 %collective-permute-done.6 = bf16[512,384]{1,0:T(8,128)(2,1)} collective-permute-done((bf16[512,384]{1,0:T(8,128)(2,1)}, bf16[512,384]{1,0:T(8,128)(2,1)}, u32[]{:S(2)}, u32[]{:S(2)}) %collective-permute-start.6) | collective-permute-done | bytes 393248 | tf_op jit(solution)/shard_map/ppermute | solution.py:24
  255.7 9.3 %collective-permute-done.7 = bf16[512,384]{1,0:T(8,128)(2,1)} collective-permute-done((bf16[512,384]{1,0:T(8,128)(2,1)}, bf16[512,384]{1,0:T(8,128)(2,1)}, u32[]{:S(2)}, u32[]{:S(2)}) %collective-permute-start.7) | collective-permute-done | bytes 393248 | tf_op jit(solution)/shard_map/ppermute | solution.py:24
  265.0 5.2 %bitcast_convert_fusion = bf16[512,1024]{1,0:T(8,128)(2,1)} fusion(bf16[4,384,1024]{2,1,0:T(8,128)(2,1)} %pad_maximum_fusion, bf16[1,512,384]{2,1,0:T(8,128)(2,1)} %bitcast.24, bf16[1,512,384]{2,1,0:T(8,128)(2,1)} %bitcast.23, bf16[1,512,384]{2,1,0:T(8,128)(2,1)} %bitcast.22, bf16[1,512,384]{2,1,0:T(8,128)(2,1)} %bitcast.21), kind=kOutput, calls=%fused_computation.11 | convolution fusion | flops 1613496320 | bytes 5767168 | tf_op jit(solution)/shard_map/dot_general | solution.py:97
  270.2 2.3 reshape.261
  272.4 3.4 copy.57
  275.8 9.2 %all-to-all-start.3 = ((bf16[64,4,2,1024]{3,2,1,0:T(2,128)(2,1)}), bf16[64,4,2,1024]{3,2,1,0:T(2,128)(2,1)}, u32[]{:S(2)}, u32[]{:S(2)}) async-start(bf16[64,4,2,1024]{3,2,1,0:T(2,128)(2,1)} %bitcast.92), calls=%async_computation.3 | async-start | bytes 2097152 | tf_op jit(solution)/shard_map/all_to_all | solution.py:106
  286.4 2.5 convolution_bitcast_fusion.2
  288.9 24.8 %all-to-all-done.3 = bf16[64,4,2,1024]{3,2,1,0:T(2,128)(2,1)} async-done(((bf16[64,4,2,1024]{3,2,1,0:T(2,128)(2,1)}), bf16[64,4,2,1024]{3,2,1,0:T(2,128)(2,1)}, u32[]{:S(2)}, u32[]{:S(2)}) %all-to-all-start.3) | async-done | bytes 1048608 | tf_op jit(solution)/shard_map/all_to_all | solution.py:106
  313.7 2.5 convolution_bitcast_fusion.1
  316.3 2.5 convolution_bitcast_fusion
  318.8 2.6 fusion.37
  321.5 10.6 %all_to_all.41 = bf16[4,4,4,1024]{3,2,1,0:T(4,128)(2,1)S(1)} all-to-all(bf16[4,4,4,1024]{3,2,1,0:T(4,128)(2,1)S(1)} %reshape.262), channel_id=1, replica_groups=mesh['dp'=4,'expert'=64] {'dp'}, dimensions={0} | all-to-all | bytes 262144 | tf_op jit(solution)/shard_map/all_to_all | solution.py:123
  332.1 0.7 copy.46
  (59 shorter events, 2.6 us)
Async XLA Ops:
  6.5 167.5 %copy-start = (bf16[1,4096,384]{2,1,0:T(8,128)(2,1)S(1)}, bf16[1,4096,384]{2,1,0:T(8,128)(2,1)}, u32[]{:S(2)}) copy-start(bf16[1,4096,384]{2,1,0:T(8,128)(2,1)} %param.15) | copy-start | bytes 9437188
  6.5 167.5 %all-gather.3.cloned.1.call-start = ((), (), s32[]{:S(2)}) async-start(), calls=%async_computation.5 | async-start | bytes 5242880 | tf_op jit(solution)/shard_map/all_gather | solution.py:92
  59.8 175.4 %all-gather.5.cloned.1.call-start = ((), (), s32[]{:S(2)}) async-start(), calls=%async_computation.6 | async-start | bytes 5242880 | tf_op jit(solution)/shard_map/all_gather | solution.py:92
  63.5 33.3 %collective-permute-start.3 = (bf16[384,1024]{1,0:T(8,128)(2,1)}, bf16[384,1024]{1,0:T(8,128)(2,1)}, u32[]{:S(2)}, u32[]{:S(2)}) collective-permute-start(bf16[384,1024]{1,0:T(8,128)(2,1)} %get-tuple-element.12), channel_id=1, source_target_pairs={{0,64},{64,128},{128,192},{192,0},{1,65},{65,129},{129,193},{193,1... | collective-permute-start | bytes 2359304 | tf_op jit(solution)/shard_map/ppermute | solution.py:16
  65.1 66.2 %collective-permute-start.4 = (bf16[384,1024]{1,0:T(8,128)(2,1)}, bf16[384,1024]{1,0:T(8,128)(2,1)}, u32[]{:S(2)}, u32[]{:S(2)}) collective-permute-start(bf16[384,1024]{1,0:T(8,128)(2,1)} %get-tuple-element.14), channel_id=1, source_target_pairs={{0,128},{64,192},{128,0},{192,64},{1,129},{65,193},{129,1},{193,65... | collective-permute-start | bytes 2359304 | tf_op jit(solution)/shard_map/ppermute | solution.py:16
  68.0 63.3 %collective-permute-start.5 = (bf16[384,1024]{1,0:T(8,128)(2,1)}, bf16[384,1024]{1,0:T(8,128)(2,1)}, u32[]{:S(2)}, u32[]{:S(2)}) collective-permute-start(bf16[384,1024]{1,0:T(8,128)(2,1)} %get-tuple-element.13), channel_id=1, source_target_pairs={{0,192},{64,0},{128,64},{192,128},{1,193},{65,1},{129,65},{193,129... | collective-permute-start | bytes 2359304 | tf_op jit(solution)/shard_map/ppermute | solution.py:16
  174.0 4.7 %copy-start.5 = (bf16[512,4096]{1,0:T(8,128)(2,1)S(1)}, bf16[512,4096]{1,0:T(8,128)(2,1)}, u32[]{:S(2)}) copy-start(bf16[512,4096]{1,0:T(8,128)(2,1)} %all-gather.3.cloned.1.call-done) | copy-start | bytes 12582916
  174.0 4.7 %copy-start.7 = (bf16[1,4096,384]{2,1,0:T(8,128)(2,1)S(1)}, bf16[1,4096,384]{2,1,0:T(8,128)(2,1)}, u32[]{:S(2)}) copy-start(bf16[1,4096,384]{2,1,0:T(8,128)(2,1)} %param.16) | copy-start | bytes 9437188
  178.7 39.0 %copy-start.1 = (bf16[1,384,1024]{2,1,0:T(8,128)(2,1)S(1)}, bf16[1,384,1024]{2,1,0:T(8,128)(2,1)}, u32[]{:S(2)}) copy-start(bf16[1,384,1024]{2,1,0:T(8,128)(2,1)} %get-tuple-element.11) | copy-start | bytes 2359300
  181.1 19.3 %collective-permute-start = (bf16[512,384]{1,0:T(8,128)(2,1)S(1)}, bf16[512,384]{1,0:T(8,128)(2,1)S(1)}, u32[]{:S(2)}, u32[]{:S(2)}) collective-permute-start(bf16[512,384]{1,0:T(8,128)(2,1)S(1)} %fusion.31), channel_id=1, source_target_pairs={{0,64},{64,128},{128,192},{192,0},{1,65},{65,129},{129,193},{193,1... | collective-permute-start | bytes 1179656 | tf_op jit(solution)/shard_map/ppermute | solution.py:24
  181.2 35.0 %collective-permute-start.1 = (bf16[512,384]{1,0:T(8,128)(2,1)S(1)}, bf16[512,384]{1,0:T(8,128)(2,1)S(1)}, u32[]{:S(2)}, u32[]{:S(2)}) collective-permute-start(bf16[512,384]{1,0:T(8,128)(2,1)S(1)} %fusion.31), channel_id=1, source_target_pairs={{0,128},{64,192},{128,0},{192,64},{1,129},{65,193},{129,1},{193,65... | collective-permute-start | bytes 1179656 | tf_op jit(solution)/shard_map/ppermute | solution.py:24
  184.8 32.9 %collective-permute-start.2 = (bf16[512,384]{1,0:T(8,128)(2,1)S(1)}, bf16[512,384]{1,0:T(8,128)(2,1)S(1)}, u32[]{:S(2)}, u32[]{:S(2)}) collective-permute-start(bf16[512,384]{1,0:T(8,128)(2,1)S(1)} %fusion.31), channel_id=1, source_target_pairs={{0,192},{64,0},{128,64},{192,128},{1,193},{65,1},{129,65},{193,129... | collective-permute-start | bytes 1179656 | tf_op jit(solution)/shard_map/ppermute | solution.py:24
  227.8 48.0 %all-to-all-start.1 = ((bf16[64,4,2,1024]{3,2,1,0:T(2,128)(2,1)}), bf16[64,4,2,1024]{3,2,1,0:T(2,128)(2,1)}, u32[]{:S(2)}, u32[]{:S(2)}) async-start(bf16[64,4,2,1024]{3,2,1,0:T(2,128)(2,1)} %bitcast.91), calls=%async_computation.1 | async-start | bytes 2097152 | tf_op jit(solution)/shard_map/all_to_all | solution.py:106
  235.3 4.7 %copy-start.6 = (bf16[512,4096]{1,0:T(8,128)(2,1)S(1)}, bf16[512,4096]{1,0:T(8,128)(2,1)}, u32[]{:S(2)}) copy-start(bf16[512,4096]{1,0:T(8,128)(2,1)} %all-gather.5.cloned.1.call-done) | copy-start | bytes 12582916
  235.3 4.7 %copy-start.8 = (bf16[1,4096,384]{2,1,0:T(8,128)(2,1)S(1)}, bf16[1,4096,384]{2,1,0:T(8,128)(2,1)}, u32[]{:S(2)}) copy-start(bf16[1,4096,384]{2,1,0:T(8,128)(2,1)} %param.16) | copy-start | bytes 9437188
  243.1 12.6 %collective-permute-start.6 = (bf16[512,384]{1,0:T(8,128)(2,1)}, bf16[512,384]{1,0:T(8,128)(2,1)}, u32[]{:S(2)}, u32[]{:S(2)}) collective-permute-start(bf16[512,384]{1,0:T(8,128)(2,1)} %fusion.28), channel_id=1, source_target_pairs={{0,64},{64,128},{128,192},{192,0},{1,65},{65,129},{129,193},{193,1... | collective-permute-start | bytes 1179656 | tf_op jit(solution)/shard_map/ppermute | solution.py:24
  244.8 20.2 %collective-permute-start.7 = (bf16[512,384]{1,0:T(8,128)(2,1)}, bf16[512,384]{1,0:T(8,128)(2,1)}, u32[]{:S(2)}, u32[]{:S(2)}) collective-permute-start(bf16[512,384]{1,0:T(8,128)(2,1)} %fusion.28), channel_id=1, source_target_pairs={{0,128},{64,192},{128,0},{192,64},{1,129},{65,193},{129,1},{193,65... | collective-permute-start | bytes 1179656 | tf_op jit(solution)/shard_map/ppermute | solution.py:24
  247.2 17.8 %collective-permute-start.8 = (bf16[512,384]{1,0:T(8,128)(2,1)}, bf16[512,384]{1,0:T(8,128)(2,1)}, u32[]{:S(2)}, u32[]{:S(2)}) collective-permute-start(bf16[512,384]{1,0:T(8,128)(2,1)} %fusion.28), channel_id=1, source_target_pairs={{0,192},{64,0},{128,64},{192,128},{1,193},{65,1},{129,65},{193,129... | collective-permute-start | bytes 1179656 | tf_op jit(solution)/shard_map/ppermute | solution.py:24
  270.2 14.8 %copy-start.9 = (s32[16]{0:T(128)S(1)}, s32[16]{0:T(128)}, u32[]{:S(2)}) copy-start(s32[16]{0:T(128)} %param.14) | copy-start | bytes 196
  270.2 15.4 %copy-start.4 = (f32[16,4,8]{0,2,1:T(8,128)S(1)}, f32[16,4,8]{0,2,1:T(8,128)}, u32[]{:S(2)}) copy-start(f32[16,4,8]{0,2,1:T(8,128)} %param.11) | copy-start | bytes 6148
  275.8 37.9 %all-to-all-start.3 = ((bf16[64,4,2,1024]{3,2,1,0:T(2,128)(2,1)}), bf16[64,4,2,1024]{3,2,1,0:T(2,128)(2,1)}, u32[]{:S(2)}, u32[]{:S(2)}) async-start(bf16[64,4,2,1024]{3,2,1,0:T(2,128)(2,1)} %bitcast.92), calls=%async_computation.3 | async-start | bytes 2097152 | tf_op jit(solution)/shard_map/all_to_all | solution.py:106
  285.2 31.0 %copy-start.2 = (f32[64,64]{1,0:T(8,128)}, f32[64,64]{1,0:T(8,128)S(1)}, u32[]{:S(2)}) copy-start(f32[64,64]{1,0:T(8,128)S(1)} %eq.138) | copy-start | bytes 49156
  286.2 30.0 %copy-start.3 = (f32[64,64]{1,0:T(8,128)}, f32[64,64]{1,0:T(8,128)S(1)}, u32[]{:S(2)}) copy-start(f32[64,64]{1,0:T(8,128)S(1)} %broadcast_in_dim.38) | copy-start | bytes 49156
Sparse Core Ops, SparseCore 0:
  60.0 74.8 all-gather.2
  174.1 61.1 all-gather.4

commit v13 on v11

--- a/solution.py
+++ b/solution.py
@@ -39,7 +39,22 @@
     slot_count = min(tokens, max(MOST_BASE, 2 * tokens * top_count // expert_count))
     slot_count = -(-slot_count // replica_count) * replica_count
     part = slot_count // replica_count
-    down_cols = exchange_gather(w_down[0], replica, replica_count)
+    by_member = lax.all_to_all(
+        w_down[0].reshape(hidden_part, replica_count, columns),
+        "dp",
+        split_axis=1,
+        concat_axis=0,
+        tiled=True,
+    ).reshape(replica_count, hidden_part, columns)
+    down_cols = jnp.stack(
+        [
+            lax.dynamic_index_in_dim(
+                by_member, (replica - shift) % replica_count, 0, keepdims=False
+            )
+            for shift in range(replica_count)
+        ],
+        axis=0,
+    )
     step_ids = lax.broadcasted_iota(jnp.int32, (row_count, step_count), 1)
     live_mask = ((step_ids < finish_step[:, None]) & (group_keep[0] == 1)).reshape(tokens)
     gate_share = route_weight / jnp.sum(route_weight, axis=2, keepdims=True)

time: 309 us -> 319 us (1.032)
  local copies, waits for them, and re-layouts: 28.9 us -> 39.9 us
    all_to_all x0 -> x1, waiting for transfers between devices: none -> 31.6 us  [body(): lax.all_to_all(w_down[0].reshape(hidden_part, replica_count, columns), 'd...]
    ppermute x3 -> x0, waiting for transfers between devices: 27 us -> none  [exchange_gather(): pieces.append(lax.ppermute(outgoing, 'dp', pairs))]
    another operation x0 -> x2, local copies, waits for them, and re-layouts: none -> 10.8 us  [body(): w_down[0].reshape(hidden_part, replica_count, columns)]
    ppermute x3 -> x0, starting transfers between devices: 5.83 us -> none  [exchange_gather(): pieces.append(lax.ppermute(outgoing, 'dp', pairs))]
    all_to_all x0 -> x1, starting transfers between devices: none -> 4.79 us  [body(): lax.all_to_all(w_down[0].reshape(hidden_part, replica_count, columns), 'd...]
  transfers between devices with their start and end apart: 13 -> 11, of which waited for: 10 -> 9; matrix products, arithmetic and copies ran while one was open for 14% -> 14% of each run, Pallas kernels for 0% -> 0%
where the time goes in v13:
time: 319 us; the launch traced here: 318 us
  waiting for transfers between devices  108 us (34%)
  blocking collectives  84.9 us (27%)
  local copies, waits for them, and re-layouts  39.9 us (13%)
  starting transfers between devices  35.9 us (11%)
  matrix products  32.2 us (10%)
  between operations  14.5 us (5%)
    all_to_all x2, blocking collectives, body(): lax.all_to_all(outgoing, 'expert', split_axis=0, concat_axis=0, tiled=True)  75.5 us
    ppermute x6, waiting for transfers between devices, exchange_all(): pieces.append(lax.ppermute(block, 'dp', pairs))  44.6 us
    all_to_all x1, waiting for transfers between devices, body(): lax.all_to_all(w_down[0].reshape(hidden_part, replica_count, columns), 'd...  31.6 us
    all_to_all x2, waiting for transfers between devices, body(): lax.all_to_all(by_source, 'expert', split_axis=0, concat_axis=0, tiled=True)  24.4 us
    all_to_all x2, starting transfers between devices, body(): lax.all_to_all(by_source, 'expert', split_axis=0, concat_axis=0, tiled=True)  21.5 us
    reshape x4, local copies, waits for them, and re-layouts, body(): expert_cols.reshape(replica_count, expert_count, sub, columns)  11.2 us
    another operation x2, local copies, waits for them, and re-layouts, body(): w_down[0].reshape(hidden_part, replica_count, columns)  10.8 us
    all_to_all x4, local copies, waits for them, and re-layouts, body(): lax.all_to_all(outgoing, 'expert', split_axis=0, concat_axis=0, tiled=True)  9.63 us
  transfers between devices with their start and end apart: 11, of which 9 were waited for; matrix products, arithmetic and copies ran while one was open for 14% of the time, Pallas kernels for 0%

profile of v13, /device:TPU:2, one launch (start us, length us, event | category | flops | bytes accessed | tf_op | source)
XLA Modules:
  0.0 318.2 jit_solution(16044923004103985322)
XLA Ops:
  6.5 6.3 %reshape_squeeze.3 = bf16[384,4,1024]{2,1,0:T(4,128)(2,1)} reshape(bf16[1,384,4096]{2,1,0:T(8,128)(2,1)} %param.17) | data formatting | bytes 6291456 | tf_op jit(solution)/shard_map/reshape;squeeze | solution.py:43
  12.8 4.5 %copy.36 = bf16[384,4,1024]{2,0,1:T(8,128)(2,1)} copy(bf16[384,4,1024]{2,1,0:T(4,128)(2,1)} %reshape_squeeze.3) | data formatting | bytes 6291456 | tf_op jit(solution)/shard_map/reshape;squeeze | solution.py:43
  17.4 4.8 %all-to-all-start.1 = ((bf16[384,4,1024]{2,0,1:T(8,128)(2,1)}), bf16[384,4,1024]{2,0,1:T(8,128)(2,1)}, u32[]{:S(2)}, u32[]{:S(2)}) async-start(bf16[384,4,1024]{2,0,1:T(8,128)(2,1)} %copy.36), calls=%async_computation.1 | async-start | bytes 6291456 | tf_op jit(solution)/shard_map/all_to_all | solution.py:42
  23.7 2.0 reshape.231
  26.0 2.4 convolution_convert_fusion
  28.4 31.6 %all-to-all-done.1 = bf16[384,4,1024]{2,0,1:T(8,128)(2,1)} async-done(((bf16[384,4,1024]{2,0,1:T(8,128)(2,1)}), bf16[384,4,1024]{2,0,1:T(8,128)(2,1)}, u32[]{:S(2)}, u32[]{:S(2)}) %all-to-all-start.1) | async-done | bytes 3145760 | tf_op jit(solution)/shard_map/all_to_all | solution.py:42
  60.1 2.1 dynamic-slice_bitcast_fusion.3
  62.3 0.9 copy-done.2
  63.9 1.9 pad_maximum_fusion
  65.7 2.6 all_to_all.37
  68.3 40.9 %all_to_all.48 = bf16[64,2,4096]{2,1,0:T(2,128)(2,1)} all-to-all(bf16[64,2,4096]{2,1,0:T(2,128)(2,1)} %all_to_all.37), channel_id=1, replica_groups=mesh['dp'=4,'expert'=64] {'expert'}, dimensions={0} | all-to-all | bytes 2097152 | tf_op jit(solution)/shard_map/all_to_all | solution.py:85
  109.2 2.3 all_to_all.39
  111.6 2.5 convolution_convert_fusion.1
  114.1 2.5 all_to_all.32
  116.6 34.6 %all_to_all.49 = bf16[64,2,4096]{2,1,0:T(2,128)(2,1)} all-to-all(bf16[64,2,4096]{2,1,0:T(2,128)(2,1)} %all_to_all.32), channel_id=1, replica_groups=mesh['dp'=4,'expert'=64] {'expert'}, dimensions={0} | all-to-all | bytes 2097152 | tf_op jit(solution)/shard_map/all_to_all | solution.py:85
  151.2 2.3 all_to_all.34
  153.5 3.6 %all-gather.5.cloned.1.call-done = bf16[512,4096]{1,0:T(8,128)(2,1)} async-done(((bf16[128,4096]{1,0:T(8,128)(2,1)}), bf16[512,4096]{1,0:T(8,128)(2,1)}) %all-gather.5.cloned.1.call-update) | async-done | bytes 4194320 | tf_op jit(solution)/shard_map/all_gather | solution.py:86
  157.1 4.7 %fusion.4 = f32[512,384]{1,0:T(8,128)S(1)} fusion(bf16[512,4096]{1,0:T(8,128)(2,1)} %all-gather.5.cloned.1.call-done, bf16[1,4096,384]{2,1,0:T(8,128)(2,1)S(1)} %copy-done), kind=kOutput, calls=%fused_computation.8 | convolution fusion | flops 1610612736 | bytes 8126464 | tf_op jit(solution)/shard_map/dot_general | solution.py:87
  161.8 2.3 fusion.28
  164.1 0.9 collective-permute-start.3
  165.1 1.7 collective-permute-start.4
  166.8 2.1 collective-permute-start.5
  168.9 12.8 %collective-permute-done.3 = bf16[512,384]{1,0:T(8,128)(2,1)S(1)} collective-permute-done((bf16[512,384]{1,0:T(8,128)(2,1)S(1)}, bf16[512,384]{1,0:T(8,128)(2,1)S(1)}, u32[]{:S(2)}, u32[]{:S(2)}) %collective-permute-start.3) | collective-permute-done | bytes 393248 | tf_op jit(solution)/shard_map/ppermute | solution.py:24
  181.7 11.1 %collective-permute-done.4 = bf16[512,384]{1,0:T(8,128)(2,1)S(1)} collective-permute-done((bf16[512,384]{1,0:T(8,128)(2,1)S(1)}, bf16[512,384]{1,0:T(8,128)(2,1)S(1)}, u32[]{:S(2)}, u32[]{:S(2)}) %collective-permute-start.4) | collective-permute-done | bytes 393248 | tf_op jit(solution)/shard_map/ppermute | solution.py:24
  192.8 3.8 %collective-permute-done.5 = bf16[512,384]{1,0:T(8,128)(2,1)S(1)} collective-permute-done((bf16[512,384]{1,0:T(8,128)(2,1)S(1)}, bf16[512,384]{1,0:T(8,128)(2,1)S(1)}, u32[]{:S(2)}, u32[]{:S(2)}) %collective-permute-start.5) | collective-permute-done | bytes 393248 | tf_op jit(solution)/shard_map/ppermute | solution.py:24
  196.6 2.8 bitcast_convert_fusion
  199.4 2.3 reshape.233
  201.7 3.4 %copy.51 = bf16[4,64,2,1024]{3,2,0,1:T(2,128)(2,1)} copy(bf16[4,64,2,1024]{3,2,1,0:T(2,128)(2,1)} %reshape.233) | data formatting | bytes 2097152 | tf_op jit(solution)/shard_map/reshape | solution.py:97
  205.0 10.7 %all-to-all-start.4 = ((bf16[64,4,2,1024]{3,2,1,0:T(2,128)(2,1)}), bf16[64,4,2,1024]{3,2,1,0:T(2,128)(2,1)}, u32[]{:S(2)}, u32[]{:S(2)}) async-start(bf16[64,4,2,1024]{3,2,1,0:T(2,128)(2,1)} %bitcast.74), calls=%async_computation.4 | async-start | bytes 2097152 | tf_op jit(solution)/shard_map/all_to_all | solution.py:100
  215.8 3.7 %all-gather.3.cloned.1.call-done = bf16[512,4096]{1,0:T(8,128)(2,1)} async-done(((bf16[128,4096]{1,0:T(8,128)(2,1)}), bf16[512,4096]{1,0:T(8,128)(2,1)}) %all-gather.3.cloned.1.call-update) | async-done | bytes 4194320 | tf_op jit(solution)/shard_map/all_gather | solution.py:86
  219.4 4.7 %fusion.6 = f32[512,384]{1,0:T(8,128)S(1)} fusion(bf16[512,4096]{1,0:T(8,128)(2,1)} %all-gather.3.cloned.1.call-done, bf16[1,4096,384]{2,1,0:T(8,128)(2,1)S(1)} %copy-done), kind=kOutput, calls=%fused_computation.10 | convolution fusion | flops 1610612736 | bytes 8126464 | tf_op jit(solution)/shard_map/dot_general | solution.py:87
  224.1 2.3 fusion.31
  226.5 1.5 collective-permute-start
  228.0 2.7 collective-permute-start.1
  230.7 0.6 collective-permute-start.2
  231.3 7.6 %collective-permute-done = bf16[512,384]{1,0:T(8,128)(2,1)S(1)} collective-permute-done((bf16[512,384]{1,0:T(8,128)(2,1)S(1)}, bf16[512,384]{1,0:T(8,128)(2,1)S(1)}, u32[]{:S(2)}, u32[]{:S(2)}) %collective-permute-start) | collective-permute-done | bytes 393248 | tf_op jit(solution)/shard_map/ppermute | solution.py:24
  238.9 9.3 %collective-permute-done.1 = bf16[512,384]{1,0:T(8,128)(2,1)S(1)} collective-permute-done((bf16[512,384]{1,0:T(8,128)(2,1)S(1)}, bf16[512,384]{1,0:T(8,128)(2,1)S(1)}, u32[]{:S(2)}, u32[]{:S(2)}) %collective-permute-start.1) | collective-permute-done | bytes 393248 | tf_op jit(solution)/shard_map/ppermute | solution.py:24
  248.2 2.8 bitcast_convert_fusion.1
  251.0 2.3 reshape.232
  253.3 3.3 %copy.52 = bf16[4,64,2,1024]{3,2,0,1:T(2,128)(2,1)} copy(bf16[4,64,2,1024]{3,2,1,0:T(2,128)(2,1)} %reshape.232) | data formatting | bytes 2097152 | tf_op jit(solution)/shard_map/reshape | solution.py:97
  256.6 10.7 %all-to-all-start.2 = ((bf16[64,4,2,1024]{3,2,1,0:T(2,128)(2,1)}), bf16[64,4,2,1024]{3,2,1,0:T(2,128)(2,1)}, u32[]{:S(2)}, u32[]{:S(2)}) async-start(bf16[64,4,2,1024]{3,2,1,0:T(2,128)(2,1)} %bitcast.75), calls=%async_computation.2 | async-start | bytes 2097152 | tf_op jit(solution)/shard_map/all_to_all | solution.py:100
  267.5 0.3 select_reduce_fusion
  267.9 3.7 %convolution_bitcast_fusion = f32[64,1024]{1,0:T(8,128)} fusion(bf16[64,4,2,1024]{3,2,1,0:T(2,128)(2,1)} %all-to-all-done.4, s32[4,2]{1,0:T(4,128)S(1)} %iota_add_fusion, f32[64,64]{1,0:T(8,128)S(1)} %select_reduce_fusion, s32[64,64]{1,0:T(8,128)S(1)} %sub.29, pred[64,64]{1,0:T(8,128)(4,1)S(1)} %broadcast_compare_fusion), kind=kOutput, calls=%fused_computation.32 | convolution fusion | flops 402751488 | bytes 1347616 | tf_op jit(solution)/shard_map/dot_general | solution.py:107
  271.6 24.4 %all-to-all-done.2 = bf16[64,4,2,1024]{3,2,1,0:T(2,128)(2,1)} async-done(((bf16[64,4,2,1024]{3,2,1,0:T(2,128)(2,1)}), bf16[64,4,2,1024]{3,2,1,0:T(2,128)(2,1)}, u32[]{:S(2)}, u32[]{:S(2)}) %all-to-all-start.2) | async-done | bytes 1048608 | tf_op jit(solution)/shard_map/all_to_all | solution.py:100
  296.0 3.7 %fusion.34 = f32[64,1024]{1,0:T(8,128)} fusion(f32[64,1024]{1,0:T(8,128)} %convolution_bitcast_fusion, bf16[64,4,2,1024]{3,2,1,0:T(2,128)(2,1)} %all-to-all-done.2, f32[64,64]{1,0:T(8,128)S(1)} %select_reduce_fusion, s32[4,2]{1,0:T(4,128)S(1)} %iota_add_fusion.1, s32[64,64]{1,0:T(8,128)S(1)} %sub.29, pred[64,64]{1,0:T(8,128)(4,1)S(1)} %broadcast_compare_fusion), kind=kOutput, calls=%fused_computation.34 | convolution fusion | flops 402817024 | bytes 1609760 | tf_op jit(solution)/shard_map/dot_general | solution.py:107
  299.8 1.1 reshape.234
  301.2 9.4 %all_to_all.50 = bf16[4,4,4,1024]{3,2,1,0:T(4,128)(2,1)S(1)} all-to-all(bf16[4,4,4,1024]{3,2,1,0:T(4,128)(2,1)S(1)} %reshape.235), channel_id=1, replica_groups=mesh['dp'=4,'expert'=64] {'dp'}, dimensions={0} | all-to-all | bytes 262144 | tf_op jit(solution)/shard_map/all_to_all | solution.py:125
  310.6 0.7 copy.44
  (64 shorter events, 2.6 us)
Async XLA Ops:
  6.5 150.6 %copy-start = (bf16[1,4096,384]{2,1,0:T(8,128)(2,1)S(1)}, bf16[1,4096,384]{2,1,0:T(8,128)(2,1)}, u32[]{:S(2)}) copy-start(bf16[1,4096,384]{2,1,0:T(8,128)(2,1)} %param.15) | copy-start | bytes 9437188
  17.4 4.9 %copy-start.11 = (s32[16,4,8]{0,2,1:T(8,128)S(1)}, s32[16,4,8]{0,2,1:T(8,128)}, u32[]{:S(2)}) copy-start(s32[16,4,8]{0,2,1:T(8,128)} %param.10) | copy-start | bytes 6148
  17.4 5.7 %copy-start.12 = (s32[16]{0:T(128)S(1)}, s32[16]{0:T(128)}, u32[]{:S(2)}) copy-start(s32[16]{0:T(128)} %param.12) | copy-start | bytes 196
  17.4 42.7 %all-to-all-start.1 = ((bf16[384,4,1024]{2,0,1:T(8,128)(2,1)}), bf16[384,4,1024]{2,0,1:T(8,128)(2,1)}, u32[]{:S(2)}, u32[]{:S(2)}) async-start(bf16[384,4,1024]{2,0,1:T(8,128)(2,1)} %copy.36), calls=%async_computation.1 | async-start | bytes 6291456 | tf_op jit(solution)/shard_map/all_to_all | solution.py:42
  22.2 134.9 %all-gather.5.cloned.1.call-start = ((), (), s32[]{:S(2)}) async-start(), calls=%async_computation.7 | async-start | bytes 5242880 | tf_op jit(solution)/shard_map/all_gather | solution.py:86
  62.2 0.9 copy-start.2
  62.2 1.2 copy-start.4
  62.2 1.4 copy-start.6
  62.3 1.6 copy-start.8
  111.5 107.9 %all-gather.3.cloned.1.call-start = ((), (), s32[]{:S(2)}) async-start(), calls=%async_computation.6 | async-start | bytes 5242880 | tf_op jit(solution)/shard_map/all_gather | solution.py:86
  157.1 4.7 %copy-start.14 = (bf16[512,4096]{1,0:T(8,128)(2,1)S(1)}, bf16[512,4096]{1,0:T(8,128)(2,1)}, u32[]{:S(2)}) copy-start(bf16[512,4096]{1,0:T(8,128)(2,1)} %all-gather.5.cloned.1.call-done) | copy-start | bytes 12582916
  157.1 4.7 %copy-start.15 = (bf16[1,4096,384]{2,1,0:T(8,128)(2,1)S(1)}, bf16[1,4096,384]{2,1,0:T(8,128)(2,1)}, u32[]{:S(2)}) copy-start(bf16[1,4096,384]{2,1,0:T(8,128)(2,1)} %param.16) | copy-start | bytes 9437188
  161.8 34.8 %copy-start.1 = (bf16[4,384,1024]{2,1,0:T(8,128)(2,1)S(1)}, bf16[4,384,1024]{2,1,0:T(8,128)(2,1)}, u32[]{:S(2)}) copy-start(bf16[4,384,1024]{2,1,0:T(8,128)(2,1)} %pad_maximum_fusion) | copy-start | bytes 9437188
  164.1 17.6 %collective-permute-start.3 = (bf16[512,384]{1,0:T(8,128)(2,1)S(1)}, bf16[512,384]{1,0:T(8,128)(2,1)S(1)}, u32[]{:S(2)}, u32[]{:S(2)}) collective-permute-start(bf16[512,384]{1,0:T(8,128)(2,1)S(1)} %fusion.28), channel_id=1, source_target_pairs={{0,64},{64,128},{128,192},{192,0},{1,65},{65,129},{129,193},{193,1... | collective-permute-start | bytes 1179656 | tf_op jit(solution)/shard_map/ppermute | solution.py:24
  165.1 27.8 %collective-permute-start.4 = (bf16[512,384]{1,0:T(8,128)(2,1)S(1)}, bf16[512,384]{1,0:T(8,128)(2,1)S(1)}, u32[]{:S(2)}, u32[]{:S(2)}) collective-permute-start(bf16[512,384]{1,0:T(8,128)(2,1)S(1)} %fusion.28), channel_id=1, source_target_pairs={{0,128},{64,192},{128,0},{192,64},{1,129},{65,193},{129,1},{193,65... | collective-permute-start | bytes 1179656 | tf_op jit(solution)/shard_map/ppermute | solution.py:24
  166.8 29.8 %collective-permute-start.5 = (bf16[512,384]{1,0:T(8,128)(2,1)S(1)}, bf16[512,384]{1,0:T(8,128)(2,1)S(1)}, u32[]{:S(2)}, u32[]{:S(2)}) collective-permute-start(bf16[512,384]{1,0:T(8,128)(2,1)S(1)} %fusion.28), channel_id=1, source_target_pairs={{0,192},{64,0},{128,64},{192,128},{1,193},{65,1},{129,65},{193,129... | collective-permute-start | bytes 1179656 | tf_op jit(solution)/shard_map/ppermute | solution.py:24
  205.0 51.6 %all-to-all-start.4 = ((bf16[64,4,2,1024]{3,2,1,0:T(2,128)(2,1)}), bf16[64,4,2,1024]{3,2,1,0:T(2,128)(2,1)}, u32[]{:S(2)}, u32[]{:S(2)}) async-start(bf16[64,4,2,1024]{3,2,1,0:T(2,128)(2,1)} %bitcast.74), calls=%async_computation.4 | async-start | bytes 2097152 | tf_op jit(solution)/shard_map/all_to_all | solution.py:100
  219.4 4.7 %copy-start.13 = (bf16[512,4096]{1,0:T(8,128)(2,1)S(1)}, bf16[512,4096]{1,0:T(8,128)(2,1)}, u32[]{:S(2)}) copy-start(bf16[512,4096]{1,0:T(8,128)(2,1)} %all-gather.3.cloned.1.call-done) | copy-start | bytes 12582916
  219.4 4.7 %copy-start.16 = (bf16[1,4096,384]{2,1,0:T(8,128)(2,1)S(1)}, bf16[1,4096,384]{2,1,0:T(8,128)(2,1)}, u32[]{:S(2)}) copy-start(bf16[1,4096,384]{2,1,0:T(8,128)(2,1)} %param.16) | copy-start | bytes 9437188
  224.1 24.0 %copy-start.3 = (bf16[1,384,1024]{2,1,0:T(8,128)(2,1)S(1)}, bf16[1,384,1024]{2,1,0:T(8,128)(2,1)}, u32[]{:S(2)}) copy-start(bf16[1,384,1024]{2,1,0:T(8,128)(2,1)} %copy-done.2) | copy-start | bytes 2359300
  224.1 24.0 %copy-start.5 = (bf16[1,384,1024]{2,1,0:T(8,128)(2,1)S(1)}, bf16[1,384,1024]{2,1,0:T(8,128)(2,1)}, u32[]{:S(2)}) copy-start(bf16[1,384,1024]{2,1,0:T(8,128)(2,1)} %copy-done.4) | copy-start | bytes 2359300
  224.1 24.0 %copy-start.7 = (bf16[1,384,1024]{2,1,0:T(8,128)(2,1)S(1)}, bf16[1,384,1024]{2,1,0:T(8,128)(2,1)}, u32[]{:S(2)}) copy-start(bf16[1,384,1024]{2,1,0:T(8,128)(2,1)} %copy-done.6) | copy-start | bytes 2359300
  224.1 24.0 %copy-start.9 = (bf16[1,384,1024]{2,1,0:T(8,128)(2,1)S(1)}, bf16[1,384,1024]{2,1,0:T(8,128)(2,1)}, u32[]{:S(2)}) copy-start(bf16[1,384,1024]{2,1,0:T(8,128)(2,1)} %copy-done.8) | copy-start | bytes 2359300
  226.5 12.4 %collective-permute-start = (bf16[512,384]{1,0:T(8,128)(2,1)S(1)}, bf16[512,384]{1,0:T(8,128)(2,1)S(1)}, u32[]{:S(2)}, u32[]{:S(2)}) collective-permute-start(bf16[512,384]{1,0:T(8,128)(2,1)S(1)} %fusion.31), channel_id=1, source_target_pairs={{0,64},{64,128},{128,192},{192,0},{1,65},{65,129},{129,193},{193,1... | collective-permute-start | bytes 1179656 | tf_op jit(solution)/shard_map/ppermute | solution.py:24
  228.0 20.2 %collective-permute-start.1 = (bf16[512,384]{1,0:T(8,128)(2,1)S(1)}, bf16[512,384]{1,0:T(8,128)(2,1)S(1)}, u32[]{:S(2)}, u32[]{:S(2)}) collective-permute-start(bf16[512,384]{1,0:T(8,128)(2,1)S(1)} %fusion.31), channel_id=1, source_target_pairs={{0,128},{64,192},{128,0},{192,64},{1,129},{65,193},{129,1},{193,65... | collective-permute-start | bytes 1179656 | tf_op jit(solution)/shard_map/ppermute | solution.py:24
  230.7 17.5 %collective-permute-start.2 = (bf16[512,384]{1,0:T(8,128)(2,1)S(1)}, bf16[512,384]{1,0:T(8,128)(2,1)S(1)}, u32[]{:S(2)}, u32[]{:S(2)}) collective-permute-start(bf16[512,384]{1,0:T(8,128)(2,1)S(1)} %fusion.31), channel_id=1, source_target_pairs={{0,192},{64,0},{128,64},{192,128},{1,193},{65,1},{129,65},{193,129... | collective-permute-start | bytes 1179656 | tf_op jit(solution)/shard_map/ppermute | solution.py:24
  251.0 16.4 %copy-start.10 = (f32[16,4,8]{0,2,1:T(8,128)S(1)}, f32[16,4,8]{0,2,1:T(8,128)}, u32[]{:S(2)}) copy-start(f32[16,4,8]{0,2,1:T(8,128)} %param.11) | copy-start | bytes 6148
  251.0 16.8 %copy-start.17 = (s32[16]{0:T(128)S(1)}, s32[16]{0:T(128)}, u32[]{:S(2)}) copy-start(s32[16]{0:T(128)} %param.14) | copy-start | bytes 196
  256.6 39.5 %all-to-all-start.2 = ((bf16[64,4,2,1024]{3,2,1,0:T(2,128)(2,1)}), bf16[64,4,2,1024]{3,2,1,0:T(2,128)(2,1)}, u32[]{:S(2)}, u32[]{:S(2)}) async-start(bf16[64,4,2,1024]{3,2,1,0:T(2,128)(2,1)} %bitcast.75), calls=%async_computation.2 | async-start | bytes 2097152 | tf_op jit(solution)/shard_map/all_to_all | solution.py:100
Sparse Core Ops, SparseCore 0:
  111.7 45.3 all-gather.4
  158.9 60.4 all-gather.2

commit v14 on v11

--- a/solution.py
+++ b/solution.py
@@ -14,7 +14,7 @@
         outgoing = lax.dynamic_slice_in_dim(matrix, start, width, axis=1)
         pairs = [(i, (i + shift) % replica_count) for i in range(replica_count)]
         pieces.append(lax.ppermute(outgoing, "dp", pairs))
-    return jnp.stack(pieces, axis=0)
+    return pieces
 
 
 def exchange_all(block, replica_count):
@@ -75,7 +75,7 @@
         hidden_all = exchange_all(activated, replica_count)
         expert_cols = lax.dot_general(
             hidden_all,
-            down_cols,
+            jnp.stack(down_cols, axis=0),
             (((0, 2), (0, 1)), ((), ())),
             preferred_element_type=jnp.float32,
         ).astype(jnp.bfloat16)

time: 309 us -> 305 us (0.987)
  other arithmetic: 4.31 us -> 1.05 us
    another operation x1 -> x0, other arithmetic: 3.26 us -> none  [exchange_gather(): return jnp.stack(pieces, axis=0)]
  transfers between devices with their start and end apart: 13 -> 13, of which waited for: 10 -> 11; matrix products, arithmetic and copies ran while one was open for 14% -> 15% of each run, Pallas kernels for 0% -> 0%
where the time goes in v14:
time: 305 us; the launch traced here: 304 us
  waiting for transfers between devices  106 us (35%)
  blocking collectives  84.3 us (28%)
  matrix products  35.5 us (12%)
  starting transfers between devices  34.2 us (11%)
  local copies, waits for them, and re-layouts  29 us (10%)
  between operations  14.3 us (5%)
    all_to_all x2, blocking collectives, body(): lax.all_to_all(outgoing, 'expert', split_axis=0, concat_axis=0, tiled=True)  75.5 us
    ppermute x6, waiting for transfers between devices, exchange_all(): pieces.append(lax.ppermute(block, 'dp', pairs))  46.3 us
    ppermute x3, waiting for transfers between devices, exchange_gather(): pieces.append(lax.ppermute(outgoing, 'dp', pairs))  27 us
    all_to_all x2, waiting for transfers between devices, body(): lax.all_to_all(by_source, 'expert', split_axis=0, concat_axis=0, tiled=True)  24.4 us
    all_to_all x2, starting transfers between devices, body(): lax.all_to_all(by_source, 'expert', split_axis=0, concat_axis=0, tiled=True)  21.5 us
    reshape x4, local copies, waits for them, and re-layouts, body(): expert_cols.reshape(replica_count, expert_count, sub, columns)  11.2 us
    all_to_all x4, local copies, waits for them, and re-layouts, body(): lax.all_to_all(outgoing, 'expert', split_axis=0, concat_axis=0, tiled=True)  9.66 us
    dot_general x2, matrix products, body(): gate_part = jnp.dot(gathered, w_gate[0], preferred_element_type=jnp.float32)  9.32 us
  transfers between devices with their start and end apart: 13, of which 11 were waited for; matrix products, arithmetic and copies ran while one was open for 15% of the time, Pallas kernels for 0%

profile of v14, /device:TPU:2, one launch (start us, length us, event | category | flops | bytes accessed | tf_op | source)
XLA Modules:
  0.0 304.2 jit_solution(5991698772404731668)
XLA Ops:
  6.5 3.7 %dynamic-slice_bitcast_fusion = (bf16[384,1024]{1,0:T(8,128)(2,1)}, bf16[384,1024]{1,0:T(8,128)(2,1)}, bf16[1,384,1024]{2,1,0:T(8,128)(2,1)}, bf16[384,1024]{1,0:T(8,128)(2,1)}) fusion(bf16[1,384,4096]{2,1,0:T(8,128)(2,1)} %param.17, s32[]{:T(128)S(6)} %select_n.63, s32[]{:T(128)S(6)} %select_n.59, s32[]{:T(128)S(6)} %select_n.57, s32[]{:T(128)S(6)} %select_n.61), kind=kLoop, calls=%fused_computation.54 | loop fusion | bytes 6291472 | tf_op jit(solution)/shard_map/dynamic_slice | solution.py:14
  10.3 1.6 collective-permute-start.3
  11.9 2.9 collective-permute-start.4
  14.8 1.3 collective-permute-start.5
  17.8 2.0 reshape.214
  19.7 2.4 convolution_convert_fusion
  22.2 9.0 %collective-permute-done.3 = bf16[384,1024]{1,0:T(8,128)(2,1)} collective-permute-done((bf16[384,1024]{1,0:T(8,128)(2,1)}, bf16[384,1024]{1,0:T(8,128)(2,1)}, u32[]{:S(2)}, u32[]{:S(2)}) %collective-permute-start.3) | collective-permute-done | bytes 786464 | tf_op jit(solution)/shard_map/ppermute | solution.py:16
  31.2 18.0 %collective-permute-done.4 = bf16[384,1024]{1,0:T(8,128)(2,1)} collective-permute-done((bf16[384,1024]{1,0:T(8,128)(2,1)}, bf16[384,1024]{1,0:T(8,128)(2,1)}, u32[]{:S(2)}, u32[]{:S(2)}) %collective-permute-start.4) | collective-permute-done | bytes 786464 | tf_op jit(solution)/shard_map/ppermute | solution.py:16
  49.2 2.5 all_to_all.29
  51.7 40.9 %all_to_all.39 = bf16[64,2,4096]{2,1,0:T(2,128)(2,1)} all-to-all(bf16[64,2,4096]{2,1,0:T(2,128)(2,1)} %all_to_all.29), channel_id=1, replica_groups=mesh['dp'=4,'expert'=64] {'expert'}, dimensions={0} | all-to-all | bytes 2097152 | tf_op jit(solution)/shard_map/all_to_all | solution.py:70
  92.7 2.3 all_to_all.31
  95.1 2.4 convolution_convert_fusion.1
  97.5 2.5 all_to_all.25
  100.1 34.6 %all_to_all.40 = bf16[64,2,4096]{2,1,0:T(2,128)(2,1)} all-to-all(bf16[64,2,4096]{2,1,0:T(2,128)(2,1)} %all_to_all.25), channel_id=1, replica_groups=mesh['dp'=4,'expert'=64] {'expert'}, dimensions={0} | all-to-all | bytes 2097152 | tf_op jit(solution)/shard_map/all_to_all | solution.py:70
  134.6 2.3 all_to_all.27
  136.9 5.0 %all-gather.5.cloned.1.call-done = bf16[512,4096]{1,0:T(8,128)(2,1)} async-done(((bf16[128,4096]{1,0:T(8,128)(2,1)}), bf16[512,4096]{1,0:T(8,128)(2,1)}) %all-gather.5.cloned.1.call-update) | async-done | bytes 4194320 | tf_op jit(solution)/shard_map/all_gather | solution.py:71
  142.0 4.7 %fusion.20 = f32[512,384]{1,0:T(8,128)S(1)} fusion(bf16[512,4096]{1,0:T(8,128)(2,1)} %all-gather.5.cloned.1.call-done, bf16[1,4096,384]{2,1,0:T(8,128)(2,1)S(1)} %copy-done), kind=kOutput, calls=%fused_computation.23 | convolution fusion | flops 1610612736 | bytes 8126464 | tf_op jit(solution)/shard_map/dot_general | solution.py:72
  146.7 2.3 fusion.48
  149.0 1.2 collective-permute-start.8
  150.2 1.8 collective-permute-start.7
  152.0 0.6 collective-permute-start.6
  152.6 9.2 %collective-permute-done.8 = bf16[512,384]{1,0:T(8,128)(2,1)S(1)} collective-permute-done((bf16[512,384]{1,0:T(8,128)(2,1)S(1)}, bf16[512,384]{1,0:T(8,128)(2,1)S(1)}, u32[]{:S(2)}, u32[]{:S(2)}) %collective-permute-start.8) | collective-permute-done | bytes 393248 | tf_op jit(solution)/shard_map/ppermute | solution.py:24
  161.8 4.5 %collective-permute-done.7 = bf16[512,384]{1,0:T(8,128)(2,1)S(1)} collective-permute-done((bf16[512,384]{1,0:T(8,128)(2,1)S(1)}, bf16[512,384]{1,0:T(8,128)(2,1)S(1)}, u32[]{:S(2)}, u32[]{:S(2)}) %collective-permute-start.7) | collective-permute-done | bytes 393248 | tf_op jit(solution)/shard_map/ppermute | solution.py:24
  166.3 14.4 %collective-permute-done.6 = bf16[512,384]{1,0:T(8,128)(2,1)S(1)} collective-permute-done((bf16[512,384]{1,0:T(8,128)(2,1)S(1)}, bf16[512,384]{1,0:T(8,128)(2,1)S(1)}, u32[]{:S(2)}, u32[]{:S(2)}) %collective-permute-start.6) | collective-permute-done | bytes 393248 | tf_op jit(solution)/shard_map/ppermute | solution.py:24
  180.7 4.5 %bitcast_convert_fusion = bf16[512,1024]{1,0:T(8,128)(2,1)} fusion(bf16[1,384,1024]{2,1,0:T(8,128)(2,1)} %bitcast.27, bf16[1,384,1024]{2,1,0:T(8,128)(2,1)} %bitcast.26, bf16[1,384,1024]{2,1,0:T(8,128)(2,1)} %bitcast.25, bf16[1,384,1024]{2,1,0:T(8,128)(2,1)S(1)} %copy-done.1, bf16[1,512,384]{2,1,0:T(8,128)(2,1)S(1)} %bitcast.89, ...), kind=kOutput, calls=%fused_computation.27 | convolution fusion | flops 1618214912 | bytes 5767168 | tf_op jit(solution)/shard_map/dot_general | solution.py:76
  185.2 2.2 reshape.216
  187.5 3.4 %copy.47 = bf16[4,64,2,1024]{3,2,0,1:T(2,128)(2,1)} copy(bf16[4,64,2,1024]{3,2,1,0:T(2,128)(2,1)} %reshape.216) | data formatting | bytes 2097152 | tf_op jit(solution)/shard_map/reshape | solution.py:82
  190.8 10.7 %all-to-all-start.3 = ((bf16[64,4,2,1024]{3,2,1,0:T(2,128)(2,1)}), bf16[64,4,2,1024]{3,2,1,0:T(2,128)(2,1)}, u32[]{:S(2)}, u32[]{:S(2)}) async-start(bf16[64,4,2,1024]{3,2,1,0:T(2,128)(2,1)} %bitcast.79), calls=%async_computation.3 | async-start | bytes 2097152 | tf_op jit(solution)/shard_map/all_to_all | solution.py:85
  201.6 3.2 %all-gather.3.cloned.1.call-done = bf16[512,4096]{1,0:T(8,128)(2,1)} async-done(((bf16[128,4096]{1,0:T(8,128)(2,1)}), bf16[512,4096]{1,0:T(8,128)(2,1)}) %all-gather.3.cloned.1.call-update) | async-done | bytes 4194320 | tf_op jit(solution)/shard_map/all_gather | solution.py:71
  204.8 4.7 %fusion.22 = f32[512,384]{1,0:T(8,128)S(1)} fusion(bf16[512,4096]{1,0:T(8,128)(2,1)} %all-gather.3.cloned.1.call-done, bf16[1,4096,384]{2,1,0:T(8,128)(2,1)S(1)} %copy-done), kind=kOutput, calls=%fused_computation.25 | convolution fusion | flops 1610612736 | bytes 8126464 | tf_op jit(solution)/shard_map/dot_general | solution.py:72
  209.5 2.3 fusion.51
  211.8 0.7 collective-permute-start.2
  212.5 1.8 collective-permute-start.1
  214.3 0.8 collective-permute-start
  215.1 8.8 %collective-permute-done.2 = bf16[512,384]{1,0:T(8,128)(2,1)S(1)} collective-permute-done((bf16[512,384]{1,0:T(8,128)(2,1)S(1)}, bf16[512,384]{1,0:T(8,128)(2,1)S(1)}, u32[]{:S(2)}, u32[]{:S(2)}) %collective-permute-start.2) | collective-permute-done | bytes 393248 | tf_op jit(solution)/shard_map/ppermute | solution.py:24
  223.9 2.2 collective-permute-done.1
  226.1 7.2 %collective-permute-done = bf16[512,384]{1,0:T(8,128)(2,1)S(1)} collective-permute-done((bf16[512,384]{1,0:T(8,128)(2,1)S(1)}, bf16[512,384]{1,0:T(8,128)(2,1)S(1)}, u32[]{:S(2)}, u32[]{:S(2)}) %collective-permute-start) | collective-permute-done | bytes 393248 | tf_op jit(solution)/shard_map/ppermute | solution.py:24
  233.3 4.4 %bitcast_convert_fusion.1 = bf16[512,1024]{1,0:T(8,128)(2,1)} fusion(bf16[1,384,1024]{2,1,0:T(8,128)(2,1)} %bitcast.14, bf16[1,384,1024]{2,1,0:T(8,128)(2,1)} %bitcast.12, bf16[1,384,1024]{2,1,0:T(8,128)(2,1)} %bitcast.10, bf16[1,384,1024]{2,1,0:T(8,128)(2,1)S(1)} %copy-done.2, bf16[1,512,384]{2,1,0:T(8,128)(2,1)S(1)} %bitcast.87, ...), kind=kOutput, calls=%fused_computation.28 | convolution fusion | flops 1618214912 | bytes 5767168 | tf_op jit(solution)/shard_map/dot_general | solution.py:76
  237.7 2.3 reshape.215
  239.9 3.4 %copy.48 = bf16[4,64,2,1024]{3,2,0,1:T(2,128)(2,1)} copy(bf16[4,64,2,1024]{3,2,1,0:T(2,128)(2,1)} %reshape.215) | data formatting | bytes 2097152 | tf_op jit(solution)/shard_map/reshape | solution.py:82
  243.3 10.7 %all-to-all-start.1 = ((bf16[64,4,2,1024]{3,2,1,0:T(2,128)(2,1)}), bf16[64,4,2,1024]{3,2,1,0:T(2,128)(2,1)}, u32[]{:S(2)}, u32[]{:S(2)}) async-start(bf16[64,4,2,1024]{3,2,1,0:T(2,128)(2,1)} %bitcast.80), calls=%async_computation.1 | async-start | bytes 2097152 | tf_op jit(solution)/shard_map/all_to_all | solution.py:85
  254.2 0.3 select_reduce_fusion
  254.7 3.7 %convolution_bitcast_fusion = f32[64,1024]{1,0:T(8,128)} fusion(bf16[64,4,2,1024]{3,2,1,0:T(2,128)(2,1)} %all-to-all-done.3, s32[4,2]{1,0:T(4,128)S(1)} %iota_add_fusion, f32[64,64]{1,0:T(8,128)S(1)} %select_reduce_fusion, s32[64,64]{1,0:T(8,128)S(1)} %sub.20, pred[64,64]{1,0:T(8,128)(4,1)S(1)} %broadcast_compare_fusion), kind=kOutput, calls=%fused_computation.47 | convolution fusion | flops 402751488 | bytes 1347616 | tf_op jit(solution)/shard_map/dot_general | solution.py:92
  258.3 24.4 %all-to-all-done.1 = bf16[64,4,2,1024]{3,2,1,0:T(2,128)(2,1)} async-done(((bf16[64,4,2,1024]{3,2,1,0:T(2,128)(2,1)}), bf16[64,4,2,1024]{3,2,1,0:T(2,128)(2,1)}, u32[]{:S(2)}, u32[]{:S(2)}) %all-to-all-start.1) | async-done | bytes 1048608 | tf_op jit(solution)/shard_map/all_to_all | solution.py:85
  282.8 3.7 %fusion.54 = f32[64,1024]{1,0:T(8,128)} fusion(f32[64,1024]{1,0:T(8,128)} %convolution_bitcast_fusion, bf16[64,4,2,1024]{3,2,1,0:T(2,128)(2,1)} %all-to-all-done.1, f32[64,64]{1,0:T(8,128)S(1)} %select_reduce_fusion, s32[4,2]{1,0:T(4,128)S(1)} %iota_add_fusion.1, s32[64,64]{1,0:T(8,128)S(1)} %sub.20, pred[64,64]{1,0:T(8,128)(4,1)S(1)} %broadcast_compare_fusion), kind=kOutput, calls=%fused_computation.49 | convolution fusion | flops 402817024 | bytes 1609760 | tf_op jit(solution)/shard_map/dot_general | solution.py:92
  286.5 1.1 reshape.217
  287.9 8.8 %all_to_all.41 = bf16[4,4,4,1024]{3,2,1,0:T(4,128)(2,1)S(1)} all-to-all(bf16[4,4,4,1024]{3,2,1,0:T(4,128)(2,1)S(1)} %reshape.218), channel_id=1, replica_groups=mesh['dp'=4,'expert'=64] {'dp'}, dimensions={0} | all-to-all | bytes 262144 | tf_op jit(solution)/shard_map/all_to_all | solution.py:110
  296.7 0.7 copy.40
  (51 shorter events, 1.7 us)
Async XLA Ops:
  6.5 135.4 %copy-start = (bf16[1,4096,384]{2,1,0:T(8,128)(2,1)S(1)}, bf16[1,4096,384]{2,1,0:T(8,128)(2,1)}, u32[]{:S(2)}) copy-start(bf16[1,4096,384]{2,1,0:T(8,128)(2,1)} %param.15) | copy-start | bytes 9437188
  6.5 135.4 %all-gather.5.cloned.1.call-start = ((), (), s32[]{:S(2)}) async-start(), calls=%async_computation.6 | async-start | bytes 5242880 | tf_op jit(solution)/shard_map/all_gather | solution.py:71
  6.5 9.6 %copy-start.4 = (s32[16,4,8]{0,2,1:T(8,128)S(1)}, s32[16,4,8]{0,2,1:T(8,128)}, u32[]{:S(2)}) copy-start(s32[16,4,8]{0,2,1:T(8,128)} %param.10) | copy-start | bytes 6148
  6.5 10.3 %copy-start.5 = (s32[16]{0:T(128)S(1)}, s32[16]{0:T(128)}, u32[]{:S(2)}) copy-start(s32[16]{0:T(128)} %param.12) | copy-start | bytes 196
  10.3 20.9 %collective-permute-start.3 = (bf16[384,1024]{1,0:T(8,128)(2,1)}, bf16[384,1024]{1,0:T(8,128)(2,1)}, u32[]{:S(2)}, u32[]{:S(2)}) collective-permute-start(bf16[384,1024]{1,0:T(8,128)(2,1)} %get-tuple-element.16), channel_id=1, source_target_pairs={{0,64},{64,128},{128,192},{192,0},{1,65},{65,129},{129,193},{193,1... | collective-permute-start | bytes 2359304 | tf_op jit(solution)/shard_map/ppermute | solution.py:16
  11.9 37.3 %collective-permute-start.4 = (bf16[384,1024]{1,0:T(8,128)(2,1)}, bf16[384,1024]{1,0:T(8,128)(2,1)}, u32[]{:S(2)}, u32[]{:S(2)}) collective-permute-start(bf16[384,1024]{1,0:T(8,128)(2,1)} %get-tuple-element.18), channel_id=1, source_target_pairs={{0,128},{64,192},{128,0},{192,64},{1,129},{65,193},{129,1},{193,65... | collective-permute-start | bytes 2359304 | tf_op jit(solution)/shard_map/ppermute | solution.py:16
  14.8 34.4 %collective-permute-start.5 = (bf16[384,1024]{1,0:T(8,128)(2,1)}, bf16[384,1024]{1,0:T(8,128)(2,1)}, u32[]{:S(2)}, u32[]{:S(2)}) collective-permute-start(bf16[384,1024]{1,0:T(8,128)(2,1)} %get-tuple-element.15), channel_id=1, source_target_pairs={{0,192},{64,0},{128,64},{192,128},{1,193},{65,1},{129,65},{193,129... | collective-permute-start | bytes 2359304 | tf_op jit(solution)/shard_map/ppermute | solution.py:16
  95.0 109.8 %all-gather.3.cloned.1.call-start = ((), (), s32[]{:S(2)}) async-start(), calls=%async_computation.5 | async-start | bytes 5242880 | tf_op jit(solution)/shard_map/all_gather | solution.py:71
  142.0 4.7 %copy-start.7 = (bf16[512,4096]{1,0:T(8,128)(2,1)S(1)}, bf16[512,4096]{1,0:T(8,128)(2,1)}, u32[]{:S(2)}) copy-start(bf16[512,4096]{1,0:T(8,128)(2,1)} %all-gather.5.cloned.1.call-done) | copy-start | bytes 12582916
  142.0 4.7 %copy-start.8 = (bf16[1,4096,384]{2,1,0:T(8,128)(2,1)S(1)}, bf16[1,4096,384]{2,1,0:T(8,128)(2,1)}, u32[]{:S(2)}) copy-start(bf16[1,4096,384]{2,1,0:T(8,128)(2,1)} %param.16) | copy-start | bytes 9437188
  146.6 34.1 %copy-start.1 = (bf16[1,384,1024]{2,1,0:T(8,128)(2,1)S(1)}, bf16[1,384,1024]{2,1,0:T(8,128)(2,1)}, u32[]{:S(2)}) copy-start(bf16[1,384,1024]{2,1,0:T(8,128)(2,1)} %get-tuple-element.17) | copy-start | bytes 2359300
  149.0 12.8 %collective-permute-start.8 = (bf16[512,384]{1,0:T(8,128)(2,1)S(1)}, bf16[512,384]{1,0:T(8,128)(2,1)S(1)}, u32[]{:S(2)}, u32[]{:S(2)}) collective-permute-start(bf16[512,384]{1,0:T(8,128)(2,1)S(1)} %fusion.48), channel_id=1, source_target_pairs={{0,192},{64,0},{128,64},{192,128},{1,193},{65,1},{129,65},{193,129... | collective-permute-start | bytes 1179656 | tf_op jit(solution)/shard_map/ppermute | solution.py:24
  150.2 16.1 %collective-permute-start.7 = (bf16[512,384]{1,0:T(8,128)(2,1)S(1)}, bf16[512,384]{1,0:T(8,128)(2,1)S(1)}, u32[]{:S(2)}, u32[]{:S(2)}) collective-permute-start(bf16[512,384]{1,0:T(8,128)(2,1)S(1)} %fusion.48), channel_id=1, source_target_pairs={{0,128},{64,192},{128,0},{192,64},{1,129},{65,193},{129,1},{193,65... | collective-permute-start | bytes 1179656 | tf_op jit(solution)/shard_map/ppermute | solution.py:24
  152.0 28.7 %collective-permute-start.6 = (bf16[512,384]{1,0:T(8,128)(2,1)S(1)}, bf16[512,384]{1,0:T(8,128)(2,1)S(1)}, u32[]{:S(2)}, u32[]{:S(2)}) collective-permute-start(bf16[512,384]{1,0:T(8,128)(2,1)S(1)} %fusion.48), channel_id=1, source_target_pairs={{0,64},{64,128},{128,192},{192,0},{1,65},{65,129},{129,193},{193,1... | collective-permute-start | bytes 1179656 | tf_op jit(solution)/shard_map/ppermute | solution.py:24
  190.8 52.5 %all-to-all-start.3 = ((bf16[64,4,2,1024]{3,2,1,0:T(2,128)(2,1)}), bf16[64,4,2,1024]{3,2,1,0:T(2,128)(2,1)}, u32[]{:S(2)}, u32[]{:S(2)}) async-start(bf16[64,4,2,1024]{3,2,1,0:T(2,128)(2,1)} %bitcast.79), calls=%async_computation.3 | async-start | bytes 2097152 | tf_op jit(solution)/shard_map/all_to_all | solution.py:85
  204.8 4.7 %copy-start.6 = (bf16[512,4096]{1,0:T(8,128)(2,1)S(1)}, bf16[512,4096]{1,0:T(8,128)(2,1)}, u32[]{:S(2)}) copy-start(bf16[512,4096]{1,0:T(8,128)(2,1)} %all-gather.3.cloned.1.call-done) | copy-start | bytes 12582916
  204.8 4.7 %copy-start.9 = (bf16[1,4096,384]{2,1,0:T(8,128)(2,1)S(1)}, bf16[1,4096,384]{2,1,0:T(8,128)(2,1)}, u32[]{:S(2)}) copy-start(bf16[1,4096,384]{2,1,0:T(8,128)(2,1)} %param.16) | copy-start | bytes 9437188
  209.5 23.8 %copy-start.2 = (bf16[1,384,1024]{2,1,0:T(8,128)(2,1)S(1)}, bf16[1,384,1024]{2,1,0:T(8,128)(2,1)}, u32[]{:S(2)}) copy-start(bf16[1,384,1024]{2,1,0:T(8,128)(2,1)} %get-tuple-element.17) | copy-start | bytes 2359300
  211.8 12.0 %collective-permute-start.2 = (bf16[512,384]{1,0:T(8,128)(2,1)S(1)}, bf16[512,384]{1,0:T(8,128)(2,1)S(1)}, u32[]{:S(2)}, u32[]{:S(2)}) collective-permute-start(bf16[512,384]{1,0:T(8,128)(2,1)S(1)} %fusion.51), channel_id=1, source_target_pairs={{0,192},{64,0},{128,64},{192,128},{1,193},{65,1},{129,65},{193,129... | collective-permute-start | bytes 1179656 | tf_op jit(solution)/shard_map/ppermute | solution.py:24
  212.5 13.6 %collective-permute-start.1 = (bf16[512,384]{1,0:T(8,128)(2,1)S(1)}, bf16[512,384]{1,0:T(8,128)(2,1)S(1)}, u32[]{:S(2)}, u32[]{:S(2)}) collective-permute-start(bf16[512,384]{1,0:T(8,128)(2,1)S(1)} %fusion.51), channel_id=1, source_target_pairs={{0,128},{64,192},{128,0},{192,64},{1,129},{65,193},{129,1},{193,65... | collective-permute-start | bytes 1179656 | tf_op jit(solution)/shard_map/ppermute | solution.py:24
  214.3 18.9 %collective-permute-start = (bf16[512,384]{1,0:T(8,128)(2,1)S(1)}, bf16[512,384]{1,0:T(8,128)(2,1)S(1)}, u32[]{:S(2)}, u32[]{:S(2)}) collective-permute-start(bf16[512,384]{1,0:T(8,128)(2,1)S(1)} %fusion.51), channel_id=1, source_target_pairs={{0,64},{64,128},{128,192},{192,0},{1,65},{65,129},{129,193},{193,1... | collective-permute-start | bytes 1179656 | tf_op jit(solution)/shard_map/ppermute | solution.py:24
  237.7 16.4 %copy-start.3 = (f32[16,4,8]{0,2,1:T(8,128)S(1)}, f32[16,4,8]{0,2,1:T(8,128)}, u32[]{:S(2)}) copy-start(f32[16,4,8]{0,2,1:T(8,128)} %param.11) | copy-start | bytes 6148
  237.7 16.8 %copy-start.10 = (s32[16]{0:T(128)S(1)}, s32[16]{0:T(128)}, u32[]{:S(2)}) copy-start(s32[16]{0:T(128)} %param.14) | copy-start | bytes 196
  243.3 39.5 %all-to-all-start.1 = ((bf16[64,4,2,1024]{3,2,1,0:T(2,128)(2,1)}), bf16[64,4,2,1024]{3,2,1,0:T(2,128)(2,1)}, u32[]{:S(2)}, u32[]{:S(2)}) async-start(bf16[64,4,2,1024]{3,2,1,0:T(2,128)(2,1)} %bitcast.80), calls=%async_computation.1 | async-start | bytes 2097152 | tf_op jit(solution)/shard_map/all_to_all | solution.py:85
Sparse Core Ops, SparseCore 0:
  95.1 46.8 all-gather.4
  143.8 60.9 all-gather.2

commit v15 on v14

--- a/solution.py
+++ b/solution.py
@@ -99,11 +99,10 @@
     flat_device = dest_slot // share_rows
     target = flat_device // expert_count * share_rows + dest_slot % share_rows
     position_ids = lax.broadcasted_iota(jnp.int32, (replica_count * share_rows, row_count), 0)
-    arrangement = (target[None, :] == position_ids).astype(jnp.float32)
+    arrangement = (target[None, :] == position_ids).astype(jnp.bfloat16)
     arranged = jnp.dot(
         arrangement,
-        combined.reshape(row_count, step_count * columns),
-        precision=lax.Precision.HIGHEST,
+        combined.astype(jnp.bfloat16).reshape(row_count, step_count * columns),
         preferred_element_type=jnp.float32,
     ).astype(jnp.bfloat16)
     arranged = arranged.reshape(replica_count, share_rows, step_count, columns)

time: 305 us -> 303 us (level)
  no operation moved by 1% of the time
where the time goes in v15:
time: 303 us; the launch traced here: 302 us
  waiting for transfers between devices  106 us (35%)
  blocking collectives  84.3 us (28%)
  matrix products  34.7 us (11%)
  starting transfers between devices  34.2 us (11%)
  local copies, waits for them, and re-layouts  28 us (9%)
  between operations  14.3 us (5%)
    all_to_all x2, blocking collectives, body(): lax.all_to_all(outgoing, 'expert', split_axis=0, concat_axis=0, tiled=True)  75.5 us
    ppermute x6, waiting for transfers between devices, exchange_all(): pieces.append(lax.ppermute(block, 'dp', pairs))  46.3 us
    ppermute x3, waiting for transfers between devices, exchange_gather(): pieces.append(lax.ppermute(outgoing, 'dp', pairs))  27 us
    all_to_all x2, waiting for transfers between devices, body(): lax.all_to_all(by_source, 'expert', split_axis=0, concat_axis=0, tiled=True)  24.4 us
    all_to_all x2, starting transfers between devices, body(): lax.all_to_all(by_source, 'expert', split_axis=0, concat_axis=0, tiled=True)  21.5 us
    reshape x4, local copies, waits for them, and re-layouts, body(): expert_cols.reshape(replica_count, expert_count, sub, columns)  11.2 us
    all_to_all x4, local copies, waits for them, and re-layouts, body(): lax.all_to_all(outgoing, 'expert', split_axis=0, concat_axis=0, tiled=True)  9.66 us
    dot_general x2, matrix products, body(): gate_part = jnp.dot(gathered, w_gate[0], preferred_element_type=jnp.float32)  9.32 us
  transfers between devices with their start and end apart: 13, of which 11 were waited for; matrix products, arithmetic and copies ran while one was open for 15% of the time, Pallas kernels for 0%

profile of v15, /device:TPU:2, one launch (start us, length us, event | category | flops | bytes accessed | tf_op | source)
XLA Modules:
  0.0 302.5 jit_solution(17572115597214870740)
XLA Ops:
  6.5 3.7 %dynamic-slice_bitcast_fusion = (bf16[384,1024]{1,0:T(8,128)(2,1)}, bf16[384,1024]{1,0:T(8,128)(2,1)}, bf16[1,384,1024]{2,1,0:T(8,128)(2,1)}, bf16[384,1024]{1,0:T(8,128)(2,1)}) fusion(bf16[1,384,4096]{2,1,0:T(8,128)(2,1)} %param.17, s32[]{:T(128)S(6)} %select_n.63, s32[]{:T(128)S(6)} %select_n.59, s32[]{:T(128)S(6)} %select_n.57, s32[]{:T(128)S(6)} %select_n.61), kind=kLoop, calls=%fused_computation.55 | loop fusion | bytes 6291472 | tf_op jit(solution)/shard_map/dynamic_slice | solution.py:14
  10.3 1.6 collective-permute-start.3
  11.9 2.9 collective-permute-start.4
  14.8 1.3 collective-permute-start.5
  17.0 0.2 convert_reduce_fusion
  17.8 2.0 reshape.214
  19.7 2.4 convolution_convert_fusion
  22.2 9.0 %collective-permute-done.3 = bf16[384,1024]{1,0:T(8,128)(2,1)} collective-permute-done((bf16[384,1024]{1,0:T(8,128)(2,1)}, bf16[384,1024]{1,0:T(8,128)(2,1)}, u32[]{:S(2)}, u32[]{:S(2)}) %collective-permute-start.3) | collective-permute-done | bytes 786464 | tf_op jit(solution)/shard_map/ppermute | solution.py:16
  31.2 18.0 %collective-permute-done.4 = bf16[384,1024]{1,0:T(8,128)(2,1)} collective-permute-done((bf16[384,1024]{1,0:T(8,128)(2,1)}, bf16[384,1024]{1,0:T(8,128)(2,1)}, u32[]{:S(2)}, u32[]{:S(2)}) %collective-permute-start.4) | collective-permute-done | bytes 786464 | tf_op jit(solution)/shard_map/ppermute | solution.py:16
  49.2 2.5 all_to_all.29
  51.7 40.9 %all_to_all.39 = bf16[64,2,4096]{2,1,0:T(2,128)(2,1)} all-to-all(bf16[64,2,4096]{2,1,0:T(2,128)(2,1)} %all_to_all.29), channel_id=1, replica_groups=mesh['dp'=4,'expert'=64] {'expert'}, dimensions={0} | all-to-all | bytes 2097152 | tf_op jit(solution)/shard_map/all_to_all | solution.py:70
  92.7 2.3 all_to_all.31
  95.1 2.4 convolution_convert_fusion.1
  97.5 2.5 all_to_all.25
  100.1 34.6 %all_to_all.40 = bf16[64,2,4096]{2,1,0:T(2,128)(2,1)} all-to-all(bf16[64,2,4096]{2,1,0:T(2,128)(2,1)} %all_to_all.25), channel_id=1, replica_groups=mesh['dp'=4,'expert'=64] {'expert'}, dimensions={0} | all-to-all | bytes 2097152 | tf_op jit(solution)/shard_map/all_to_all | solution.py:70
  134.6 2.3 all_to_all.27
  136.9 5.0 %all-gather.5.cloned.1.call-done = bf16[512,4096]{1,0:T(8,128)(2,1)} async-done(((bf16[128,4096]{1,0:T(8,128)(2,1)}), bf16[512,4096]{1,0:T(8,128)(2,1)}) %all-gather.5.cloned.1.call-update) | async-done | bytes 4194320 | tf_op jit(solution)/shard_map/all_gather | solution.py:71
  142.0 4.7 %fusion.20 = f32[512,384]{1,0:T(8,128)S(1)} fusion(bf16[512,4096]{1,0:T(8,128)(2,1)} %all-gather.5.cloned.1.call-done, bf16[1,4096,384]{2,1,0:T(8,128)(2,1)S(1)} %copy-done), kind=kOutput, calls=%fused_computation.23 | convolution fusion | flops 1610612736 | bytes 8126464 | tf_op jit(solution)/shard_map/dot_general | solution.py:72
  146.7 2.3 fusion.48
  149.0 1.2 collective-permute-start.8
  150.2 1.8 collective-permute-start.7
  152.0 0.6 collective-permute-start.6
  152.6 9.2 %collective-permute-done.8 = bf16[512,384]{1,0:T(8,128)(2,1)S(1)} collective-permute-done((bf16[512,384]{1,0:T(8,128)(2,1)S(1)}, bf16[512,384]{1,0:T(8,128)(2,1)S(1)}, u32[]{:S(2)}, u32[]{:S(2)}) %collective-permute-start.8) | collective-permute-done | bytes 393248 | tf_op jit(solution)/shard_map/ppermute | solution.py:24
  161.8 4.5 %collective-permute-done.7 = bf16[512,384]{1,0:T(8,128)(2,1)S(1)} collective-permute-done((bf16[512,384]{1,0:T(8,128)(2,1)S(1)}, bf16[512,384]{1,0:T(8,128)(2,1)S(1)}, u32[]{:S(2)}, u32[]{:S(2)}) %collective-permute-start.7) | collective-permute-done | bytes 393248 | tf_op jit(solution)/shard_map/ppermute | solution.py:24
  166.3 14.4 %collective-permute-done.6 = bf16[512,384]{1,0:T(8,128)(2,1)S(1)} collective-permute-done((bf16[512,384]{1,0:T(8,128)(2,1)S(1)}, bf16[512,384]{1,0:T(8,128)(2,1)S(1)}, u32[]{:S(2)}, u32[]{:S(2)}) %collective-permute-start.6) | collective-permute-done | bytes 393248 | tf_op jit(solution)/shard_map/ppermute | solution.py:24
  180.7 4.5 %bitcast_convert_fusion = bf16[512,1024]{1,0:T(8,128)(2,1)} fusion(bf16[1,384,1024]{2,1,0:T(8,128)(2,1)} %bitcast.27, bf16[1,384,1024]{2,1,0:T(8,128)(2,1)} %bitcast.26, bf16[1,384,1024]{2,1,0:T(8,128)(2,1)} %bitcast.25, bf16[1,384,1024]{2,1,0:T(8,128)(2,1)S(1)} %copy-done.1, bf16[1,512,384]{2,1,0:T(8,128)(2,1)S(1)} %bitcast.91, ...), kind=kOutput, calls=%fused_computation.27 | convolution fusion | flops 1618214912 | bytes 5767168 | tf_op jit(solution)/shard_map/dot_general | solution.py:76
  185.2 2.2 reshape.216
  187.5 3.4 %copy.47 = bf16[4,64,2,1024]{3,2,0,1:T(2,128)(2,1)} copy(bf16[4,64,2,1024]{3,2,1,0:T(2,128)(2,1)} %reshape.216) | data formatting | bytes 2097152 | tf_op jit(solution)/shard_map/reshape | solution.py:82
  190.8 10.7 %all-to-all-start.3 = ((bf16[64,4,2,1024]{3,2,1,0:T(2,128)(2,1)}), bf16[64,4,2,1024]{3,2,1,0:T(2,128)(2,1)}, u32[]{:S(2)}, u32[]{:S(2)}) async-start(bf16[64,4,2,1024]{3,2,1,0:T(2,128)(2,1)} %bitcast.81), calls=%async_computation.3 | async-start | bytes 2097152 | tf_op jit(solution)/shard_map/all_to_all | solution.py:85
  201.6 3.2 %all-gather.3.cloned.1.call-done = bf16[512,4096]{1,0:T(8,128)(2,1)} async-done(((bf16[128,4096]{1,0:T(8,128)(2,1)}), bf16[512,4096]{1,0:T(8,128)(2,1)}) %all-gather.3.cloned.1.call-update) | async-done | bytes 4194320 | tf_op jit(solution)/shard_map/all_gather | solution.py:71
  204.8 4.7 %fusion.22 = f32[512,384]{1,0:T(8,128)S(1)} fusion(bf16[512,4096]{1,0:T(8,128)(2,1)} %all-gather.3.cloned.1.call-done, bf16[1,4096,384]{2,1,0:T(8,128)(2,1)S(1)} %copy-done), kind=kOutput, calls=%fused_computation.25 | convolution fusion | flops 1610612736 | bytes 8126464 | tf_op jit(solution)/shard_map/dot_general | solution.py:72
  209.5 2.3 fusion.51
  211.8 0.7 collective-permute-start.2
  212.5 1.8 collective-permute-start.1
  214.3 0.8 collective-permute-start
  215.1 8.8 %collective-permute-done.2 = bf16[512,384]{1,0:T(8,128)(2,1)S(1)} collective-permute-done((bf16[512,384]{1,0:T(8,128)(2,1)S(1)}, bf16[512,384]{1,0:T(8,128)(2,1)S(1)}, u32[]{:S(2)}, u32[]{:S(2)}) %collective-permute-start.2) | collective-permute-done | bytes 393248 | tf_op jit(solution)/shard_map/ppermute | solution.py:24
  223.9 2.2 collective-permute-done.1
  226.1 7.2 %collective-permute-done = bf16[512,384]{1,0:T(8,128)(2,1)S(1)} collective-permute-done((bf16[512,384]{1,0:T(8,128)(2,1)S(1)}, bf16[512,384]{1,0:T(8,128)(2,1)S(1)}, u32[]{:S(2)}, u32[]{:S(2)}) %collective-permute-start) | collective-permute-done | bytes 393248 | tf_op jit(solution)/shard_map/ppermute | solution.py:24
  233.3 4.4 %bitcast_convert_fusion.1 = bf16[512,1024]{1,0:T(8,128)(2,1)} fusion(bf16[1,384,1024]{2,1,0:T(8,128)(2,1)} %bitcast.14, bf16[1,384,1024]{2,1,0:T(8,128)(2,1)} %bitcast.12, bf16[1,384,1024]{2,1,0:T(8,128)(2,1)} %bitcast.10, bf16[1,384,1024]{2,1,0:T(8,128)(2,1)S(1)} %copy-done.2, bf16[1,512,384]{2,1,0:T(8,128)(2,1)S(1)} %bitcast.89, ...), kind=kOutput, calls=%fused_computation.28 | convolution fusion | flops 1618214912 | bytes 5767168 | tf_op jit(solution)/shard_map/dot_general | solution.py:76
  237.7 2.3 reshape.215
  239.9 3.4 %copy.48 = bf16[4,64,2,1024]{3,2,0,1:T(2,128)(2,1)} copy(bf16[4,64,2,1024]{3,2,1,0:T(2,128)(2,1)} %reshape.215) | data formatting | bytes 2097152 | tf_op jit(solution)/shard_map/reshape | solution.py:82
  243.3 10.7 %all-to-all-start.1 = ((bf16[64,4,2,1024]{3,2,1,0:T(2,128)(2,1)}), bf16[64,4,2,1024]{3,2,1,0:T(2,128)(2,1)}, u32[]{:S(2)}, u32[]{:S(2)}) async-start(bf16[64,4,2,1024]{3,2,1,0:T(2,128)(2,1)} %bitcast.82), calls=%async_computation.1 | async-start | bytes 2097152 | tf_op jit(solution)/shard_map/all_to_all | solution.py:85
  254.2 0.3 select_reduce_fusion
  254.7 3.7 %convolution_bitcast_fusion = f32[64,1024]{1,0:T(8,128)} fusion(bf16[64,4,2,1024]{3,2,1,0:T(2,128)(2,1)} %all-to-all-done.3, s32[4,2]{1,0:T(4,128)S(1)} %iota_add_fusion, f32[64,64]{1,0:T(8,128)S(1)} %select_reduce_fusion, s32[64,64]{1,0:T(8,128)S(1)} %sub.20, pred[64,64]{1,0:T(8,128)(4,1)S(1)} %broadcast_compare_fusion), kind=kOutput, calls=%fused_computation.47 | convolution fusion | flops 402751488 | bytes 1347616 | tf_op jit(solution)/shard_map/dot_general | solution.py:92
  258.3 24.4 %all-to-all-done.1 = bf16[64,4,2,1024]{3,2,1,0:T(2,128)(2,1)} async-done(((bf16[64,4,2,1024]{3,2,1,0:T(2,128)(2,1)}), bf16[64,4,2,1024]{3,2,1,0:T(2,128)(2,1)}, u32[]{:S(2)}, u32[]{:S(2)}) %all-to-all-start.1) | async-done | bytes 1048608 | tf_op jit(solution)/shard_map/all_to_all | solution.py:85
  282.8 3.0 %fusion.55 = bf16[64,1024]{1,0:T(8,128)(2,1)S(1)} fusion(f32[64,1024]{1,0:T(8,128)} %convolution_bitcast_fusion, bf16[64,4,2,1024]{3,2,1,0:T(2,128)(2,1)} %all-to-all-done.1, f32[64,64]{1,0:T(8,128)S(1)} %select_reduce_fusion, s32[4,2]{1,0:T(4,128)S(1)} %iota_add_fusion.1, s32[64,64]{1,0:T(8,128)S(1)} %sub.20, pred[64,64]{1,0:T(8,128)(4,1)S(1)} %broadcast_compare_fusion), kind=kOutput, calls=%fused_computation.50 | convolution fusion | flops 402882560 | bytes 1478688 | tf_op jit(solution)/shard_map/dot_general | solution.py:92
  286.1 8.8 %all_to_all.41 = bf16[4,4,4,1024]{3,2,1,0:T(4,128)(2,1)S(1)} all-to-all(bf16[4,4,4,1024]{3,2,1,0:T(4,128)(2,1)S(1)} %reshape.218), channel_id=1, replica_groups=mesh['dp'=4,'expert'=64] {'dp'}, dimensions={0} | all-to-all | bytes 262144 | tf_op jit(solution)/shard_map/all_to_all | solution.py:109
  294.9 0.7 copy.40
  (51 shorter events, 1.5 us)
Async XLA Ops:
  6.5 135.4 %copy-start = (bf16[1,4096,384]{2,1,0:T(8,128)(2,1)S(1)}, bf16[1,4096,384]{2,1,0:T(8,128)(2,1)}, u32[]{:S(2)}) copy-start(bf16[1,4096,384]{2,1,0:T(8,128)(2,1)} %param.15) | copy-start | bytes 9437188
  6.5 135.4 %all-gather.5.cloned.1.call-start = ((), (), s32[]{:S(2)}) async-start(), calls=%async_computation.6 | async-start | bytes 5242880 | tf_op jit(solution)/shard_map/all_gather | solution.py:71
  6.5 9.6 %copy-start.4 = (s32[16,4,8]{0,2,1:T(8,128)S(1)}, s32[16,4,8]{0,2,1:T(8,128)}, u32[]{:S(2)}) copy-start(s32[16,4,8]{0,2,1:T(8,128)} %param.10) | copy-start | bytes 6148
  6.5 10.3 %copy-start.5 = (s32[16]{0:T(128)S(1)}, s32[16]{0:T(128)}, u32[]{:S(2)}) copy-start(s32[16]{0:T(128)} %param.12) | copy-start | bytes 196
  10.3 20.9 %collective-permute-start.3 = (bf16[384,1024]{1,0:T(8,128)(2,1)}, bf16[384,1024]{1,0:T(8,128)(2,1)}, u32[]{:S(2)}, u32[]{:S(2)}) collective-permute-start(bf16[384,1024]{1,0:T(8,128)(2,1)} %get-tuple-element.16), channel_id=1, source_target_pairs={{0,64},{64,128},{128,192},{192,0},{1,65},{65,129},{129,193},{193,1... | collective-permute-start | bytes 2359304 | tf_op jit(solution)/shard_map/ppermute | solution.py:16
  11.9 37.3 %collective-permute-start.4 = (bf16[384,1024]{1,0:T(8,128)(2,1)}, bf16[384,1024]{1,0:T(8,128)(2,1)}, u32[]{:S(2)}, u32[]{:S(2)}) collective-permute-start(bf16[384,1024]{1,0:T(8,128)(2,1)} %get-tuple-element.18), channel_id=1, source_target_pairs={{0,128},{64,192},{128,0},{192,64},{1,129},{65,193},{129,1},{193,65... | collective-permute-start | bytes 2359304 | tf_op jit(solution)/shard_map/ppermute | solution.py:16
  14.8 34.4 %collective-permute-start.5 = (bf16[384,1024]{1,0:T(8,128)(2,1)}, bf16[384,1024]{1,0:T(8,128)(2,1)}, u32[]{:S(2)}, u32[]{:S(2)}) collective-permute-start(bf16[384,1024]{1,0:T(8,128)(2,1)} %get-tuple-element.15), channel_id=1, source_target_pairs={{0,192},{64,0},{128,64},{192,128},{1,193},{65,1},{129,65},{193,129... | collective-permute-start | bytes 2359304 | tf_op jit(solution)/shard_map/ppermute | solution.py:16
  95.0 109.8 %all-gather.3.cloned.1.call-start = ((), (), s32[]{:S(2)}) async-start(), calls=%async_computation.5 | async-start | bytes 5242880 | tf_op jit(solution)/shard_map/all_gather | solution.py:71
  142.0 4.7 %copy-start.7 = (bf16[512,4096]{1,0:T(8,128)(2,1)S(1)}, bf16[512,4096]{1,0:T(8,128)(2,1)}, u32[]{:S(2)}) copy-start(bf16[512,4096]{1,0:T(8,128)(2,1)} %all-gather.5.cloned.1.call-done) | copy-start | bytes 12582916
  142.0 4.7 %copy-start.8 = (bf16[1,4096,384]{2,1,0:T(8,128)(2,1)S(1)}, bf16[1,4096,384]{2,1,0:T(8,128)(2,1)}, u32[]{:S(2)}) copy-start(bf16[1,4096,384]{2,1,0:T(8,128)(2,1)} %param.16) | copy-start | bytes 9437188
  146.6 34.1 %copy-start.1 = (bf16[1,384,1024]{2,1,0:T(8,128)(2,1)S(1)}, bf16[1,384,1024]{2,1,0:T(8,128)(2,1)}, u32[]{:S(2)}) copy-start(bf16[1,384,1024]{2,1,0:T(8,128)(2,1)} %get-tuple-element.17) | copy-start | bytes 2359300
  149.0 12.8 %collective-permute-start.8 = (bf16[512,384]{1,0:T(8,128)(2,1)S(1)}, bf16[512,384]{1,0:T(8,128)(2,1)S(1)}, u32[]{:S(2)}, u32[]{:S(2)}) collective-permute-start(bf16[512,384]{1,0:T(8,128)(2,1)S(1)} %fusion.48), channel_id=1, source_target_pairs={{0,192},{64,0},{128,64},{192,128},{1,193},{65,1},{129,65},{193,129... | collective-permute-start | bytes 1179656 | tf_op jit(solution)/shard_map/ppermute | solution.py:24
  150.2 16.1 %collective-permute-start.7 = (bf16[512,384]{1,0:T(8,128)(2,1)S(1)}, bf16[512,384]{1,0:T(8,128)(2,1)S(1)}, u32[]{:S(2)}, u32[]{:S(2)}) collective-permute-start(bf16[512,384]{1,0:T(8,128)(2,1)S(1)} %fusion.48), channel_id=1, source_target_pairs={{0,128},{64,192},{128,0},{192,64},{1,129},{65,193},{129,1},{193,65... | collective-permute-start | bytes 1179656 | tf_op jit(solution)/shard_map/ppermute | solution.py:24
  152.0 28.7 %collective-permute-start.6 = (bf16[512,384]{1,0:T(8,128)(2,1)S(1)}, bf16[512,384]{1,0:T(8,128)(2,1)S(1)}, u32[]{:S(2)}, u32[]{:S(2)}) collective-permute-start(bf16[512,384]{1,0:T(8,128)(2,1)S(1)} %fusion.48), channel_id=1, source_target_pairs={{0,64},{64,128},{128,192},{192,0},{1,65},{65,129},{129,193},{193,1... | collective-permute-start | bytes 1179656 | tf_op jit(solution)/shard_map/ppermute | solution.py:24
  190.8 52.5 %all-to-all-start.3 = ((bf16[64,4,2,1024]{3,2,1,0:T(2,128)(2,1)}), bf16[64,4,2,1024]{3,2,1,0:T(2,128)(2,1)}, u32[]{:S(2)}, u32[]{:S(2)}) async-start(bf16[64,4,2,1024]{3,2,1,0:T(2,128)(2,1)} %bitcast.81), calls=%async_computation.3 | async-start | bytes 2097152 | tf_op jit(solution)/shard_map/all_to_all | solution.py:85
  204.8 4.7 %copy-start.6 = (bf16[512,4096]{1,0:T(8,128)(2,1)S(1)}, bf16[512,4096]{1,0:T(8,128)(2,1)}, u32[]{:S(2)}) copy-start(bf16[512,4096]{1,0:T(8,128)(2,1)} %all-gather.3.cloned.1.call-done) | copy-start | bytes 12582916
  204.8 4.7 %copy-start.9 = (bf16[1,4096,384]{2,1,0:T(8,128)(2,1)S(1)}, bf16[1,4096,384]{2,1,0:T(8,128)(2,1)}, u32[]{:S(2)}) copy-start(bf16[1,4096,384]{2,1,0:T(8,128)(2,1)} %param.16) | copy-start | bytes 9437188
  209.5 23.8 %copy-start.2 = (bf16[1,384,1024]{2,1,0:T(8,128)(2,1)S(1)}, bf16[1,384,1024]{2,1,0:T(8,128)(2,1)}, u32[]{:S(2)}) copy-start(bf16[1,384,1024]{2,1,0:T(8,128)(2,1)} %get-tuple-element.17) | copy-start | bytes 2359300
  211.8 12.0 %collective-permute-start.2 = (bf16[512,384]{1,0:T(8,128)(2,1)S(1)}, bf16[512,384]{1,0:T(8,128)(2,1)S(1)}, u32[]{:S(2)}, u32[]{:S(2)}) collective-permute-start(bf16[512,384]{1,0:T(8,128)(2,1)S(1)} %fusion.51), channel_id=1, source_target_pairs={{0,192},{64,0},{128,64},{192,128},{1,193},{65,1},{129,65},{193,129... | collective-permute-start | bytes 1179656 | tf_op jit(solution)/shard_map/ppermute | solution.py:24
  212.5 13.6 %collective-permute-start.1 = (bf16[512,384]{1,0:T(8,128)(2,1)S(1)}, bf16[512,384]{1,0:T(8,128)(2,1)S(1)}, u32[]{:S(2)}, u32[]{:S(2)}) collective-permute-start(bf16[512,384]{1,0:T(8,128)(2,1)S(1)} %fusion.51), channel_id=1, source_target_pairs={{0,128},{64,192},{128,0},{192,64},{1,129},{65,193},{129,1},{193,65... | collective-permute-start | bytes 1179656 | tf_op jit(solution)/shard_map/ppermute | solution.py:24
  214.3 18.9 %collective-permute-start = (bf16[512,384]{1,0:T(8,128)(2,1)S(1)}, bf16[512,384]{1,0:T(8,128)(2,1)S(1)}, u32[]{:S(2)}, u32[]{:S(2)}) collective-permute-start(bf16[512,384]{1,0:T(8,128)(2,1)S(1)} %fusion.51), channel_id=1, source_target_pairs={{0,64},{64,128},{128,192},{192,0},{1,65},{65,129},{129,193},{193,1... | collective-permute-start | bytes 1179656 | tf_op jit(solution)/shard_map/ppermute | solution.py:24
  237.7 16.4 %copy-start.3 = (f32[16,4,8]{0,2,1:T(8,128)S(1)}, f32[16,4,8]{0,2,1:T(8,128)}, u32[]{:S(2)}) copy-start(f32[16,4,8]{0,2,1:T(8,128)} %param.11) | copy-start | bytes 6148
  237.7 16.8 %copy-start.10 = (s32[16]{0:T(128)S(1)}, s32[16]{0:T(128)}, u32[]{:S(2)}) copy-start(s32[16]{0:T(128)} %param.14) | copy-start | bytes 196
  243.3 39.5 %all-to-all-start.1 = ((bf16[64,4,2,1024]{3,2,1,0:T(2,128)(2,1)}), bf16[64,4,2,1024]{3,2,1,0:T(2,128)(2,1)}, u32[]{:S(2)}, u32[]{:S(2)}) async-start(bf16[64,4,2,1024]{3,2,1,0:T(2,128)(2,1)} %bitcast.82), calls=%async_computation.1 | async-start | bytes 2097152 | tf_op jit(solution)/shard_map/all_to_all | solution.py:85
Sparse Core Ops, SparseCore 0:
  95.1 46.8 all-gather.4
  143.8 60.9 all-gather.2

commit v16 on v15

--- a/solution.py
+++ b/solution.py
@@ -55,18 +55,24 @@
     member_ids = lax.broadcasted_iota(jnp.int32, (1, 1, replica_count, 1), 2)
     within_ids = lax.broadcasted_iota(jnp.int32, (1, 1, 1, sub), 3)
     combined = jnp.zeros((tokens, columns), jnp.float32)
+    outgoings = []
     for chunk in range(chunks):
         slot_ids = replica * part + chunk * sub + lax.broadcasted_iota(jnp.int32, (1, 1, sub), 2)
         placement = (hit_mask[:, :, None] == 1) & (prior_hits[:, :, None] == slot_ids)
         placement = placement.reshape(tokens, expert_count * sub)
-        outgoing = lax.dot_general(
-            placement.astype(jnp.bfloat16),
-            flat_inputs,
-            (((0,), (0,)), ((), ())),
-            preferred_element_type=jnp.float32,
-        ).astype(jnp.bfloat16)
-        if chunk == 1:
-            down_cols, outgoing = lax.optimization_barrier((down_cols, outgoing))
+        outgoings.append(
+            lax.dot_general(
+                placement.astype(jnp.bfloat16),
+                flat_inputs,
+                (((0,), (0,)), ((), ())),
+                preferred_element_type=jnp.float32,
+            ).astype(jnp.bfloat16)
+        )
+    if chunks > 1:
+        down_cols, outgoings[1] = lax.optimization_barrier((down_cols, outgoings[1]))
+    down_stack = jnp.stack(down_cols, axis=0)
+    for chunk in range(chunks):
+        outgoing = outgoings[chunk]
         arrived = lax.all_to_all(outgoing, "expert", split_axis=0, concat_axis=0, tiled=True)
         gathered = lax.all_gather(arrived, "dp", axis=0, tiled=True)
         gate_part = jnp.dot(gathered, w_gate[0], preferred_element_type=jnp.float32)
@@ -75,7 +81,7 @@
         hidden_all = exchange_all(activated, replica_count)
         expert_cols = lax.dot_general(
             hidden_all,
-            jnp.stack(down_cols, axis=0),
+            down_stack,
             (((0, 2), (0, 1)), ((), ())),
             preferred_element_type=jnp.float32,
         ).astype(jnp.bfloat16)

time: 303 us -> 303 us (level)
  no operation moved by 1% of the time
where the time goes in v16:
time: 303 us; the launch traced here: 302 us
  waiting for transfers between devices  106 us (35%)
  blocking collectives  84.3 us (28%)
  matrix products  34.7 us (11%)
  starting transfers between devices  34.2 us (11%)
  local copies, waits for them, and re-layouts  28 us (9%)
  between operations  14.3 us (5%)
    all_to_all x2, blocking collectives, body(): lax.all_to_all(outgoing, 'expert', split_axis=0, concat_axis=0, tiled=True)  75.5 us
    ppermute x6, waiting for transfers between devices, exchange_all(): pieces.append(lax.ppermute(block, 'dp', pairs))  46.3 us
    ppermute x3, waiting for transfers between devices, exchange_gather(): pieces.append(lax.ppermute(outgoing, 'dp', pairs))  27 us
    all_to_all x2, waiting for transfers between devices, body(): lax.all_to_all(by_source, 'expert', split_axis=0, concat_axis=0, tiled=True)  24.4 us
    all_to_all x2, starting transfers between devices, body(): lax.all_to_all(by_source, 'expert', split_axis=0, concat_axis=0, tiled=True)  21.5 us
    reshape x4, local copies, waits for them, and re-layouts, body(): expert_cols.reshape(replica_count, expert_count, sub, columns)  11.2 us
    all_to_all x4, local copies, waits for them, and re-layouts, body(): lax.all_to_all(outgoing, 'expert', split_axis=0, concat_axis=0, tiled=True)  9.66 us
    dot_general x2, matrix products, body(): gate_part = jnp.dot(gathered, w_gate[0], preferred_element_type=jnp.float32)  9.32 us
  transfers between devices with their start and end apart: 13, of which 11 were waited for; matrix products, arithmetic and copies ran while one was open for 15% of the time, Pallas kernels for 0%

profile of v16, /device:TPU:2, one launch (start us, length us, event | category | flops | bytes accessed | tf_op | source)
XLA Modules:
  0.0 302.5 jit_solution(11170726233700323488)
XLA Ops:
  6.5 3.7 %dynamic-slice_bitcast_fusion = (bf16[384,1024]{1,0:T(8,128)(2,1)}, bf16[384,1024]{1,0:T(8,128)(2,1)}, bf16[384,1024]{1,0:T(8,128)(2,1)}, bf16[384,1024]{1,0:T(8,128)(2,1)}) fusion(bf16[1,384,4096]{2,1,0:T(8,128)(2,1)} %param.17, s32[]{:T(128)S(6)} %select_n.63, s32[]{:T(128)S(6)} %select_n.59, s32[]{:T(128)S(6)} %select_n.57, s32[]{:T(128)S(6)} %select_n.61), kind=kLoop, calls=%fused_computation.40 | loop fusion | bytes 6291472 | tf_op jit(solution)/shard_map/dynamic_slice | solution.py:14
  10.3 1.6 collective-permute-start.3
  11.9 2.9 collective-permute-start.4
  14.8 1.3 collective-permute-start.5
  17.0 0.2 convert_reduce_fusion
  17.8 2.0 reshape.213
  19.7 2.4 convolution_convert_fusion
  22.2 9.0 %collective-permute-done.3 = bf16[384,1024]{1,0:T(8,128)(2,1)} collective-permute-done((bf16[384,1024]{1,0:T(8,128)(2,1)}, bf16[384,1024]{1,0:T(8,128)(2,1)}, u32[]{:S(2)}, u32[]{:S(2)}) %collective-permute-start.3) | collective-permute-done | bytes 786464 | tf_op jit(solution)/shard_map/ppermute | solution.py:16
  31.2 18.0 %collective-permute-done.4 = bf16[384,1024]{1,0:T(8,128)(2,1)} collective-permute-done((bf16[384,1024]{1,0:T(8,128)(2,1)}, bf16[384,1024]{1,0:T(8,128)(2,1)}, u32[]{:S(2)}, u32[]{:S(2)}) %collective-permute-start.4) | collective-permute-done | bytes 786464 | tf_op jit(solution)/shard_map/ppermute | solution.py:16
  49.2 2.5 all_to_all.29
  51.7 40.9 %all_to_all.39 = bf16[64,2,4096]{2,1,0:T(2,128)(2,1)} all-to-all(bf16[64,2,4096]{2,1,0:T(2,128)(2,1)} %all_to_all.29), channel_id=1, replica_groups=mesh['dp'=4,'expert'=64] {'expert'}, dimensions={0} | all-to-all | bytes 2097152 | tf_op jit(solution)/shard_map/all_to_all | solution.py:76
  92.7 2.3 all_to_all.31
  95.1 2.4 convolution_convert_fusion.1
  97.5 2.5 all_to_all.25
  100.1 34.6 %all_to_all.40 = bf16[64,2,4096]{2,1,0:T(2,128)(2,1)} all-to-all(bf16[64,2,4096]{2,1,0:T(2,128)(2,1)} %all_to_all.25), channel_id=1, replica_groups=mesh['dp'=4,'expert'=64] {'expert'}, dimensions={0} | all-to-all | bytes 2097152 | tf_op jit(solution)/shard_map/all_to_all | solution.py:76
  134.6 2.3 all_to_all.27
  136.9 5.0 %all-gather.5.cloned.1.call-done = bf16[512,4096]{1,0:T(8,128)(2,1)} async-done(((bf16[128,4096]{1,0:T(8,128)(2,1)}), bf16[512,4096]{1,0:T(8,128)(2,1)}) %all-gather.5.cloned.1.call-update) | async-done | bytes 4194320 | tf_op jit(solution)/shard_map/all_gather | solution.py:77
  142.0 4.7 %fusion.4 = f32[512,384]{1,0:T(8,128)S(1)} fusion(bf16[512,4096]{1,0:T(8,128)(2,1)} %all-gather.5.cloned.1.call-done, bf16[1,4096,384]{2,1,0:T(8,128)(2,1)S(1)} %copy-done), kind=kOutput, calls=%fused_computation.8 | convolution fusion | flops 1610612736 | bytes 8126464 | tf_op jit(solution)/shard_map/dot_general | solution.py:78
  146.7 2.3 fusion.28
  149.0 1.2 collective-permute-start.8
  150.2 1.8 collective-permute-start.7
  152.0 0.6 collective-permute-start.6
  152.6 9.2 %collective-permute-done.8 = bf16[512,384]{1,0:T(8,128)(2,1)S(1)} collective-permute-done((bf16[512,384]{1,0:T(8,128)(2,1)S(1)}, bf16[512,384]{1,0:T(8,128)(2,1)S(1)}, u32[]{:S(2)}, u32[]{:S(2)}) %collective-permute-start.8) | collective-permute-done | bytes 393248 | tf_op jit(solution)/shard_map/ppermute | solution.py:24
  161.8 4.5 %collective-permute-done.7 = bf16[512,384]{1,0:T(8,128)(2,1)S(1)} collective-permute-done((bf16[512,384]{1,0:T(8,128)(2,1)S(1)}, bf16[512,384]{1,0:T(8,128)(2,1)S(1)}, u32[]{:S(2)}, u32[]{:S(2)}) %collective-permute-start.7) | collective-permute-done | bytes 393248 | tf_op jit(solution)/shard_map/ppermute | solution.py:24
  166.3 14.4 %collective-permute-done.6 = bf16[512,384]{1,0:T(8,128)(2,1)S(1)} collective-permute-done((bf16[512,384]{1,0:T(8,128)(2,1)S(1)}, bf16[512,384]{1,0:T(8,128)(2,1)S(1)}, u32[]{:S(2)}, u32[]{:S(2)}) %collective-permute-start.6) | collective-permute-done | bytes 393248 | tf_op jit(solution)/shard_map/ppermute | solution.py:24
  180.7 4.5 %bitcast_convert_fusion = bf16[512,1024]{1,0:T(8,128)(2,1)} fusion(bf16[1,512,384]{2,1,0:T(8,128)(2,1)S(1)} %bitcast.91, bf16[1,512,384]{2,1,0:T(8,128)(2,1)S(1)} %bitcast.93, bf16[1,512,384]{2,1,0:T(8,128)(2,1)S(1)} %bitcast.94, bf16[1,512,384]{2,1,0:T(8,128)(2,1)S(1)} %bitcast.88, bf16[1,384,1024]{2,1,0:T(8,128)(2,1)} %bitcast.16, ...), kind=kOutput, calls=%fused_computation.12 | convolution fusion | flops 1618214912 | bytes 5767168 | tf_op jit(solution)/shard_map/dot_general | solution.py:82
  185.2 2.2 reshape.215
  187.5 3.4 %copy.47 = bf16[4,64,2,1024]{3,2,0,1:T(2,128)(2,1)} copy(bf16[4,64,2,1024]{3,2,1,0:T(2,128)(2,1)} %reshape.215) | data formatting | bytes 2097152 | tf_op jit(solution)/shard_map/reshape | solution.py:88
  190.8 10.7 %all-to-all-start.3 = ((bf16[64,4,2,1024]{3,2,1,0:T(2,128)(2,1)}), bf16[64,4,2,1024]{3,2,1,0:T(2,128)(2,1)}, u32[]{:S(2)}, u32[]{:S(2)}) async-start(bf16[64,4,2,1024]{3,2,1,0:T(2,128)(2,1)} %bitcast.79), calls=%async_computation.3 | async-start | bytes 2097152 | tf_op jit(solution)/shard_map/all_to_all | solution.py:91
  201.6 3.2 %all-gather.3.cloned.1.call-done = bf16[512,4096]{1,0:T(8,128)(2,1)} async-done(((bf16[128,4096]{1,0:T(8,128)(2,1)}), bf16[512,4096]{1,0:T(8,128)(2,1)}) %all-gather.3.cloned.1.call-update) | async-done | bytes 4194320 | tf_op jit(solution)/shard_map/all_gather | solution.py:77
  204.8 4.7 %fusion.6 = f32[512,384]{1,0:T(8,128)S(1)} fusion(bf16[512,4096]{1,0:T(8,128)(2,1)} %all-gather.3.cloned.1.call-done, bf16[1,4096,384]{2,1,0:T(8,128)(2,1)S(1)} %copy-done), kind=kOutput, calls=%fused_computation.10 | convolution fusion | flops 1610612736 | bytes 8126464 | tf_op jit(solution)/shard_map/dot_general | solution.py:78
  209.5 2.3 fusion.31
  211.8 0.7 collective-permute-start.2
  212.5 1.8 collective-permute-start.1
  214.3 0.8 collective-permute-start
  215.1 8.8 %collective-permute-done.2 = bf16[512,384]{1,0:T(8,128)(2,1)S(1)} collective-permute-done((bf16[512,384]{1,0:T(8,128)(2,1)S(1)}, bf16[512,384]{1,0:T(8,128)(2,1)S(1)}, u32[]{:S(2)}, u32[]{:S(2)}) %collective-permute-start.2) | collective-permute-done | bytes 393248 | tf_op jit(solution)/shard_map/ppermute | solution.py:24
  223.9 2.2 collective-permute-done.1
  226.1 7.2 %collective-permute-done = bf16[512,384]{1,0:T(8,128)(2,1)S(1)} collective-permute-done((bf16[512,384]{1,0:T(8,128)(2,1)S(1)}, bf16[512,384]{1,0:T(8,128)(2,1)S(1)}, u32[]{:S(2)}, u32[]{:S(2)}) %collective-permute-start) | collective-permute-done | bytes 393248 | tf_op jit(solution)/shard_map/ppermute | solution.py:24
  233.3 4.4 %bitcast_convert_fusion.1 = bf16[512,1024]{1,0:T(8,128)(2,1)} fusion(bf16[1,512,384]{2,1,0:T(8,128)(2,1)S(1)} %bitcast.89, bf16[1,512,384]{2,1,0:T(8,128)(2,1)S(1)} %bitcast.90, bf16[1,512,384]{2,1,0:T(8,128)(2,1)S(1)} %bitcast.92, bf16[1,512,384]{2,1,0:T(8,128)(2,1)S(1)} %bitcast.87, bf16[1,384,1024]{2,1,0:T(8,128)(2,1)} %bitcast.16, ...), kind=kOutput, calls=%fused_computation.13 | convolution fusion | flops 1618214912 | bytes 5767168 | tf_op jit(solution)/shard_map/dot_general | solution.py:82
  237.7 2.3 reshape.214
  239.9 3.4 %copy.48 = bf16[4,64,2,1024]{3,2,0,1:T(2,128)(2,1)} copy(bf16[4,64,2,1024]{3,2,1,0:T(2,128)(2,1)} %reshape.214) | data formatting | bytes 2097152 | tf_op jit(solution)/shard_map/reshape | solution.py:88
  243.3 10.7 %all-to-all-start.1 = ((bf16[64,4,2,1024]{3,2,1,0:T(2,128)(2,1)}), bf16[64,4,2,1024]{3,2,1,0:T(2,128)(2,1)}, u32[]{:S(2)}, u32[]{:S(2)}) async-start(bf16[64,4,2,1024]{3,2,1,0:T(2,128)(2,1)} %bitcast.80), calls=%async_computation.1 | async-start | bytes 2097152 | tf_op jit(solution)/shard_map/all_to_all | solution.py:91
  254.2 0.3 select_reduce_fusion
  254.7 3.7 %convolution_bitcast_fusion = f32[64,1024]{1,0:T(8,128)} fusion(bf16[64,4,2,1024]{3,2,1,0:T(2,128)(2,1)} %all-to-all-done.3, s32[4,2]{1,0:T(4,128)S(1)} %iota_add_fusion, f32[64,64]{1,0:T(8,128)S(1)} %select_reduce_fusion, s32[64,64]{1,0:T(8,128)S(1)} %sub.20, pred[64,64]{1,0:T(8,128)(4,1)S(1)} %broadcast_compare_fusion), kind=kOutput, calls=%fused_computation.32 | convolution fusion | flops 402751488 | bytes 1347616 | tf_op jit(solution)/shard_map/dot_general | solution.py:98
  258.3 24.4 %all-to-all-done.1 = bf16[64,4,2,1024]{3,2,1,0:T(2,128)(2,1)} async-done(((bf16[64,4,2,1024]{3,2,1,0:T(2,128)(2,1)}), bf16[64,4,2,1024]{3,2,1,0:T(2,128)(2,1)}, u32[]{:S(2)}, u32[]{:S(2)}) %all-to-all-start.1) | async-done | bytes 1048608 | tf_op jit(solution)/shard_map/all_to_all | solution.py:91
  282.8 3.0 %fusion.35 = bf16[64,1024]{1,0:T(8,128)(2,1)S(1)} fusion(f32[64,1024]{1,0:T(8,128)} %convolution_bitcast_fusion, bf16[64,4,2,1024]{3,2,1,0:T(2,128)(2,1)} %all-to-all-done.1, f32[64,64]{1,0:T(8,128)S(1)} %select_reduce_fusion, s32[4,2]{1,0:T(4,128)S(1)} %iota_add_fusion.1, s32[64,64]{1,0:T(8,128)S(1)} %sub.20, pred[64,64]{1,0:T(8,128)(4,1)S(1)} %broadcast_compare_fusion), kind=kOutput, calls=%fused_computation.35 | convolution fusion | flops 402882560 | bytes 1478688 | tf_op jit(solution)/shard_map/dot_general | solution.py:98
  286.1 8.8 %all_to_all.41 = bf16[4,4,4,1024]{3,2,1,0:T(4,128)(2,1)S(1)} all-to-all(bf16[4,4,4,1024]{3,2,1,0:T(4,128)(2,1)S(1)} %reshape.217), channel_id=1, replica_groups=mesh['dp'=4,'expert'=64] {'dp'}, dimensions={0} | all-to-all | bytes 262144 | tf_op jit(solution)/shard_map/all_to_all | solution.py:115
  294.9 0.7 copy.40
  (51 shorter events, 1.5 us)
Async XLA Ops:
  6.5 135.4 %copy-start = (bf16[1,4096,384]{2,1,0:T(8,128)(2,1)S(1)}, bf16[1,4096,384]{2,1,0:T(8,128)(2,1)}, u32[]{:S(2)}) copy-start(bf16[1,4096,384]{2,1,0:T(8,128)(2,1)} %param.15) | copy-start | bytes 9437188
  6.5 135.4 %all-gather.5.cloned.1.call-start = ((), (), s32[]{:S(2)}) async-start(), calls=%async_computation.6 | async-start | bytes 5242880 | tf_op jit(solution)/shard_map/all_gather | solution.py:77
  6.5 9.6 %copy-start.4 = (s32[16,4,8]{0,2,1:T(8,128)S(1)}, s32[16,4,8]{0,2,1:T(8,128)}, u32[]{:S(2)}) copy-start(s32[16,4,8]{0,2,1:T(8,128)} %param.10) | copy-start | bytes 6148
  6.5 10.3 %copy-start.5 = (s32[16]{0:T(128)S(1)}, s32[16]{0:T(128)}, u32[]{:S(2)}) copy-start(s32[16]{0:T(128)} %param.12) | copy-start | bytes 196
  10.3 20.9 %collective-permute-start.3 = (bf16[384,1024]{1,0:T(8,128)(2,1)}, bf16[384,1024]{1,0:T(8,128)(2,1)}, u32[]{:S(2)}, u32[]{:S(2)}) collective-permute-start(bf16[384,1024]{1,0:T(8,128)(2,1)} %get-tuple-element.16), channel_id=1, source_target_pairs={{0,64},{64,128},{128,192},{192,0},{1,65},{65,129},{129,193},{193,1... | collective-permute-start | bytes 2359304 | tf_op jit(solution)/shard_map/ppermute | solution.py:16
  11.9 37.3 %collective-permute-start.4 = (bf16[384,1024]{1,0:T(8,128)(2,1)}, bf16[384,1024]{1,0:T(8,128)(2,1)}, u32[]{:S(2)}, u32[]{:S(2)}) collective-permute-start(bf16[384,1024]{1,0:T(8,128)(2,1)} %get-tuple-element.18), channel_id=1, source_target_pairs={{0,128},{64,192},{128,0},{192,64},{1,129},{65,193},{129,1},{193,65... | collective-permute-start | bytes 2359304 | tf_op jit(solution)/shard_map/ppermute | solution.py:16
  14.8 34.4 %collective-permute-start.5 = (bf16[384,1024]{1,0:T(8,128)(2,1)}, bf16[384,1024]{1,0:T(8,128)(2,1)}, u32[]{:S(2)}, u32[]{:S(2)}) collective-permute-start(bf16[384,1024]{1,0:T(8,128)(2,1)} %get-tuple-element.15), channel_id=1, source_target_pairs={{0,192},{64,0},{128,64},{192,128},{1,193},{65,1},{129,65},{193,129... | collective-permute-start | bytes 2359304 | tf_op jit(solution)/shard_map/ppermute | solution.py:16
  95.0 109.8 %all-gather.3.cloned.1.call-start = ((), (), s32[]{:S(2)}) async-start(), calls=%async_computation.5 | async-start | bytes 5242880 | tf_op jit(solution)/shard_map/all_gather | solution.py:77
  142.0 4.7 %copy-start.7 = (bf16[512,4096]{1,0:T(8,128)(2,1)S(1)}, bf16[512,4096]{1,0:T(8,128)(2,1)}, u32[]{:S(2)}) copy-start(bf16[512,4096]{1,0:T(8,128)(2,1)} %all-gather.5.cloned.1.call-done) | copy-start | bytes 12582916
  142.0 4.7 %copy-start.8 = (bf16[1,4096,384]{2,1,0:T(8,128)(2,1)S(1)}, bf16[1,4096,384]{2,1,0:T(8,128)(2,1)}, u32[]{:S(2)}) copy-start(bf16[1,4096,384]{2,1,0:T(8,128)(2,1)} %param.16) | copy-start | bytes 9437188
  146.6 34.1 %copy-start.1 = (bf16[384,1024]{1,0:T(8,128)(2,1)S(1)}, bf16[384,1024]{1,0:T(8,128)(2,1)}, u32[]{:S(2)}) copy-start(bf16[384,1024]{1,0:T(8,128)(2,1)} %get-tuple-element.10) | copy-start | bytes 2359300
  149.0 12.8 %collective-permute-start.8 = (bf16[512,384]{1,0:T(8,128)(2,1)S(1)}, bf16[512,384]{1,0:T(8,128)(2,1)S(1)}, u32[]{:S(2)}, u32[]{:S(2)}) collective-permute-start(bf16[512,384]{1,0:T(8,128)(2,1)S(1)} %fusion.28), channel_id=1, source_target_pairs={{0,192},{64,0},{128,64},{192,128},{1,193},{65,1},{129,65},{193,129... | collective-permute-start | bytes 1179656 | tf_op jit(solution)/shard_map/ppermute | solution.py:24
  150.2 16.1 %collective-permute-start.7 = (bf16[512,384]{1,0:T(8,128)(2,1)S(1)}, bf16[512,384]{1,0:T(8,128)(2,1)S(1)}, u32[]{:S(2)}, u32[]{:S(2)}) collective-permute-start(bf16[512,384]{1,0:T(8,128)(2,1)S(1)} %fusion.28), channel_id=1, source_target_pairs={{0,128},{64,192},{128,0},{192,64},{1,129},{65,193},{129,1},{193,65... | collective-permute-start | bytes 1179656 | tf_op jit(solution)/shard_map/ppermute | solution.py:24
  152.0 28.7 %collective-permute-start.6 = (bf16[512,384]{1,0:T(8,128)(2,1)S(1)}, bf16[512,384]{1,0:T(8,128)(2,1)S(1)}, u32[]{:S(2)}, u32[]{:S(2)}) collective-permute-start(bf16[512,384]{1,0:T(8,128)(2,1)S(1)} %fusion.28), channel_id=1, source_target_pairs={{0,64},{64,128},{128,192},{192,0},{1,65},{65,129},{129,193},{193,1... | collective-permute-start | bytes 1179656 | tf_op jit(solution)/shard_map/ppermute | solution.py:24
  190.8 52.5 %all-to-all-start.3 = ((bf16[64,4,2,1024]{3,2,1,0:T(2,128)(2,1)}), bf16[64,4,2,1024]{3,2,1,0:T(2,128)(2,1)}, u32[]{:S(2)}, u32[]{:S(2)}) async-start(bf16[64,4,2,1024]{3,2,1,0:T(2,128)(2,1)} %bitcast.79), calls=%async_computation.3 | async-start | bytes 2097152 | tf_op jit(solution)/shard_map/all_to_all | solution.py:91
  204.8 4.7 %copy-start.6 = (bf16[512,4096]{1,0:T(8,128)(2,1)S(1)}, bf16[512,4096]{1,0:T(8,128)(2,1)}, u32[]{:S(2)}) copy-start(bf16[512,4096]{1,0:T(8,128)(2,1)} %all-gather.3.cloned.1.call-done) | copy-start | bytes 12582916
  204.8 4.7 %copy-start.9 = (bf16[1,4096,384]{2,1,0:T(8,128)(2,1)S(1)}, bf16[1,4096,384]{2,1,0:T(8,128)(2,1)}, u32[]{:S(2)}) copy-start(bf16[1,4096,384]{2,1,0:T(8,128)(2,1)} %param.16) | copy-start | bytes 9437188
  209.5 23.8 %copy-start.2 = (bf16[384,1024]{1,0:T(8,128)(2,1)S(1)}, bf16[384,1024]{1,0:T(8,128)(2,1)}, u32[]{:S(2)}) copy-start(bf16[384,1024]{1,0:T(8,128)(2,1)} %get-tuple-element.10) | copy-start | bytes 2359300
  211.8 12.0 %collective-permute-start.2 = (bf16[512,384]{1,0:T(8,128)(2,1)S(1)}, bf16[512,384]{1,0:T(8,128)(2,1)S(1)}, u32[]{:S(2)}, u32[]{:S(2)}) collective-permute-start(bf16[512,384]{1,0:T(8,128)(2,1)S(1)} %fusion.31), channel_id=1, source_target_pairs={{0,192},{64,0},{128,64},{192,128},{1,193},{65,1},{129,65},{193,129... | collective-permute-start | bytes 1179656 | tf_op jit(solution)/shard_map/ppermute | solution.py:24
  212.5 13.6 %collective-permute-start.1 = (bf16[512,384]{1,0:T(8,128)(2,1)S(1)}, bf16[512,384]{1,0:T(8,128)(2,1)S(1)}, u32[]{:S(2)}, u32[]{:S(2)}) collective-permute-start(bf16[512,384]{1,0:T(8,128)(2,1)S(1)} %fusion.31), channel_id=1, source_target_pairs={{0,128},{64,192},{128,0},{192,64},{1,129},{65,193},{129,1},{193,65... | collective-permute-start | bytes 1179656 | tf_op jit(solution)/shard_map/ppermute | solution.py:24
  214.3 18.9 %collective-permute-start = (bf16[512,384]{1,0:T(8,128)(2,1)S(1)}, bf16[512,384]{1,0:T(8,128)(2,1)S(1)}, u32[]{:S(2)}, u32[]{:S(2)}) collective-permute-start(bf16[512,384]{1,0:T(8,128)(2,1)S(1)} %fusion.31), channel_id=1, source_target_pairs={{0,64},{64,128},{128,192},{192,0},{1,65},{65,129},{129,193},{193,1... | collective-permute-start | bytes 1179656 | tf_op jit(solution)/shard_map/ppermute | solution.py:24
  237.7 16.4 %copy-start.3 = (f32[16,4,8]{0,2,1:T(8,128)S(1)}, f32[16,4,8]{0,2,1:T(8,128)}, u32[]{:S(2)}) copy-start(f32[16,4,8]{0,2,1:T(8,128)} %param.11) | copy-start | bytes 6148
  237.7 16.8 %copy-start.10 = (s32[16]{0:T(128)S(1)}, s32[16]{0:T(128)}, u32[]{:S(2)}) copy-start(s32[16]{0:T(128)} %param.14) | copy-start | bytes 196
  243.3 39.5 %all-to-all-start.1 = ((bf16[64,4,2,1024]{3,2,1,0:T(2,128)(2,1)}), bf16[64,4,2,1024]{3,2,1,0:T(2,128)(2,1)}, u32[]{:S(2)}, u32[]{:S(2)}) async-start(bf16[64,4,2,1024]{3,2,1,0:T(2,128)(2,1)} %bitcast.80), calls=%async_computation.1 | async-start | bytes 2097152 | tf_op jit(solution)/shard_map/all_to_all | solution.py:91
Sparse Core Ops, SparseCore 0:
  95.1 46.8 all-gather.4
  143.8 60.9 all-gather.2

commit v17 on v16

--- a/solution.py
+++ b/solution.py
@@ -98,7 +98,7 @@
         combined = combined + jnp.dot(
             weighted_place,
             returned_rows.reshape(expert_count * replica_count * sub, columns).astype(jnp.float32),
-            precision=lax.Precision.HIGHEST,
+            precision=lax.Precision.HIGH,
             preferred_element_type=jnp.float32,
         )
     share_rows = row_count // replica_count

time: 303 us -> 303 us (level)
  no operation moved by 1% of the time
where the time goes in v17:
time: 303 us; the launch traced here: 302 us
  waiting for transfers between devices  106 us (35%)
  blocking collectives  84.3 us (28%)
  matrix products  34.3 us (11%)
  starting transfers between devices  34.2 us (11%)
  local copies, waits for them, and re-layouts  28 us (9%)
  between operations  14.3 us (5%)
    all_to_all x2, blocking collectives, body(): lax.all_to_all(outgoing, 'expert', split_axis=0, concat_axis=0, tiled=True)  75.5 us
    ppermute x6, waiting for transfers between devices, exchange_all(): pieces.append(lax.ppermute(block, 'dp', pairs))  46.3 us
    ppermute x3, waiting for transfers between devices, exchange_gather(): pieces.append(lax.ppermute(outgoing, 'dp', pairs))  27 us
    all_to_all x2, waiting for transfers between devices, body(): lax.all_to_all(by_source, 'expert', split_axis=0, concat_axis=0, tiled=True)  24.6 us
    all_to_all x2, starting transfers between devices, body(): lax.all_to_all(by_source, 'expert', split_axis=0, concat_axis=0, tiled=True)  21.5 us
    reshape x4, local copies, waits for them, and re-layouts, body(): expert_cols.reshape(replica_count, expert_count, sub, columns)  11.2 us
    all_to_all x4, local copies, waits for them, and re-layouts, body(): lax.all_to_all(outgoing, 'expert', split_axis=0, concat_axis=0, tiled=True)  9.66 us
    dot_general x2, matrix products, body(): gate_part = jnp.dot(gathered, w_gate[0], preferred_element_type=jnp.float32)  9.32 us
  transfers between devices with their start and end apart: 13, of which 11 were waited for; matrix products, arithmetic and copies ran while one was open for 15% of the time, Pallas kernels for 0%

profile of v17, /device:TPU:2, one launch (start us, length us, event | category | flops | bytes accessed | tf_op | source)
XLA Modules:
  0.0 302.3 jit_solution(9261390843322471953)
XLA Ops:
  6.5 3.7 %dynamic-slice_bitcast_fusion = (bf16[384,1024]{1,0:T(8,128)(2,1)}, bf16[384,1024]{1,0:T(8,128)(2,1)}, bf16[384,1024]{1,0:T(8,128)(2,1)}, bf16[384,1024]{1,0:T(8,128)(2,1)}) fusion(bf16[1,384,4096]{2,1,0:T(8,128)(2,1)} %param.17, s32[]{:T(128)S(6)} %select_n.63, s32[]{:T(128)S(6)} %select_n.59, s32[]{:T(128)S(6)} %select_n.57, s32[]{:T(128)S(6)} %select_n.61), kind=kLoop, calls=%fused_computation.40 | loop fusion | bytes 6291472 | tf_op jit(solution)/shard_map/dynamic_slice | solution.py:14
  10.3 1.6 collective-permute-start.3
  11.9 2.9 collective-permute-start.4
  14.8 1.3 collective-permute-start.5
  17.0 0.2 convert_reduce_fusion
  17.8 2.0 reshape.213
  19.7 2.4 convolution_convert_fusion
  22.2 9.0 %collective-permute-done.3 = bf16[384,1024]{1,0:T(8,128)(2,1)} collective-permute-done((bf16[384,1024]{1,0:T(8,128)(2,1)}, bf16[384,1024]{1,0:T(8,128)(2,1)}, u32[]{:S(2)}, u32[]{:S(2)}) %collective-permute-start.3) | collective-permute-done | bytes 786464 | tf_op jit(solution)/shard_map/ppermute | solution.py:16
  31.2 18.0 %collective-permute-done.4 = bf16[384,1024]{1,0:T(8,128)(2,1)} collective-permute-done((bf16[384,1024]{1,0:T(8,128)(2,1)}, bf16[384,1024]{1,0:T(8,128)(2,1)}, u32[]{:S(2)}, u32[]{:S(2)}) %collective-permute-start.4) | collective-permute-done | bytes 786464 | tf_op jit(solution)/shard_map/ppermute | solution.py:16
  49.2 2.5 all_to_all.29
  51.7 40.9 %all_to_all.39 = bf16[64,2,4096]{2,1,0:T(2,128)(2,1)} all-to-all(bf16[64,2,4096]{2,1,0:T(2,128)(2,1)} %all_to_all.29), channel_id=1, replica_groups=mesh['dp'=4,'expert'=64] {'expert'}, dimensions={0} | all-to-all | bytes 2097152 | tf_op jit(solution)/shard_map/all_to_all | solution.py:76
  92.7 2.3 all_to_all.31
  95.1 2.4 convolution_convert_fusion.1
  97.5 2.5 all_to_all.25
  100.1 34.6 %all_to_all.40 = bf16[64,2,4096]{2,1,0:T(2,128)(2,1)} all-to-all(bf16[64,2,4096]{2,1,0:T(2,128)(2,1)} %all_to_all.25), channel_id=1, replica_groups=mesh['dp'=4,'expert'=64] {'expert'}, dimensions={0} | all-to-all | bytes 2097152 | tf_op jit(solution)/shard_map/all_to_all | solution.py:76
  134.6 2.3 all_to_all.27
  136.9 5.0 %all-gather.5.cloned.1.call-done = bf16[512,4096]{1,0:T(8,128)(2,1)} async-done(((bf16[128,4096]{1,0:T(8,128)(2,1)}), bf16[512,4096]{1,0:T(8,128)(2,1)}) %all-gather.5.cloned.1.call-update) | async-done | bytes 4194320 | tf_op jit(solution)/shard_map/all_gather | solution.py:77
  142.0 4.7 %fusion.4 = f32[512,384]{1,0:T(8,128)S(1)} fusion(bf16[512,4096]{1,0:T(8,128)(2,1)} %all-gather.5.cloned.1.call-done, bf16[1,4096,384]{2,1,0:T(8,128)(2,1)S(1)} %copy-done), kind=kOutput, calls=%fused_computation.8 | convolution fusion | flops 1610612736 | bytes 8126464 | tf_op jit(solution)/shard_map/dot_general | solution.py:78
  146.7 2.3 fusion.28
  149.0 1.2 collective-permute-start.8
  150.2 1.8 collective-permute-start.7
  152.0 0.6 collective-permute-start.6
  152.6 9.2 %collective-permute-done.8 = bf16[512,384]{1,0:T(8,128)(2,1)S(1)} collective-permute-done((bf16[512,384]{1,0:T(8,128)(2,1)S(1)}, bf16[512,384]{1,0:T(8,128)(2,1)S(1)}, u32[]{:S(2)}, u32[]{:S(2)}) %collective-permute-start.8) | collective-permute-done | bytes 393248 | tf_op jit(solution)/shard_map/ppermute | solution.py:24
  161.8 4.5 %collective-permute-done.7 = bf16[512,384]{1,0:T(8,128)(2,1)S(1)} collective-permute-done((bf16[512,384]{1,0:T(8,128)(2,1)S(1)}, bf16[512,384]{1,0:T(8,128)(2,1)S(1)}, u32[]{:S(2)}, u32[]{:S(2)}) %collective-permute-start.7) | collective-permute-done | bytes 393248 | tf_op jit(solution)/shard_map/ppermute | solution.py:24
  166.3 14.4 %collective-permute-done.6 = bf16[512,384]{1,0:T(8,128)(2,1)S(1)} collective-permute-done((bf16[512,384]{1,0:T(8,128)(2,1)S(1)}, bf16[512,384]{1,0:T(8,128)(2,1)S(1)}, u32[]{:S(2)}, u32[]{:S(2)}) %collective-permute-start.6) | collective-permute-done | bytes 393248 | tf_op jit(solution)/shard_map/ppermute | solution.py:24
  180.7 4.5 %bitcast_convert_fusion = bf16[512,1024]{1,0:T(8,128)(2,1)} fusion(bf16[1,512,384]{2,1,0:T(8,128)(2,1)S(1)} %bitcast.91, bf16[1,512,384]{2,1,0:T(8,128)(2,1)S(1)} %bitcast.93, bf16[1,512,384]{2,1,0:T(8,128)(2,1)S(1)} %bitcast.94, bf16[1,512,384]{2,1,0:T(8,128)(2,1)S(1)} %bitcast.88, bf16[1,384,1024]{2,1,0:T(8,128)(2,1)} %bitcast.16, ...), kind=kOutput, calls=%fused_computation.12 | convolution fusion | flops 1618214912 | bytes 5767168 | tf_op jit(solution)/shard_map/dot_general | solution.py:82
  185.2 2.2 reshape.215
  187.5 3.4 %copy.47 = bf16[4,64,2,1024]{3,2,0,1:T(2,128)(2,1)} copy(bf16[4,64,2,1024]{3,2,1,0:T(2,128)(2,1)} %reshape.215) | data formatting | bytes 2097152 | tf_op jit(solution)/shard_map/reshape | solution.py:88
  190.8 10.7 %all-to-all-start.3 = ((bf16[64,4,2,1024]{3,2,1,0:T(2,128)(2,1)}), bf16[64,4,2,1024]{3,2,1,0:T(2,128)(2,1)}, u32[]{:S(2)}, u32[]{:S(2)}) async-start(bf16[64,4,2,1024]{3,2,1,0:T(2,128)(2,1)} %bitcast.79), calls=%async_computation.3 | async-start | bytes 2097152 | tf_op jit(solution)/shard_map/all_to_all | solution.py:91
  201.6 3.2 %all-gather.3.cloned.1.call-done = bf16[512,4096]{1,0:T(8,128)(2,1)} async-done(((bf16[128,4096]{1,0:T(8,128)(2,1)}), bf16[512,4096]{1,0:T(8,128)(2,1)}) %all-gather.3.cloned.1.call-update) | async-done | bytes 4194320 | tf_op jit(solution)/shard_map/all_gather | solution.py:77
  204.8 4.7 %fusion.6 = f32[512,384]{1,0:T(8,128)S(1)} fusion(bf16[512,4096]{1,0:T(8,128)(2,1)} %all-gather.3.cloned.1.call-done, bf16[1,4096,384]{2,1,0:T(8,128)(2,1)S(1)} %copy-done), kind=kOutput, calls=%fused_computation.10 | convolution fusion | flops 1610612736 | bytes 8126464 | tf_op jit(solution)/shard_map/dot_general | solution.py:78
  209.5 2.3 fusion.31
  211.8 0.7 collective-permute-start.2
  212.5 1.8 collective-permute-start.1
  214.3 0.8 collective-permute-start
  215.1 8.8 %collective-permute-done.2 = bf16[512,384]{1,0:T(8,128)(2,1)S(1)} collective-permute-done((bf16[512,384]{1,0:T(8,128)(2,1)S(1)}, bf16[512,384]{1,0:T(8,128)(2,1)S(1)}, u32[]{:S(2)}, u32[]{:S(2)}) %collective-permute-start.2) | collective-permute-done | bytes 393248 | tf_op jit(solution)/shard_map/ppermute | solution.py:24
  223.9 2.2 collective-permute-done.1
  226.1 7.2 %collective-permute-done = bf16[512,384]{1,0:T(8,128)(2,1)S(1)} collective-permute-done((bf16[512,384]{1,0:T(8,128)(2,1)S(1)}, bf16[512,384]{1,0:T(8,128)(2,1)S(1)}, u32[]{:S(2)}, u32[]{:S(2)}) %collective-permute-start) | collective-permute-done | bytes 393248 | tf_op jit(solution)/shard_map/ppermute | solution.py:24
  233.3 4.4 %bitcast_convert_fusion.1 = bf16[512,1024]{1,0:T(8,128)(2,1)} fusion(bf16[1,512,384]{2,1,0:T(8,128)(2,1)S(1)} %bitcast.89, bf16[1,512,384]{2,1,0:T(8,128)(2,1)S(1)} %bitcast.90, bf16[1,512,384]{2,1,0:T(8,128)(2,1)S(1)} %bitcast.92, bf16[1,512,384]{2,1,0:T(8,128)(2,1)S(1)} %bitcast.87, bf16[1,384,1024]{2,1,0:T(8,128)(2,1)} %bitcast.16, ...), kind=kOutput, calls=%fused_computation.13 | convolution fusion | flops 1618214912 | bytes 5767168 | tf_op jit(solution)/shard_map/dot_general | solution.py:82
  237.7 2.3 reshape.214
  239.9 3.4 %copy.48 = bf16[4,64,2,1024]{3,2,0,1:T(2,128)(2,1)} copy(bf16[4,64,2,1024]{3,2,1,0:T(2,128)(2,1)} %reshape.214) | data formatting | bytes 2097152 | tf_op jit(solution)/shard_map/reshape | solution.py:88
  243.3 10.7 %all-to-all-start.1 = ((bf16[64,4,2,1024]{3,2,1,0:T(2,128)(2,1)}), bf16[64,4,2,1024]{3,2,1,0:T(2,128)(2,1)}, u32[]{:S(2)}, u32[]{:S(2)}) async-start(bf16[64,4,2,1024]{3,2,1,0:T(2,128)(2,1)} %bitcast.80), calls=%async_computation.1 | async-start | bytes 2097152 | tf_op jit(solution)/shard_map/all_to_all | solution.py:91
  254.2 0.3 select_reduce_fusion
  254.7 3.5 %convolution_bitcast_fusion = f32[64,1024]{1,0:T(8,128)} fusion(bf16[64,4,2,1024]{3,2,1,0:T(2,128)(2,1)} %all-to-all-done.3, s32[4,2]{1,0:T(4,128)S(1)} %iota_add_fusion, f32[64,64]{1,0:T(8,128)S(1)} %select_reduce_fusion, s32[64,64]{1,0:T(8,128)S(1)} %sub.20, pred[64,64]{1,0:T(8,128)(4,1)S(1)} %broadcast_compare_fusion), kind=kOutput, calls=%fused_computation.32 | convolution fusion | flops 201424896 | bytes 1347616 | tf_op jit(solution)/shard_map/dot_general | solution.py:98
  258.2 24.6 %all-to-all-done.1 = bf16[64,4,2,1024]{3,2,1,0:T(2,128)(2,1)} async-done(((bf16[64,4,2,1024]{3,2,1,0:T(2,128)(2,1)}), bf16[64,4,2,1024]{3,2,1,0:T(2,128)(2,1)}, u32[]{:S(2)}, u32[]{:S(2)}) %all-to-all-start.1) | async-done | bytes 1048608 | tf_op jit(solution)/shard_map/all_to_all | solution.py:91
  282.8 2.8 fusion.35
  285.9 8.8 %all_to_all.41 = bf16[4,4,4,1024]{3,2,1,0:T(4,128)(2,1)S(1)} all-to-all(bf16[4,4,4,1024]{3,2,1,0:T(4,128)(2,1)S(1)} %reshape.217), channel_id=1, replica_groups=mesh['dp'=4,'expert'=64] {'dp'}, dimensions={0} | all-to-all | bytes 262144 | tf_op jit(solution)/shard_map/all_to_all | solution.py:115
  294.7 0.7 copy.40
  (51 shorter events, 1.5 us)
Async XLA Ops:
  6.5 135.4 %copy-start = (bf16[1,4096,384]{2,1,0:T(8,128)(2,1)S(1)}, bf16[1,4096,384]{2,1,0:T(8,128)(2,1)}, u32[]{:S(2)}) copy-start(bf16[1,4096,384]{2,1,0:T(8,128)(2,1)} %param.15) | copy-start | bytes 9437188
  6.5 135.4 %all-gather.5.cloned.1.call-start = ((), (), s32[]{:S(2)}) async-start(), calls=%async_computation.6 | async-start | bytes 5242880 | tf_op jit(solution)/shard_map/all_gather | solution.py:77
  6.5 9.6 %copy-start.4 = (s32[16,4,8]{0,2,1:T(8,128)S(1)}, s32[16,4,8]{0,2,1:T(8,128)}, u32[]{:S(2)}) copy-start(s32[16,4,8]{0,2,1:T(8,128)} %param.10) | copy-start | bytes 6148
  6.5 10.3 %copy-start.5 = (s32[16]{0:T(128)S(1)}, s32[16]{0:T(128)}, u32[]{:S(2)}) copy-start(s32[16]{0:T(128)} %param.12) | copy-start | bytes 196
  10.3 20.9 %collective-permute-start.3 = (bf16[384,1024]{1,0:T(8,128)(2,1)}, bf16[384,1024]{1,0:T(8,128)(2,1)}, u32[]{:S(2)}, u32[]{:S(2)}) collective-permute-start(bf16[384,1024]{1,0:T(8,128)(2,1)} %get-tuple-element.16), channel_id=1, source_target_pairs={{0,64},{64,128},{128,192},{192,0},{1,65},{65,129},{129,193},{193,1... | collective-permute-start | bytes 2359304 | tf_op jit(solution)/shard_map/ppermute | solution.py:16
  11.9 37.3 %collective-permute-start.4 = (bf16[384,1024]{1,0:T(8,128)(2,1)}, bf16[384,1024]{1,0:T(8,128)(2,1)}, u32[]{:S(2)}, u32[]{:S(2)}) collective-permute-start(bf16[384,1024]{1,0:T(8,128)(2,1)} %get-tuple-element.18), channel_id=1, source_target_pairs={{0,128},{64,192},{128,0},{192,64},{1,129},{65,193},{129,1},{193,65... | collective-permute-start | bytes 2359304 | tf_op jit(solution)/shard_map/ppermute | solution.py:16
  14.8 34.4 %collective-permute-start.5 = (bf16[384,1024]{1,0:T(8,128)(2,1)}, bf16[384,1024]{1,0:T(8,128)(2,1)}, u32[]{:S(2)}, u32[]{:S(2)}) collective-permute-start(bf16[384,1024]{1,0:T(8,128)(2,1)} %get-tuple-element.15), channel_id=1, source_target_pairs={{0,192},{64,0},{128,64},{192,128},{1,193},{65,1},{129,65},{193,129... | collective-permute-start | bytes 2359304 | tf_op jit(solution)/shard_map/ppermute | solution.py:16
  95.0 109.8 %all-gather.3.cloned.1.call-start = ((), (), s32[]{:S(2)}) async-start(), calls=%async_computation.5 | async-start | bytes 5242880 | tf_op jit(solution)/shard_map/all_gather | solution.py:77
  142.0 4.7 %copy-start.7 = (bf16[512,4096]{1,0:T(8,128)(2,1)S(1)}, bf16[512,4096]{1,0:T(8,128)(2,1)}, u32[]{:S(2)}) copy-start(bf16[512,4096]{1,0:T(8,128)(2,1)} %all-gather.5.cloned.1.call-done) | copy-start | bytes 12582916
  142.0 4.7 %copy-start.8 = (bf16[1,4096,384]{2,1,0:T(8,128)(2,1)S(1)}, bf16[1,4096,384]{2,1,0:T(8,128)(2,1)}, u32[]{:S(2)}) copy-start(bf16[1,4096,384]{2,1,0:T(8,128)(2,1)} %param.16) | copy-start | bytes 9437188
  146.6 34.1 %copy-start.1 = (bf16[384,1024]{1,0:T(8,128)(2,1)S(1)}, bf16[384,1024]{1,0:T(8,128)(2,1)}, u32[]{:S(2)}) copy-start(bf16[384,1024]{1,0:T(8,128)(2,1)} %get-tuple-element.10) | copy-start | bytes 2359300
  149.0 12.8 %collective-permute-start.8 = (bf16[512,384]{1,0:T(8,128)(2,1)S(1)}, bf16[512,384]{1,0:T(8,128)(2,1)S(1)}, u32[]{:S(2)}, u32[]{:S(2)}) collective-permute-start(bf16[512,384]{1,0:T(8,128)(2,1)S(1)} %fusion.28), channel_id=1, source_target_pairs={{0,192},{64,0},{128,64},{192,128},{1,193},{65,1},{129,65},{193,129... | collective-permute-start | bytes 1179656 | tf_op jit(solution)/shard_map/ppermute | solution.py:24
  150.2 16.1 %collective-permute-start.7 = (bf16[512,384]{1,0:T(8,128)(2,1)S(1)}, bf16[512,384]{1,0:T(8,128)(2,1)S(1)}, u32[]{:S(2)}, u32[]{:S(2)}) collective-permute-start(bf16[512,384]{1,0:T(8,128)(2,1)S(1)} %fusion.28), channel_id=1, source_target_pairs={{0,128},{64,192},{128,0},{192,64},{1,129},{65,193},{129,1},{193,65... | collective-permute-start | bytes 1179656 | tf_op jit(solution)/shard_map/ppermute | solution.py:24
  152.0 28.7 %collective-permute-start.6 = (bf16[512,384]{1,0:T(8,128)(2,1)S(1)}, bf16[512,384]{1,0:T(8,128)(2,1)S(1)}, u32[]{:S(2)}, u32[]{:S(2)}) collective-permute-start(bf16[512,384]{1,0:T(8,128)(2,1)S(1)} %fusion.28), channel_id=1, source_target_pairs={{0,64},{64,128},{128,192},{192,0},{1,65},{65,129},{129,193},{193,1... | collective-permute-start | bytes 1179656 | tf_op jit(solution)/shard_map/ppermute | solution.py:24
  190.8 52.5 %all-to-all-start.3 = ((bf16[64,4,2,1024]{3,2,1,0:T(2,128)(2,1)}), bf16[64,4,2,1024]{3,2,1,0:T(2,128)(2,1)}, u32[]{:S(2)}, u32[]{:S(2)}) async-start(bf16[64,4,2,1024]{3,2,1,0:T(2,128)(2,1)} %bitcast.79), calls=%async_computation.3 | async-start | bytes 2097152 | tf_op jit(solution)/shard_map/all_to_all | solution.py:91
  204.8 4.7 %copy-start.6 = (bf16[512,4096]{1,0:T(8,128)(2,1)S(1)}, bf16[512,4096]{1,0:T(8,128)(2,1)}, u32[]{:S(2)}) copy-start(bf16[512,4096]{1,0:T(8,128)(2,1)} %all-gather.3.cloned.1.call-done) | copy-start | bytes 12582916
  204.8 4.7 %copy-start.9 = (bf16[1,4096,384]{2,1,0:T(8,128)(2,1)S(1)}, bf16[1,4096,384]{2,1,0:T(8,128)(2,1)}, u32[]{:S(2)}) copy-start(bf16[1,4096,384]{2,1,0:T(8,128)(2,1)} %param.16) | copy-start | bytes 9437188
  209.5 23.8 %copy-start.2 = (bf16[384,1024]{1,0:T(8,128)(2,1)S(1)}, bf16[384,1024]{1,0:T(8,128)(2,1)}, u32[]{:S(2)}) copy-start(bf16[384,1024]{1,0:T(8,128)(2,1)} %get-tuple-element.10) | copy-start | bytes 2359300
  211.8 12.0 %collective-permute-start.2 = (bf16[512,384]{1,0:T(8,128)(2,1)S(1)}, bf16[512,384]{1,0:T(8,128)(2,1)S(1)}, u32[]{:S(2)}, u32[]{:S(2)}) collective-permute-start(bf16[512,384]{1,0:T(8,128)(2,1)S(1)} %fusion.31), channel_id=1, source_target_pairs={{0,192},{64,0},{128,64},{192,128},{1,193},{65,1},{129,65},{193,129... | collective-permute-start | bytes 1179656 | tf_op jit(solution)/shard_map/ppermute | solution.py:24
  212.5 13.6 %collective-permute-start.1 = (bf16[512,384]{1,0:T(8,128)(2,1)S(1)}, bf16[512,384]{1,0:T(8,128)(2,1)S(1)}, u32[]{:S(2)}, u32[]{:S(2)}) collective-permute-start(bf16[512,384]{1,0:T(8,128)(2,1)S(1)} %fusion.31), channel_id=1, source_target_pairs={{0,128},{64,192},{128,0},{192,64},{1,129},{65,193},{129,1},{193,65... | collective-permute-start | bytes 1179656 | tf_op jit(solution)/shard_map/ppermute | solution.py:24
  214.3 18.9 %collective-permute-start = (bf16[512,384]{1,0:T(8,128)(2,1)S(1)}, bf16[512,384]{1,0:T(8,128)(2,1)S(1)}, u32[]{:S(2)}, u32[]{:S(2)}) collective-permute-start(bf16[512,384]{1,0:T(8,128)(2,1)S(1)} %fusion.31), channel_id=1, source_target_pairs={{0,64},{64,128},{128,192},{192,0},{1,65},{65,129},{129,193},{193,1... | collective-permute-start | bytes 1179656 | tf_op jit(solution)/shard_map/ppermute | solution.py:24
  237.7 16.4 %copy-start.3 = (f32[16,4,8]{0,2,1:T(8,128)S(1)}, f32[16,4,8]{0,2,1:T(8,128)}, u32[]{:S(2)}) copy-start(f32[16,4,8]{0,2,1:T(8,128)} %param.11) | copy-start | bytes 6148
  237.7 16.8 %copy-start.10 = (s32[16]{0:T(128)S(1)}, s32[16]{0:T(128)}, u32[]{:S(2)}) copy-start(s32[16]{0:T(128)} %param.14) | copy-start | bytes 196
  243.3 39.5 %all-to-all-start.1 = ((bf16[64,4,2,1024]{3,2,1,0:T(2,128)(2,1)}), bf16[64,4,2,1024]{3,2,1,0:T(2,128)(2,1)}, u32[]{:S(2)}, u32[]{:S(2)}) async-start(bf16[64,4,2,1024]{3,2,1,0:T(2,128)(2,1)} %bitcast.80), calls=%async_computation.1 | async-start | bytes 2097152 | tf_op jit(solution)/shard_map/all_to_all | solution.py:91
Sparse Core Ops, SparseCore 0:
  95.1 46.8 all-gather.4
  143.8 60.9 all-gather.2

commit v18 on v16

--- a/solution.py
+++ b/solution.py
@@ -112,8 +112,8 @@
         preferred_element_type=jnp.float32,
     ).astype(jnp.bfloat16)
     arranged = arranged.reshape(replica_count, share_rows, step_count, columns)
-    quarters = lax.all_to_all(arranged, "dp", split_axis=0, concat_axis=0, tiled=True)
-    return quarters.transpose(1, 2, 0, 3).reshape(share_rows, step_count, model_width)
+    quarters = lax.all_to_all(arranged, "dp", split_axis=0, concat_axis=3, tiled=True)
+    return quarters.reshape(share_rows, step_count, model_width)
 
 
 def solution(mesh):

time: 303 us -> 304 us (level)
  no operation moved by 1% of the time
where the time goes in v18:
time: 304 us; the launch traced here: 303 us
  waiting for transfers between devices  106 us (35%)
  blocking collectives  84.3 us (28%)
  matrix products  34.7 us (11%)
  starting transfers between devices  34.2 us (11%)
  local copies, waits for them, and re-layouts  28.2 us (9%)
  between operations  14.3 us (5%)
    all_to_all x2, blocking collectives, body(): lax.all_to_all(outgoing, 'expert', split_axis=0, concat_axis=0, tiled=True)  75.5 us
    ppermute x6, waiting for transfers between devices, exchange_all(): pieces.append(lax.ppermute(block, 'dp', pairs))  46.3 us
    ppermute x3, waiting for transfers between devices, exchange_gather(): pieces.append(lax.ppermute(outgoing, 'dp', pairs))  27 us
    all_to_all x2, waiting for transfers between devices, body(): lax.all_to_all(by_source, 'expert', split_axis=0, concat_axis=0, tiled=True)  24.4 us
    all_to_all x2, starting transfers between devices, body(): lax.all_to_all(by_source, 'expert', split_axis=0, concat_axis=0, tiled=True)  21.5 us
    reshape x4, local copies, waits for them, and re-layouts, body(): expert_cols.reshape(replica_count, expert_count, sub, columns)  11.2 us
    all_to_all x4, local copies, waits for them, and re-layouts, body(): lax.all_to_all(outgoing, 'expert', split_axis=0, concat_axis=0, tiled=True)  9.66 us
    dot_general x2, matrix products, body(): gate_part = jnp.dot(gathered, w_gate[0], preferred_element_type=jnp.float32)  9.32 us
  transfers between devices with their start and end apart: 13, of which 11 were waited for; matrix products, arithmetic and copies ran while one was open for 15% of the time, Pallas kernels for 0%

profile of v18, /device:TPU:2, one launch (start us, length us, event | category | flops | bytes accessed | tf_op | source)
XLA Modules:
  0.0 302.6 jit_solution(8033966577052828724)
XLA Ops:
  6.5 3.7 %dynamic-slice_bitcast_fusion = (bf16[384,1024]{1,0:T(8,128)(2,1)}, bf16[384,1024]{1,0:T(8,128)(2,1)}, bf16[384,1024]{1,0:T(8,128)(2,1)}, bf16[384,1024]{1,0:T(8,128)(2,1)}) fusion(bf16[1,384,4096]{2,1,0:T(8,128)(2,1)} %param.17, s32[]{:T(128)S(6)} %select_n.63, s32[]{:T(128)S(6)} %select_n.59, s32[]{:T(128)S(6)} %select_n.57, s32[]{:T(128)S(6)} %select_n.61), kind=kLoop, calls=%fused_computation.40 | loop fusion | bytes 6291472 | tf_op jit(solution)/shard_map/dynamic_slice | solution.py:14
  10.3 1.6 collective-permute-start.3
  11.9 2.9 collective-permute-start.4
  14.8 1.3 collective-permute-start.5
  17.0 0.2 convert_reduce_fusion
  17.8 2.0 reshape.214
  19.7 2.4 convolution_convert_fusion
  22.2 9.0 %collective-permute-done.3 = bf16[384,1024]{1,0:T(8,128)(2,1)} collective-permute-done((bf16[384,1024]{1,0:T(8,128)(2,1)}, bf16[384,1024]{1,0:T(8,128)(2,1)}, u32[]{:S(2)}, u32[]{:S(2)}) %collective-permute-start.3) | collective-permute-done | bytes 786464 | tf_op jit(solution)/shard_map/ppermute | solution.py:16
  31.2 18.0 %collective-permute-done.4 = bf16[384,1024]{1,0:T(8,128)(2,1)} collective-permute-done((bf16[384,1024]{1,0:T(8,128)(2,1)}, bf16[384,1024]{1,0:T(8,128)(2,1)}, u32[]{:S(2)}, u32[]{:S(2)}) %collective-permute-start.4) | collective-permute-done | bytes 786464 | tf_op jit(solution)/shard_map/ppermute | solution.py:16
  49.2 2.5 all_to_all.37
  51.7 40.9 %all_to_all.49 = bf16[64,2,4096]{2,1,0:T(2,128)(2,1)} all-to-all(bf16[64,2,4096]{2,1,0:T(2,128)(2,1)} %all_to_all.37), channel_id=1, replica_groups=mesh['dp'=4,'expert'=64] {'expert'}, dimensions={0} | all-to-all | bytes 2097152 | tf_op jit(solution)/shard_map/all_to_all | solution.py:76
  92.7 2.3 all_to_all.39
  95.1 2.4 convolution_convert_fusion.1
  97.5 2.5 all_to_all.33
  100.1 34.6 %all_to_all.50 = bf16[64,2,4096]{2,1,0:T(2,128)(2,1)} all-to-all(bf16[64,2,4096]{2,1,0:T(2,128)(2,1)} %all_to_all.33), channel_id=1, replica_groups=mesh['dp'=4,'expert'=64] {'expert'}, dimensions={0} | all-to-all | bytes 2097152 | tf_op jit(solution)/shard_map/all_to_all | solution.py:76
  134.6 2.3 all_to_all.35
  136.9 5.0 %all-gather.5.cloned.1.call-done = bf16[512,4096]{1,0:T(8,128)(2,1)} async-done(((bf16[128,4096]{1,0:T(8,128)(2,1)}), bf16[512,4096]{1,0:T(8,128)(2,1)}) %all-gather.5.cloned.1.call-update) | async-done | bytes 4194320 | tf_op jit(solution)/shard_map/all_gather | solution.py:77
  142.0 4.7 %fusion.4 = f32[512,384]{1,0:T(8,128)S(1)} fusion(bf16[512,4096]{1,0:T(8,128)(2,1)} %all-gather.5.cloned.1.call-done, bf16[1,4096,384]{2,1,0:T(8,128)(2,1)S(1)} %copy-done), kind=kOutput, calls=%fused_computation.8 | convolution fusion | flops 1610612736 | bytes 8126464 | tf_op jit(solution)/shard_map/dot_general | solution.py:78
  146.7 2.3 fusion.28
  149.0 1.2 collective-permute-start.8
  150.2 1.8 collective-permute-start.7
  152.0 0.6 collective-permute-start.6
  152.6 9.2 %collective-permute-done.8 = bf16[512,384]{1,0:T(8,128)(2,1)S(1)} collective-permute-done((bf16[512,384]{1,0:T(8,128)(2,1)S(1)}, bf16[512,384]{1,0:T(8,128)(2,1)S(1)}, u32[]{:S(2)}, u32[]{:S(2)}) %collective-permute-start.8) | collective-permute-done | bytes 393248 | tf_op jit(solution)/shard_map/ppermute | solution.py:24
  161.8 4.5 %collective-permute-done.7 = bf16[512,384]{1,0:T(8,128)(2,1)S(1)} collective-permute-done((bf16[512,384]{1,0:T(8,128)(2,1)S(1)}, bf16[512,384]{1,0:T(8,128)(2,1)S(1)}, u32[]{:S(2)}, u32[]{:S(2)}) %collective-permute-start.7) | collective-permute-done | bytes 393248 | tf_op jit(solution)/shard_map/ppermute | solution.py:24
  166.3 14.4 %collective-permute-done.6 = bf16[512,384]{1,0:T(8,128)(2,1)S(1)} collective-permute-done((bf16[512,384]{1,0:T(8,128)(2,1)S(1)}, bf16[512,384]{1,0:T(8,128)(2,1)S(1)}, u32[]{:S(2)}, u32[]{:S(2)}) %collective-permute-start.6) | collective-permute-done | bytes 393248 | tf_op jit(solution)/shard_map/ppermute | solution.py:24
  180.7 4.5 %bitcast_convert_fusion = bf16[512,1024]{1,0:T(8,128)(2,1)} fusion(bf16[1,512,384]{2,1,0:T(8,128)(2,1)S(1)} %bitcast.91, bf16[1,512,384]{2,1,0:T(8,128)(2,1)S(1)} %bitcast.93, bf16[1,512,384]{2,1,0:T(8,128)(2,1)S(1)} %bitcast.94, bf16[1,512,384]{2,1,0:T(8,128)(2,1)S(1)} %bitcast.88, bf16[1,384,1024]{2,1,0:T(8,128)(2,1)} %bitcast.16, ...), kind=kOutput, calls=%fused_computation.12 | convolution fusion | flops 1618214912 | bytes 5767168 | tf_op jit(solution)/shard_map/dot_general | solution.py:82
  185.2 2.2 reshape.216
  187.5 3.4 %copy.46 = bf16[4,64,2,1024]{3,2,0,1:T(2,128)(2,1)} copy(bf16[4,64,2,1024]{3,2,1,0:T(2,128)(2,1)} %reshape.216) | data formatting | bytes 2097152 | tf_op jit(solution)/shard_map/reshape | solution.py:88
  190.8 10.7 %all-to-all-start.3 = ((bf16[64,4,2,1024]{3,2,1,0:T(2,128)(2,1)}), bf16[64,4,2,1024]{3,2,1,0:T(2,128)(2,1)}, u32[]{:S(2)}, u32[]{:S(2)}) async-start(bf16[64,4,2,1024]{3,2,1,0:T(2,128)(2,1)} %bitcast.79), calls=%async_computation.3 | async-start | bytes 2097152 | tf_op jit(solution)/shard_map/all_to_all | solution.py:91
  201.6 3.2 %all-gather.3.cloned.1.call-done = bf16[512,4096]{1,0:T(8,128)(2,1)} async-done(((bf16[128,4096]{1,0:T(8,128)(2,1)}), bf16[512,4096]{1,0:T(8,128)(2,1)}) %all-gather.3.cloned.1.call-update) | async-done | bytes 4194320 | tf_op jit(solution)/shard_map/all_gather | solution.py:77
  204.8 4.7 %fusion.6 = f32[512,384]{1,0:T(8,128)S(1)} fusion(bf16[512,4096]{1,0:T(8,128)(2,1)} %all-gather.3.cloned.1.call-done, bf16[1,4096,384]{2,1,0:T(8,128)(2,1)S(1)} %copy-done), kind=kOutput, calls=%fused_computation.10 | convolution fusion | flops 1610612736 | bytes 8126464 | tf_op jit(solution)/shard_map/dot_general | solution.py:78
  209.5 2.3 fusion.31
  211.8 0.7 collective-permute-start.2
  212.5 1.8 collective-permute-start.1
  214.3 0.8 collective-permute-start
  215.1 8.8 %collective-permute-done.2 = bf16[512,384]{1,0:T(8,128)(2,1)S(1)} collective-permute-done((bf16[512,384]{1,0:T(8,128)(2,1)S(1)}, bf16[512,384]{1,0:T(8,128)(2,1)S(1)}, u32[]{:S(2)}, u32[]{:S(2)}) %collective-permute-start.2) | collective-permute-done | bytes 393248 | tf_op jit(solution)/shard_map/ppermute | solution.py:24
  223.9 2.2 collective-permute-done.1
  226.1 7.2 %collective-permute-done = bf16[512,384]{1,0:T(8,128)(2,1)S(1)} collective-permute-done((bf16[512,384]{1,0:T(8,128)(2,1)S(1)}, bf16[512,384]{1,0:T(8,128)(2,1)S(1)}, u32[]{:S(2)}, u32[]{:S(2)}) %collective-permute-start) | collective-permute-done | bytes 393248 | tf_op jit(solution)/shard_map/ppermute | solution.py:24
  233.3 4.4 %bitcast_convert_fusion.1 = bf16[512,1024]{1,0:T(8,128)(2,1)} fusion(bf16[1,512,384]{2,1,0:T(8,128)(2,1)S(1)} %bitcast.89, bf16[1,512,384]{2,1,0:T(8,128)(2,1)S(1)} %bitcast.90, bf16[1,512,384]{2,1,0:T(8,128)(2,1)S(1)} %bitcast.92, bf16[1,512,384]{2,1,0:T(8,128)(2,1)S(1)} %bitcast.87, bf16[1,384,1024]{2,1,0:T(8,128)(2,1)} %bitcast.16, ...), kind=kOutput, calls=%fused_computation.13 | convolution fusion | flops 1618214912 | bytes 5767168 | tf_op jit(solution)/shard_map/dot_general | solution.py:82
  237.7 2.3 reshape.215
  239.9 3.4 %copy.47 = bf16[4,64,2,1024]{3,2,0,1:T(2,128)(2,1)} copy(bf16[4,64,2,1024]{3,2,1,0:T(2,128)(2,1)} %reshape.215) | data formatting | bytes 2097152 | tf_op jit(solution)/shard_map/reshape | solution.py:88
  243.3 10.7 %all-to-all-start.1 = ((bf16[64,4,2,1024]{3,2,1,0:T(2,128)(2,1)}), bf16[64,4,2,1024]{3,2,1,0:T(2,128)(2,1)}, u32[]{:S(2)}, u32[]{:S(2)}) async-start(bf16[64,4,2,1024]{3,2,1,0:T(2,128)(2,1)} %bitcast.80), calls=%async_computation.1 | async-start | bytes 2097152 | tf_op jit(solution)/shard_map/all_to_all | solution.py:91
  254.2 0.3 select_reduce_fusion
  254.7 3.7 %convolution_bitcast_fusion = f32[64,1024]{1,0:T(8,128)} fusion(bf16[64,4,2,1024]{3,2,1,0:T(2,128)(2,1)} %all-to-all-done.3, s32[4,2]{1,0:T(4,128)S(1)} %iota_add_fusion, f32[64,64]{1,0:T(8,128)S(1)} %select_reduce_fusion, s32[64,64]{1,0:T(8,128)S(1)} %sub.20, pred[64,64]{1,0:T(8,128)(4,1)S(1)} %broadcast_compare_fusion), kind=kOutput, calls=%fused_computation.32 | convolution fusion | flops 402751488 | bytes 1347616 | tf_op jit(solution)/shard_map/dot_general | solution.py:98
  258.3 24.4 %all-to-all-done.1 = bf16[64,4,2,1024]{3,2,1,0:T(2,128)(2,1)} async-done(((bf16[64,4,2,1024]{3,2,1,0:T(2,128)(2,1)}), bf16[64,4,2,1024]{3,2,1,0:T(2,128)(2,1)}, u32[]{:S(2)}, u32[]{:S(2)}) %all-to-all-start.1) | async-done | bytes 1048608 | tf_op jit(solution)/shard_map/all_to_all | solution.py:91
  282.8 3.0 %fusion.35 = bf16[64,1024]{1,0:T(8,128)(2,1)S(1)} fusion(f32[64,1024]{1,0:T(8,128)} %convolution_bitcast_fusion, bf16[64,4,2,1024]{3,2,1,0:T(2,128)(2,1)} %all-to-all-done.1, f32[64,64]{1,0:T(8,128)S(1)} %select_reduce_fusion, s32[4,2]{1,0:T(4,128)S(1)} %iota_add_fusion.1, s32[64,64]{1,0:T(8,128)S(1)} %sub.20, pred[64,64]{1,0:T(8,128)(4,1)S(1)} %broadcast_compare_fusion), kind=kOutput, calls=%fused_computation.35 | convolution fusion | flops 402882560 | bytes 1478688 | tf_op jit(solution)/shard_map/dot_general | solution.py:98
  286.1 8.8 %all_to_all.51 = bf16[4,4,4,1024]{3,2,1,0:T(4,128)(2,1)S(1)} all-to-all(bf16[4,4,4,1024]{3,2,1,0:T(4,128)(2,1)S(1)} %reshape.218), channel_id=1, replica_groups=mesh['dp'=4,'expert'=64] {'dp'}, dimensions={0} | all-to-all | bytes 262144 | tf_op jit(solution)/shard_map/all_to_all | solution.py:115
  295.0 0.8 reshape.219
  (52 shorter events, 1.6 us)
Async XLA Ops:
  6.5 135.4 %copy-start = (bf16[1,4096,384]{2,1,0:T(8,128)(2,1)S(1)}, bf16[1,4096,384]{2,1,0:T(8,128)(2,1)}, u32[]{:S(2)}) copy-start(bf16[1,4096,384]{2,1,0:T(8,128)(2,1)} %param.15) | copy-start | bytes 9437188
  6.5 135.4 %all-gather.5.cloned.1.call-start = ((), (), s32[]{:S(2)}) async-start(), calls=%async_computation.6 | async-start | bytes 5242880 | tf_op jit(solution)/shard_map/all_gather | solution.py:77
  6.5 9.6 %copy-start.4 = (s32[16,4,8]{0,2,1:T(8,128)S(1)}, s32[16,4,8]{0,2,1:T(8,128)}, u32[]{:S(2)}) copy-start(s32[16,4,8]{0,2,1:T(8,128)} %param.10) | copy-start | bytes 6148
  6.5 10.3 %copy-start.5 = (s32[16]{0:T(128)S(1)}, s32[16]{0:T(128)}, u32[]{:S(2)}) copy-start(s32[16]{0:T(128)} %param.12) | copy-start | bytes 196
  10.3 20.9 %collective-permute-start.3 = (bf16[384,1024]{1,0:T(8,128)(2,1)}, bf16[384,1024]{1,0:T(8,128)(2,1)}, u32[]{:S(2)}, u32[]{:S(2)}) collective-permute-start(bf16[384,1024]{1,0:T(8,128)(2,1)} %get-tuple-element.16), channel_id=1, source_target_pairs={{0,64},{64,128},{128,192},{192,0},{1,65},{65,129},{129,193},{193,1... | collective-permute-start | bytes 2359304 | tf_op jit(solution)/shard_map/ppermute | solution.py:16
  11.9 37.3 %collective-permute-start.4 = (bf16[384,1024]{1,0:T(8,128)(2,1)}, bf16[384,1024]{1,0:T(8,128)(2,1)}, u32[]{:S(2)}, u32[]{:S(2)}) collective-permute-start(bf16[384,1024]{1,0:T(8,128)(2,1)} %get-tuple-element.18), channel_id=1, source_target_pairs={{0,128},{64,192},{128,0},{192,64},{1,129},{65,193},{129,1},{193,65... | collective-permute-start | bytes 2359304 | tf_op jit(solution)/shard_map/ppermute | solution.py:16
  14.8 34.4 %collective-permute-start.5 = (bf16[384,1024]{1,0:T(8,128)(2,1)}, bf16[384,1024]{1,0:T(8,128)(2,1)}, u32[]{:S(2)}, u32[]{:S(2)}) collective-permute-start(bf16[384,1024]{1,0:T(8,128)(2,1)} %get-tuple-element.15), channel_id=1, source_target_pairs={{0,192},{64,0},{128,64},{192,128},{1,193},{65,1},{129,65},{193,129... | collective-permute-start | bytes 2359304 | tf_op jit(solution)/shard_map/ppermute | solution.py:16
  95.0 109.8 %all-gather.3.cloned.1.call-start = ((), (), s32[]{:S(2)}) async-start(), calls=%async_computation.5 | async-start | bytes 5242880 | tf_op jit(solution)/shard_map/all_gather | solution.py:77
  142.0 4.7 %copy-start.7 = (bf16[512,4096]{1,0:T(8,128)(2,1)S(1)}, bf16[512,4096]{1,0:T(8,128)(2,1)}, u32[]{:S(2)}) copy-start(bf16[512,4096]{1,0:T(8,128)(2,1)} %all-gather.5.cloned.1.call-done) | copy-start | bytes 12582916
  142.0 4.7 %copy-start.8 = (bf16[1,4096,384]{2,1,0:T(8,128)(2,1)S(1)}, bf16[1,4096,384]{2,1,0:T(8,128)(2,1)}, u32[]{:S(2)}) copy-start(bf16[1,4096,384]{2,1,0:T(8,128)(2,1)} %param.16) | copy-start | bytes 9437188
  146.6 34.1 %copy-start.1 = (bf16[384,1024]{1,0:T(8,128)(2,1)S(1)}, bf16[384,1024]{1,0:T(8,128)(2,1)}, u32[]{:S(2)}) copy-start(bf16[384,1024]{1,0:T(8,128)(2,1)} %get-tuple-element.10) | copy-start | bytes 2359300
  149.0 12.8 %collective-permute-start.8 = (bf16[512,384]{1,0:T(8,128)(2,1)S(1)}, bf16[512,384]{1,0:T(8,128)(2,1)S(1)}, u32[]{:S(2)}, u32[]{:S(2)}) collective-permute-start(bf16[512,384]{1,0:T(8,128)(2,1)S(1)} %fusion.28), channel_id=1, source_target_pairs={{0,192},{64,0},{128,64},{192,128},{1,193},{65,1},{129,65},{193,129... | collective-permute-start | bytes 1179656 | tf_op jit(solution)/shard_map/ppermute | solution.py:24
  150.2 16.1 %collective-permute-start.7 = (bf16[512,384]{1,0:T(8,128)(2,1)S(1)}, bf16[512,384]{1,0:T(8,128)(2,1)S(1)}, u32[]{:S(2)}, u32[]{:S(2)}) collective-permute-start(bf16[512,384]{1,0:T(8,128)(2,1)S(1)} %fusion.28), channel_id=1, source_target_pairs={{0,128},{64,192},{128,0},{192,64},{1,129},{65,193},{129,1},{193,65... | collective-permute-start | bytes 1179656 | tf_op jit(solution)/shard_map/ppermute | solution.py:24
  152.0 28.7 %collective-permute-start.6 = (bf16[512,384]{1,0:T(8,128)(2,1)S(1)}, bf16[512,384]{1,0:T(8,128)(2,1)S(1)}, u32[]{:S(2)}, u32[]{:S(2)}) collective-permute-start(bf16[512,384]{1,0:T(8,128)(2,1)S(1)} %fusion.28), channel_id=1, source_target_pairs={{0,64},{64,128},{128,192},{192,0},{1,65},{65,129},{129,193},{193,1... | collective-permute-start | bytes 1179656 | tf_op jit(solution)/shard_map/ppermute | solution.py:24
  190.8 52.5 %all-to-all-start.3 = ((bf16[64,4,2,1024]{3,2,1,0:T(2,128)(2,1)}), bf16[64,4,2,1024]{3,2,1,0:T(2,128)(2,1)}, u32[]{:S(2)}, u32[]{:S(2)}) async-start(bf16[64,4,2,1024]{3,2,1,0:T(2,128)(2,1)} %bitcast.79), calls=%async_computation.3 | async-start | bytes 2097152 | tf_op jit(solution)/shard_map/all_to_all | solution.py:91
  204.8 4.7 %copy-start.6 = (bf16[512,4096]{1,0:T(8,128)(2,1)S(1)}, bf16[512,4096]{1,0:T(8,128)(2,1)}, u32[]{:S(2)}) copy-start(bf16[512,4096]{1,0:T(8,128)(2,1)} %all-gather.3.cloned.1.call-done) | copy-start | bytes 12582916
  204.8 4.7 %copy-start.9 = (bf16[1,4096,384]{2,1,0:T(8,128)(2,1)S(1)}, bf16[1,4096,384]{2,1,0:T(8,128)(2,1)}, u32[]{:S(2)}) copy-start(bf16[1,4096,384]{2,1,0:T(8,128)(2,1)} %param.16) | copy-start | bytes 9437188
  209.5 23.8 %copy-start.2 = (bf16[384,1024]{1,0:T(8,128)(2,1)S(1)}, bf16[384,1024]{1,0:T(8,128)(2,1)}, u32[]{:S(2)}) copy-start(bf16[384,1024]{1,0:T(8,128)(2,1)} %get-tuple-element.10) | copy-start | bytes 2359300
  211.8 12.0 %collective-permute-start.2 = (bf16[512,384]{1,0:T(8,128)(2,1)S(1)}, bf16[512,384]{1,0:T(8,128)(2,1)S(1)}, u32[]{:S(2)}, u32[]{:S(2)}) collective-permute-start(bf16[512,384]{1,0:T(8,128)(2,1)S(1)} %fusion.31), channel_id=1, source_target_pairs={{0,192},{64,0},{128,64},{192,128},{1,193},{65,1},{129,65},{193,129... | collective-permute-start | bytes 1179656 | tf_op jit(solution)/shard_map/ppermute | solution.py:24
  212.5 13.6 %collective-permute-start.1 = (bf16[512,384]{1,0:T(8,128)(2,1)S(1)}, bf16[512,384]{1,0:T(8,128)(2,1)S(1)}, u32[]{:S(2)}, u32[]{:S(2)}) collective-permute-start(bf16[512,384]{1,0:T(8,128)(2,1)S(1)} %fusion.31), channel_id=1, source_target_pairs={{0,128},{64,192},{128,0},{192,64},{1,129},{65,193},{129,1},{193,65... | collective-permute-start | bytes 1179656 | tf_op jit(solution)/shard_map/ppermute | solution.py:24
  214.3 18.9 %collective-permute-start = (bf16[512,384]{1,0:T(8,128)(2,1)S(1)}, bf16[512,384]{1,0:T(8,128)(2,1)S(1)}, u32[]{:S(2)}, u32[]{:S(2)}) collective-permute-start(bf16[512,384]{1,0:T(8,128)(2,1)S(1)} %fusion.31), channel_id=1, source_target_pairs={{0,64},{64,128},{128,192},{192,0},{1,65},{65,129},{129,193},{193,1... | collective-permute-start | bytes 1179656 | tf_op jit(solution)/shard_map/ppermute | solution.py:24
  237.7 16.4 %copy-start.3 = (f32[16,4,8]{0,2,1:T(8,128)S(1)}, f32[16,4,8]{0,2,1:T(8,128)}, u32[]{:S(2)}) copy-start(f32[16,4,8]{0,2,1:T(8,128)} %param.11) | copy-start | bytes 6148
  237.7 16.8 %copy-start.10 = (s32[16]{0:T(128)S(1)}, s32[16]{0:T(128)}, u32[]{:S(2)}) copy-start(s32[16]{0:T(128)} %param.14) | copy-start | bytes 196
  243.3 39.5 %all-to-all-start.1 = ((bf16[64,4,2,1024]{3,2,1,0:T(2,128)(2,1)}), bf16[64,4,2,1024]{3,2,1,0:T(2,128)(2,1)}, u32[]{:S(2)}, u32[]{:S(2)}) async-start(bf16[64,4,2,1024]{3,2,1,0:T(2,128)(2,1)} %bitcast.80), calls=%async_computation.1 | async-start | bytes 2097152 | tf_op jit(solution)/shard_map/all_to_all | solution.py:91
Sparse Core Ops, SparseCore 0:
  95.1 46.8 all-gather.4
  143.8 60.9 all-gather.2
